TPU v7x, 32 devices: a whole 2x2x4 slice. The times are simulated.
32 devices in a mesh: groups: 2 (over y), tm: 4 (over x, core), width: 4 (over z).
Axes of the slice: x: 2, y: 2, z: 4, core: 2. Of those that a mesh axis runs over, the one named last changes fastest.
Arguments:
- video: bfloat16 [32, 12, 48, 256], P(('groups', 'tm'), None, 'width'), parts along dimension 0, may hold values from -6 to 6
- conv_w: bfloat16 [2, 3, 3, 256, 256], replicated, may hold values from -0.125 to 0.125
- depth_k: float32 [2, 16, 256], replicated, may hold values from -1.5 to 1.5
- proj_w: bfloat16 [2, 256, 256], replicated, may hold values from -0.375 to 0.375
Outputs:
- result: bfloat16 [32, 12, 48, 256], P(('groups', 'tm'), None, 'width'), parts along dimension 0
There are 2 independent parts, one for each index of `groups`. A program takes and returns all parts, laid end to end along the dimension named above; an argument that names none is the same for every part. Nothing has to cross between parts.
All inputs are finite; a program needn't handle non-finite values.
Results may differ from a plain program's by a relative error of at most 0.0058.
Values may be sent and summed in bfloat16 or wider, within the bound.
No kernel may reach another device: no remote copies, remote signals or barrier semaphores. Data moves between devices by JAX's collectives and lax.ppermute only.
A program may use at most 64 MiB of HBM per device.

v0:
```python
from functools import partial

import jax
import jax.numpy as jnp
from jax import lax
from jax.sharding import PartitionSpec as P

BLOCKS = 2


def with_halo(shard, sides, width):
    for axis, dim in sides:
        peers, length = (lax.axis_size(axis), shard.shape[dim])
        up = [(i, (i + 1) % peers) for i in range(peers - 1)]
        down = [(j, i) for i, j in up]
        last = lax.slice_in_dim(shard, length - width, length, axis=dim)
        leading = lax.slice_in_dim(shard, 0, width, axis=dim)
        before = lax.ppermute(last, axis, up)
        after = lax.ppermute(leading, axis, down)
        shard = jnp.concatenate([before, shard, after], axis=dim)
    return shard


def spatial(padded, weight):
    frames = padded.shape[0]
    rows = padded.shape[1] - 2
    cols = padded.shape[2] - 2
    chans = padded.shape[3]
    total = jnp.zeros((frames * rows * cols, chans), jnp.float32)
    for dy in range(3):
        for dx in range(3):
            piece = padded[:, dy : dy + rows, dx : dx + cols, :].reshape(-1, chans)
            total = total + jnp.dot(piece, weight[dy, dx], preferred_element_type=jnp.float32)
    return total.reshape(frames, rows, cols, chans)


def toeplitz_table(kernel):
    frames = kernel.shape[0]
    later = jnp.arange(frames, dtype=jnp.int32)[:, None]
    earlier = jnp.arange(frames, dtype=jnp.int32)[None, :]
    offset = (later - earlier) % frames
    return jnp.where((later >= earlier)[:, :, None], kernel[offset], jnp.zeros((), jnp.float32))


def temporal(kernel, proj, hidden):
    chans = hidden.shape[-1]
    table = toeplitz_table(kernel)
    values = hidden.astype(jnp.float32)
    total = jnp.einsum("tsc,sijc->tijc", table, values, precision=lax.Precision.HIGHEST)
    depth = total.astype(jnp.bfloat16)
    mixed = jnp.dot(depth.reshape(-1, chans), proj, preferred_element_type=jnp.float32)
    return mixed.reshape(hidden.shape).astype(jnp.bfloat16)


def add_branch(state, mixed):
    return (state.astype(jnp.float32) + mixed.astype(jnp.float32)).astype(jnp.bfloat16)


def shards(video, conv_w, depth_k, proj_w):
    state = video
    for block in range(BLOCKS):
        extended = with_halo(state, (("width", 2),), 1)
        extended = jnp.pad(extended, ((0, 0), (1, 1), (0, 0), (0, 0)))
        hidden = jax.nn.silu(spatial(extended, conv_w[block])).astype(jnp.bfloat16)
        mixer = partial(temporal, depth_k[block], proj_w[block])
        mixed = mixer(lax.all_to_all(hidden, "tm", split_axis=1, concat_axis=0, tiled=True))
        returned = lax.all_to_all(mixed, "tm", split_axis=0, concat_axis=1, tiled=True)
        state = add_branch(state, returned)
    return state


def solution(mesh):
    return jax.shard_map(
        shards,
        mesh=mesh,
        in_specs=(P(("groups", "tm"), None, "width", None), P(), P(), P()),
        out_specs=P(("groups", "tm"), None, "width", None),
        check_vma=False,
    )
```

profile of v0, /device:TPU:0, one launch (start us, length us, event | category | flops | bytes accessed | tf_op | source)
XLA Modules:
  0.0 109.8 jit_solution(14615664582587126943)
XLA Ops:
  0.8 5.0 %collective-permute-start = (bf16[4,12,1,256]{3,0,2,1:T(4,128)(2,1)S(1)}, bf16[4,12,1,256]{3,0,2,1:T(4,128)(2,1)S(1)}, u32[]{:S(2)}, u32[]{:S(2)}) collective-permute-start(bf16[4,12,1,256]{3,0,2,1:T(4,128)(2,1)S(1)} %get-tuple-element.25), channel_id=1, source_target_pairs={{0,1},{1,2},{2,3},{4,5},{5,6},{6,7},{8,9},{9,10},{10,11},{12,13},{... | collective-permute-start | bytes 73736 | tf_op jit(solution)/shard_map/ppermute | solution.py:18
  5.8 1.4 %collective-permute-start.1 = (bf16[4,12,1,256]{3,0,2,1:T(4,128)(2,1)S(1)}, bf16[4,12,1,256]{3,0,2,1:T(4,128)(2,1)S(1)}, u32[]{:S(2)}, u32[]{:S(2)}) collective-permute-start(bf16[4,12,1,256]{3,0,2,1:T(4,128)(2,1)S(1)} %get-tuple-element.26), channel_id=1, source_target_pairs={{1,0},{2,1},{3,2},{5,4},{6,5},{7,6},{9,8},{10,9},{11,10},{13,12},{... | collective-permute-start | bytes 73736 | tf_op jit(solution)/shard_map/ppermute | solution.py:19
  7.2 2.9 %slice_bitcast_fusion = (bf16[3,3,256,256]{3,2,1,0:T(8,128)(2,1)}, bf16[3,3,256,256]{3,2,1,0:T(8,128)(2,1)S(1)}) fusion(bf16[2,3,3,256,256]{4,3,2,1,0:T(8,128)(2,1)} %param.5), kind=kLoop, calls=%fused_computation.32 | loop fusion | bytes 4718592 | tf_op jit(solution)/shard_map/squeeze | solution.py:64
  12.3 0.8 reshape.146
  13.1 0.8 reshape.147
  14.4 0.8 reshape.149
  15.2 0.8 reshape.151
  16.3 0.8 reshape.154
  22.5 0.9 copy.38
  23.4 3.5 %all-to-all-start = ((bf16[4,12,12,256]{3,0,2,1:T(4,128)(2,1)}), bf16[4,12,12,256]{3,0,2,1:T(4,128)(2,1)S(1)}, u32[]{:S(2)}, u32[]{:S(2)}) async-start(bf16[4,12,12,256]{3,0,2,1:T(4,128)(2,1)} %copy.38), calls=%async_computation | async-start | bytes 589824 | tf_op jit(solution)/shard_map/all_to_all | solution.py:66
  26.9 1.0 gather_fusion
  27.9 2.5 %copy.40 = f32[16,16,256]{1,0,2:T(8,128)} copy(f32[16,16,256]{2,1,0:T(8,128)S(1)} %bitcast.149) | data formatting | bytes 524288 | tf_op jit(solution)/shard_map/gather | solution.py:42
  30.4 2.8 %all-to-all-done = bf16[4,12,12,256]{3,0,2,1:T(4,128)(2,1)S(1)} async-done(((bf16[4,12,12,256]{3,0,2,1:T(4,128)(2,1)}), bf16[4,12,12,256]{3,0,2,1:T(4,128)(2,1)S(1)}, u32[]{:S(2)}, u32[]{:S(2)}) %all-to-all-start) | async-done | bytes 294944 | tf_op jit(solution)/shard_map/all_to_all | solution.py:66
  33.4 2.9 %copy.41 = bf16[16,3,12,256]{0,2,1,3:T(8,128)(2,1)S(1)} copy(bf16[16,3,12,256]{3,0,2,1:T(8,128)(2,1)S(1)} %all_to_all.43) | data formatting | bytes 589824 | tf_op jit(solution)/shard_map/all_to_all | solution.py:66
  36.3 6.9 %convert_bitcast_fusion.1 = bf16[16,3,12,256]{0,2,1,3:T(8,128)(2,1)S(1)} fusion(bf16[16,3,12,256]{0,2,1,3:T(8,128)(2,1)S(1)} %copy.41, f32[16,16,256]{1,0,2:T(8,128)} %copy.40, pred[16,16]{1,0:T(8,128)(4,1)S(1)} %iota_compare_fusion.2), kind=kOutput, calls=%fused_computation.3 | convolution fusion | flops 28524544 | bytes 852224 | tf_op jit(solution)/shard_map/tsc,sijc->tijc/dot_general | solution.py:49
  44.1 9.8 %all_to_all.54 = bf16[16,3,12,256]{3,2,1,0:T(8,128)(2,1)S(1)} all-to-all(bf16[16,3,12,256]{3,2,1,0:T(8,128)(2,1)S(1)} %copy.43), channel_id=1, replica_groups=mesh['groups'=2,'tm'=4,'width'=4] {'tm'}, dimensions={0} | all-to-all | bytes 589824 | tf_op jit(solution)/shard_map/all_to_all | solution.py:67
  55.1 3.9 %collective-permute-start.2 = (bf16[4,12,1,256]{3,0,2,1:T(4,128)(2,1)S(1)}, bf16[4,12,1,256]{3,0,2,1:T(4,128)(2,1)S(1)}, u32[]{:S(2)}, u32[]{:S(2)}) collective-permute-start(bf16[4,12,1,256]{3,0,2,1:T(4,128)(2,1)S(1)} %get-tuple-element.21), channel_id=1, source_target_pairs={{0,1},{1,2},{2,3},{4,5},{5,6},{6,7},{8,9},{9,10},{10,11},{12,13},{... | collective-permute-start | bytes 73736 | tf_op jit(solution)/shard_map/ppermute | solution.py:18
  59.0 1.5 %collective-permute-start.3 = (bf16[4,12,1,256]{3,0,2,1:T(4,128)(2,1)S(1)}, bf16[4,12,1,256]{3,0,2,1:T(4,128)(2,1)S(1)}, u32[]{:S(2)}, u32[]{:S(2)}) collective-permute-start(bf16[4,12,1,256]{3,0,2,1:T(4,128)(2,1)S(1)} %get-tuple-element.22), channel_id=1, source_target_pairs={{1,0},{2,1},{3,2},{5,4},{6,5},{7,6},{9,8},{10,9},{11,10},{13,12},{... | collective-permute-start | bytes 73736 | tf_op jit(solution)/shard_map/ppermute | solution.py:19
  60.7 4.1 %collective-permute-done.3 = bf16[4,12,1,256]{3,0,2,1:T(4,128)(2,1)S(1)} collective-permute-done((bf16[4,12,1,256]{3,0,2,1:T(4,128)(2,1)S(1)}, bf16[4,12,1,256]{3,0,2,1:T(4,128)(2,1)S(1)}, u32[]{:S(2)}, u32[]{:S(2)}) %collective-permute-start.3) | collective-permute-done | bytes 24608 | tf_op jit(solution)/shard_map/ppermute | solution.py:19
  66.0 0.8 reshape.157
  68.6 0.8 reshape.163
  69.4 0.8 reshape.164
  75.4 0.9 copy.54
  76.3 3.5 %all-to-all-start.2 = ((bf16[4,12,12,256]{3,0,2,1:T(4,128)(2,1)}), bf16[4,12,12,256]{3,0,2,1:T(4,128)(2,1)S(1)}, u32[]{:S(2)}, u32[]{:S(2)}) async-start(bf16[4,12,12,256]{3,0,2,1:T(4,128)(2,1)} %copy.54), calls=%async_computation.2 | async-start | bytes 589824 | tf_op jit(solution)/shard_map/all_to_all | solution.py:66
  79.8 1.0 gather_fusion.1
  80.7 2.5 %copy.56 = f32[16,16,256]{1,0,2:T(8,128)} copy(f32[16,16,256]{2,1,0:T(8,128)S(1)} %bitcast.148) | data formatting | bytes 524288 | tf_op jit(solution)/shard_map/gather | solution.py:42
  83.2 2.9 %all-to-all-done.2 = bf16[4,12,12,256]{3,0,2,1:T(4,128)(2,1)S(1)} async-done(((bf16[4,12,12,256]{3,0,2,1:T(4,128)(2,1)}), bf16[4,12,12,256]{3,0,2,1:T(4,128)(2,1)S(1)}, u32[]{:S(2)}, u32[]{:S(2)}) %all-to-all-start.2) | async-done | bytes 294944 | tf_op jit(solution)/shard_map/all_to_all | solution.py:66
  86.2 0.8 all_to_all.48
  87.0 3.8 %copy.57 = bf16[16,3,12,256]{0,2,1,3:T(8,128)(2,1)S(1)} copy(bf16[16,3,12,256]{3,0,2,1:T(8,128)(2,1)} %all_to_all.48) | data formatting | bytes 589824 | tf_op jit(solution)/shard_map/all_to_all | solution.py:66
  90.8 6.9 %convert_bitcast_fusion = bf16[16,3,12,256]{0,2,1,3:T(8,128)(2,1)S(1)} fusion(bf16[16,3,12,256]{0,2,1,3:T(8,128)(2,1)S(1)} %copy.57, f32[16,16,256]{1,0,2:T(8,128)} %copy.56, pred[16,16]{1,0:T(8,128)(4,1)S(1)} %iota_compare_fusion.2), kind=kOutput, calls=%fused_computation.2 | convolution fusion | flops 28524544 | bytes 852224 | tf_op jit(solution)/shard_map/tsc,sijc->tijc/dot_general | solution.py:49
  98.6 9.8 %all_to_all.55 = bf16[16,3,12,256]{3,2,1,0:T(8,128)(2,1)S(1)} all-to-all(bf16[16,3,12,256]{3,2,1,0:T(8,128)(2,1)S(1)} %copy.59), channel_id=1, replica_groups=mesh['groups'=2,'tm'=4,'width'=4] {'tm'}, dimensions={0} | all-to-all | bytes 589824 | tf_op jit(solution)/shard_map/all_to_all | solution.py:67
  108.9 0.9 fusion.19
  (112 shorter events, 20.9 us)
Async XLA Ops:
  0.8 10.2 %collective-permute-start = (bf16[4,12,1,256]{3,0,2,1:T(4,128)(2,1)S(1)}, bf16[4,12,1,256]{3,0,2,1:T(4,128)(2,1)S(1)}, u32[]{:S(2)}, u32[]{:S(2)}) collective-permute-start(bf16[4,12,1,256]{3,0,2,1:T(4,128)(2,1)S(1)} %get-tuple-element.25), channel_id=1, source_target_pairs={{0,1},{1,2},{2,3},{4,5},{5,6},{6,7},{8,9},{9,10},{10,11},{12,13},{... | collective-permute-start | bytes 73736 | tf_op jit(solution)/shard_map/ppermute | solution.py:18
  5.7 4.3 %copy-start.14 = (f32[2,16,256]{2,1,0:T(8,128)S(1)}, f32[2,16,256]{2,1,0:T(8,128)}, u32[]{:S(2)}) copy-start(f32[2,16,256]{2,1,0:T(8,128)} %param.6) | copy-start | bytes 98308
  5.8 4.3 %copy-start = (bf16[4,12,12,256]{3,0,2,1:T(4,128)(2,1)S(1)}, bf16[4,12,12,256]{3,0,2,1:T(4,128)(2,1)}, u32[]{:S(2)}) copy-start(bf16[4,12,12,256]{3,0,2,1:T(4,128)(2,1)} %param.4) | copy-start | bytes 884740
  5.8 5.9 %collective-permute-start.1 = (bf16[4,12,1,256]{3,0,2,1:T(4,128)(2,1)S(1)}, bf16[4,12,1,256]{3,0,2,1:T(4,128)(2,1)S(1)}, u32[]{:S(2)}, u32[]{:S(2)}) collective-permute-start(bf16[4,12,1,256]{3,0,2,1:T(4,128)(2,1)S(1)} %get-tuple-element.26), channel_id=1, source_target_pairs={{1,0},{2,1},{3,2},{5,4},{6,5},{7,6},{9,8},{10,9},{11,10},{13,12},{... | collective-permute-start | bytes 73736 | tf_op jit(solution)/shard_map/ppermute | solution.py:19
  16.1 1.0 copy-start.4
  16.2 1.1 %copy-start.5 = (bf16[576,256]{1,0:T(8,128)(2,1)S(1)}, bf16[576,256]{1,0:T(8,128)(2,1)}, u32[]{:S(2)}) copy-start(bf16[576,256]{1,0:T(8,128)(2,1)} %reshape.147) | copy-start | bytes 884740
  17.6 1.0 copy-start.8
  18.6 1.0 copy-start.3
  19.5 1.0 copy-start.6
  21.0 1.0 copy-start.12
  23.4 9.8 %all-to-all-start = ((bf16[4,12,12,256]{3,0,2,1:T(4,128)(2,1)}), bf16[4,12,12,256]{3,0,2,1:T(4,128)(2,1)S(1)}, u32[]{:S(2)}, u32[]{:S(2)}) async-start(bf16[4,12,12,256]{3,0,2,1:T(4,128)(2,1)} %copy.38), calls=%async_computation | async-start | bytes 589824 | tf_op jit(solution)/shard_map/all_to_all | solution.py:66
  36.3 6.9 %copy-start.15 = (bf16[2,256,256]{2,1,0:T(8,128)(2,1)S(1)}, bf16[2,256,256]{2,1,0:T(8,128)(2,1)}, u32[]{:S(2)}) copy-start(bf16[2,256,256]{2,1,0:T(8,128)(2,1)} %param.7) | copy-start | bytes 786436
  53.9 1.0 copy-start.1
  55.1 5.6 %collective-permute-start.2 = (bf16[4,12,1,256]{3,0,2,1:T(4,128)(2,1)S(1)}, bf16[4,12,1,256]{3,0,2,1:T(4,128)(2,1)S(1)}, u32[]{:S(2)}, u32[]{:S(2)}) collective-permute-start(bf16[4,12,1,256]{3,0,2,1:T(4,128)(2,1)S(1)} %get-tuple-element.21), channel_id=1, source_target_pairs={{0,1},{1,2},{2,3},{4,5},{5,6},{6,7},{8,9},{9,10},{10,11},{12,13},{... | collective-permute-start | bytes 73736 | tf_op jit(solution)/shard_map/ppermute | solution.py:18
  59.0 5.7 %collective-permute-start.3 = (bf16[4,12,1,256]{3,0,2,1:T(4,128)(2,1)S(1)}, bf16[4,12,1,256]{3,0,2,1:T(4,128)(2,1)S(1)}, u32[]{:S(2)}, u32[]{:S(2)}) collective-permute-start(bf16[4,12,1,256]{3,0,2,1:T(4,128)(2,1)S(1)} %get-tuple-element.22), channel_id=1, source_target_pairs={{1,0},{2,1},{3,2},{5,4},{6,5},{7,6},{9,8},{10,9},{11,10},{13,12},{... | collective-permute-start | bytes 73736 | tf_op jit(solution)/shard_map/ppermute | solution.py:19
  68.6 1.6 %copy-start.2 = (bf16[3,3,256,256]{3,2,1,0:T(8,128)(2,1)S(1)}, bf16[3,3,256,256]{3,2,1,0:T(8,128)(2,1)}, u32[]{:S(2)}) copy-start(bf16[3,3,256,256]{3,2,1,0:T(8,128)(2,1)} %get-tuple-element.5) | copy-start | bytes 3538948
  69.4 1.1 copy-start.10
  70.2 1.0 copy-start.13
  71.9 1.0 copy-start.7
  72.9 1.0 copy-start.9
  73.9 1.0 copy-start.11
  76.3 9.8 %all-to-all-start.2 = ((bf16[4,12,12,256]{3,0,2,1:T(4,128)(2,1)}), bf16[4,12,12,256]{3,0,2,1:T(4,128)(2,1)S(1)}, u32[]{:S(2)}, u32[]{:S(2)}) async-start(bf16[4,12,12,256]{3,0,2,1:T(4,128)(2,1)} %copy.54), calls=%async_computation.2 | async-start | bytes 589824 | tf_op jit(solution)/shard_map/all_to_all | solution.py:66
  90.8 6.9 %copy-start.16 = (bf16[2,256,256]{2,1,0:T(8,128)(2,1)S(1)}, bf16[2,256,256]{2,1,0:T(8,128)(2,1)}, u32[]{:S(2)}) copy-start(bf16[2,256,256]{2,1,0:T(8,128)(2,1)} %param.7) | copy-start | bytes 786436
where the time goes:
time: 111 us; the launch traced here: 110 us
  local copies, waits for them, and re-layouts  38.4 us (35%)
  blocking collectives  19.6 us (18%)
  matrix products  19.4 us (17%)
  starting transfers between devices  18.7 us (17%)
  waiting for transfers between devices  10.4 us (9%)
  other arithmetic  2.54 us (2%)
    all_to_all x2, blocking collectives, shards(): lax.all_to_all(mixed, 'tm', split_axis=0, concat_axis=1, tiled=True)  19.6 us
    dot_general x2, matrix products, temporal(): jnp.einsum('tsc,sijc->tijc', table, values, precision=lax.Precision.HIGHEST)  13.7 us
    reshape x18, local copies, waits for them, and re-layouts, spatial(): piece = padded[:, dy:dy + rows, dx:dx + cols, :].reshape(-1, chans)  9.05 us
    ppermute x2, starting transfers between devices, with_halo(): before = lax.ppermute(last, axis, up)  8.9 us
    all_to_all x6, local copies, waits for them, and re-layouts, shards(): lax.all_to_all(hidden, 'tm', split_axis=1, concat_axis=0, tiled=True)  7.8 us
    gather x4, local copies, waits for them, and re-layouts, toeplitz_table(): kernel[offset]  6.91 us
    all_to_all x2, starting transfers between devices, shards(): lax.all_to_all(hidden, 'tm', split_axis=1, concat_axis=0, tiled=True)  6.9 us
    unnamed x35, local copies, waits for them, and re-layouts  6.14 us
  transfers between devices with their start and end apart: 6, of which 4 were waited for; matrix products, arithmetic and copies ran while one was open for 10% of the time, Pallas kernels for 0%

commit v1 on v0

v1 whole, which is shorter than its diff:
```python
import jax
import jax.numpy as jnp
from jax import lax
from jax.sharding import PartitionSpec as P

BLOCKS = 2


def conv3x3(x, weight):
    return lax.conv_general_dilated(
        x,
        weight,
        window_strides=(1, 1),
        padding="VALID",
        dimension_numbers=("NHWC", "HWIO", "NHWC"),
        preferred_element_type=jnp.float32,
    )


def block(x, weight, kernel, proj):
    chans = x.shape[-1]
    hidden = jax.nn.silu(conv3x3(x, weight)).astype(jnp.bfloat16)
    frames = hidden.shape[0]
    values = hidden.astype(jnp.float32)
    depth = values * kernel[0]
    for lag in range(1, frames):
        shifted = jnp.pad(values[: frames - lag], ((lag, 0), (0, 0), (0, 0), (0, 0)))
        depth = depth + shifted * kernel[lag]
    depth = depth.astype(jnp.bfloat16)
    mixed = jnp.dot(depth.reshape(-1, chans), proj, preferred_element_type=jnp.float32)
    mixed = mixed.reshape(hidden.shape).astype(jnp.bfloat16)
    inner = x[:, 1:-1, 1:-1, :]
    return (inner.astype(jnp.float32) + mixed.astype(jnp.float32)).astype(jnp.bfloat16)


def shards(video, conv_w, depth_k, proj_w):
    bands = lax.axis_size("tm")
    sides = lax.axis_size("width")
    band = lax.axis_index("tm")
    side = lax.axis_index("width")
    frames, height, cols, chans = video.shape
    rows = height // bands
    halo = BLOCKS

    padded = jnp.pad(video, ((0, 0), (halo, halo), (0, 0), (0, 0)))
    pieces = jnp.stack([padded[:, r * rows : r * rows + rows + 2 * halo] for r in range(bands)])
    gathered = lax.all_to_all(pieces, "tm", 0, 0, tiled=False)
    gathered = gathered.reshape(bands * frames, rows + 2 * halo, cols, chans)

    up = [(i, i + 1) for i in range(sides - 1)]
    down = [(i + 1, i) for i in range(sides - 1)]
    before = lax.ppermute(gathered[:, :, cols - halo :], "width", up)
    after = lax.ppermute(gathered[:, :, :halo], "width", down)
    state = jnp.concatenate([before, gathered, after], axis=2)

    for b in range(BLOCKS):
        state = block(state, conv_w[b], depth_k[b], proj_w[b])
        left = halo - 1 - b
        if left > 0:
            n_rows, n_cols = state.shape[1], state.shape[2]
            row = band * rows - left + lax.broadcasted_iota(jnp.int32, (n_rows, n_cols), 0)
            col = side * cols - left + lax.broadcasted_iota(jnp.int32, (n_rows, n_cols), 1)
            inside = (row >= 0) & (row < height) & (col >= 0) & (col < sides * cols)
            state = jnp.where(inside[None, :, :, None], state, jnp.zeros((), state.dtype))

    return lax.all_to_all(state, "tm", 0, 1, tiled=True)


def solution(mesh):
    return jax.shard_map(
        shards,
        mesh=mesh,
        in_specs=(P(("groups", "tm"), None, "width", None), P(), P(), P()),
        out_specs=P(("groups", "tm"), None, "width", None),
        check_vma=False,
    )
```

time: 111 us -> 49.6 us (0.45)
  local copies, waits for them, and re-layouts: 38.4 us -> 4.22 us
  matrix products: 19.4 us -> 7.86 us
  blocking collectives: 19.6 us -> 9.8 us
  starting transfers between devices: 18.7 us -> 9.7 us
  waiting for transfers between devices: 10.4 us -> 15.8 us
    dot_general x22 -> x2, matrix products: 19.4 us -> 4.19 us  [block(): jnp.dot(depth.reshape(-1, chans), proj, preferred_element_type=jnp.float32)]
    all_to_all x2 -> x1, blocking collectives: 19.6 us -> 9.8 us  [shards(): return lax.all_to_all(state, 'tm', 0, 1, tiled=True)]
    reshape x20 -> x1, local copies, waits for them, and re-layouts: 9.19 us -> 0.16 us  [shards(): gathered = gathered.reshape(bands * frames, rows + 2 * halo, cols, chans)]
    gather x4 -> x0, local copies, waits for them, and re-layouts: 6.91 us -> none  [toeplitz_table(): kernel[offset]]
    all_to_all x6 -> x2, local copies, waits for them, and re-layouts: 7.8 us -> 1.12 us  [the longest x1 0.87 us: shards(): return lax.all_to_all(state, 'tm', 0, 1, tiled=True)]
    ppermute x4 -> x2, starting transfers between devices: 11.8 us -> 5.47 us  [the longest x1 4.18 us: shards(): before = lax.ppermute(gathered[:, :, cols - halo:], 'width', up)]
    unnamed x35 -> x8, local copies, waits for them, and re-layouts: 6.14 us -> 0.92 us
    all_to_all x2 -> x1, waiting for transfers between devices: 5.7 us -> 10.5 us  [shards(): gathered = lax.all_to_all(pieces, 'tm', 0, 0, tiled=False)]
  transfers between devices with their start and end apart: 6 -> 3, of which waited for: 4 -> 3; matrix products, arithmetic and copies ran while one was open for 10% -> 0% of each run, Pallas kernels for 0% -> 0%
where the time goes in v1:
time: 49.6 us; the launch traced here: 49.2 us
  waiting for transfers between devices  15.8 us (32%)
  blocking collectives  9.8 us (20%)
  starting transfers between devices  9.7 us (20%)
  matrix products  7.86 us (16%)
  local copies, waits for them, and re-layouts  4.22 us (9%)
  other arithmetic  1.57 us (3%)
    all_to_all x1, waiting for transfers between devices, shards(): gathered = lax.all_to_all(pieces, 'tm', 0, 0, tiled=False)  10.5 us
    all_to_all x1, blocking collectives, shards(): return lax.all_to_all(state, 'tm', 0, 1, tiled=True)  9.8 us
    ppermute x1, waiting for transfers between devices, shards(): after = lax.ppermute(gathered[:, :, :halo], 'width', down)  4.33 us
    all_to_all x1, starting transfers between devices, shards(): gathered = lax.all_to_all(pieces, 'tm', 0, 0, tiled=False)  4.24 us
    dot_general x2, matrix products, block(): jnp.dot(depth.reshape(-1, chans), proj, preferred_element_type=jnp.float32)  4.19 us
    ppermute x1, starting transfers between devices, shards(): before = lax.ppermute(gathered[:, :, cols - halo:], 'width', up)  4.18 us
    conv_general_dilated x2, matrix products, conv3x3(): lax.conv_general_dilated(x, weight, window_strides=(1, 1), padding='VALID...  3.68 us
    another operation x1, other arithmetic, shards(): jnp.stack([padded[:, r * rows:r * rows + rows + 2 * halo] for r in range(...  1.48 us
  transfers between devices with their start and end apart: 3, of which 3 were waited for; matrix products, arithmetic and copies ran while one was open for 0% of the time, Pallas kernels for 0%

profile of v1, /device:TPU:0, one launch (start us, length us, event | category | flops | bytes accessed | tf_op | source)
XLA Modules:
  0.0 49.2 jit_solution(16001688779777614391)
XLA Ops:
  0.0 1.4 %fusion.21 = (bf16[1,4,7,12,256]{4,1,3,2,0:T(4,128)(2,1)S(1)}, bf16[1,4,7,12,256]{4,1,3,2,0:T(4,128)(2,1)S(1)}, bf16[1,4,7,12,256]{4,1,3,2,0:T(4,128)(2,1)S(1)}, bf16[1,4,7,12,256]{4,1,3,2,0:T(4,128)(2,1)S(1)}) fusion(bf16[4,12,12,256]{3,0,2,1:T(4,128)(2,1)} %param.4), kind=kLoop, calls=%fused_computation.23 | loop fusion | bytes 1327104 | tf_op jit(solution)/shard_map/stack | solution.py:46
  1.4 0.0 copy-start
  1.4 1.5 %pad_maximum_fusion = bf16[4,4,7,12,256]{4,1,3,2,0:T(4,128)(2,1)} fusion(bf16[1,4,7,12,256]{4,1,3,2,0:T(4,128)(2,1)S(1)} %get-tuple-element.8, bf16[1,4,7,12,256]{4,1,3,2,0:T(4,128)(2,1)S(1)} %get-tuple-element.9, bf16[1,4,7,12,256]{4,1,3,2,0:T(4,128)(2,1)S(1)} %get-tuple-element.10, bf16[1,4,7,12,256]{4,1,3,2,0:T(4,128)(2,1)S(1)} %get-tuple-element.7), kind=kLoop, calls=%fused_computation.16 | loop fusion | flops 1032192 | bytes 1376256 | tf_op jit(solution)/shard_map/stack | solution.py:46
  2.9 4.2 %all-to-all-start = ((bf16[4,4,7,12,256]{4,1,3,2,0:T(4,128)(2,1)}), bf16[4,4,7,12,256]{4,1,3,2,0:T(4,128)(2,1)S(1)}, u32[]{:S(2)}, u32[]{:S(2)}) async-start(bf16[4,4,7,12,256]{4,1,3,2,0:T(4,128)(2,1)} %pad_maximum_fusion), calls=%async_computation | async-start | bytes 1376256 | tf_op jit(solution)/shard_map/all_to_all | solution.py:47
  7.1 0.0 copy-done
  7.2 10.5 %all-to-all-done = bf16[4,4,7,12,256]{4,1,3,2,0:T(4,128)(2,1)S(1)} async-done(((bf16[4,4,7,12,256]{4,1,3,2,0:T(4,128)(2,1)}), bf16[4,4,7,12,256]{4,1,3,2,0:T(4,128)(2,1)S(1)}, u32[]{:S(2)}, u32[]{:S(2)}) %all-to-all-start) | async-done | bytes 688160 | tf_op jit(solution)/shard_map/all_to_all | solution.py:47
  17.7 0.3 copy.7
  17.9 0.2 reshape.150
  18.1 4.2 %collective-permute-start = (bf16[16,7,2,256]{3,0,2,1:T(8,128)(2,1)S(1)}, bf16[16,7,2,256]{3,0,2,1:T(8,128)(2,1)S(1)}, u32[]{:S(2)}, u32[]{:S(2)}) collective-permute-start(bf16[16,7,2,256]{3,0,2,1:T(8,128)(2,1)S(1)} %get-tuple-element.6), channel_id=1, source_target_pairs={{0,1},{1,2},{2,3},{4,5},{5,6},{6,7},{8,9},{9,10},{10,11},{12,13},{... | collective-permute-start | bytes 344072 | tf_op jit(solution)/shard_map/ppermute | solution.py:52
  22.3 0.1 and_and_fusion
  22.4 1.3 %collective-permute-start.1 = (bf16[16,7,2,256]{3,0,2,1:T(8,128)(2,1)S(1)}, bf16[16,7,2,256]{3,0,2,1:T(8,128)(2,1)S(1)}, u32[]{:S(2)}, u32[]{:S(2)}) collective-permute-start(bf16[16,7,2,256]{3,0,2,1:T(8,128)(2,1)S(1)} %get-tuple-element.5), channel_id=1, source_target_pairs={{1,0},{2,1},{3,2},{5,4},{6,5},{7,6},{9,8},{10,9},{11,10},{13,12},{... | collective-permute-start | bytes 344072 | tf_op jit(solution)/shard_map/ppermute | solution.py:53
  23.7 1.0 %collective-permute-done = bf16[16,7,2,256]{3,0,2,1:T(8,128)(2,1)S(1)} collective-permute-done((bf16[16,7,2,256]{3,0,2,1:T(8,128)(2,1)S(1)}, bf16[16,7,2,256]{3,0,2,1:T(8,128)(2,1)S(1)}, u32[]{:S(2)}, u32[]{:S(2)}) %collective-permute-start) | collective-permute-done | bytes 114720 | tf_op jit(solution)/shard_map/ppermute | solution.py:52
  24.7 0.1 constant_dynamic-update-slice_fusion.1
  24.7 4.3 %collective-permute-done.1 = bf16[16,7,2,256]{3,0,2,1:T(8,128)(2,1)S(1)} collective-permute-done((bf16[16,7,2,256]{3,0,2,1:T(8,128)(2,1)S(1)}, bf16[16,7,2,256]{3,0,2,1:T(8,128)(2,1)S(1)}, u32[]{:S(2)}, u32[]{:S(2)}) %collective-permute-start.1) | collective-permute-done | bytes 114720 | tf_op jit(solution)/shard_map/ppermute | solution.py:53
  29.1 2.8 %fusion.12 = f32[16,5,14,256]{3,0,2,1:T(8,128)S(1)} fusion(bf16[16,7,16,256]{3,0,2,1:T(8,128)(2,1)S(1)} %constant_dynamic-update-slice_fusion, bf16[2,3,3,256,256]{4,3,2,1,0:T(8,128)(2,1)} %param.5), kind=kOutput, calls=%fused_computation.15 | convolution fusion | flops 1322926080 | bytes 3244032 | tf_op jit(solution)/shard_map/conv_general_dilated | solution.py:10
  32.2 0.0 copy-start.2
  32.3 0.8 %copy-done.2 = bf16[2,256,256]{2,1,0:T(8,128)(2,1)S(1)} copy-done((bf16[2,256,256]{2,1,0:T(8,128)(2,1)S(1)}, bf16[2,256,256]{2,1,0:T(8,128)(2,1)}, u32[]{:S(2)}) %copy-start.2) | copy-done | bytes 262168
  33.2 0.0 copy-start.1
  33.2 2.7 %fusion.20 = bf16[16,5,14,256]{3,0,2,1:T(8,128)(2,1)S(1)} fusion(bf16[16,7,16,256]{3,0,2,1:T(8,128)(2,1)S(1)} %constant_dynamic-update-slice_fusion, pred[5,14]{1,0:T(8,128)(4,1)S(1)} %and_and_fusion, f32[1,5,14,256]{3,0,2,1:T(1,128)S(1)} %slice.381, f32[2,5,14,256]{3,0,2,1:T(2,128)S(1)} %slice.380, f32[3,5,14,256]{3,0,2,1:T(4,128)S(1)} %slice.379, ...), kind=kOutput, calls=%fused_computation.20 | convolution fusion | flops 157696000 | bytes 13552640 | tf_op jit(solution)/shard_map/dot_general | solution.py:30
  35.9 0.0 copy-done.1
  35.9 0.9 %fusion.17 = f32[16,3,12,256]{3,0,2,1:T(8,128)S(1)} fusion(bf16[16,5,14,256]{3,0,2,1:T(8,128)(2,1)S(1)} %fusion.20, bf16[2,3,3,256,256]{4,3,2,1,0:T(8,128)(2,1)S(1)} %copy-done.1), kind=kOutput, calls=%fused_computation.19 | convolution fusion | flops 680361984 | bytes 2342912 | tf_op jit(solution)/shard_map/conv_general_dilated | solution.py:10
  37.0 1.5 %fusion.3 = bf16[16,3,12,256]{3,0,2,1:T(8,128)(2,1)S(1)} fusion(bf16[16,5,14,256]{3,0,2,1:T(8,128)(2,1)S(1)} %fusion.20, f32[1,3,12,256]{3,0,2,1:T(1,128)S(1)} %slice.397, f32[2,3,12,256]{3,0,2,1:T(2,128)S(1)} %slice.396, f32[3,3,12,256]{3,0,2,1:T(4,128)S(1)} %slice.395, f32[4,3,12,256]{3,0,2,1:T(4,128)S(1)} %slice.394, f32[5,3,12,256]{3,0,2,1:T(8,128)S(1)} %slice.393, ...), kind=kOutput, calls=%fused_computation.5 | convolution fusion | flops 80953344 | bytes 7041024 | tf_op jit(solution)/shard_map/dot_general | solution.py:30
  38.5 0.1 copy.8
  38.6 9.8 %all_to_all.23 = bf16[16,3,12,256]{3,2,1,0:T(8,128)(2,1)S(1)} all-to-all(bf16[16,3,12,256]{3,2,1,0:T(8,128)(2,1)S(1)} %copy.8), channel_id=1, replica_groups=mesh['groups'=2,'tm'=4,'width'=4] {'tm'}, dimensions={0} | all-to-all | bytes 589824 | tf_op jit(solution)/shard_map/all_to_all | solution.py:66
  48.4 0.9 %copy.9 = bf16[4,4,3,12,256]{4,0,3,2,1:T(4,128)(2,1)} copy(bf16[4,4,3,12,256]{4,3,2,0,1:T(8,128)(2,1)S(1)} %bitcast.104) | data formatting | bytes 589824 | tf_op jit(solution)/shard_map/all_to_all | solution.py:66
  (23 shorter events, 0.6 us)
Async XLA Ops:
  1.4 5.8 %copy-start = (f32[2,16,256]{2,1,0:T(8,128)S(1)}, f32[2,16,256]{2,1,0:T(8,128)}, u32[]{:S(2)}) copy-start(f32[2,16,256]{2,1,0:T(8,128)} %param.6) | copy-start | bytes 98308
  2.9 14.8 %all-to-all-start = ((bf16[4,4,7,12,256]{4,1,3,2,0:T(4,128)(2,1)}), bf16[4,4,7,12,256]{4,1,3,2,0:T(4,128)(2,1)S(1)}, u32[]{:S(2)}, u32[]{:S(2)}) async-start(bf16[4,4,7,12,256]{4,1,3,2,0:T(4,128)(2,1)} %pad_maximum_fusion), calls=%async_computation | async-start | bytes 1376256 | tf_op jit(solution)/shard_map/all_to_all | solution.py:47
  18.1 6.5 %collective-permute-start = (bf16[16,7,2,256]{3,0,2,1:T(8,128)(2,1)S(1)}, bf16[16,7,2,256]{3,0,2,1:T(8,128)(2,1)S(1)}, u32[]{:S(2)}, u32[]{:S(2)}) collective-permute-start(bf16[16,7,2,256]{3,0,2,1:T(8,128)(2,1)S(1)} %get-tuple-element.6), channel_id=1, source_target_pairs={{0,1},{1,2},{2,3},{4,5},{5,6},{6,7},{8,9},{9,10},{10,11},{12,13},{... | collective-permute-start | bytes 344072 | tf_op jit(solution)/shard_map/ppermute | solution.py:52
  22.4 6.7 %collective-permute-start.1 = (bf16[16,7,2,256]{3,0,2,1:T(8,128)(2,1)S(1)}, bf16[16,7,2,256]{3,0,2,1:T(8,128)(2,1)S(1)}, u32[]{:S(2)}, u32[]{:S(2)}) collective-permute-start(bf16[16,7,2,256]{3,0,2,1:T(8,128)(2,1)S(1)} %get-tuple-element.5), channel_id=1, source_target_pairs={{1,0},{2,1},{3,2},{5,4},{6,5},{7,6},{9,8},{10,9},{11,10},{13,12},{... | collective-permute-start | bytes 344072 | tf_op jit(solution)/shard_map/ppermute | solution.py:53
  32.2 1.0 %copy-start.2 = (bf16[2,256,256]{2,1,0:T(8,128)(2,1)S(1)}, bf16[2,256,256]{2,1,0:T(8,128)(2,1)}, u32[]{:S(2)}) copy-start(bf16[2,256,256]{2,1,0:T(8,128)(2,1)} %param.7) | copy-start | bytes 786436
  33.2 2.7 %copy-start.1 = (bf16[2,3,3,256,256]{4,3,2,1,0:T(8,128)(2,1)S(1)}, bf16[2,3,3,256,256]{4,3,2,1,0:T(8,128)(2,1)}, u32[]{:S(2)}) copy-start(bf16[2,3,3,256,256]{4,3,2,1,0:T(8,128)(2,1)} %param.5) | copy-start | bytes 7077892

commit v2 on v1

--- a/solution.py
+++ b/solution.py
@@ -43,14 +43,23 @@
     halo = BLOCKS
 
     padded = jnp.pad(video, ((0, 0), (halo, halo), (0, 0), (0, 0)))
-    pieces = jnp.stack([padded[:, r * rows : r * rows + rows + 2 * halo] for r in range(bands)])
+    starts = [r * rows for r in range(bands)]
+    pieces = jnp.stack([padded[:, s : s + rows + 2 * halo] for s in starts])
     gathered = lax.all_to_all(pieces, "tm", 0, 0, tiled=False)
     gathered = gathered.reshape(bands * frames, rows + 2 * halo, cols, chans)
 
-    up = [(i, i + 1) for i in range(sides - 1)]
-    down = [(i + 1, i) for i in range(sides - 1)]
-    before = lax.ppermute(gathered[:, :, cols - halo :], "width", up)
-    after = lax.ppermute(gathered[:, :, :halo], "width", down)
+    target = lax.broadcasted_iota(jnp.int32, (1, sides, 1, 1, 1, 1), 1)
+    lead = pieces[:, :, :, :halo]
+    tail = pieces[:, :, :, cols - halo :]
+    zero = jnp.zeros((), pieces.dtype)
+    edges = jnp.where(target == side + 1, tail[:, None], jnp.where(target == side - 1, lead[:, None], zero))
+    edges = edges.reshape((bands * sides,) + edges.shape[2:])
+    edges = lax.all_to_all(edges, ("tm", "width"), 0, 0, tiled=False)
+    edges = edges.reshape((bands, sides) + edges.shape[1:])
+    before = lax.dynamic_index_in_dim(edges, jnp.maximum(side - 1, 0), axis=1, keepdims=False)
+    after = lax.dynamic_index_in_dim(edges, jnp.minimum(side + 1, sides - 1), axis=1, keepdims=False)
+    before = jnp.where(side > 0, before, zero).reshape(bands * frames, rows + 2 * halo, halo, chans)
+    after = jnp.where(side < sides - 1, after, zero).reshape(bands * frames, rows + 2 * halo, halo, chans)
     state = jnp.concatenate([before, gathered, after], axis=2)
 
     for b in range(BLOCKS):

time: 49.6 us -> 58.4 us (1.18)
  waiting for transfers between devices: 15.8 us -> 21.4 us
  other arithmetic: 1.57 us -> 3.08 us
  local copies, waits for them, and re-layouts: 4.22 us -> 5.63 us
    all_to_all x0 -> x1, waiting for transfers between devices: none -> 13.6 us  [shards(): edges = lax.all_to_all(edges, ('tm', 'width'), 0, 0, tiled=False)]
    all_to_all x0 -> x1, starting transfers between devices: none -> 5.68 us  [shards(): edges = lax.all_to_all(edges, ('tm', 'width'), 0, 0, tiled=False)]
    ppermute x2 -> x0, starting transfers between devices: 5.47 us -> none  [the longest x1 4.18 us: shards(): before = lax.ppermute(gathered[:, :, cols - halo:], 'width', up)]
    ppermute x2 -> x0, waiting for transfers between devices: 5.31 us -> none  [the longest x1 4.33 us: shards(): after = lax.ppermute(gathered[:, :, :halo], 'width', down)]
    all_to_all x1, waiting for transfers between devices: 10.5 us -> 7.8 us  [shards(): gathered = lax.all_to_all(pieces, 'tm', 0, 0, tiled=False)]
    select_n x0 -> x2, other arithmetic: none -> 1.5 us  [the longest x1 1.3 us: shards(): jnp.where(target == side + 1, tail[:, None], jnp.where(target == side - 1...]
    slice x1 -> x3, local copies, waits for them, and re-layouts: 0.02 us -> 1.22 us  [the longest x2 1.13 us: shards(): tail = pieces[:, :, :, cols - halo:]]
  transfers between devices with their start and end apart: 3 -> 2, of which waited for: 3 -> 2; matrix products, arithmetic and copies ran while one was open for 0% -> 6% of each run, Pallas kernels for 0% -> 0%
where the time goes in v2:
time: 58.4 us; the launch traced here: 57.9 us
  waiting for transfers between devices  21.4 us (37%)
  starting transfers between devices  9.92 us (17%)
  blocking collectives  9.8 us (17%)
  matrix products  7.87 us (13%)
  local copies, waits for them, and re-layouts  5.63 us (10%)
  other arithmetic  3.08 us (5%)
    all_to_all x1, waiting for transfers between devices, shards(): edges = lax.all_to_all(edges, ('tm', 'width'), 0, 0, tiled=False)  13.6 us
    all_to_all x1, blocking collectives, shards(): return lax.all_to_all(state, 'tm', 0, 1, tiled=True)  9.8 us
    all_to_all x1, waiting for transfers between devices, shards(): gathered = lax.all_to_all(pieces, 'tm', 0, 0, tiled=False)  7.8 us
    all_to_all x1, starting transfers between devices, shards(): edges = lax.all_to_all(edges, ('tm', 'width'), 0, 0, tiled=False)  5.68 us
    all_to_all x1, starting transfers between devices, shards(): gathered = lax.all_to_all(pieces, 'tm', 0, 0, tiled=False)  4.24 us
    dot_general x2, matrix products, block(): jnp.dot(depth.reshape(-1, chans), proj, preferred_element_type=jnp.float32)  4.18 us
    conv_general_dilated x2, matrix products, conv3x3(): lax.conv_general_dilated(x, weight, window_strides=(1, 1), padding='VALID...  3.68 us
    another operation x1, other arithmetic, shards(): pieces = jnp.stack([padded[:, s:s + rows + 2 * halo] for s in starts])  1.48 us
  transfers between devices with their start and end apart: 2, of which 2 were waited for; matrix products, arithmetic and copies ran while one was open for 6% of the time, Pallas kernels for 0%

profile of v2, /device:TPU:0, one launch (start us, length us, event | category | flops | bytes accessed | tf_op | source)
XLA Modules:
  0.0 57.9 jit_solution(7836990991193878556)
XLA Ops:
  0.0 1.4 %fusion.23 = (bf16[1,4,7,12,256]{4,1,3,2,0:T(4,128)(2,1)S(1)}, bf16[1,4,7,12,256]{4,1,3,2,0:T(4,128)(2,1)S(1)}, bf16[1,4,7,12,256]{4,1,3,2,0:T(4,128)(2,1)S(1)}, bf16[1,4,7,12,256]{4,1,3,2,0:T(4,128)(2,1)S(1)}) fusion(bf16[4,12,12,256]{3,0,2,1:T(4,128)(2,1)} %param.4), kind=kLoop, calls=%fused_computation.28 | loop fusion | bytes 1327104 | tf_op jit(solution)/shard_map/stack | solution.py:47
  1.4 1.5 %pad_maximum_fusion = bf16[4,4,7,12,256]{4,1,3,2,0:T(4,128)(2,1)} fusion(bf16[1,4,7,12,256]{4,1,3,2,0:T(4,128)(2,1)S(1)} %get-tuple-element.10, bf16[1,4,7,12,256]{4,1,3,2,0:T(4,128)(2,1)S(1)} %get-tuple-element.11, bf16[1,4,7,12,256]{4,1,3,2,0:T(4,128)(2,1)S(1)} %get-tuple-element.12, bf16[1,4,7,12,256]{4,1,3,2,0:T(4,128)(2,1)S(1)} %get-tuple-element.9), kind=kLoop, calls=%fused_computation.20 | loop fusion | flops 1032192 | bytes 1376256 | tf_op jit(solution)/shard_map/stack | solution.py:47
  2.8 4.2 %all-to-all-start.1 = ((bf16[4,4,7,12,256]{4,1,3,2,0:T(4,128)(2,1)}), bf16[4,4,7,12,256]{4,1,3,2,0:T(4,128)(2,1)S(1)}, u32[]{:S(2)}, u32[]{:S(2)}) async-start(bf16[4,4,7,12,256]{4,1,3,2,0:T(4,128)(2,1)} %pad_maximum_fusion), calls=%async_computation.1 | async-start | bytes 1376256 | tf_op jit(solution)/shard_map/all_to_all | solution.py:48
  7.1 0.1 broadcast_in_dim.70
  7.2 0.1 broadcast_in_dim.75
  7.3 1.0 %fusion.33 = (bf16[4,4,7,2,256]{4,1,3,2,0:T(4,128)(2,1)S(1)}, bf16[4,4,7,2,256]{4,1,3,2,0:T(4,128)(2,1)S(1)}) fusion(bf16[4,4,7,12,256]{4,1,3,2,0:T(4,128)(2,1)} %pad_maximum_fusion), kind=kLoop, calls=%fused_computation.48 | loop fusion | bytes 458752 | tf_op jit(solution)/shard_map/slice | solution.py:53
  8.3 0.0 copy-start
  8.4 0.1 copy.15
  8.4 0.1 copy.16
  8.5 1.3 %broadcast_select_fusion = bf16[16,4,7,2,256]{4,3,2,1,0:T(2,128)(2,1)} fusion(pred[16]{0:T(512)(128)(4,1)S(1)} %broadcast_in_dim.70, pred[16]{0:T(512)(128)(4,1)S(1)} %broadcast_in_dim.75, bf16[4,4,7,2,256]{4,3,2,1,0:T(2,128)(2,1)S(1)} %copy.16, bf16[4,4,7,2,256]{4,3,2,1,0:T(2,128)(2,1)S(1)} %copy.15), kind=kLoop, calls=%fused_computation.18 | loop fusion | flops 458752 | bytes 688160 | tf_op jit(solution)/shard_map/jit(_where)/select_n | solution.py:55
  9.9 7.8 %all-to-all-done.1 = bf16[4,4,7,12,256]{4,1,3,2,0:T(4,128)(2,1)S(1)} async-done(((bf16[4,4,7,12,256]{4,1,3,2,0:T(4,128)(2,1)}), bf16[4,4,7,12,256]{4,1,3,2,0:T(4,128)(2,1)S(1)}, u32[]{:S(2)}, u32[]{:S(2)}) %all-to-all-start.1) | async-done | bytes 688160 | tf_op jit(solution)/shard_map/all_to_all | solution.py:48
  17.7 5.7 %all-to-all-start = ((bf16[16,4,7,2,256]{4,3,2,1,0:T(2,128)(2,1)}), bf16[16,4,7,2,256]{4,3,2,1,0:T(2,128)(2,1)S(1)}, u32[]{:S(2)}, u32[]{:S(2)}) async-start(bf16[16,4,7,2,256]{4,3,2,1,0:T(2,128)(2,1)} %broadcast_select_fusion), calls=%async_computation | async-start | bytes 917504 | tf_op jit(solution)/shard_map/all_to_all | solution.py:57
  23.4 0.1 and_and_fusion
  23.5 0.0 copy-done
  23.5 0.3 copy.18
  23.8 0.2 reshape.181
  23.9 13.6 %all-to-all-done = bf16[16,4,7,2,256]{4,3,2,1,0:T(2,128)(2,1)S(1)} async-done(((bf16[16,4,7,2,256]{4,3,2,1,0:T(2,128)(2,1)}), bf16[16,4,7,2,256]{4,3,2,1,0:T(2,128)(2,1)S(1)}, u32[]{:S(2)}, u32[]{:S(2)}) %all-to-all-start) | async-done | bytes 458784 | tf_op jit(solution)/shard_map/all_to_all | solution.py:57
  37.5 0.2 broadcast_select_fusion.2
  37.7 0.1 constant_dynamic-update-slice_fusion
  37.8 2.8 %fusion.15 = f32[16,5,14,256]{3,0,2,1:T(8,128)S(1)} fusion(bf16[16,7,16,256]{3,0,2,1:T(8,128)(2,1)S(1)} %copy_dynamic-update-slice_fusion, bf16[2,3,3,256,256]{4,3,2,1,0:T(8,128)(2,1)} %param.5), kind=kOutput, calls=%fused_computation.17 | convolution fusion | flops 1322926080 | bytes 3244032 | tf_op jit(solution)/shard_map/conv_general_dilated | solution.py:10
  40.9 0.0 copy-start.2
  41.0 0.8 %copy-done.2 = bf16[2,256,256]{2,1,0:T(8,128)(2,1)S(1)} copy-done((bf16[2,256,256]{2,1,0:T(8,128)(2,1)S(1)}, bf16[2,256,256]{2,1,0:T(8,128)(2,1)}, u32[]{:S(2)}) %copy-start.2) | copy-done | bytes 262168
  41.9 0.0 copy-start.1
  41.9 2.7 %fusion.3 = bf16[16,5,14,256]{3,0,2,1:T(8,128)(2,1)S(1)} fusion(bf16[16,7,16,256]{3,0,2,1:T(8,128)(2,1)S(1)} %copy_dynamic-update-slice_fusion, pred[5,14]{1,0:T(8,128)(4,1)S(1)} %and_and_fusion, f32[1,5,14,256]{3,0,2,1:T(1,128)S(1)} %slice.381, f32[2,5,14,256]{3,0,2,1:T(2,128)S(1)} %slice.380, f32[3,5,14,256]{3,0,2,1:T(4,128)S(1)} %slice.379, ...), kind=kOutput, calls=%fused_computation.4 | convolution fusion | flops 157696000 | bytes 13552640 | tf_op jit(solution)/shard_map/dot_general | solution.py:30
  44.6 0.0 copy-done.1
  44.6 0.9 %fusion.20 = f32[16,3,12,256]{3,0,2,1:T(8,128)S(1)} fusion(bf16[16,5,14,256]{3,0,2,1:T(8,128)(2,1)S(1)} %fusion.3, bf16[2,3,3,256,256]{4,3,2,1,0:T(8,128)(2,1)S(1)} %copy-done.1), kind=kOutput, calls=%fused_computation.23 | convolution fusion | flops 680361984 | bytes 2342912 | tf_op jit(solution)/shard_map/conv_general_dilated | solution.py:10
  45.7 1.5 %fusion.6 = bf16[16,3,12,256]{3,0,2,1:T(8,128)(2,1)S(1)} fusion(bf16[16,5,14,256]{3,0,2,1:T(8,128)(2,1)S(1)} %fusion.3, f32[1,3,12,256]{3,0,2,1:T(1,128)S(1)} %slice.397, f32[2,3,12,256]{3,0,2,1:T(2,128)S(1)} %slice.396, f32[3,3,12,256]{3,0,2,1:T(4,128)S(1)} %slice.395, f32[4,3,12,256]{3,0,2,1:T(4,128)S(1)} %slice.394, f32[5,3,12,256]{3,0,2,1:T(8,128)S(1)} %slice.393, ...), kind=kOutput, calls=%fused_computation.8 | convolution fusion | flops 80953344 | bytes 7041024 | tf_op jit(solution)/shard_map/dot_general | solution.py:30
  47.2 0.1 copy.20
  47.3 9.8 %all_to_all.28 = bf16[16,3,12,256]{3,2,1,0:T(8,128)(2,1)S(1)} all-to-all(bf16[16,3,12,256]{3,2,1,0:T(8,128)(2,1)S(1)} %copy.20), channel_id=1, replica_groups=mesh['groups'=2,'tm'=4,'width'=4] {'tm'}, dimensions={0} | all-to-all | bytes 589824 | tf_op jit(solution)/shard_map/all_to_all | solution.py:75
  57.1 0.9 %copy.21 = bf16[4,4,3,12,256]{4,0,3,2,1:T(4,128)(2,1)} copy(bf16[4,4,3,12,256]{4,3,2,0,1:T(8,128)(2,1)S(1)} %bitcast.111) | data formatting | bytes 589824 | tf_op jit(solution)/shard_map/all_to_all | solution.py:75
  (26 shorter events, 0.6 us)
Async XLA Ops:
  2.8 14.8 %all-to-all-start.1 = ((bf16[4,4,7,12,256]{4,1,3,2,0:T(4,128)(2,1)}), bf16[4,4,7,12,256]{4,1,3,2,0:T(4,128)(2,1)S(1)}, u32[]{:S(2)}, u32[]{:S(2)}) async-start(bf16[4,4,7,12,256]{4,1,3,2,0:T(4,128)(2,1)} %pad_maximum_fusion), calls=%async_computation.1 | async-start | bytes 1376256 | tf_op jit(solution)/shard_map/all_to_all | solution.py:48
  8.3 15.1 %copy-start = (f32[2,16,256]{2,1,0:T(8,128)S(1)}, f32[2,16,256]{2,1,0:T(8,128)}, u32[]{:S(2)}) copy-start(f32[2,16,256]{2,1,0:T(8,128)} %param.6) | copy-start | bytes 98308
  17.7 19.8 %all-to-all-start = ((bf16[16,4,7,2,256]{4,3,2,1,0:T(2,128)(2,1)}), bf16[16,4,7,2,256]{4,3,2,1,0:T(2,128)(2,1)S(1)}, u32[]{:S(2)}, u32[]{:S(2)}) async-start(bf16[16,4,7,2,256]{4,3,2,1,0:T(2,128)(2,1)} %broadcast_select_fusion), calls=%async_computation | async-start | bytes 917504 | tf_op jit(solution)/shard_map/all_to_all | solution.py:57
  40.9 1.0 %copy-start.2 = (bf16[2,256,256]{2,1,0:T(8,128)(2,1)S(1)}, bf16[2,256,256]{2,1,0:T(8,128)(2,1)}, u32[]{:S(2)}) copy-start(bf16[2,256,256]{2,1,0:T(8,128)(2,1)} %param.7) | copy-start | bytes 786436
  41.9 2.7 %copy-start.1 = (bf16[2,3,3,256,256]{4,3,2,1,0:T(8,128)(2,1)S(1)}, bf16[2,3,3,256,256]{4,3,2,1,0:T(8,128)(2,1)}, u32[]{:S(2)}) copy-start(bf16[2,3,3,256,256]{4,3,2,1,0:T(8,128)(2,1)} %param.5) | copy-start | bytes 7077892

commit v3 on v1

--- a/solution.py
+++ b/solution.py
@@ -51,17 +51,21 @@
     down = [(i + 1, i) for i in range(sides - 1)]
     before = lax.ppermute(gathered[:, :, cols - halo :], "width", up)
     after = lax.ppermute(gathered[:, :, :halo], "width", down)
-    state = jnp.concatenate([before, gathered, after], axis=2)
 
-    for b in range(BLOCKS):
+    inner = block(gathered, conv_w[0], depth_k[0], proj_w[0])
+    reach = 2 * halo
+    rims = jnp.concatenate([before, gathered[:, :, :reach], gathered[:, :, cols - reach :], after], axis=2)
+    rims = block(rims, conv_w[0], depth_k[0], proj_w[0])
+    state = jnp.concatenate([rims[:, :, :halo], inner, rims[:, :, rims.shape[2] - halo :]], axis=2)
+
+    for b in range(1, BLOCKS):
+        left = halo - b
+        n_rows, n_cols = state.shape[1], state.shape[2]
+        row = band * rows - left + lax.broadcasted_iota(jnp.int32, (n_rows, n_cols), 0)
+        col = side * cols - left + lax.broadcasted_iota(jnp.int32, (n_rows, n_cols), 1)
+        inside = (row >= 0) & (row < height) & (col >= 0) & (col < sides * cols)
+        state = jnp.where(inside[None, :, :, None], state, jnp.zeros((), state.dtype))
         state = block(state, conv_w[b], depth_k[b], proj_w[b])
-        left = halo - 1 - b
-        if left > 0:
-            n_rows, n_cols = state.shape[1], state.shape[2]
-            row = band * rows - left + lax.broadcasted_iota(jnp.int32, (n_rows, n_cols), 0)
-            col = side * cols - left + lax.broadcasted_iota(jnp.int32, (n_rows, n_cols), 1)
-            inside = (row >= 0) & (row < height) & (col >= 0) & (col < sides * cols)
-            state = jnp.where(inside[None, :, :, None], state, jnp.zeros((), state.dtype))
 
     return lax.all_to_all(state, "tm", 0, 1, tiled=True)
 

time: 49.6 us -> 49.2 us (level)
  matrix products: 7.86 us -> 10.1 us
  waiting for transfers between devices: 15.8 us -> 13.8 us
  local copies, waits for them, and re-layouts: 4.22 us -> 3.47 us
    dot_general x2 -> x3, matrix products: 4.19 us -> 5.69 us  [block(): jnp.dot(depth.reshape(-1, chans), proj, preferred_element_type=jnp.float32)]
    ppermute x1, waiting for transfers between devices: 4.33 us -> 3.36 us  [shards(): after = lax.ppermute(gathered[:, :, :halo], 'width', down)]
    ppermute x1, waiting for transfers between devices: 0.98 us -> 0.01 us  [shards(): before = lax.ppermute(gathered[:, :, cols - halo:], 'width', up)]
    unnamed x8 -> x6, local copies, waits for them, and re-layouts: 0.92 us -> 0.02 us
    conv_general_dilated x2 -> x3, matrix products: 3.68 us -> 4.41 us  [conv3x3(): lax.conv_general_dilated(x, weight, window_strides=(1, 1), padding='VALID...]
  transfers between devices with their start and end apart: 3 -> 3, of which waited for: 3 -> 2; matrix products, arithmetic and copies ran while one was open for 0% -> 4% of each run, Pallas kernels for 0% -> 0%
where the time goes in v3:
time: 49.2 us; the launch traced here: 48.9 us
  waiting for transfers between devices  13.8 us (28%)
  matrix products  10.1 us (21%)
  blocking collectives  9.8 us (20%)
  starting transfers between devices  9.71 us (20%)
  local copies, waits for them, and re-layouts  3.47 us (7%)
  other arithmetic  1.71 us (3%)
    all_to_all x1, waiting for transfers between devices, shards(): gathered = lax.all_to_all(pieces, 'tm', 0, 0, tiled=False)  10.4 us
    all_to_all x1, blocking collectives, shards(): return lax.all_to_all(state, 'tm', 0, 1, tiled=True)  9.8 us
    dot_general x3, matrix products, block(): jnp.dot(depth.reshape(-1, chans), proj, preferred_element_type=jnp.float32)  5.69 us
    conv_general_dilated x3, matrix products, conv3x3(): lax.conv_general_dilated(x, weight, window_strides=(1, 1), padding='VALID...  4.41 us
    all_to_all x1, starting transfers between devices, shards(): gathered = lax.all_to_all(pieces, 'tm', 0, 0, tiled=False)  4.24 us
    ppermute x1, starting transfers between devices, shards(): before = lax.ppermute(gathered[:, :, cols - halo:], 'width', up)  4.18 us
    ppermute x1, waiting for transfers between devices, shards(): after = lax.ppermute(gathered[:, :, :halo], 'width', down)  3.36 us
    another operation x1, other arithmetic, shards(): jnp.stack([padded[:, r * rows:r * rows + rows + 2 * halo] for r in range(...  1.47 us
  transfers between devices with their start and end apart: 3, of which 2 were waited for; matrix products, arithmetic and copies ran while one was open for 4% of the time, Pallas kernels for 0%

profile of v3, /device:TPU:0, one launch (start us, length us, event | category | flops | bytes accessed | tf_op | source)
XLA Modules:
  0.0 48.9 jit_solution(6434809782838823936)
XLA Ops:
  0.0 0.0 copy-start
  0.0 1.4 %fusion.38 = (bf16[1,4,7,12,256]{4,1,3,2,0:T(4,128)(2,1)S(1)}, bf16[1,4,7,12,256]{4,1,3,2,0:T(4,128)(2,1)S(1)}, bf16[1,4,7,12,256]{4,1,3,2,0:T(4,128)(2,1)S(1)}, bf16[1,4,7,12,256]{4,1,3,2,0:T(4,128)(2,1)S(1)}) fusion(bf16[4,12,12,256]{3,0,2,1:T(4,128)(2,1)} %param.4), kind=kLoop, calls=%fused_computation.40 | loop fusion | bytes 1327104 | tf_op jit(solution)/shard_map/stack | solution.py:46
  1.4 1.5 %pad_maximum_fusion = bf16[4,4,7,12,256]{4,1,3,2,0:T(4,128)(2,1)} fusion(bf16[1,4,7,12,256]{4,1,3,2,0:T(4,128)(2,1)S(1)} %get-tuple-element.12, bf16[1,4,7,12,256]{4,1,3,2,0:T(4,128)(2,1)S(1)} %get-tuple-element.13, bf16[1,4,7,12,256]{4,1,3,2,0:T(4,128)(2,1)S(1)} %get-tuple-element.14, bf16[1,4,7,12,256]{4,1,3,2,0:T(4,128)(2,1)S(1)} %get-tuple-element.11), kind=kLoop, calls=%fused_computation.26 | loop fusion | flops 1032192 | bytes 1376256 | tf_op jit(solution)/shard_map/stack | solution.py:46
  2.8 4.2 %all-to-all-start = ((bf16[4,4,7,12,256]{4,1,3,2,0:T(4,128)(2,1)}), bf16[4,4,7,12,256]{4,1,3,2,0:T(4,128)(2,1)S(1)}, u32[]{:S(2)}, u32[]{:S(2)}) async-start(bf16[4,4,7,12,256]{4,1,3,2,0:T(4,128)(2,1)} %pad_maximum_fusion), calls=%async_computation | async-start | bytes 1376256 | tf_op jit(solution)/shard_map/all_to_all | solution.py:47
  7.1 0.1 and_and_fusion
  7.2 0.0 copy-done
  7.2 10.4 %all-to-all-done = bf16[4,4,7,12,256]{4,1,3,2,0:T(4,128)(2,1)S(1)} async-done(((bf16[4,4,7,12,256]{4,1,3,2,0:T(4,128)(2,1)}), bf16[4,4,7,12,256]{4,1,3,2,0:T(4,128)(2,1)S(1)}, u32[]{:S(2)}, u32[]{:S(2)}) %all-to-all-start) | async-done | bytes 688160 | tf_op jit(solution)/shard_map/all_to_all | solution.py:47
  17.7 0.3 copy.7
  17.9 0.2 reshape.154
  18.1 2.4 %fusion.18 = f32[16,5,10,256]{3,0,2,1:T(8,128)S(1)} fusion(bf16[16,7,12,256]{3,0,2,1:T(8,128)(2,1)S(1)} %reshape.154, bf16[2,3,3,256,256]{4,3,2,1,0:T(8,128)(2,1)} %param.5), kind=kOutput, calls=%fused_computation.21 | convolution fusion | flops 944947200 | bytes 2686976 | tf_op jit(solution)/shard_map/conv_general_dilated | solution.py:10
  20.5 0.0 copy-start.2
  20.8 4.2 %collective-permute-start = (bf16[16,7,2,256]{3,0,2,1:T(8,128)(2,1)S(1)}, bf16[16,7,2,256]{3,0,2,1:T(8,128)(2,1)S(1)}, u32[]{:S(2)}, u32[]{:S(2)}) collective-permute-start(bf16[16,7,2,256]{3,0,2,1:T(8,128)(2,1)S(1)} %get-tuple-element.5), channel_id=1, source_target_pairs={{0,1},{1,2},{2,3},{4,5},{5,6},{6,7},{8,9},{9,10},{10,11},{12,13},{... | collective-permute-start | bytes 344072 | tf_op jit(solution)/shard_map/ppermute | solution.py:52
  25.0 1.3 %collective-permute-start.1 = (bf16[16,7,2,256]{3,0,2,1:T(8,128)(2,1)S(1)}, bf16[16,7,2,256]{3,0,2,1:T(8,128)(2,1)S(1)}, u32[]{:S(2)}, u32[]{:S(2)}) collective-permute-start(bf16[16,7,2,256]{3,0,2,1:T(8,128)(2,1)S(1)} %get-tuple-element.6), channel_id=1, source_target_pairs={{1,0},{2,1},{3,2},{5,4},{6,5},{7,6},{9,8},{10,9},{11,10},{13,12},{... | collective-permute-start | bytes 344072 | tf_op jit(solution)/shard_map/ppermute | solution.py:53
  26.3 0.0 copy-done.2
  26.3 0.0 copy-start.1
  26.3 2.0 %fusion.2 = bf16[16,5,10,256]{3,0,2,1:T(8,128)(2,1)S(1)} fusion(bf16[16,7,12,256]{3,0,2,1:T(8,128)(2,1)S(1)} %reshape.154, f32[1,5,10,256]{3,0,2,1:T(1,128)S(1)} %slice.498, f32[2,5,10,256]{3,0,2,1:T(2,128)S(1)} %slice.497, f32[3,5,10,256]{3,0,2,1:T(4,128)S(1)} %slice.496, f32[4,5,10,256]{3,0,2,1:T(4,128)S(1)} %slice.495, f32[5,5,10,256]{3,0,2,1:T(8,128)S(1)} %slice.494, ...), kind=kOutput, calls=%fused_computation.3 | convolution fusion | flops 112435200 | bytes 9721856 | tf_op jit(solution)/shard_map/dot_general | solution.py:30
  28.3 0.0 collective-permute-done
  28.3 3.4 %collective-permute-done.1 = bf16[16,7,2,256]{3,0,2,1:T(8,128)(2,1)S(1)} collective-permute-done((bf16[16,7,2,256]{3,0,2,1:T(8,128)(2,1)S(1)}, bf16[16,7,2,256]{3,0,2,1:T(8,128)(2,1)S(1)}, u32[]{:S(2)}, u32[]{:S(2)}) %collective-permute-start.1) | collective-permute-done | bytes 114720 | tf_op jit(solution)/shard_map/ppermute | solution.py:53
  31.7 0.0 copy-done.1
  31.7 1.1 %fusion.23 = f32[16,5,10,256]{3,0,2,1:T(8,128)S(1)} fusion(bf16[2,3,3,256,256]{4,3,2,1,0:T(8,128)(2,1)S(1)} %copy-done.1, bf16[16,7,2,256]{3,0,2,1:T(8,128)(2,1)S(1)} %collective-permute-done.1, bf16[16,7,4,256]{3,0,2,1:T(8,128)(2,1)S(1)} %get-tuple-element.8, bf16[16,7,4,256]{3,0,2,1:T(8,128)(2,1)S(1)} %get-tuple-element.7, ...), kind=kOutput, calls=%fused_computation.25 | convolution fusion | flops 945979392 | bytes 2686976 | tf_op jit(solution)/shard_map/conv_general_dilated | solution.py:10
  33.1 2.3 %add_convert_fusion.1 = bf16[16,5,10,256]{3,0,2,1:T(8,128)(2,1)S(1)} fusion(bf16[16,7,2,256]{3,0,2,1:T(8,128)(2,1)S(1)} %collective-permute-done.1, bf16[16,7,4,256]{3,0,2,1:T(8,128)(2,1)S(1)} %get-tuple-element.8, bf16[16,7,4,256]{3,0,2,1:T(8,128)(2,1)S(1)} %get-tuple-element.7, bf16[16,7,2,256]{3,0,2,1:T(8,128)(2,1)S(1)} %collective-permute-done, ...), kind=kOutput, calls=%fused_computation.22 | convolution fusion | flops 113049600 | bytes 10000384 | tf_op jit(solution)/shard_map/dot_general | solution.py:30
  35.5 0.1 maximum_select_fusion
  35.6 0.9 %fusion.35 = f32[16,3,12,256]{3,0,2,1:T(8,128)S(1)} fusion(bf16[16,5,14,256]{3,0,2,1:T(8,128)(2,1)S(1)} %maximum_select_fusion, bf16[2,3,3,256,256]{4,3,2,1,0:T(8,128)(2,1)S(1)} %copy-done.1), kind=kOutput, calls=%fused_computation.36 | convolution fusion | flops 680361984 | bytes 2342912 | tf_op jit(solution)/shard_map/conv_general_dilated | solution.py:10
  36.7 1.4 %fusion.6 = bf16[16,3,12,256]{3,0,2,1:T(8,128)(2,1)S(1)} fusion(bf16[16,5,14,256]{3,0,2,1:T(8,128)(2,1)S(1)} %maximum_select_fusion, f32[1,3,12,256]{3,0,2,1:T(1,128)S(1)} %slice.515, f32[2,3,12,256]{3,0,2,1:T(2,128)S(1)} %slice.514, f32[3,3,12,256]{3,0,2,1:T(4,128)S(1)} %slice.513, f32[4,3,12,256]{3,0,2,1:T(4,128)S(1)} %slice.512, ...), kind=kOutput, calls=%fused_computation.9 | convolution fusion | flops 80953344 | bytes 7041024 | tf_op jit(solution)/shard_map/dot_general | solution.py:30
  38.2 0.1 copy.8
  38.3 9.8 %all_to_all.23 = bf16[16,3,12,256]{3,2,1,0:T(8,128)(2,1)S(1)} all-to-all(bf16[16,3,12,256]{3,2,1,0:T(8,128)(2,1)S(1)} %copy.8), channel_id=1, replica_groups=mesh['groups'=2,'tm'=4,'width'=4] {'tm'}, dimensions={0} | all-to-all | bytes 589824 | tf_op jit(solution)/shard_map/all_to_all | solution.py:70
  48.1 0.9 %copy.9 = bf16[4,4,3,12,256]{4,0,3,2,1:T(4,128)(2,1)} copy(bf16[4,4,3,12,256]{4,3,2,0,1:T(8,128)(2,1)S(1)} %bitcast.126) | data formatting | bytes 589824 | tf_op jit(solution)/shard_map/all_to_all | solution.py:70
  (31 shorter events, 0.7 us)
Async XLA Ops:
  0.0 7.2 %copy-start = (f32[2,16,256]{2,1,0:T(8,128)S(1)}, f32[2,16,256]{2,1,0:T(8,128)}, u32[]{:S(2)}) copy-start(f32[2,16,256]{2,1,0:T(8,128)} %param.6) | copy-start | bytes 98308
  2.8 14.8 %all-to-all-start = ((bf16[4,4,7,12,256]{4,1,3,2,0:T(4,128)(2,1)}), bf16[4,4,7,12,256]{4,1,3,2,0:T(4,128)(2,1)S(1)}, u32[]{:S(2)}, u32[]{:S(2)}) async-start(bf16[4,4,7,12,256]{4,1,3,2,0:T(4,128)(2,1)} %pad_maximum_fusion), calls=%async_computation | async-start | bytes 1376256 | tf_op jit(solution)/shard_map/all_to_all | solution.py:47
  20.5 5.8 %copy-start.2 = (bf16[2,256,256]{2,1,0:T(8,128)(2,1)S(1)}, bf16[2,256,256]{2,1,0:T(8,128)(2,1)}, u32[]{:S(2)}) copy-start(bf16[2,256,256]{2,1,0:T(8,128)(2,1)} %param.7) | copy-start | bytes 786436
  20.8 7.5 %collective-permute-start = (bf16[16,7,2,256]{3,0,2,1:T(8,128)(2,1)S(1)}, bf16[16,7,2,256]{3,0,2,1:T(8,128)(2,1)S(1)}, u32[]{:S(2)}, u32[]{:S(2)}) collective-permute-start(bf16[16,7,2,256]{3,0,2,1:T(8,128)(2,1)S(1)} %get-tuple-element.5), channel_id=1, source_target_pairs={{0,1},{1,2},{2,3},{4,5},{5,6},{6,7},{8,9},{9,10},{10,11},{12,13},{... | collective-permute-start | bytes 344072 | tf_op jit(solution)/shard_map/ppermute | solution.py:52
  25.0 6.7 %collective-permute-start.1 = (bf16[16,7,2,256]{3,0,2,1:T(8,128)(2,1)S(1)}, bf16[16,7,2,256]{3,0,2,1:T(8,128)(2,1)S(1)}, u32[]{:S(2)}, u32[]{:S(2)}) collective-permute-start(bf16[16,7,2,256]{3,0,2,1:T(8,128)(2,1)S(1)} %get-tuple-element.6), channel_id=1, source_target_pairs={{1,0},{2,1},{3,2},{5,4},{6,5},{7,6},{9,8},{10,9},{11,10},{13,12},{... | collective-permute-start | bytes 344072 | tf_op jit(solution)/shard_map/ppermute | solution.py:53
  26.3 5.4 %copy-start.1 = (bf16[2,3,3,256,256]{4,3,2,1,0:T(8,128)(2,1)S(1)}, bf16[2,3,3,256,256]{4,3,2,1,0:T(8,128)(2,1)}, u32[]{:S(2)}) copy-start(bf16[2,3,3,256,256]{4,3,2,1,0:T(8,128)(2,1)} %param.5) | copy-start | bytes 7077892

commit v4 on v1

v4 whole, which is shorter than its diff:
```python
import functools

import jax
import jax.numpy as jnp
from jax import lax
from jax.experimental import pallas as pl
from jax.experimental.pallas import tpu as pltpu
from jax.sharding import PartitionSpec as P

BLOCKS = 2
LANES = 16


def block_kernel(x_ref, w_ref, k_ref, p_ref, m_ref, o_ref, *, count, pitch):
    frames, _, chans = x_ref.shape
    total = frames * count

    def window(dy):
        return x_ref[:, dy * pitch : dy * pitch + count, :].reshape(total, chans)

    taps = [None, None, None]
    for dy in range(3):
        piece = window(dy)
        for dx in range(3):
            part = jnp.dot(piece, w_ref[dy, dx], preferred_element_type=jnp.float32)
            taps[dx] = part if taps[dx] is None else taps[dx] + part
    conv = taps[0] + pltpu.roll(taps[1], total - 1, 0) + pltpu.roll(taps[2], total - 2, 0)
    hidden = (conv / (1.0 + jnp.exp(-conv))).astype(jnp.bfloat16)

    values = hidden.astype(jnp.float32).reshape(frames, count, chans)
    kernel = k_ref[...]
    depth = []
    for t in range(frames):
        acc = values[t] * kernel[0:1]
        for lag in range(1, t + 1):
            acc = acc + values[t - lag] * kernel[lag : lag + 1]
        depth.append(acc.astype(jnp.bfloat16))
    depth = jnp.stack(depth).reshape(total, chans)

    mixed = jnp.dot(depth, p_ref[...], preferred_element_type=jnp.float32).astype(jnp.bfloat16)
    center = pltpu.roll(window(1).astype(jnp.float32), total - 1, 0)
    state = (center + mixed.astype(jnp.float32)).astype(jnp.bfloat16).reshape(frames, count, chans)
    o_ref[...] = jnp.where(m_ref[...][None] > 0, state, jnp.zeros((), state.dtype))


def block(x, weight, kernel, proj, mask, pitch):
    frames, length, chans = x.shape
    count = length - 2 * pitch
    flops = 2 * frames * count * chans * chans * 10
    vmem = pltpu.VMEM
    return pl.pallas_call(
        functools.partial(block_kernel, count=count, pitch=pitch),
        out_shape=jax.ShapeDtypeStruct((frames, count, chans), x.dtype),
        in_specs=[pl.BlockSpec(memory_space=vmem)] * 5,
        out_specs=pl.BlockSpec(memory_space=vmem),
        compiler_params=pltpu.CompilerParams(vmem_limit_bytes=48 * 1024 * 1024),
        cost_estimate=pl.CostEstimate(
            flops=flops,
            transcendentals=frames * count * chans,
            bytes_accessed=2 * frames * (length + count) * chans + 2 * 10 * chans * chans,
        ),
    )(x, weight, kernel, proj, mask)


def shards(video, conv_w, depth_k, proj_w):
    bands = lax.axis_size("tm")
    sides = lax.axis_size("width")
    band = lax.axis_index("tm")
    side = lax.axis_index("width")
    frames, height, cols, chans = video.shape
    rows = height // bands
    halo = BLOCKS
    pitch = -(-(cols + 2 * halo) // LANES) * LANES

    padded = jnp.pad(video, ((0, 0), (halo, halo), (0, 0), (0, 0)))
    pieces = jnp.stack([padded[:, r * rows : r * rows + rows + 2 * halo] for r in range(bands)])
    gathered = lax.all_to_all(pieces, "tm", 0, 0, tiled=False)
    gathered = gathered.reshape(bands * frames, rows + 2 * halo, cols, chans)

    up = [(i, i + 1) for i in range(sides - 1)]
    down = [(i + 1, i) for i in range(sides - 1)]
    before = lax.ppermute(gathered[:, :, cols - halo :], "width", up)
    after = lax.ppermute(gathered[:, :, :halo], "width", down)
    spare = jnp.zeros(gathered.shape[:2] + (pitch - cols - 2 * halo, chans), gathered.dtype)
    state = jnp.concatenate([before, gathered, after, spare], axis=2)
    state = state.reshape(state.shape[0], -1, chans)

    for b in range(BLOCKS):
        left = halo - 1 - b
        n_rows = rows + 2 * left
        row = band * rows - left + lax.broadcasted_iota(jnp.int32, (n_rows, pitch), 0)
        col = side * cols - left + lax.broadcasted_iota(jnp.int32, (n_rows, pitch), 1)
        inside = (row >= 0) & (row < height) & (col >= 0) & (col < sides * cols)
        inside = inside & (lax.broadcasted_iota(jnp.int32, (n_rows, pitch), 1) < cols + 2 * left)
        mask = jnp.broadcast_to(inside.reshape(-1, 1), (n_rows * pitch, chans)).astype(jnp.float32)
        state = block(state, conv_w[b], depth_k[b], proj_w[b], mask, pitch)

    state = state.reshape(state.shape[0], rows, pitch, chans)[:, :, :cols]
    return lax.all_to_all(state, "tm", 0, 1, tiled=True)


def solution(mesh):
    return jax.shard_map(
        shards,
        mesh=mesh,
        in_specs=(P(("groups", "tm"), None, "width", None), P(), P(), P()),
        out_specs=P(("groups", "tm"), None, "width", None),
        check_vma=False,
    )
```

time: 49.6 us -> 47.8 us (0.964)
  matrix products: 7.86 us -> 0 us
  Pallas kernels: 0 us -> 5.04 us
  local copies, waits for them, and re-layouts: 4.22 us -> 7.29 us
  waiting for transfers between devices: 15.8 us -> 13.7 us
    pallas_call x0 -> x2, Pallas kernels: none -> 5.04 us  [block(): pl.pallas_call(functools.partial(block_kernel, count=count, pitch=pitch),...]
    dot_general x2 -> x0, matrix products: 4.19 us -> none  [block(): jnp.dot(depth.reshape(-1, chans), proj, preferred_element_type=jnp.float32)]
    conv_general_dilated x2 -> x0, matrix products: 3.68 us -> none  [conv3x3(): lax.conv_general_dilated(x, weight, window_strides=(1, 1), padding='VALID...]
    all_to_all x1, waiting for transfers between devices: 10.5 us -> 8.36 us  [shards(): gathered = lax.all_to_all(pieces, 'tm', 0, 0, tiled=False)]
    squeeze x0 -> x3, local copies, waits for them, and re-layouts: none -> 1.81 us  [shards(): state = block(state, conv_w[b], depth_k[b], proj_w[b], mask, pitch)]
    reshape x1, local copies, waits for them, and re-layouts: 0.16 us -> 1.51 us  [shards(): gathered = gathered.reshape(bands * frames, rows + 2 * halo, cols, chans)]
    unnamed x8 -> x4, local copies, waits for them, and re-layouts: 0.92 us -> 0.01 us
    all_to_all x1, local copies, waits for them, and re-layouts: 0.25 us -> 1.12 us  [shards(): gathered = lax.all_to_all(pieces, 'tm', 0, 0, tiled=False)]
  transfers between devices with their start and end apart: 3 -> 3, of which waited for: 3 -> 3; matrix products, arithmetic and copies ran while one was open for 0% -> 5% of each run, Pallas kernels for 0% -> 0%
where the time goes in v4:
time: 47.8 us; the launch traced here: 47.5 us
  waiting for transfers between devices  13.7 us (29%)
  blocking collectives  9.8 us (21%)
  starting transfers between devices  9.71 us (20%)
  local copies, waits for them, and re-layouts  7.29 us (15%)
  Pallas kernels  5.04 us (11%)
  other arithmetic  1.79 us (4%)
    all_to_all x1, blocking collectives, shards(): return lax.all_to_all(state, 'tm', 0, 1, tiled=True)  9.8 us
    all_to_all x1, waiting for transfers between devices, shards(): gathered = lax.all_to_all(pieces, 'tm', 0, 0, tiled=False)  8.36 us
    pallas_call x2, Pallas kernels, block(): pl.pallas_call(functools.partial(block_kernel, count=count, pitch=pitch),...  5.04 us
    ppermute x1, waiting for transfers between devices, shards(): after = lax.ppermute(gathered[:, :, :halo], 'width', down)  4.34 us
    all_to_all x1, starting transfers between devices, shards(): gathered = lax.all_to_all(pieces, 'tm', 0, 0, tiled=False)  4.24 us
    ppermute x1, starting transfers between devices, shards(): before = lax.ppermute(gathered[:, :, cols - halo:], 'width', up)  4.18 us
    squeeze x3, local copies, waits for them, and re-layouts, shards(): state = block(state, conv_w[b], depth_k[b], proj_w[b], mask, pitch)  1.81 us
    reshape x1, local copies, waits for them, and re-layouts, shards(): gathered = gathered.reshape(bands * frames, rows + 2 * halo, cols, chans)  1.51 us
  transfers between devices with their start and end apart: 3, of which 3 were waited for; matrix products, arithmetic and copies ran while one was open for 5% of the time, Pallas kernels for 0%

profile of v4, /device:TPU:0, one launch (start us, length us, event | category | flops | bytes accessed | tf_op | source)
XLA Modules:
  0.0 47.5 jit_solution(301359374089711006)
XLA Ops:
  0.0 1.4 %fusion = (bf16[1,4,7,12,256]{4,1,3,2,0:T(4,128)(2,1)S(1)}, bf16[1,4,7,12,256]{4,1,3,2,0:T(4,128)(2,1)S(1)}, bf16[1,4,7,12,256]{4,1,3,2,0:T(4,128)(2,1)S(1)}, bf16[1,4,7,12,256]{4,1,3,2,0:T(4,128)(2,1)S(1)}) fusion(bf16[4,12,12,256]{3,0,2,1:T(4,128)(2,1)} %param.4), kind=kLoop, calls=%fused_computation.6 | loop fusion | bytes 1327104 | tf_op jit(solution)/shard_map/stack | solution.py:76
  1.4 0.0 copy-start
  1.4 1.5 %pad_maximum_fusion.1 = bf16[4,4,7,12,256]{4,1,3,2,0:T(4,128)(2,1)} fusion(bf16[1,4,7,12,256]{4,1,3,2,0:T(4,128)(2,1)S(1)} %get-tuple-element.10, bf16[1,4,7,12,256]{4,1,3,2,0:T(4,128)(2,1)S(1)} %get-tuple-element.11, bf16[1,4,7,12,256]{4,1,3,2,0:T(4,128)(2,1)S(1)} %get-tuple-element.12, bf16[1,4,7,12,256]{4,1,3,2,0:T(4,128)(2,1)S(1)} %get-tuple-element.9), kind=kLoop, calls=%fused_computation.3 | loop fusion | flops 1032192 | bytes 1376256 | tf_op jit(solution)/shard_map/stack | solution.py:76
  2.9 4.2 %all-to-all-start = ((bf16[4,4,7,12,256]{4,1,3,2,0:T(4,128)(2,1)}), bf16[4,4,7,12,256]{4,1,3,2,0:T(4,128)(2,1)S(1)}, u32[]{:S(2)}, u32[]{:S(2)}) async-start(bf16[4,4,7,12,256]{4,1,3,2,0:T(4,128)(2,1)} %pad_maximum_fusion.1), calls=%async_computation | async-start | bytes 1376256 | tf_op jit(solution)/shard_map/all_to_all | solution.py:77
  7.2 0.1 and_convert_fusion
  7.2 0.1 reshape.90
  7.3 0.1 and_convert_fusion.1
  7.4 0.1 reshape.91
  7.5 0.0 copy-done
  7.5 1.8 %slice_bitcast_fusion = (bf16[3,3,256,256]{3,2,1,0:T(8,128)(2,1)S(1)}, bf16[3,3,256,256]{3,2,1,0:T(8,128)(2,1)S(1)}) fusion(bf16[2,3,3,256,256]{4,3,2,1,0:T(8,128)(2,1)} %param.5), kind=kLoop, calls=%fused_computation | loop fusion | bytes 4718592 | tf_op jit(solution)/shard_map/squeeze | solution.py:96
  9.3 8.4 %all-to-all-done = bf16[4,4,7,12,256]{4,1,3,2,0:T(4,128)(2,1)S(1)} async-done(((bf16[4,4,7,12,256]{4,1,3,2,0:T(4,128)(2,1)}), bf16[4,4,7,12,256]{4,1,3,2,0:T(4,128)(2,1)S(1)}, u32[]{:S(2)}, u32[]{:S(2)}) %all-to-all-start) | async-done | bytes 688160 | tf_op jit(solution)/shard_map/all_to_all | solution.py:77
  17.7 1.1 %copy.6 = bf16[4,4,7,12,256]{4,1,0,3,2:T(4,128)(2,1)} copy(bf16[4,4,7,12,256]{4,1,3,2,0:T(4,128)(2,1)S(1)} %all-to-all-done) | data formatting | bytes 1376256 | tf_op jit(solution)/shard_map/all_to_all | solution.py:77
  18.8 0.0 copy-start.1
  18.8 1.5 %reshape.87 = bf16[16,7,12,256]{3,0,2,1:T(8,128)(2,1)S(1)} reshape(bf16[4,4,7,12,256]{4,1,0,3,2:T(4,128)(2,1)} %copy.6) | data formatting | bytes 1376256 | tf_op jit(solution)/shard_map/reshape | solution.py:78
  20.3 4.2 %collective-permute-start = (bf16[16,7,2,256]{3,0,2,1:T(8,128)(2,1)S(1)}, bf16[16,7,2,256]{3,0,2,1:T(8,128)(2,1)S(1)}, u32[]{:S(2)}, u32[]{:S(2)}) collective-permute-start(bf16[16,7,2,256]{3,0,2,1:T(8,128)(2,1)S(1)} %get-tuple-element.7), channel_id=1, source_target_pairs={{0,1},{1,2},{2,3},{4,5},{5,6},{6,7},{8,9},{9,10},{10,11},{12,13},{... | collective-permute-start | bytes 344072 | tf_op jit(solution)/shard_map/ppermute | solution.py:82
  24.5 1.3 %collective-permute-start.1 = (bf16[16,7,2,256]{3,0,2,1:T(8,128)(2,1)S(1)}, bf16[16,7,2,256]{3,0,2,1:T(8,128)(2,1)S(1)}, u32[]{:S(2)}, u32[]{:S(2)}) collective-permute-start(bf16[16,7,2,256]{3,0,2,1:T(8,128)(2,1)S(1)} %get-tuple-element.8), channel_id=1, source_target_pairs={{1,0},{2,1},{3,2},{5,4},{6,5},{7,6},{9,8},{10,9},{11,10},{13,12},{... | collective-permute-start | bytes 344072 | tf_op jit(solution)/shard_map/ppermute | solution.py:83
  25.8 0.0 copy-done.1
  25.8 1.0 %collective-permute-done = bf16[16,7,2,256]{3,0,2,1:T(8,128)(2,1)S(1)} collective-permute-done((bf16[16,7,2,256]{3,0,2,1:T(8,128)(2,1)S(1)}, bf16[16,7,2,256]{3,0,2,1:T(8,128)(2,1)S(1)}, u32[]{:S(2)}, u32[]{:S(2)}) %collective-permute-start) | collective-permute-done | bytes 114720 | tf_op jit(solution)/shard_map/ppermute | solution.py:82
  26.9 4.3 %collective-permute-done.1 = bf16[16,7,2,256]{3,0,2,1:T(8,128)(2,1)S(1)} collective-permute-done((bf16[16,7,2,256]{3,0,2,1:T(8,128)(2,1)S(1)}, bf16[16,7,2,256]{3,0,2,1:T(8,128)(2,1)S(1)}, u32[]{:S(2)}, u32[]{:S(2)}) %collective-permute-start.1) | collective-permute-done | bytes 114720 | tf_op jit(solution)/shard_map/ppermute | solution.py:83
  31.2 0.1 pad_maximum_fusion
  31.3 0.3 copy.7
  31.6 0.1 broadcast_in_dim.4.m_ref
  31.7 3.1 %shard_map.46.x_ref = bf16[16,80,256]{2,1,0:T(8,128)(2,1)S(1)} custom-call(bf16[16,112,256]{2,1,0:T(8,128)(2,1)S(1)} %bitcast.29, bf16[3,3,256,256]{3,2,1,0:T(8,128)(2,1)S(1)} %get-tuple-element.6.w_ref, f32[16,256]{1,0:T(8,128)S(1)} %get-tuple-element.16.k_ref, bf16[256,256]{1,0:T(8,128)(2,1)S(1)} %get-tuple-element.14.p_ref, ...), custom_call_target="tpu_custom_call" | custom-call | flops 1677721600 | bytes 2883584 | tf_op jit(solution)/shard_map/pallas_call | solution.py:51
  34.8 0.1 broadcast_in_dim.5.m_ref
  34.9 1.9 %shard_map.47 = bf16[16,48,256]{2,1,0:T(8,128)(2,1)S(1)} custom-call(bf16[16,80,256]{2,1,0:T(8,128)(2,1)S(1)} %shard_map.46.x_ref, bf16[3,3,256,256]{3,2,1,0:T(8,128)(2,1)S(1)} %get-tuple-element.5.w_ref, f32[16,256]{1,0:T(8,128)S(1)} %get-tuple-element.15.k_ref, bf16[256,256]{1,0:T(8,128)(2,1)S(1)} %get-tuple-element.13.p_ref, ...), custom_call_target="tpu_custom_call" | custom-call | flops 1006632960 | bytes 2359296 | tf_op jit(solution)/shard_map/pallas_call | solution.py:51
  36.8 9.8 %all_to_all.23 = bf16[16,3,12,256]{3,2,1,0:T(8,128)(2,1)S(1)} all-to-all(bf16[16,3,12,256]{3,2,1,0:T(8,128)(2,1)S(1)} %bitcast.30), channel_id=1, replica_groups=mesh['groups'=2,'tm'=4,'width'=4] {'tm'}, dimensions={0} | all-to-all | bytes 589824 | tf_op jit(solution)/shard_map/all_to_all | solution.py:99
  46.6 0.9 %copy.8 = bf16[4,4,3,12,256]{4,1,3,2,0:T(4,128)(2,1)} copy(bf16[4,4,3,12,256]{4,3,2,1,0:T(8,128)(2,1)S(1)} %bitcast.31) | data formatting | bytes 589824 | tf_op jit(solution)/shard_map/all_to_all | solution.py:99
  (9 shorter events, 0.1 us)
Async XLA Ops:
  1.4 6.1 %copy-start = (bf16[2,256,256]{2,1,0:T(8,128)(2,1)S(1)}, bf16[2,256,256]{2,1,0:T(8,128)(2,1)}, u32[]{:S(2)}) copy-start(bf16[2,256,256]{2,1,0:T(8,128)(2,1)} %param.7) | copy-start | bytes 786436
  2.9 14.8 %all-to-all-start = ((bf16[4,4,7,12,256]{4,1,3,2,0:T(4,128)(2,1)}), bf16[4,4,7,12,256]{4,1,3,2,0:T(4,128)(2,1)S(1)}, u32[]{:S(2)}, u32[]{:S(2)}) async-start(bf16[4,4,7,12,256]{4,1,3,2,0:T(4,128)(2,1)} %pad_maximum_fusion.1), calls=%async_computation | async-start | bytes 1376256 | tf_op jit(solution)/shard_map/all_to_all | solution.py:77
  18.8 7.0 %copy-start.1 = (f32[2,16,256]{2,1,0:T(8,128)S(1)}, f32[2,16,256]{2,1,0:T(8,128)}, u32[]{:S(2)}) copy-start(f32[2,16,256]{2,1,0:T(8,128)} %param.6) | copy-start | bytes 98308
  20.3 6.5 %collective-permute-start = (bf16[16,7,2,256]{3,0,2,1:T(8,128)(2,1)S(1)}, bf16[16,7,2,256]{3,0,2,1:T(8,128)(2,1)S(1)}, u32[]{:S(2)}, u32[]{:S(2)}) collective-permute-start(bf16[16,7,2,256]{3,0,2,1:T(8,128)(2,1)S(1)} %get-tuple-element.7), channel_id=1, source_target_pairs={{0,1},{1,2},{2,3},{4,5},{5,6},{6,7},{8,9},{9,10},{10,11},{12,13},{... | collective-permute-start | bytes 344072 | tf_op jit(solution)/shard_map/ppermute | solution.py:82
  24.5 6.7 %collective-permute-start.1 = (bf16[16,7,2,256]{3,0,2,1:T(8,128)(2,1)S(1)}, bf16[16,7,2,256]{3,0,2,1:T(8,128)(2,1)S(1)}, u32[]{:S(2)}, u32[]{:S(2)}) collective-permute-start(bf16[16,7,2,256]{3,0,2,1:T(8,128)(2,1)S(1)} %get-tuple-element.8), channel_id=1, source_target_pairs={{1,0},{2,1},{3,2},{5,4},{6,5},{7,6},{9,8},{10,9},{11,10},{13,12},{... | collective-permute-start | bytes 344072 | tf_op jit(solution)/shard_map/ppermute | solution.py:83

commit v5 on v4

--- a/solution.py
+++ b/solution.py
@@ -74,13 +74,14 @@
 
     padded = jnp.pad(video, ((0, 0), (halo, halo), (0, 0), (0, 0)))
     pieces = jnp.stack([padded[:, r * rows : r * rows + rows + 2 * halo] for r in range(bands)])
-    gathered = lax.all_to_all(pieces, "tm", 0, 0, tiled=False)
-    gathered = gathered.reshape(bands * frames, rows + 2 * halo, cols, chans)
+    received = lax.all_to_all(pieces, "tm", 0, 0, tiled=False)
 
     up = [(i, i + 1) for i in range(sides - 1)]
     down = [(i + 1, i) for i in range(sides - 1)]
-    before = lax.ppermute(gathered[:, :, cols - halo :], "width", up)
-    after = lax.ppermute(gathered[:, :, :halo], "width", down)
+    edge = (bands * frames, rows + 2 * halo, halo, chans)
+    before = lax.ppermute(received[:, :, :, cols - halo :], "width", up).reshape(edge)
+    after = lax.ppermute(received[:, :, :, :halo], "width", down).reshape(edge)
+    gathered = received.reshape(bands * frames, rows + 2 * halo, cols, chans)
     spare = jnp.zeros(gathered.shape[:2] + (pitch - cols - 2 * halo, chans), gathered.dtype)
     state = jnp.concatenate([before, gathered, after, spare], axis=2)
     state = state.reshape(state.shape[0], -1, chans)

time: 47.8 us -> 46.5 us (0.973)
  waiting for transfers between devices: 13.7 us -> 8.36 us
  local copies, waits for them, and re-layouts: 7.29 us -> 10 us
  starting transfers between devices: 9.71 us -> 11 us
    ppermute x2, waiting for transfers between devices: 5.36 us -> 0.01 us  [the longest x1 0.01 us: shards(): after = lax.ppermute(received[:, :, :, :halo], 'width', down).reshape(edge)]
    ppermute x0 -> x2, local copies, waits for them, and re-layouts: none -> 1.98 us  [the longest x1 0.99 us: shards(): after = lax.ppermute(received[:, :, :, :halo], 'width', down).reshape(edge)]
    ppermute x2, starting transfers between devices: 5.48 us -> 6.75 us  [the longest x1 5.47 us: shards(): lax.ppermute(received[:, :, :, cols - halo:], 'width', up).reshape(edge)]
    slice x1, local copies, waits for them, and re-layouts: 0.02 us -> 0.73 us  [shards(): received[:, :, :, cols - halo:]]
    reshape x1 -> x3, local copies, waits for them, and re-layouts: 1.51 us -> 1.53 us  [the longest x1 1.5 us: shards(): gathered = received.reshape(bands * frames, rows + 2 * halo, cols, chans)]
  transfers between devices with their start and end apart: 3 -> 3, of which waited for: 3 -> 1; matrix products, arithmetic and copies ran while one was open for 5% -> 13% of each run, Pallas kernels for 0% -> 0%
where the time goes in v5:
time: 46.5 us; the launch traced here: 46.1 us
  starting transfers between devices  11 us (24%)
  local copies, waits for them, and re-layouts  10 us (22%)
  blocking collectives  9.8 us (21%)
  waiting for transfers between devices  8.36 us (18%)
  Pallas kernels  5.04 us (11%)
  other arithmetic  1.79 us (4%)
    all_to_all x1, blocking collectives, shards(): return lax.all_to_all(state, 'tm', 0, 1, tiled=True)  9.8 us
    all_to_all x1, waiting for transfers between devices, shards(): received = lax.all_to_all(pieces, 'tm', 0, 0, tiled=False)  8.35 us
    ppermute x1, starting transfers between devices, shards(): lax.ppermute(received[:, :, :, cols - halo:], 'width', up).reshape(edge)  5.47 us
    pallas_call x2, Pallas kernels, block(): pl.pallas_call(functools.partial(block_kernel, count=count, pitch=pitch),...  5.04 us
    all_to_all x1, starting transfers between devices, shards(): received = lax.all_to_all(pieces, 'tm', 0, 0, tiled=False)  4.24 us
    squeeze x3, local copies, waits for them, and re-layouts, shards(): state = block(state, conv_w[b], depth_k[b], proj_w[b], mask, pitch)  1.81 us
    reshape x1, local copies, waits for them, and re-layouts, shards(): gathered = received.reshape(bands * frames, rows + 2 * halo, cols, chans)  1.5 us
    another operation x1, other arithmetic, shards(): jnp.stack([padded[:, r * rows:r * rows + rows + 2 * halo] for r in range(...  1.48 us
  transfers between devices with their start and end apart: 3, of which 1 were waited for; matrix products, arithmetic and copies ran while one was open for 13% of the time, Pallas kernels for 0%

profile of v5, /device:TPU:0, one launch (start us, length us, event | category | flops | bytes accessed | tf_op | source)
XLA Modules:
  0.0 46.1 jit_solution(2039450833018118376)
XLA Ops:
  0.0 1.4 %fusion = (bf16[1,4,7,12,256]{4,1,3,2,0:T(4,128)(2,1)S(1)}, bf16[1,4,7,12,256]{4,1,3,2,0:T(4,128)(2,1)S(1)}, bf16[1,4,7,12,256]{4,1,3,2,0:T(4,128)(2,1)S(1)}, bf16[1,4,7,12,256]{4,1,3,2,0:T(4,128)(2,1)S(1)}) fusion(bf16[4,12,12,256]{3,0,2,1:T(4,128)(2,1)} %param.4), kind=kLoop, calls=%fused_computation.6 | loop fusion | bytes 1327104 | tf_op jit(solution)/shard_map/stack | solution.py:76
  1.4 0.0 copy-start
  1.4 1.5 %pad_maximum_fusion.1 = bf16[4,4,7,12,256]{4,1,3,2,0:T(4,128)(2,1)} fusion(bf16[1,4,7,12,256]{4,1,3,2,0:T(4,128)(2,1)S(1)} %get-tuple-element.10, bf16[1,4,7,12,256]{4,1,3,2,0:T(4,128)(2,1)S(1)} %get-tuple-element.11, bf16[1,4,7,12,256]{4,1,3,2,0:T(4,128)(2,1)S(1)} %get-tuple-element.12, bf16[1,4,7,12,256]{4,1,3,2,0:T(4,128)(2,1)S(1)} %get-tuple-element.9), kind=kLoop, calls=%fused_computation.3 | loop fusion | flops 1032192 | bytes 1376256 | tf_op jit(solution)/shard_map/stack | solution.py:76
  2.9 4.2 %all-to-all-start = ((bf16[4,4,7,12,256]{4,1,3,2,0:T(4,128)(2,1)}), bf16[4,4,7,12,256]{4,1,3,2,0:T(4,128)(2,1)S(1)}, u32[]{:S(2)}, u32[]{:S(2)}) async-start(bf16[4,4,7,12,256]{4,1,3,2,0:T(4,128)(2,1)} %pad_maximum_fusion.1), calls=%async_computation | async-start | bytes 1376256 | tf_op jit(solution)/shard_map/all_to_all | solution.py:77
  7.2 0.1 and_convert_fusion
  7.2 0.1 reshape.98
  7.3 0.1 and_convert_fusion.1
  7.4 0.1 reshape.99
  7.5 0.0 copy-done
  7.5 0.0 copy-start.1
  7.5 1.8 %slice_bitcast_fusion = (bf16[3,3,256,256]{3,2,1,0:T(8,128)(2,1)S(1)}, bf16[3,3,256,256]{3,2,1,0:T(8,128)(2,1)S(1)}) fusion(bf16[2,3,3,256,256]{4,3,2,1,0:T(8,128)(2,1)} %param.5), kind=kLoop, calls=%fused_computation | loop fusion | bytes 4718592 | tf_op jit(solution)/shard_map/squeeze | solution.py:97
  9.3 8.3 %all-to-all-done = bf16[4,4,7,12,256]{4,1,3,2,0:T(4,128)(2,1)S(1)} async-done(((bf16[4,4,7,12,256]{4,1,3,2,0:T(4,128)(2,1)}), bf16[4,4,7,12,256]{4,1,3,2,0:T(4,128)(2,1)S(1)}, u32[]{:S(2)}, u32[]{:S(2)}) %all-to-all-start) | async-done | bytes 688160 | tf_op jit(solution)/shard_map/all_to_all | solution.py:77
  17.7 0.7 %fusion.6 = (bf16[4,4,7,2,256]{4,1,3,2,0:T(4,128)(2,1)S(1)}, bf16[4,4,7,2,256]{4,1,3,2,0:T(4,128)(2,1)}) fusion(bf16[4,4,7,12,256]{4,1,3,2,0:T(4,128)(2,1)S(1)} %all-to-all-done), kind=kLoop, calls=%fused_computation.26 | loop fusion | bytes 458752 | tf_op jit(solution)/shard_map/slice | solution.py:82
  18.4 1.3 %collective-permute-start.1 = (bf16[4,4,7,2,256]{4,1,3,2,0:T(4,128)(2,1)}, bf16[4,4,7,2,256]{4,1,3,2,0:T(4,128)(2,1)}, u32[]{:S(2)}, u32[]{:S(2)}) collective-permute-start(bf16[4,4,7,2,256]{4,1,3,2,0:T(4,128)(2,1)} %get-tuple-element.8), channel_id=1, source_target_pairs={{1,0},{2,1},{3,2},{5,4},{6,5},{7,6},{9,8},{10,9},{11,10},{13,12},{... | collective-permute-start | bytes 344072 | tf_op jit(solution)/shard_map/ppermute | solution.py:83
  19.7 5.5 %collective-permute-start = (bf16[4,4,7,2,256]{4,1,3,2,0:T(4,128)(2,1)S(1)}, bf16[4,4,7,2,256]{4,1,3,2,0:T(4,128)(2,1)}, u32[]{:S(2)}, u32[]{:S(2)}) collective-permute-start(bf16[4,4,7,2,256]{4,1,3,2,0:T(4,128)(2,1)S(1)} %get-tuple-element.7), channel_id=1, source_target_pairs={{0,1},{1,2},{2,3},{4,5},{5,6},{6,7},{8,9},{9,10},{10,11},{12,13},{... | collective-permute-start | bytes 344072 | tf_op jit(solution)/shard_map/ppermute | solution.py:82
  25.2 0.0 copy-done.1
  25.2 1.1 %copy.7 = bf16[4,4,7,12,256]{4,1,0,3,2:T(4,128)(2,1)} copy(bf16[4,4,7,12,256]{4,1,3,2,0:T(4,128)(2,1)S(1)} %all-to-all-done) | data formatting | bytes 1376256 | tf_op jit(solution)/shard_map/all_to_all | solution.py:77
  26.3 1.5 %reshape.94 = bf16[16,7,12,256]{3,0,2,1:T(8,128)(2,1)S(1)} reshape(bf16[4,4,7,12,256]{4,1,0,3,2:T(4,128)(2,1)} %copy.7) | data formatting | bytes 1376256 | tf_op jit(solution)/shard_map/reshape | solution.py:84
  27.8 0.0 collective-permute-done.1
  27.8 1.0 %copy.8 = bf16[4,4,7,2,256]{4,3,2,1,0:T(2,128)(2,1)S(1)} copy(bf16[4,4,7,2,256]{4,1,3,2,0:T(4,128)(2,1)} %collective-permute-done.1) | data formatting | bytes 229376 | tf_op jit(solution)/shard_map/ppermute | solution.py:83
  28.8 0.0 collective-permute-done
  28.8 1.0 %copy.6 = bf16[4,4,7,2,256]{4,3,2,1,0:T(2,128)(2,1)S(1)} copy(bf16[4,4,7,2,256]{4,1,3,2,0:T(4,128)(2,1)} %collective-permute-done) | data formatting | bytes 229376 | tf_op jit(solution)/shard_map/ppermute | solution.py:82
  29.8 0.1 pad_maximum_fusion
  30.0 0.3 copy.11
  30.3 0.1 broadcast_in_dim.4.m_ref
  30.3 3.1 %shard_map.46.x_ref = bf16[16,80,256]{2,1,0:T(8,128)(2,1)S(1)} custom-call(bf16[16,112,256]{2,1,0:T(8,128)(2,1)S(1)} %bitcast.31, bf16[3,3,256,256]{3,2,1,0:T(8,128)(2,1)S(1)} %get-tuple-element.6.w_ref, f32[16,256]{1,0:T(8,128)S(1)} %get-tuple-element.16.k_ref, bf16[256,256]{1,0:T(8,128)(2,1)S(1)} %get-tuple-element.14.p_ref, ...), custom_call_target="tpu_custom_call" | custom-call | flops 1677721600 | bytes 2883584 | tf_op jit(solution)/shard_map/pallas_call | solution.py:51
  33.5 0.1 broadcast_in_dim.5.m_ref
  33.5 1.9 %shard_map.47 = bf16[16,48,256]{2,1,0:T(8,128)(2,1)S(1)} custom-call(bf16[16,80,256]{2,1,0:T(8,128)(2,1)S(1)} %shard_map.46.x_ref, bf16[3,3,256,256]{3,2,1,0:T(8,128)(2,1)S(1)} %get-tuple-element.5.w_ref, f32[16,256]{1,0:T(8,128)S(1)} %get-tuple-element.15.k_ref, bf16[256,256]{1,0:T(8,128)(2,1)S(1)} %get-tuple-element.13.p_ref, ...), custom_call_target="tpu_custom_call" | custom-call | flops 1006632960 | bytes 2359296 | tf_op jit(solution)/shard_map/pallas_call | solution.py:51
  35.5 9.8 %all_to_all.23 = bf16[16,3,12,256]{3,2,1,0:T(8,128)(2,1)S(1)} all-to-all(bf16[16,3,12,256]{3,2,1,0:T(8,128)(2,1)S(1)} %bitcast.32), channel_id=1, replica_groups=mesh['groups'=2,'tm'=4,'width'=4] {'tm'}, dimensions={0} | all-to-all | bytes 589824 | tf_op jit(solution)/shard_map/all_to_all | solution.py:100
  45.3 0.9 %copy.12 = bf16[4,4,3,12,256]{4,1,3,2,0:T(4,128)(2,1)} copy(bf16[4,4,3,12,256]{4,3,2,1,0:T(8,128)(2,1)S(1)} %bitcast.33) | data formatting | bytes 589824 | tf_op jit(solution)/shard_map/all_to_all | solution.py:100
  (10 shorter events, 0.1 us)
Async XLA Ops:
  1.4 6.1 %copy-start = (bf16[2,256,256]{2,1,0:T(8,128)(2,1)S(1)}, bf16[2,256,256]{2,1,0:T(8,128)(2,1)}, u32[]{:S(2)}) copy-start(bf16[2,256,256]{2,1,0:T(8,128)(2,1)} %param.7) | copy-start | bytes 786436
  2.9 14.8 %all-to-all-start = ((bf16[4,4,7,12,256]{4,1,3,2,0:T(4,128)(2,1)}), bf16[4,4,7,12,256]{4,1,3,2,0:T(4,128)(2,1)S(1)}, u32[]{:S(2)}, u32[]{:S(2)}) async-start(bf16[4,4,7,12,256]{4,1,3,2,0:T(4,128)(2,1)} %pad_maximum_fusion.1), calls=%async_computation | async-start | bytes 1376256 | tf_op jit(solution)/shard_map/all_to_all | solution.py:77
  7.5 17.6 %copy-start.1 = (f32[2,16,256]{2,1,0:T(8,128)S(1)}, f32[2,16,256]{2,1,0:T(8,128)}, u32[]{:S(2)}) copy-start(f32[2,16,256]{2,1,0:T(8,128)} %param.6) | copy-start | bytes 98308
  18.4 9.4 %collective-permute-start.1 = (bf16[4,4,7,2,256]{4,1,3,2,0:T(4,128)(2,1)}, bf16[4,4,7,2,256]{4,1,3,2,0:T(4,128)(2,1)}, u32[]{:S(2)}, u32[]{:S(2)}) collective-permute-start(bf16[4,4,7,2,256]{4,1,3,2,0:T(4,128)(2,1)} %get-tuple-element.8), channel_id=1, source_target_pairs={{1,0},{2,1},{3,2},{5,4},{6,5},{7,6},{9,8},{10,9},{11,10},{13,12},{... | collective-permute-start | bytes 344072 | tf_op jit(solution)/shard_map/ppermute | solution.py:83
  19.7 9.1 %collective-permute-start = (bf16[4,4,7,2,256]{4,1,3,2,0:T(4,128)(2,1)S(1)}, bf16[4,4,7,2,256]{4,1,3,2,0:T(4,128)(2,1)}, u32[]{:S(2)}, u32[]{:S(2)}) collective-permute-start(bf16[4,4,7,2,256]{4,1,3,2,0:T(4,128)(2,1)S(1)} %get-tuple-element.7), channel_id=1, source_target_pairs={{0,1},{1,2},{2,3},{4,5},{5,6},{6,7},{8,9},{9,10},{10,11},{12,13},{... | collective-permute-start | bytes 344072 | tf_op jit(solution)/shard_map/ppermute | solution.py:82

commit v6 on v5

--- a/solution.py
+++ b/solution.py
@@ -78,13 +78,11 @@
 
     up = [(i, i + 1) for i in range(sides - 1)]
     down = [(i + 1, i) for i in range(sides - 1)]
-    edge = (bands * frames, rows + 2 * halo, halo, chans)
-    before = lax.ppermute(received[:, :, :, cols - halo :], "width", up).reshape(edge)
-    after = lax.ppermute(received[:, :, :, :halo], "width", down).reshape(edge)
-    gathered = received.reshape(bands * frames, rows + 2 * halo, cols, chans)
-    spare = jnp.zeros(gathered.shape[:2] + (pitch - cols - 2 * halo, chans), gathered.dtype)
-    state = jnp.concatenate([before, gathered, after, spare], axis=2)
-    state = state.reshape(state.shape[0], -1, chans)
+    before = lax.ppermute(received[:, :, :, cols - halo :], "width", up)
+    after = lax.ppermute(received[:, :, :, :halo], "width", down)
+    spare = jnp.zeros(received.shape[:3] + (pitch - cols - 2 * halo, chans), received.dtype)
+    state = jnp.concatenate([before, received, after, spare], axis=3)
+    state = state.reshape(bands * frames, -1, chans)
 
     for b in range(BLOCKS):
         left = halo - 1 - b

time: 46.5 us -> 45.6 us (0.981)
  local copies, waits for them, and re-layouts: 10 us -> 4.57 us
  waiting for transfers between devices: 8.36 us -> 13.7 us
  starting transfers between devices: 11 us -> 9.71 us
  other arithmetic: 1.79 us -> 2.32 us
    ppermute x2, waiting for transfers between devices: 0.01 us -> 5.36 us  [the longest x1 4.34 us: shards(): after = lax.ppermute(received[:, :, :, :halo], 'width', down)]
    ppermute x2 -> x0, local copies, waits for them, and re-layouts: 1.98 us -> none  [the longest x1 0.99 us: shards(): after = lax.ppermute(received[:, :, :, :halo], 'width', down).reshape(edge)]
    reshape x3 -> x0, local copies, waits for them, and re-layouts: 1.53 us -> none  [the longest x1 1.5 us: shards(): gathered = received.reshape(bands * frames, rows + 2 * halo, cols, chans)]
    ppermute x2, starting transfers between devices: 6.75 us -> 5.48 us  [the longest x1 4.18 us: shards(): before = lax.ppermute(received[:, :, :, cols - halo:], 'width', up)]
    all_to_all x1 -> x0, local copies, waits for them, and re-layouts: 1.12 us -> none  [shards(): received = lax.all_to_all(pieces, 'tm', 0, 0, tiled=False)]
    slice x1, local copies, waits for them, and re-layouts: 0.73 us -> 0.08 us  [shards(): before = lax.ppermute(received[:, :, :, cols - halo:], 'width', up)]
    concatenate x1, other arithmetic: 0.11 us -> 0.65 us  [shards(): state = jnp.concatenate([before, received, after, spare], axis=3)]
  transfers between devices with their start and end apart: 3 -> 3, of which waited for: 1 -> 3; matrix products, arithmetic and copies ran while one was open for 13% -> 5% of each run, Pallas kernels for 0% -> 0%
where the time goes in v6:
time: 45.6 us; the launch traced here: 45.3 us
  waiting for transfers between devices  13.7 us (30%)
  blocking collectives  9.8 us (21%)
  starting transfers between devices  9.71 us (21%)
  Pallas kernels  5.04 us (11%)
  local copies, waits for them, and re-layouts  4.57 us (10%)
  other arithmetic  2.32 us (5%)
    all_to_all x1, blocking collectives, shards(): return lax.all_to_all(state, 'tm', 0, 1, tiled=True)  9.8 us
    all_to_all x1, waiting for transfers between devices, shards(): received = lax.all_to_all(pieces, 'tm', 0, 0, tiled=False)  8.35 us
    pallas_call x2, Pallas kernels, block(): pl.pallas_call(functools.partial(block_kernel, count=count, pitch=pitch),...  5.04 us
    ppermute x1, waiting for transfers between devices, shards(): after = lax.ppermute(received[:, :, :, :halo], 'width', down)  4.34 us
    all_to_all x1, starting transfers between devices, shards(): received = lax.all_to_all(pieces, 'tm', 0, 0, tiled=False)  4.24 us
    ppermute x1, starting transfers between devices, shards(): before = lax.ppermute(received[:, :, :, cols - halo:], 'width', up)  4.18 us
    squeeze x3, local copies, waits for them, and re-layouts, shards(): state = block(state, conv_w[b], depth_k[b], proj_w[b], mask, pitch)  1.81 us
    another operation x1, other arithmetic, shards(): jnp.stack([padded[:, r * rows:r * rows + rows + 2 * halo] for r in range(...  1.48 us
  transfers between devices with their start and end apart: 3, of which 3 were waited for; matrix products, arithmetic and copies ran while one was open for 5% of the time, Pallas kernels for 0%

profile of v6, /device:TPU:0, one launch (start us, length us, event | category | flops | bytes accessed | tf_op | source)
XLA Modules:
  0.0 45.3 jit_solution(16512225481435892342)
XLA Ops:
  0.0 1.4 %fusion = (bf16[1,4,7,12,256]{4,1,3,2,0:T(4,128)(2,1)S(1)}, bf16[1,4,7,12,256]{4,1,3,2,0:T(4,128)(2,1)S(1)}, bf16[1,4,7,12,256]{4,1,3,2,0:T(4,128)(2,1)S(1)}, bf16[1,4,7,12,256]{4,1,3,2,0:T(4,128)(2,1)S(1)}) fusion(bf16[4,12,12,256]{3,0,2,1:T(4,128)(2,1)} %param.4), kind=kLoop, calls=%fused_computation.6 | loop fusion | bytes 1327104 | tf_op jit(solution)/shard_map/stack | solution.py:76
  1.4 0.0 copy-start
  1.4 1.5 %pad_maximum_fusion.1 = bf16[4,4,7,12,256]{4,1,3,2,0:T(4,128)(2,1)} fusion(bf16[1,4,7,12,256]{4,1,3,2,0:T(4,128)(2,1)S(1)} %get-tuple-element.10, bf16[1,4,7,12,256]{4,1,3,2,0:T(4,128)(2,1)S(1)} %get-tuple-element.11, bf16[1,4,7,12,256]{4,1,3,2,0:T(4,128)(2,1)S(1)} %get-tuple-element.12, bf16[1,4,7,12,256]{4,1,3,2,0:T(4,128)(2,1)S(1)} %get-tuple-element.9), kind=kLoop, calls=%fused_computation.3 | loop fusion | flops 1032192 | bytes 1376256 | tf_op jit(solution)/shard_map/stack | solution.py:76
  2.9 4.2 %all-to-all-start = ((bf16[4,4,7,12,256]{4,1,3,2,0:T(4,128)(2,1)}), bf16[4,4,7,12,256]{4,1,3,2,0:T(4,128)(2,1)S(1)}, u32[]{:S(2)}, u32[]{:S(2)}) async-start(bf16[4,4,7,12,256]{4,1,3,2,0:T(4,128)(2,1)} %pad_maximum_fusion.1), calls=%async_computation | async-start | bytes 1376256 | tf_op jit(solution)/shard_map/all_to_all | solution.py:77
  7.2 0.1 and_convert_fusion
  7.2 0.1 reshape.86
  7.3 0.1 and_convert_fusion.1
  7.4 0.1 reshape.87
  7.5 0.0 copy-done
  7.5 0.0 copy-start.1
  7.5 1.8 %slice_bitcast_fusion = (bf16[3,3,256,256]{3,2,1,0:T(8,128)(2,1)S(1)}, bf16[3,3,256,256]{3,2,1,0:T(8,128)(2,1)S(1)}) fusion(bf16[2,3,3,256,256]{4,3,2,1,0:T(8,128)(2,1)} %param.5), kind=kLoop, calls=%fused_computation | loop fusion | bytes 4718592 | tf_op jit(solution)/shard_map/squeeze | solution.py:95
  9.3 8.3 %all-to-all-done = bf16[4,4,7,12,256]{4,1,3,2,0:T(4,128)(2,1)S(1)} async-done(((bf16[4,4,7,12,256]{4,1,3,2,0:T(4,128)(2,1)}), bf16[4,4,7,12,256]{4,1,3,2,0:T(4,128)(2,1)S(1)}, u32[]{:S(2)}, u32[]{:S(2)}) %all-to-all-start) | async-done | bytes 688160 | tf_op jit(solution)/shard_map/all_to_all | solution.py:77
  17.7 0.1 fusion.6
  17.8 4.2 %collective-permute-start = (bf16[4,4,7,2,256]{4,1,3,2,0:T(4,128)(2,1)S(1)}, bf16[4,4,7,2,256]{4,1,3,2,0:T(4,128)(2,1)S(1)}, u32[]{:S(2)}, u32[]{:S(2)}) collective-permute-start(bf16[4,4,7,2,256]{4,1,3,2,0:T(4,128)(2,1)S(1)} %get-tuple-element.7), channel_id=1, source_target_pairs={{0,1},{1,2},{2,3},{4,5},{5,6},{6,7},{8,9},{9,10},{10,11},{12,13},{... | collective-permute-start | bytes 344072 | tf_op jit(solution)/shard_map/ppermute | solution.py:81
  21.9 1.3 %collective-permute-start.1 = (bf16[4,4,7,2,256]{4,1,3,2,0:T(4,128)(2,1)S(1)}, bf16[4,4,7,2,256]{4,1,3,2,0:T(4,128)(2,1)S(1)}, u32[]{:S(2)}, u32[]{:S(2)}) collective-permute-start(bf16[4,4,7,2,256]{4,1,3,2,0:T(4,128)(2,1)S(1)} %get-tuple-element.8), channel_id=1, source_target_pairs={{1,0},{2,1},{3,2},{5,4},{6,5},{7,6},{9,8},{10,9},{11,10},{13,12},{... | collective-permute-start | bytes 344072 | tf_op jit(solution)/shard_map/ppermute | solution.py:82
  23.2 0.0 copy-done.1
  23.3 1.0 %collective-permute-done = bf16[4,4,7,2,256]{4,1,3,2,0:T(4,128)(2,1)S(1)} collective-permute-done((bf16[4,4,7,2,256]{4,1,3,2,0:T(4,128)(2,1)S(1)}, bf16[4,4,7,2,256]{4,1,3,2,0:T(4,128)(2,1)S(1)}, u32[]{:S(2)}, u32[]{:S(2)}) %collective-permute-start) | collective-permute-done | bytes 114720 | tf_op jit(solution)/shard_map/ppermute | solution.py:81
  24.3 4.3 %collective-permute-done.1 = bf16[4,4,7,2,256]{4,1,3,2,0:T(4,128)(2,1)S(1)} collective-permute-done((bf16[4,4,7,2,256]{4,1,3,2,0:T(4,128)(2,1)S(1)}, bf16[4,4,7,2,256]{4,1,3,2,0:T(4,128)(2,1)S(1)}, u32[]{:S(2)}, u32[]{:S(2)}) %collective-permute-start.1) | collective-permute-done | bytes 114720 | tf_op jit(solution)/shard_map/ppermute | solution.py:82
  28.6 0.6 %pad_maximum_fusion = bf16[4,4,7,16,256]{4,1,3,2,0:T(4,128)(2,1)S(1)} fusion(bf16[4,4,7,2,256]{4,1,3,2,0:T(4,128)(2,1)S(1)} %collective-permute-done.1, bf16[4,4,7,12,256]{4,1,3,2,0:T(4,128)(2,1)S(1)} %all-to-all-done, bf16[4,4,7,2,256]{4,1,3,2,0:T(4,128)(2,1)S(1)} %collective-permute-done), kind=kLoop, calls=%fused_computation.2 | loop fusion | flops 917504 | bytes 1835008 | tf_op jit(solution)/shard_map/concatenate | solution.py:84
  29.3 0.1 copy.5
  29.4 0.1 broadcast_in_dim.4.m_ref
  29.5 3.1 %shard_map.46.x_ref = bf16[16,80,256]{2,1,0:T(8,128)(2,1)S(1)} custom-call(bf16[16,112,256]{2,1,0:T(8,128)(2,1)S(1)} %bitcast.27, bf16[3,3,256,256]{3,2,1,0:T(8,128)(2,1)S(1)} %get-tuple-element.6.w_ref, f32[16,256]{1,0:T(8,128)S(1)} %get-tuple-element.16.k_ref, bf16[256,256]{1,0:T(8,128)(2,1)S(1)} %get-tuple-element.14.p_ref, ...), custom_call_target="tpu_custom_call" | custom-call | flops 1677721600 | bytes 2883584 | tf_op jit(solution)/shard_map/pallas_call | solution.py:51
  32.6 0.1 broadcast_in_dim.5.m_ref
  32.7 1.9 %shard_map.47 = bf16[16,48,256]{2,1,0:T(8,128)(2,1)S(1)} custom-call(bf16[16,80,256]{2,1,0:T(8,128)(2,1)S(1)} %shard_map.46.x_ref, bf16[3,3,256,256]{3,2,1,0:T(8,128)(2,1)S(1)} %get-tuple-element.5.w_ref, f32[16,256]{1,0:T(8,128)S(1)} %get-tuple-element.15.k_ref, bf16[256,256]{1,0:T(8,128)(2,1)S(1)} %get-tuple-element.13.p_ref, ...), custom_call_target="tpu_custom_call" | custom-call | flops 1006632960 | bytes 2359296 | tf_op jit(solution)/shard_map/pallas_call | solution.py:51
  34.6 9.8 %all_to_all.23 = bf16[16,3,12,256]{3,2,1,0:T(8,128)(2,1)S(1)} all-to-all(bf16[16,3,12,256]{3,2,1,0:T(8,128)(2,1)S(1)} %bitcast.28), channel_id=1, replica_groups=mesh['groups'=2,'tm'=4,'width'=4] {'tm'}, dimensions={0} | all-to-all | bytes 589824 | tf_op jit(solution)/shard_map/all_to_all | solution.py:98
  44.4 0.9 %copy.6 = bf16[4,4,3,12,256]{4,1,3,2,0:T(4,128)(2,1)} copy(bf16[4,4,3,12,256]{4,3,2,1,0:T(8,128)(2,1)S(1)} %bitcast.29) | data formatting | bytes 589824 | tf_op jit(solution)/shard_map/all_to_all | solution.py:98
  (8 shorter events, 0.1 us)
Async XLA Ops:
  1.4 6.1 %copy-start = (bf16[2,256,256]{2,1,0:T(8,128)(2,1)S(1)}, bf16[2,256,256]{2,1,0:T(8,128)(2,1)}, u32[]{:S(2)}) copy-start(bf16[2,256,256]{2,1,0:T(8,128)(2,1)} %param.7) | copy-start | bytes 786436
  2.9 14.8 %all-to-all-start = ((bf16[4,4,7,12,256]{4,1,3,2,0:T(4,128)(2,1)}), bf16[4,4,7,12,256]{4,1,3,2,0:T(4,128)(2,1)S(1)}, u32[]{:S(2)}, u32[]{:S(2)}) async-start(bf16[4,4,7,12,256]{4,1,3,2,0:T(4,128)(2,1)} %pad_maximum_fusion.1), calls=%async_computation | async-start | bytes 1376256 | tf_op jit(solution)/shard_map/all_to_all | solution.py:77
  7.5 15.7 %copy-start.1 = (f32[2,16,256]{2,1,0:T(8,128)S(1)}, f32[2,16,256]{2,1,0:T(8,128)}, u32[]{:S(2)}) copy-start(f32[2,16,256]{2,1,0:T(8,128)} %param.6) | copy-start | bytes 98308
  17.8 6.5 %collective-permute-start = (bf16[4,4,7,2,256]{4,1,3,2,0:T(4,128)(2,1)S(1)}, bf16[4,4,7,2,256]{4,1,3,2,0:T(4,128)(2,1)S(1)}, u32[]{:S(2)}, u32[]{:S(2)}) collective-permute-start(bf16[4,4,7,2,256]{4,1,3,2,0:T(4,128)(2,1)S(1)} %get-tuple-element.7), channel_id=1, source_target_pairs={{0,1},{1,2},{2,3},{4,5},{5,6},{6,7},{8,9},{9,10},{10,11},{12,13},{... | collective-permute-start | bytes 344072 | tf_op jit(solution)/shard_map/ppermute | solution.py:81
  21.9 6.7 %collective-permute-start.1 = (bf16[4,4,7,2,256]{4,1,3,2,0:T(4,128)(2,1)S(1)}, bf16[4,4,7,2,256]{4,1,3,2,0:T(4,128)(2,1)S(1)}, u32[]{:S(2)}, u32[]{:S(2)}) collective-permute-start(bf16[4,4,7,2,256]{4,1,3,2,0:T(4,128)(2,1)S(1)} %get-tuple-element.8), channel_id=1, source_target_pairs={{1,0},{2,1},{3,2},{5,4},{6,5},{7,6},{9,8},{10,9},{11,10},{13,12},{... | collective-permute-start | bytes 344072 | tf_op jit(solution)/shard_map/ppermute | solution.py:82

commit v7 on v6

--- a/solution.py
+++ b/solution.py
@@ -76,10 +76,16 @@
     pieces = jnp.stack([padded[:, r * rows : r * rows + rows + 2 * halo] for r in range(bands)])
     received = lax.all_to_all(pieces, "tm", 0, 0, tiled=False)
 
-    up = [(i, i + 1) for i in range(sides - 1)]
-    down = [(i + 1, i) for i in range(sides - 1)]
-    before = lax.ppermute(received[:, :, :, cols - halo :], "width", up)
-    after = lax.ppermute(received[:, :, :, :halo], "width", down)
+    lead = received[:, :, :, :halo]
+    tail = received[:, :, :, cols - halo :]
+    target = lax.broadcasted_iota(jnp.int32, (sides,) + (1,) * lead.ndim, 0)
+    zero = jnp.zeros((), lead.dtype)
+    edges = jnp.where(target == side + 1, tail[None], jnp.where(target == side - 1, lead[None], zero))
+    edges = lax.all_to_all(edges, "width", 0, 0, tiled=False)
+    before = lax.dynamic_index_in_dim(edges, jnp.maximum(side - 1, 0), 0, keepdims=False)
+    after = lax.dynamic_index_in_dim(edges, jnp.minimum(side + 1, sides - 1), 0, keepdims=False)
+    before = jnp.where(side > 0, before, zero)
+    after = jnp.where(side < sides - 1, after, zero)
     spare = jnp.zeros(received.shape[:3] + (pitch - cols - 2 * halo, chans), received.dtype)
     state = jnp.concatenate([before, received, after, spare], axis=3)
     state = state.reshape(bands * frames, -1, chans)

time: 45.6 us -> 55.3 us (1.21)
  waiting for transfers between devices: 13.7 us -> 21.2 us
  other arithmetic: 2.32 us -> 4.44 us
    all_to_all x0 -> x1, waiting for transfers between devices: none -> 11 us  [shards(): edges = lax.all_to_all(edges, 'width', 0, 0, tiled=False)]
    all_to_all x0 -> x1, starting transfers between devices: none -> 5.57 us  [shards(): edges = lax.all_to_all(edges, 'width', 0, 0, tiled=False)]
    ppermute x2 -> x0, starting transfers between devices: 5.48 us -> none  [the longest x1 4.18 us: shards(): before = lax.ppermute(received[:, :, :, cols - halo:], 'width', up)]
    ppermute x2 -> x0, waiting for transfers between devices: 5.36 us -> none  [the longest x1 4.34 us: shards(): after = lax.ppermute(received[:, :, :, :halo], 'width', down)]
    select_n x0 -> x2, other arithmetic: none -> 2.11 us  [the longest x1 1.06 us: shards(): jnp.where(target == side + 1, tail[None], jnp.where(target == side - 1, l...]
    all_to_all x1, waiting for transfers between devices: 8.35 us -> 10.1 us  [shards(): received = lax.all_to_all(pieces, 'tm', 0, 0, tiled=False)]
  transfers between devices with their start and end apart: 3 -> 2, of which waited for: 3 -> 2; matrix products, arithmetic and copies ran while one was open for 5% -> 4% of each run, Pallas kernels for 0% -> 0%
where the time goes in v7:
time: 55.3 us; the launch traced here: 55 us
  waiting for transfers between devices  21.2 us (38%)
  starting transfers between devices  9.8 us (18%)
  blocking collectives  9.8 us (18%)
  Pallas kernels  5.04 us (9%)
  local copies, waits for them, and re-layouts  4.59 us (8%)
  other arithmetic  4.44 us (8%)
    all_to_all x1, waiting for transfers between devices, shards(): edges = lax.all_to_all(edges, 'width', 0, 0, tiled=False)  11 us
    all_to_all x1, waiting for transfers between devices, shards(): received = lax.all_to_all(pieces, 'tm', 0, 0, tiled=False)  10.1 us
    all_to_all x1, blocking collectives, shards(): return lax.all_to_all(state, 'tm', 0, 1, tiled=True)  9.8 us
    all_to_all x1, starting transfers between devices, shards(): edges = lax.all_to_all(edges, 'width', 0, 0, tiled=False)  5.57 us
    pallas_call x2, Pallas kernels, block(): pl.pallas_call(functools.partial(block_kernel, count=count, pitch=pitch),...  5.04 us
    all_to_all x1, starting transfers between devices, shards(): received = lax.all_to_all(pieces, 'tm', 0, 0, tiled=False)  4.24 us
    squeeze x3, local copies, waits for them, and re-layouts, shards(): state = block(state, conv_w[b], depth_k[b], proj_w[b], mask, pitch)  1.83 us
    another operation x1, other arithmetic, shards(): jnp.stack([padded[:, r * rows:r * rows + rows + 2 * halo] for r in range(...  1.47 us
  transfers between devices with their start and end apart: 2, of which 2 were waited for; matrix products, arithmetic and copies ran while one was open for 4% of the time, Pallas kernels for 0%

profile of v7, /device:TPU:0, one launch (start us, length us, event | category | flops | bytes accessed | tf_op | source)
XLA Modules:
  0.0 55.0 jit_solution(15879176408985920446)
XLA Ops:
  0.0 1.4 %fusion = (bf16[1,4,7,12,256]{4,1,3,2,0:T(4,128)(2,1)S(1)}, bf16[1,4,7,12,256]{4,1,3,2,0:T(4,128)(2,1)S(1)}, bf16[1,4,7,12,256]{4,1,3,2,0:T(4,128)(2,1)S(1)}, bf16[1,4,7,12,256]{4,1,3,2,0:T(4,128)(2,1)S(1)}) fusion(bf16[4,12,12,256]{3,0,2,1:T(4,128)(2,1)} %param.4), kind=kLoop, calls=%fused_computation.7 | loop fusion | bytes 1327104 | tf_op jit(solution)/shard_map/stack | solution.py:76
  1.4 1.5 %pad_maximum_fusion.1 = bf16[4,4,7,12,256]{4,1,3,2,0:T(4,128)(2,1)} fusion(bf16[1,4,7,12,256]{4,1,3,2,0:T(4,128)(2,1)S(1)} %get-tuple-element.12, bf16[1,4,7,12,256]{4,1,3,2,0:T(4,128)(2,1)S(1)} %get-tuple-element.13, bf16[1,4,7,12,256]{4,1,3,2,0:T(4,128)(2,1)S(1)} %get-tuple-element.14, bf16[1,4,7,12,256]{4,1,3,2,0:T(4,128)(2,1)S(1)} %get-tuple-element.11), kind=kLoop, calls=%fused_computation.3 | loop fusion | flops 1032192 | bytes 1376256 | tf_op jit(solution)/shard_map/stack | solution.py:76
  2.8 4.2 %all-to-all-start = ((bf16[4,4,7,12,256]{4,1,3,2,0:T(4,128)(2,1)}), bf16[4,4,7,12,256]{4,1,3,2,0:T(4,128)(2,1)S(1)}, u32[]{:S(2)}, u32[]{:S(2)}) async-start(bf16[4,4,7,12,256]{4,1,3,2,0:T(4,128)(2,1)} %pad_maximum_fusion.1), calls=%async_computation | async-start | bytes 1376256 | tf_op jit(solution)/shard_map/all_to_all | solution.py:77
  7.1 0.0 copy-start.1
  7.1 0.0 copy-start
  7.2 0.1 and_convert_fusion
  7.2 0.1 reshape.104
  7.3 0.1 and_convert_fusion.1
  7.4 0.1 reshape.105
  7.5 10.1 %all-to-all-done = bf16[4,4,7,12,256]{4,1,3,2,0:T(4,128)(2,1)S(1)} async-done(((bf16[4,4,7,12,256]{4,1,3,2,0:T(4,128)(2,1)}), bf16[4,4,7,12,256]{4,1,3,2,0:T(4,128)(2,1)S(1)}, u32[]{:S(2)}, u32[]{:S(2)}) %all-to-all-start) | async-done | bytes 688160 | tf_op jit(solution)/shard_map/all_to_all | solution.py:77
  17.6 0.1 fusion.6
  17.7 1.1 %select_select_fusion = bf16[4,4,4,7,2,256]{5,2,4,3,1,0:T(4,128)(2,1)} fusion(pred[4]{0:T(512)(128)(4,1)S(1)} %get-tuple-element.20, pred[4]{0:T(512)(128)(4,1)S(1)} %get-tuple-element.19, bf16[4,4,7,2,256]{4,1,3,2,0:T(4,128)(2,1)S(1)} %get-tuple-element.8, bf16[4,4,7,2,256]{4,1,3,2,0:T(4,128)(2,1)S(1)} %get-tuple-element.7), kind=kLoop, calls=%fused_computation.4 | loop fusion | flops 458752 | bytes 688136 | tf_op jit(solution)/shard_map/jit(_where)/select_n | solution.py:83
  18.8 5.6 %all-to-all-start.1 = ((bf16[4,4,4,7,2,256]{5,2,4,3,1,0:T(4,128)(2,1)}), bf16[4,4,4,7,2,256]{5,2,4,3,1,0:T(4,128)(2,1)}, u32[]{:S(2)}, u32[]{:S(2)}) async-start(bf16[4,4,4,7,2,256]{5,2,4,3,1,0:T(4,128)(2,1)} %select_select_fusion), calls=%async_computation.1 | async-start | bytes 917504 | tf_op jit(solution)/shard_map/all_to_all | solution.py:84
  24.4 0.0 copy-done.1
  24.4 0.0 copy-done
  24.4 1.8 %slice_bitcast_fusion = (bf16[3,3,256,256]{3,2,1,0:T(8,128)(2,1)S(1)}, bf16[3,3,256,256]{3,2,1,0:T(8,128)(2,1)S(1)}) fusion(bf16[2,3,3,256,256]{4,3,2,1,0:T(8,128)(2,1)} %param.5), kind=kLoop, calls=%fused_computation | loop fusion | bytes 4718592 | tf_op jit(solution)/shard_map/squeeze | solution.py:101
  26.2 11.0 %all-to-all-done.1 = bf16[4,4,4,7,2,256]{5,2,4,3,1,0:T(4,128)(2,1)} async-done(((bf16[4,4,4,7,2,256]{5,2,4,3,1,0:T(4,128)(2,1)}), bf16[4,4,4,7,2,256]{5,2,4,3,1,0:T(4,128)(2,1)}, u32[]{:S(2)}, u32[]{:S(2)}) %all-to-all-start.1) | async-done | bytes 458784 | tf_op jit(solution)/shard_map/all_to_all | solution.py:84
  37.3 1.1 %select_bitcast_fusion.1 = (bf16[4,4,7,2,256]{4,1,3,2,0:T(4,128)(2,1)S(1)}, bf16[4,4,7,2,256]{4,1,3,2,0:T(4,128)(2,1)S(1)}) fusion(bf16[4,4,4,7,2,256]{5,2,4,3,1,0:T(4,128)(2,1)} %all-to-all-done.1, s32[]{:T(128)S(6)} %max.3, pred[]{:T(512)S(6)} %gt.3, s32[]{:T(128)S(6)} %select_n.39, pred[]{:T(512)S(6)} %lt.42), kind=kLoop, calls=%fused_computation.14 | loop fusion | flops 114688 | bytes 458762 | tf_op jit(solution)/shard_map/jit(_where)/select_n | solution.py:87
  38.3 0.6 %pad_maximum_fusion = bf16[4,4,7,16,256]{4,1,3,2,0:T(4,128)(2,1)S(1)} fusion(bf16[4,4,7,2,256]{4,1,3,2,0:T(4,128)(2,1)S(1)} %get-tuple-element.10, bf16[4,4,7,12,256]{4,1,3,2,0:T(4,128)(2,1)S(1)} %all-to-all-done, bf16[4,4,7,2,256]{4,1,3,2,0:T(4,128)(2,1)S(1)} %get-tuple-element.9), kind=kLoop, calls=%fused_computation.2 | loop fusion | flops 917504 | bytes 1835008 | tf_op jit(solution)/shard_map/concatenate | solution.py:90
  39.0 0.1 copy.5
  39.1 0.1 broadcast_in_dim.59.m_ref
  39.2 3.1 %shard_map.46.x_ref = bf16[16,80,256]{2,1,0:T(8,128)(2,1)S(1)} custom-call(bf16[16,112,256]{2,1,0:T(8,128)(2,1)S(1)} %bitcast.31, bf16[3,3,256,256]{3,2,1,0:T(8,128)(2,1)S(1)} %get-tuple-element.6.w_ref, f32[16,256]{1,0:T(8,128)S(1)} %get-tuple-element.18.k_ref, bf16[256,256]{1,0:T(8,128)(2,1)S(1)} %get-tuple-element.16.p_ref, ...), custom_call_target="tpu_custom_call" | custom-call | flops 1677721600 | bytes 2883584 | tf_op jit(solution)/shard_map/pallas_call | solution.py:51
  42.3 0.1 broadcast_in_dim.60.m_ref
  42.4 1.9 %shard_map.47 = bf16[16,48,256]{2,1,0:T(8,128)(2,1)S(1)} custom-call(bf16[16,80,256]{2,1,0:T(8,128)(2,1)S(1)} %shard_map.46.x_ref, bf16[3,3,256,256]{3,2,1,0:T(8,128)(2,1)S(1)} %get-tuple-element.5.w_ref, f32[16,256]{1,0:T(8,128)S(1)} %get-tuple-element.17.k_ref, bf16[256,256]{1,0:T(8,128)(2,1)S(1)} %get-tuple-element.15.p_ref, ...), custom_call_target="tpu_custom_call" | custom-call | flops 1006632960 | bytes 2359296 | tf_op jit(solution)/shard_map/pallas_call | solution.py:51
  44.3 9.8 %all_to_all.28 = bf16[16,3,12,256]{3,2,1,0:T(8,128)(2,1)S(1)} all-to-all(bf16[16,3,12,256]{3,2,1,0:T(8,128)(2,1)S(1)} %bitcast.32), channel_id=1, replica_groups=mesh['groups'=2,'tm'=4,'width'=4] {'tm'}, dimensions={0} | all-to-all | bytes 589824 | tf_op jit(solution)/shard_map/all_to_all | solution.py:104
  54.1 0.9 %copy.6 = bf16[4,4,3,12,256]{4,1,3,2,0:T(4,128)(2,1)} copy(bf16[4,4,3,12,256]{4,3,2,1,0:T(8,128)(2,1)S(1)} %bitcast.33) | data formatting | bytes 589824 | tf_op jit(solution)/shard_map/all_to_all | solution.py:104
  (10 shorter events, 0.1 us)
Async XLA Ops:
  2.8 14.8 %all-to-all-start = ((bf16[4,4,7,12,256]{4,1,3,2,0:T(4,128)(2,1)}), bf16[4,4,7,12,256]{4,1,3,2,0:T(4,128)(2,1)S(1)}, u32[]{:S(2)}, u32[]{:S(2)}) async-start(bf16[4,4,7,12,256]{4,1,3,2,0:T(4,128)(2,1)} %pad_maximum_fusion.1), calls=%async_computation | async-start | bytes 1376256 | tf_op jit(solution)/shard_map/all_to_all | solution.py:77
  7.1 17.3 %copy-start.1 = (f32[2,16,256]{2,1,0:T(8,128)S(1)}, f32[2,16,256]{2,1,0:T(8,128)}, u32[]{:S(2)}) copy-start(f32[2,16,256]{2,1,0:T(8,128)} %param.6) | copy-start | bytes 98308
  7.1 17.3 %copy-start = (bf16[2,256,256]{2,1,0:T(8,128)(2,1)S(1)}, bf16[2,256,256]{2,1,0:T(8,128)(2,1)}, u32[]{:S(2)}) copy-start(bf16[2,256,256]{2,1,0:T(8,128)(2,1)} %param.7) | copy-start | bytes 786436
  18.8 18.5 %all-to-all-start.1 = ((bf16[4,4,4,7,2,256]{5,2,4,3,1,0:T(4,128)(2,1)}), bf16[4,4,4,7,2,256]{5,2,4,3,1,0:T(4,128)(2,1)}, u32[]{:S(2)}, u32[]{:S(2)}) async-start(bf16[4,4,4,7,2,256]{5,2,4,3,1,0:T(4,128)(2,1)} %select_select_fusion), calls=%async_computation.1 | async-start | bytes 917504 | tf_op jit(solution)/shard_map/all_to_all | solution.py:84

commit v8 on v6

--- a/solution.py
+++ b/solution.py
@@ -72,8 +72,11 @@
     halo = BLOCKS
     pitch = -(-(cols + 2 * halo) // LANES) * LANES
 
-    padded = jnp.pad(video, ((0, 0), (halo, halo), (0, 0), (0, 0)))
-    pieces = jnp.stack([padded[:, r * rows : r * rows + rows + 2 * halo] for r in range(bands)])
+    spans = -(-(rows + 2 * halo) // rows)
+    padded = jnp.pad(video, ((0, 0), (halo, (bands + spans - 1) * rows - height - halo), (0, 0), (0, 0)))
+    windows = [padded[:, j * rows : (j + bands) * rows].reshape(frames, bands, rows, cols, chans) for j in range(spans)]
+    pieces = jnp.concatenate(windows, axis=2)[:, :, : rows + 2 * halo]
+    pieces = jnp.transpose(pieces, (1, 0, 2, 3, 4))
     received = lax.all_to_all(pieces, "tm", 0, 0, tiled=False)
 
     up = [(i, i + 1) for i in range(sides - 1)]

time: 45.6 us -> 45.6 us (level)
    another operation x1 -> x0, other arithmetic: 1.48 us -> none  [shards(): jnp.stack([padded[:, r * rows:r * rows + rows + 2 * halo] for r in range(...]
    slice x0 -> x1, local copies, waits for them, and re-layouts: none -> 1.47 us  [shards(): padded[:, j * rows:(j + bands) * rows]]
    another operation x1 -> x0, local copies, waits for them, and re-layouts: 1.36 us -> none  [shards(): jnp.stack([padded[:, r * rows:r * rows + rows + 2 * halo] for r in range(...]
    transpose x0 -> x1, other arithmetic: none -> 1.35 us  [shards(): pieces = jnp.transpose(pieces, (1, 0, 2, 3, 4))]
where the time goes in v8:
time: 45.6 us; the launch traced here: 45.3 us
  waiting for transfers between devices  13.7 us (30%)
  blocking collectives  9.8 us (21%)
  starting transfers between devices  9.71 us (21%)
  Pallas kernels  5.04 us (11%)
  local copies, waits for them, and re-layouts  4.67 us (10%)
  other arithmetic  2.18 us (5%)
    all_to_all x1, blocking collectives, shards(): return lax.all_to_all(state, 'tm', 0, 1, tiled=True)  9.8 us
    all_to_all x1, waiting for transfers between devices, shards(): received = lax.all_to_all(pieces, 'tm', 0, 0, tiled=False)  8.35 us
    pallas_call x2, Pallas kernels, block(): pl.pallas_call(functools.partial(block_kernel, count=count, pitch=pitch),...  5.04 us
    ppermute x1, waiting for transfers between devices, shards(): after = lax.ppermute(received[:, :, :, :halo], 'width', down)  4.34 us
    all_to_all x1, starting transfers between devices, shards(): received = lax.all_to_all(pieces, 'tm', 0, 0, tiled=False)  4.24 us
    ppermute x1, starting transfers between devices, shards(): before = lax.ppermute(received[:, :, :, cols - halo:], 'width', up)  4.18 us
    squeeze x3, local copies, waits for them, and re-layouts, shards(): state = block(state, conv_w[b], depth_k[b], proj_w[b], mask, pitch)  1.81 us
    slice x1, local copies, waits for them, and re-layouts, shards(): padded[:, j * rows:(j + bands) * rows]  1.47 us
  transfers between devices with their start and end apart: 3, of which 3 were waited for; matrix products, arithmetic and copies ran while one was open for 5% of the time, Pallas kernels for 0%

profile of v8, /device:TPU:0, one launch (start us, length us, event | category | flops | bytes accessed | tf_op | source)
XLA Modules:
  0.0 45.3 jit_solution(13667446849407237083)
XLA Ops:
  0.0 1.5 %pad_slice_fusion.2 = (bf16[4,12,12,256]{3,0,2,1:T(4,128)(2,1)S(1)}, bf16[4,12,12,256]{3,0,2,1:T(4,128)(2,1)S(1)}, bf16[4,12,12,256]{3,0,2,1:T(4,128)(2,1)S(1)}) fusion(bf16[4,12,12,256]{3,0,2,1:T(4,128)(2,1)} %param.4), kind=kLoop, calls=%fused_computation.8 | loop fusion | bytes 1179648 | tf_op jit(solution)/shard_map/slice | solution.py:77
  1.5 0.0 copy-start
  1.5 1.3 %fusion = bf16[4,4,7,12,256]{4,1,3,2,0:T(4,128)(2,1)} fusion(bf16[4,4,3,12,256]{4,0,3,2,1:T(4,128)(2,1)S(1)} %bitcast.29, bf16[4,4,3,12,256]{4,0,3,2,1:T(4,128)(2,1)S(1)} %bitcast.28, bf16[4,4,3,12,256]{4,0,3,2,1:T(4,128)(2,1)S(1)} %bitcast.27), kind=kLoop, calls=%fused_computation.4 | loop fusion | flops 688128 | bytes 1572864 | tf_op jit(solution)/shard_map/transpose | solution.py:79
  2.8 4.2 %all-to-all-start = ((bf16[4,4,7,12,256]{4,1,3,2,0:T(4,128)(2,1)}), bf16[4,4,7,12,256]{4,1,3,2,0:T(4,128)(2,1)S(1)}, u32[]{:S(2)}, u32[]{:S(2)}) async-start(bf16[4,4,7,12,256]{4,1,3,2,0:T(4,128)(2,1)} %fusion), calls=%async_computation | async-start | bytes 1376256 | tf_op jit(solution)/shard_map/all_to_all | solution.py:80
  7.1 0.1 and_convert_fusion
  7.2 0.1 reshape.98
  7.3 0.1 and_convert_fusion.1
  7.4 0.1 reshape.99
  7.5 0.0 copy-done
  7.5 0.0 copy-start.1
  7.5 1.8 %slice_bitcast_fusion = (bf16[3,3,256,256]{3,2,1,0:T(8,128)(2,1)S(1)}, bf16[3,3,256,256]{3,2,1,0:T(8,128)(2,1)S(1)}) fusion(bf16[2,3,3,256,256]{4,3,2,1,0:T(8,128)(2,1)} %param.5), kind=kLoop, calls=%fused_computation | loop fusion | bytes 4718592 | tf_op jit(solution)/shard_map/squeeze | solution.py:98
  9.3 8.3 %all-to-all-done = bf16[4,4,7,12,256]{4,1,3,2,0:T(4,128)(2,1)S(1)} async-done(((bf16[4,4,7,12,256]{4,1,3,2,0:T(4,128)(2,1)}), bf16[4,4,7,12,256]{4,1,3,2,0:T(4,128)(2,1)S(1)}, u32[]{:S(2)}, u32[]{:S(2)}) %all-to-all-start) | async-done | bytes 688160 | tf_op jit(solution)/shard_map/all_to_all | solution.py:80
  17.6 0.1 fusion.5
  17.7 4.2 %collective-permute-start = (bf16[4,4,7,2,256]{4,1,3,2,0:T(4,128)(2,1)S(1)}, bf16[4,4,7,2,256]{4,1,3,2,0:T(4,128)(2,1)S(1)}, u32[]{:S(2)}, u32[]{:S(2)}) collective-permute-start(bf16[4,4,7,2,256]{4,1,3,2,0:T(4,128)(2,1)S(1)} %get-tuple-element.7), channel_id=1, source_target_pairs={{0,1},{1,2},{2,3},{4,5},{5,6},{6,7},{8,9},{9,10},{10,11},{12,13},{... | collective-permute-start | bytes 344072 | tf_op jit(solution)/shard_map/ppermute | solution.py:84
  21.9 1.3 %collective-permute-start.1 = (bf16[4,4,7,2,256]{4,1,3,2,0:T(4,128)(2,1)S(1)}, bf16[4,4,7,2,256]{4,1,3,2,0:T(4,128)(2,1)S(1)}, u32[]{:S(2)}, u32[]{:S(2)}) collective-permute-start(bf16[4,4,7,2,256]{4,1,3,2,0:T(4,128)(2,1)S(1)} %get-tuple-element.8), channel_id=1, source_target_pairs={{1,0},{2,1},{3,2},{5,4},{6,5},{7,6},{9,8},{10,9},{11,10},{13,12},{... | collective-permute-start | bytes 344072 | tf_op jit(solution)/shard_map/ppermute | solution.py:85
  23.2 0.0 copy-done.1
  23.2 1.0 %collective-permute-done = bf16[4,4,7,2,256]{4,1,3,2,0:T(4,128)(2,1)S(1)} collective-permute-done((bf16[4,4,7,2,256]{4,1,3,2,0:T(4,128)(2,1)S(1)}, bf16[4,4,7,2,256]{4,1,3,2,0:T(4,128)(2,1)S(1)}, u32[]{:S(2)}, u32[]{:S(2)}) %collective-permute-start) | collective-permute-done | bytes 114720 | tf_op jit(solution)/shard_map/ppermute | solution.py:84
  24.3 4.3 %collective-permute-done.1 = bf16[4,4,7,2,256]{4,1,3,2,0:T(4,128)(2,1)S(1)} collective-permute-done((bf16[4,4,7,2,256]{4,1,3,2,0:T(4,128)(2,1)S(1)}, bf16[4,4,7,2,256]{4,1,3,2,0:T(4,128)(2,1)S(1)}, u32[]{:S(2)}, u32[]{:S(2)}) %collective-permute-start.1) | collective-permute-done | bytes 114720 | tf_op jit(solution)/shard_map/ppermute | solution.py:85
  28.6 0.6 %pad_maximum_fusion = bf16[4,4,7,16,256]{4,1,3,2,0:T(4,128)(2,1)S(1)} fusion(bf16[4,4,7,2,256]{4,1,3,2,0:T(4,128)(2,1)S(1)} %collective-permute-done.1, bf16[4,4,7,12,256]{4,1,3,2,0:T(4,128)(2,1)S(1)} %all-to-all-done, bf16[4,4,7,2,256]{4,1,3,2,0:T(4,128)(2,1)S(1)} %collective-permute-done), kind=kLoop, calls=%fused_computation.2 | loop fusion | flops 917504 | bytes 1835008 | tf_op jit(solution)/shard_map/concatenate | solution.py:87
  29.3 0.1 copy.9
  29.4 0.1 broadcast_in_dim.4.m_ref
  29.5 3.1 %shard_map.46.x_ref = bf16[16,80,256]{2,1,0:T(8,128)(2,1)S(1)} custom-call(bf16[16,112,256]{2,1,0:T(8,128)(2,1)S(1)} %bitcast.24, bf16[3,3,256,256]{3,2,1,0:T(8,128)(2,1)S(1)} %get-tuple-element.6.w_ref, f32[16,256]{1,0:T(8,128)S(1)} %get-tuple-element.15.k_ref, bf16[256,256]{1,0:T(8,128)(2,1)S(1)} %get-tuple-element.13.p_ref, ...), custom_call_target="tpu_custom_call" | custom-call | flops 1677721600 | bytes 2883584 | tf_op jit(solution)/shard_map/pallas_call | solution.py:51
  32.6 0.1 broadcast_in_dim.5.m_ref
  32.7 1.9 %shard_map.47 = bf16[16,48,256]{2,1,0:T(8,128)(2,1)S(1)} custom-call(bf16[16,80,256]{2,1,0:T(8,128)(2,1)S(1)} %shard_map.46.x_ref, bf16[3,3,256,256]{3,2,1,0:T(8,128)(2,1)S(1)} %get-tuple-element.5.w_ref, f32[16,256]{1,0:T(8,128)S(1)} %get-tuple-element.14.k_ref, bf16[256,256]{1,0:T(8,128)(2,1)S(1)} %get-tuple-element.12.p_ref, ...), custom_call_target="tpu_custom_call" | custom-call | flops 1006632960 | bytes 2359296 | tf_op jit(solution)/shard_map/pallas_call | solution.py:51
  34.6 9.8 %all_to_all.23 = bf16[16,3,12,256]{3,2,1,0:T(8,128)(2,1)S(1)} all-to-all(bf16[16,3,12,256]{3,2,1,0:T(8,128)(2,1)S(1)} %bitcast.25), channel_id=1, replica_groups=mesh['groups'=2,'tm'=4,'width'=4] {'tm'}, dimensions={0} | all-to-all | bytes 589824 | tf_op jit(solution)/shard_map/all_to_all | solution.py:101
  44.4 0.9 %copy.10 = bf16[4,4,3,12,256]{4,1,3,2,0:T(4,128)(2,1)} copy(bf16[4,4,3,12,256]{4,3,2,1,0:T(8,128)(2,1)S(1)} %bitcast.26) | data formatting | bytes 589824 | tf_op jit(solution)/shard_map/all_to_all | solution.py:101
  (8 shorter events, 0.1 us)
Async XLA Ops:
  1.5 6.0 %copy-start = (bf16[2,256,256]{2,1,0:T(8,128)(2,1)S(1)}, bf16[2,256,256]{2,1,0:T(8,128)(2,1)}, u32[]{:S(2)}) copy-start(bf16[2,256,256]{2,1,0:T(8,128)(2,1)} %param.7) | copy-start | bytes 786436
  2.8 14.8 %all-to-all-start = ((bf16[4,4,7,12,256]{4,1,3,2,0:T(4,128)(2,1)}), bf16[4,4,7,12,256]{4,1,3,2,0:T(4,128)(2,1)S(1)}, u32[]{:S(2)}, u32[]{:S(2)}) async-start(bf16[4,4,7,12,256]{4,1,3,2,0:T(4,128)(2,1)} %fusion), calls=%async_computation | async-start | bytes 1376256 | tf_op jit(solution)/shard_map/all_to_all | solution.py:80
  7.5 15.7 %copy-start.1 = (f32[2,16,256]{2,1,0:T(8,128)S(1)}, f32[2,16,256]{2,1,0:T(8,128)}, u32[]{:S(2)}) copy-start(f32[2,16,256]{2,1,0:T(8,128)} %param.6) | copy-start | bytes 98308
  17.7 6.5 %collective-permute-start = (bf16[4,4,7,2,256]{4,1,3,2,0:T(4,128)(2,1)S(1)}, bf16[4,4,7,2,256]{4,1,3,2,0:T(4,128)(2,1)S(1)}, u32[]{:S(2)}, u32[]{:S(2)}) collective-permute-start(bf16[4,4,7,2,256]{4,1,3,2,0:T(4,128)(2,1)S(1)} %get-tuple-element.7), channel_id=1, source_target_pairs={{0,1},{1,2},{2,3},{4,5},{5,6},{6,7},{8,9},{9,10},{10,11},{12,13},{... | collective-permute-start | bytes 344072 | tf_op jit(solution)/shard_map/ppermute | solution.py:84
  21.9 6.7 %collective-permute-start.1 = (bf16[4,4,7,2,256]{4,1,3,2,0:T(4,128)(2,1)S(1)}, bf16[4,4,7,2,256]{4,1,3,2,0:T(4,128)(2,1)S(1)}, u32[]{:S(2)}, u32[]{:S(2)}) collective-permute-start(bf16[4,4,7,2,256]{4,1,3,2,0:T(4,128)(2,1)S(1)} %get-tuple-element.8), channel_id=1, source_target_pairs={{1,0},{2,1},{3,2},{5,4},{6,5},{7,6},{9,8},{10,9},{11,10},{13,12},{... | collective-permute-start | bytes 344072 | tf_op jit(solution)/shard_map/ppermute | solution.py:85

commit v9 on v6

--- a/solution.py
+++ b/solution.py
@@ -11,7 +11,7 @@
 LANES = 16
 
 
-def block_kernel(x_ref, w_ref, k_ref, p_ref, m_ref, o_ref, *, count, pitch):
+def run_block(x_ref, w_ref, k_ref, p_ref, b, count, pitch):
     frames, _, chans = x_ref.shape
     total = frames * count
 
@@ -22,13 +22,13 @@
     for dy in range(3):
         piece = window(dy)
         for dx in range(3):
-            part = jnp.dot(piece, w_ref[dy, dx], preferred_element_type=jnp.float32)
+            part = jnp.dot(piece, w_ref[b, dy, dx], preferred_element_type=jnp.float32)
             taps[dx] = part if taps[dx] is None else taps[dx] + part
     conv = taps[0] + pltpu.roll(taps[1], total - 1, 0) + pltpu.roll(taps[2], total - 2, 0)
     hidden = (conv / (1.0 + jnp.exp(-conv))).astype(jnp.bfloat16)
 
     values = hidden.astype(jnp.float32).reshape(frames, count, chans)
-    kernel = k_ref[...]
+    kernel = k_ref[b]
     depth = []
     for t in range(frames):
         acc = values[t] * kernel[0:1]
@@ -37,29 +37,44 @@
         depth.append(acc.astype(jnp.bfloat16))
     depth = jnp.stack(depth).reshape(total, chans)
 
-    mixed = jnp.dot(depth, p_ref[...], preferred_element_type=jnp.float32).astype(jnp.bfloat16)
+    mixed = jnp.dot(depth, p_ref[b], preferred_element_type=jnp.float32).astype(jnp.bfloat16)
     center = pltpu.roll(window(1).astype(jnp.float32), total - 1, 0)
-    state = (center + mixed.astype(jnp.float32)).astype(jnp.bfloat16).reshape(frames, count, chans)
-    o_ref[...] = jnp.where(m_ref[...][None] > 0, state, jnp.zeros((), state.dtype))
+    return (center + mixed.astype(jnp.float32)).astype(jnp.bfloat16).reshape(frames, count, chans)
 
 
-def block(x, weight, kernel, proj, mask, pitch):
+def blocks_kernel(x_ref, w_ref, k_ref, p_ref, *rest, pitch):
+    masks = rest[: BLOCKS - 1]
+    o_ref = rest[BLOCKS - 1]
+    held = rest[BLOCKS:]
+    source = x_ref
+    for b in range(BLOCKS):
+        target = o_ref if b == BLOCKS - 1 else held[b]
+        count = target.shape[1]
+        state = run_block(source, w_ref, k_ref, p_ref, b, count, pitch)
+        if b < BLOCKS - 1:
+            state = jnp.where(masks[b][...][None] > 0, state, jnp.zeros((), state.dtype))
+        target[...] = state
+        source = target
+
+
+def all_blocks(x, conv_w, depth_k, proj_w, masks, pitch):
     frames, length, chans = x.shape
-    count = length - 2 * pitch
-    flops = 2 * frames * count * chans * chans * 10
+    counts = [length - 2 * pitch * (b + 1) for b in range(BLOCKS)]
+    flops = sum(2 * frames * n * chans * chans * 10 for n in counts)
     vmem = pltpu.VMEM
     return pl.pallas_call(
-        functools.partial(block_kernel, count=count, pitch=pitch),
-        out_shape=jax.ShapeDtypeStruct((frames, count, chans), x.dtype),
-        in_specs=[pl.BlockSpec(memory_space=vmem)] * 5,
+        functools.partial(blocks_kernel, pitch=pitch),
+        out_shape=jax.ShapeDtypeStruct((frames, counts[-1], chans), x.dtype),
+        in_specs=[pl.BlockSpec(memory_space=vmem)] * (4 + len(masks)),
         out_specs=pl.BlockSpec(memory_space=vmem),
+        scratch_shapes=[pltpu.VMEM((frames, n, chans), x.dtype) for n in counts[:-1]],
         compiler_params=pltpu.CompilerParams(vmem_limit_bytes=48 * 1024 * 1024),
         cost_estimate=pl.CostEstimate(
             flops=flops,
-            transcendentals=frames * count * chans,
-            bytes_accessed=2 * frames * (length + count) * chans + 2 * 10 * chans * chans,
+            transcendentals=frames * sum(counts) * chans,
+            bytes_accessed=2 * frames * (length + counts[-1]) * chans + 2 * BLOCKS * 10 * chans * chans,
         ),
-    )(x, weight, kernel, proj, mask)
+    )(x, conv_w, depth_k, proj_w, *masks)
 
 
 def shards(video, conv_w, depth_k, proj_w):
@@ -84,15 +99,16 @@
     state = jnp.concatenate([before, received, after, spare], axis=3)
     state = state.reshape(bands * frames, -1, chans)
 
-    for b in range(BLOCKS):
+    masks = []
+    for b in range(BLOCKS - 1):
         left = halo - 1 - b
         n_rows = rows + 2 * left
         row = band * rows - left + lax.broadcasted_iota(jnp.int32, (n_rows, pitch), 0)
         col = side * cols - left + lax.broadcasted_iota(jnp.int32, (n_rows, pitch), 1)
         inside = (row >= 0) & (row < height) & (col >= 0) & (col < sides * cols)
         inside = inside & (lax.broadcasted_iota(jnp.int32, (n_rows, pitch), 1) < cols + 2 * left)
-        mask = jnp.broadcast_to(inside.reshape(-1, 1), (n_rows * pitch, chans)).astype(jnp.float32)
-        state = block(state, conv_w[b], depth_k[b], proj_w[b], mask, pitch)
+        masks.append(jnp.broadcast_to(inside.reshape(-1, 1), (n_rows * pitch, chans)).astype(jnp.float32))
+    state = all_blocks(state, conv_w, depth_k, proj_w, masks, pitch)
 
     state = state.reshape(state.shape[0], rows, pitch, chans)[:, :, :cols]
     return lax.all_to_all(state, "tm", 0, 1, tiled=True)

time: 45.6 us -> 47.7 us (1.046)
  waiting for transfers between devices: 13.7 us -> 16.1 us
  local copies, waits for them, and re-layouts: 4.57 us -> 3.28 us
  other arithmetic: 2.32 us -> 3.12 us
    all_to_all x1, waiting for transfers between devices: 8.35 us -> 10.5 us  [shards(): received = lax.all_to_all(pieces, 'tm', 0, 0, tiled=False)]
    squeeze x3 -> x0, local copies, waits for them, and re-layouts: 1.81 us -> none  [shards(): state = block(state, conv_w[b], depth_k[b], proj_w[b], mask, pitch)]
    concatenate x1, other arithmetic: 0.65 us -> 1.54 us  [shards(): state = jnp.concatenate([before, received, after, spare], axis=3)]
    slice x1, local copies, waits for them, and re-layouts: 0.08 us -> 0.76 us  [shards(): before = lax.ppermute(received[:, :, :, cols - halo:], 'width', up)]
    pallas_call x2 -> x1, Pallas kernels: 5.04 us -> 5.39 us  [all_blocks(): pl.pallas_call(functools.partial(blocks_kernel, pitch=pitch), out_shape=j...]
  transfers between devices with their start and end apart: 3 -> 3, of which waited for: 3 -> 3; matrix products, arithmetic and copies ran while one was open for 5% -> 0% of each run, Pallas kernels for 0% -> 0%
where the time goes in v9:
time: 47.7 us; the launch traced here: 47.4 us
  waiting for transfers between devices  16.1 us (34%)
  blocking collectives  9.8 us (21%)
  starting transfers between devices  9.7 us (20%)
  Pallas kernels  5.39 us (11%)
  local copies, waits for them, and re-layouts  3.28 us (7%)
  other arithmetic  3.12 us (7%)
    all_to_all x1, waiting for transfers between devices, shards(): received = lax.all_to_all(pieces, 'tm', 0, 0, tiled=False)  10.5 us
    all_to_all x1, blocking collectives, shards(): return lax.all_to_all(state, 'tm', 0, 1, tiled=True)  9.8 us
    pallas_call x1, Pallas kernels, all_blocks(): pl.pallas_call(functools.partial(blocks_kernel, pitch=pitch), out_shape=j...  5.39 us
    ppermute x1, waiting for transfers between devices, shards(): after = lax.ppermute(received[:, :, :, :halo], 'width', down)  4.34 us
    all_to_all x1, starting transfers between devices, shards(): received = lax.all_to_all(pieces, 'tm', 0, 0, tiled=False)  4.24 us
    ppermute x1, starting transfers between devices, shards(): before = lax.ppermute(received[:, :, :, cols - halo:], 'width', up)  4.17 us
    concatenate x1, other arithmetic, shards(): state = jnp.concatenate([before, received, after, spare], axis=3)  1.54 us
    another operation x1, other arithmetic, shards(): jnp.stack([padded[:, r * rows:r * rows + rows + 2 * halo] for r in range(...  1.48 us
  transfers between devices with their start and end apart: 3, of which 3 were waited for; matrix products, arithmetic and copies ran while one was open for 0% of the time, Pallas kernels for 0%

profile of v9, /device:TPU:0, one launch (start us, length us, event | category | flops | bytes accessed | tf_op | source)
XLA Modules:
  0.0 47.4 jit_solution(10460735162961793029)
XLA Ops:
  0.0 1.4 %fusion = (bf16[1,4,7,12,256]{4,1,3,2,0:T(4,128)(2,1)S(1)}, bf16[1,4,7,12,256]{4,1,3,2,0:T(4,128)(2,1)S(1)}, bf16[1,4,7,12,256]{4,1,3,2,0:T(4,128)(2,1)S(1)}, bf16[1,4,7,12,256]{4,1,3,2,0:T(4,128)(2,1)S(1)}) fusion(bf16[4,12,12,256]{3,0,2,1:T(4,128)(2,1)} %param.4), kind=kLoop, calls=%fused_computation.4 | loop fusion | bytes 1327104 | tf_op jit(solution)/shard_map/stack | solution.py:91
  1.4 1.5 %pad_maximum_fusion.1 = bf16[4,4,7,12,256]{4,1,3,2,0:T(4,128)(2,1)} fusion(bf16[1,4,7,12,256]{4,1,3,2,0:T(4,128)(2,1)S(1)} %get-tuple-element.8, bf16[1,4,7,12,256]{4,1,3,2,0:T(4,128)(2,1)S(1)} %get-tuple-element.9, bf16[1,4,7,12,256]{4,1,3,2,0:T(4,128)(2,1)S(1)} %get-tuple-element.10, bf16[1,4,7,12,256]{4,1,3,2,0:T(4,128)(2,1)S(1)} %get-tuple-element.7), kind=kLoop, calls=%fused_computation.1 | loop fusion | flops 1032192 | bytes 1376256 | tf_op jit(solution)/shard_map/stack | solution.py:91
  2.8 4.2 %all-to-all-start = ((bf16[4,4,7,12,256]{4,1,3,2,0:T(4,128)(2,1)}), bf16[4,4,7,12,256]{4,1,3,2,0:T(4,128)(2,1)S(1)}, u32[]{:S(2)}, u32[]{:S(2)}) async-start(bf16[4,4,7,12,256]{4,1,3,2,0:T(4,128)(2,1)} %pad_maximum_fusion.1), calls=%async_computation | async-start | bytes 1376256 | tf_op jit(solution)/shard_map/all_to_all | solution.py:92
  7.1 0.0 copy-start
  7.1 0.0 copy-start.1
  7.1 0.0 copy-start.2
  7.1 10.5 %all-to-all-done = bf16[4,4,7,12,256]{4,1,3,2,0:T(4,128)(2,1)S(1)} async-done(((bf16[4,4,7,12,256]{4,1,3,2,0:T(4,128)(2,1)}), bf16[4,4,7,12,256]{4,1,3,2,0:T(4,128)(2,1)S(1)}, u32[]{:S(2)}, u32[]{:S(2)}) %all-to-all-start) | async-done | bytes 688160 | tf_op jit(solution)/shard_map/all_to_all | solution.py:92
  17.6 0.8 %fusion.4 = (bf16[4,4,7,2,256]{4,1,3,2,0:T(4,128)(2,1)}, bf16[4,4,7,2,256]{4,1,3,2,0:T(4,128)(2,1)}) fusion(bf16[4,4,7,12,256]{4,1,3,2,0:T(4,128)(2,1)S(1)} %all-to-all-done), kind=kLoop, calls=%fused_computation.14 | loop fusion | bytes 458752 | tf_op jit(solution)/shard_map/slice | solution.py:96
  18.4 4.2 %collective-permute-start = (bf16[4,4,7,2,256]{4,1,3,2,0:T(4,128)(2,1)}, bf16[4,4,7,2,256]{4,1,3,2,0:T(4,128)(2,1)S(1)}, u32[]{:S(2)}, u32[]{:S(2)}) collective-permute-start(bf16[4,4,7,2,256]{4,1,3,2,0:T(4,128)(2,1)} %get-tuple-element.5), channel_id=1, source_target_pairs={{0,1},{1,2},{2,3},{4,5},{5,6},{6,7},{8,9},{9,10},{10,11},{12,13},{... | collective-permute-start | bytes 344072 | tf_op jit(solution)/shard_map/ppermute | solution.py:96
  22.6 1.3 %collective-permute-start.1 = (bf16[4,4,7,2,256]{4,1,3,2,0:T(4,128)(2,1)}, bf16[4,4,7,2,256]{4,1,3,2,0:T(4,128)(2,1)}, u32[]{:S(2)}, u32[]{:S(2)}) collective-permute-start(bf16[4,4,7,2,256]{4,1,3,2,0:T(4,128)(2,1)} %get-tuple-element.6), channel_id=1, source_target_pairs={{1,0},{2,1},{3,2},{5,4},{6,5},{7,6},{9,8},{10,9},{11,10},{13,12},{... | collective-permute-start | bytes 344072 | tf_op jit(solution)/shard_map/ppermute | solution.py:97
  23.9 0.1 and_convert_fusion
  24.0 0.1 reshape.47
  24.0 1.2 %collective-permute-done = bf16[4,4,7,2,256]{4,1,3,2,0:T(4,128)(2,1)S(1)} collective-permute-done((bf16[4,4,7,2,256]{4,1,3,2,0:T(4,128)(2,1)}, bf16[4,4,7,2,256]{4,1,3,2,0:T(4,128)(2,1)S(1)}, u32[]{:S(2)}, u32[]{:S(2)}) %collective-permute-start) | collective-permute-done | bytes 114720 | tf_op jit(solution)/shard_map/ppermute | solution.py:96
  25.3 4.3 %collective-permute-done.1 = bf16[4,4,7,2,256]{4,1,3,2,0:T(4,128)(2,1)} collective-permute-done((bf16[4,4,7,2,256]{4,1,3,2,0:T(4,128)(2,1)}, bf16[4,4,7,2,256]{4,1,3,2,0:T(4,128)(2,1)}, u32[]{:S(2)}, u32[]{:S(2)}) %collective-permute-start.1) | collective-permute-done | bytes 114720 | tf_op jit(solution)/shard_map/ppermute | solution.py:97
  29.6 1.5 %pad_maximum_fusion = bf16[4,4,7,16,256]{4,1,3,2,0:T(4,128)(2,1)S(1)} fusion(bf16[4,4,7,2,256]{4,1,3,2,0:T(4,128)(2,1)} %collective-permute-done.1, bf16[4,4,7,12,256]{4,1,3,2,0:T(4,128)(2,1)S(1)} %all-to-all-done, bf16[4,4,7,2,256]{4,1,3,2,0:T(4,128)(2,1)S(1)} %collective-permute-done), kind=kLoop, calls=%fused_computation | loop fusion | flops 917504 | bytes 1835008 | tf_op jit(solution)/shard_map/concatenate | solution.py:99
  31.1 0.1 copy.5
  31.3 0.1 broadcast_in_dim.2.rest_0_
  31.4 0.0 copy-done
  31.4 0.0 copy-done.1
  31.4 0.0 copy-done.2
  31.4 5.4 %shard_map.46 = bf16[16,48,256]{2,1,0:T(8,128)(2,1)S(1)} custom-call(bf16[16,112,256]{2,1,0:T(8,128)(2,1)S(1)} %bitcast.15, bf16[2,3,3,256,256]{4,3,2,1,0:T(8,128)(2,1)S(1)} %copy-done, f32[2,16,256]{2,1,0:T(8,128)S(1)} %copy-done.2, bf16[2,256,256]{2,1,0:T(8,128)(2,1)S(1)} %copy-done.1, f32[80,256]{1,0:T(8,128)S(1)} %broadcast_in_dim.2.rest_0_), custom_call_target="tpu_custom_call" | custom-call | flops 2684354560 | bytes 3932160 | tf_op jit(solution)/shard_map/pallas_call | solution.py:65
  36.8 9.8 %all_to_all.23 = bf16[16,3,12,256]{3,2,1,0:T(8,128)(2,1)S(1)} all-to-all(bf16[16,3,12,256]{3,2,1,0:T(8,128)(2,1)S(1)} %bitcast.16), channel_id=1, replica_groups=mesh['groups'=2,'tm'=4,'width'=4] {'tm'}, dimensions={0} | all-to-all | bytes 589824 | tf_op jit(solution)/shard_map/all_to_all | solution.py:114
  46.6 0.9 %copy.6 = bf16[4,4,3,12,256]{4,1,3,2,0:T(4,128)(2,1)} copy(bf16[4,4,3,12,256]{4,3,2,1,0:T(8,128)(2,1)S(1)} %bitcast.17) | data formatting | bytes 589824 | tf_op jit(solution)/shard_map/all_to_all | solution.py:114
  (3 shorter events, 0.0 us)
Async XLA Ops:
  2.8 14.8 %all-to-all-start = ((bf16[4,4,7,12,256]{4,1,3,2,0:T(4,128)(2,1)}), bf16[4,4,7,12,256]{4,1,3,2,0:T(4,128)(2,1)S(1)}, u32[]{:S(2)}, u32[]{:S(2)}) async-start(bf16[4,4,7,12,256]{4,1,3,2,0:T(4,128)(2,1)} %pad_maximum_fusion.1), calls=%async_computation | async-start | bytes 1376256 | tf_op jit(solution)/shard_map/all_to_all | solution.py:92
  7.1 24.3 %copy-start = (bf16[2,3,3,256,256]{4,3,2,1,0:T(8,128)(2,1)S(1)}, bf16[2,3,3,256,256]{4,3,2,1,0:T(8,128)(2,1)}, u32[]{:S(2)}) copy-start(bf16[2,3,3,256,256]{4,3,2,1,0:T(8,128)(2,1)} %w_ref.1) | copy-start | bytes 7077892
  7.1 24.3 %copy-start.1 = (bf16[2,256,256]{2,1,0:T(8,128)(2,1)S(1)}, bf16[2,256,256]{2,1,0:T(8,128)(2,1)}, u32[]{:S(2)}) copy-start(bf16[2,256,256]{2,1,0:T(8,128)(2,1)} %p_ref.1) | copy-start | bytes 786436
  7.1 24.3 %copy-start.2 = (f32[2,16,256]{2,1,0:T(8,128)S(1)}, f32[2,16,256]{2,1,0:T(8,128)}, u32[]{:S(2)}) copy-start(f32[2,16,256]{2,1,0:T(8,128)} %k_ref.1) | copy-start | bytes 98308
  18.4 6.8 %collective-permute-start = (bf16[4,4,7,2,256]{4,1,3,2,0:T(4,128)(2,1)}, bf16[4,4,7,2,256]{4,1,3,2,0:T(4,128)(2,1)S(1)}, u32[]{:S(2)}, u32[]{:S(2)}) collective-permute-start(bf16[4,4,7,2,256]{4,1,3,2,0:T(4,128)(2,1)} %get-tuple-element.5), channel_id=1, source_target_pairs={{0,1},{1,2},{2,3},{4,5},{5,6},{6,7},{8,9},{9,10},{10,11},{12,13},{... | collective-permute-start | bytes 344072 | tf_op jit(solution)/shard_map/ppermute | solution.py:96
  22.6 7.0 %collective-permute-start.1 = (bf16[4,4,7,2,256]{4,1,3,2,0:T(4,128)(2,1)}, bf16[4,4,7,2,256]{4,1,3,2,0:T(4,128)(2,1)}, u32[]{:S(2)}, u32[]{:S(2)}) collective-permute-start(bf16[4,4,7,2,256]{4,1,3,2,0:T(4,128)(2,1)} %get-tuple-element.6), channel_id=1, source_target_pairs={{1,0},{2,1},{3,2},{5,4},{6,5},{7,6},{9,8},{10,9},{11,10},{13,12},{... | collective-permute-start | bytes 344072 | tf_op jit(solution)/shard_map/ppermute | solution.py:97

commit v10 on v6

--- a/solution.py
+++ b/solution.py
@@ -62,6 +62,39 @@
     )(x, weight, kernel, proj, mask)
 
 
+def bands_kernel(v_ref, o_ref, zero_ref, sems, *, rows, halo):
+    height = v_ref.shape[0]
+    zero_ref[...] = jnp.zeros(zero_ref.shape, zero_ref.dtype)
+    copies = []
+    for r in range(o_ref.shape[0]):
+        lo = r * rows - halo
+        hi = lo + rows + 2 * halo
+        first, last = max(lo, 0), min(hi, height)
+        parts = [(v_ref.at[first:last], o_ref.at[r, first - lo : last - lo])]
+        if first > lo:
+            parts.append((zero_ref.at[: first - lo], o_ref.at[r, : first - lo]))
+        if last < hi:
+            parts.append((zero_ref.at[: hi - last], o_ref.at[r, last - lo :]))
+        for src, dst in parts:
+            copy = pltpu.make_async_copy(src, dst, sems.at[len(copies)])
+            copy.start()
+            copies.append(copy)
+    for copy in copies:
+        copy.wait()
+
+
+def row_bands(video_t, bands, rows, halo):
+    height, cols, frames, chans = video_t.shape
+    count = bands + 2 * sum(1 for r in range(bands) for edge in (r * rows - halo < 0, r * rows + rows + halo > height) if edge)
+    return pl.pallas_call(
+        functools.partial(bands_kernel, rows=rows, halo=halo),
+        out_shape=jax.ShapeDtypeStruct((bands, rows + 2 * halo, cols, frames, chans), video_t.dtype),
+        in_specs=[pl.BlockSpec(memory_space=pl.ANY)],
+        out_specs=pl.BlockSpec(memory_space=pl.ANY),
+        scratch_shapes=[pltpu.VMEM((halo, cols, frames, chans), video_t.dtype), pltpu.SemaphoreType.DMA((count,))],
+    )(video_t)
+
+
 def shards(video, conv_w, depth_k, proj_w):
     bands = lax.axis_size("tm")
     sides = lax.axis_size("width")
@@ -72,9 +105,9 @@
     halo = BLOCKS
     pitch = -(-(cols + 2 * halo) // LANES) * LANES
 
-    padded = jnp.pad(video, ((0, 0), (halo, halo), (0, 0), (0, 0)))
-    pieces = jnp.stack([padded[:, r * rows : r * rows + rows + 2 * halo] for r in range(bands)])
+    pieces = row_bands(jnp.transpose(video, (1, 2, 0, 3)), bands, rows, halo)
     received = lax.all_to_all(pieces, "tm", 0, 0, tiled=False)
+    received = jnp.transpose(received, (0, 3, 1, 2, 4))
 
     up = [(i, i + 1) for i in range(sides - 1)]
     down = [(i + 1, i) for i in range(sides - 1)]

time: 45.6 us -> 61.8 us (1.36)
  Pallas kernels: 5.04 us -> 24.1 us
  other arithmetic: 2.32 us -> 0.84 us
  local copies, waits for them, and re-layouts: 4.57 us -> 3.2 us
    pallas_call x0 -> x1, Pallas kernels: none -> 19 us  [row_bands(): pl.pallas_call(functools.partial(bands_kernel, rows=rows, halo=halo), out...]
    another operation x1 -> x0, other arithmetic: 1.48 us -> none  [shards(): jnp.stack([padded[:, r * rows:r * rows + rows + 2 * halo] for r in range(...]
    another operation x1 -> x0, local copies, waits for them, and re-layouts: 1.36 us -> none  [shards(): jnp.stack([padded[:, r * rows:r * rows + rows + 2 * halo] for r in range(...]
  transfers between devices with their start and end apart: 3 -> 3, of which waited for: 3 -> 3; matrix products, arithmetic and copies ran while one was open for 5% -> 4% of each run, Pallas kernels for 0% -> 0%
where the time goes in v10:
time: 61.8 us; the launch traced here: 61.5 us
  Pallas kernels  24.1 us (39%)
  waiting for transfers between devices  13.7 us (22%)
  blocking collectives  9.8 us (16%)
  starting transfers between devices  9.72 us (16%)
  local copies, waits for them, and re-layouts  3.2 us (5%)
  other arithmetic  0.84 us (1%)
    pallas_call x1, Pallas kernels, row_bands(): pl.pallas_call(functools.partial(bands_kernel, rows=rows, halo=halo), out...  19 us
    all_to_all x1, blocking collectives, shards(): return lax.all_to_all(state, 'tm', 0, 1, tiled=True)  9.8 us
    all_to_all x1, waiting for transfers between devices, shards(): received = lax.all_to_all(pieces, 'tm', 0, 0, tiled=False)  8.35 us
    pallas_call x2, Pallas kernels, block(): pl.pallas_call(functools.partial(block_kernel, count=count, pitch=pitch),...  5.04 us
    ppermute x1, waiting for transfers between devices, shards(): after = lax.ppermute(received[:, :, :, :halo], 'width', down)  4.34 us
    all_to_all x1, starting transfers between devices, shards(): received = lax.all_to_all(pieces, 'tm', 0, 0, tiled=False)  4.25 us
    ppermute x1, starting transfers between devices, shards(): before = lax.ppermute(received[:, :, :, cols - halo:], 'width', up)  4.18 us
    squeeze x3, local copies, waits for them, and re-layouts, shards(): state = block(state, conv_w[b], depth_k[b], proj_w[b], mask, pitch)  1.81 us
  transfers between devices with their start and end apart: 3, of which 3 were waited for; matrix products, arithmetic and copies ran while one was open for 4% of the time, Pallas kernels for 0%

profile of v10, /device:TPU:0, one launch (start us, length us, event | category | flops | bytes accessed | tf_op | source)
XLA Modules:
  0.0 61.5 jit_solution(10636992732769363052)
XLA Ops:
  0.0 0.0 copy-start
  0.0 19.0 %shard_map.46 = bf16[4,7,12,4,256]{4,3,2,1,0:T(4,128)(2,1)} custom-call(bf16[12,12,4,256]{3,2,1,0:T(4,128)(2,1)} %bitcast.26), custom_call_target="tpu_custom_call" | custom-call | tf_op jit(solution)/shard_map/pallas_call | solution.py:89
  19.1 4.2 %all-to-all-start = ((bf16[4,7,12,4,256]{4,3,2,1,0:T(4,128)(2,1)}), bf16[4,7,12,4,256]{4,3,2,1,0:T(4,128)(2,1)S(1)}, u32[]{:S(2)}, u32[]{:S(2)}) async-start(bf16[4,7,12,4,256]{4,3,2,1,0:T(4,128)(2,1)} %shard_map.46), calls=%async_computation | async-start | bytes 1376256 | tf_op jit(solution)/shard_map/all_to_all | solution.py:109
  23.4 0.1 and_convert_fusion
  23.5 0.1 reshape.86
  23.5 0.1 and_convert_fusion.1
  23.6 0.1 reshape.87
  23.7 0.0 copy-done
  23.7 0.0 copy-start.1
  23.7 1.8 %slice_bitcast_fusion = (bf16[3,3,256,256]{3,2,1,0:T(8,128)(2,1)S(1)}, bf16[3,3,256,256]{3,2,1,0:T(8,128)(2,1)S(1)}) fusion(bf16[2,3,3,256,256]{4,3,2,1,0:T(8,128)(2,1)} %param.5), kind=kLoop, calls=%fused_computation | loop fusion | bytes 4718592 | tf_op jit(solution)/shard_map/squeeze | solution.py:128
  25.5 8.3 %all-to-all-done = bf16[4,7,12,4,256]{4,3,2,1,0:T(4,128)(2,1)S(1)} async-done(((bf16[4,7,12,4,256]{4,3,2,1,0:T(4,128)(2,1)}), bf16[4,7,12,4,256]{4,3,2,1,0:T(4,128)(2,1)S(1)}, u32[]{:S(2)}, u32[]{:S(2)}) %all-to-all-start) | async-done | bytes 688160 | tf_op jit(solution)/shard_map/all_to_all | solution.py:109
  33.9 0.1 fusion.4
  34.0 4.2 %collective-permute-start = (bf16[4,4,7,2,256]{4,1,3,2,0:T(4,128)(2,1)S(1)}, bf16[4,4,7,2,256]{4,1,3,2,0:T(4,128)(2,1)S(1)}, u32[]{:S(2)}, u32[]{:S(2)}) collective-permute-start(bf16[4,4,7,2,256]{4,1,3,2,0:T(4,128)(2,1)S(1)} %get-tuple-element.7), channel_id=1, source_target_pairs={{0,1},{1,2},{2,3},{4,5},{5,6},{6,7},{8,9},{9,10},{10,11},{12,13},{... | collective-permute-start | bytes 344072 | tf_op jit(solution)/shard_map/ppermute | solution.py:114
  38.2 1.3 %collective-permute-start.1 = (bf16[4,4,7,2,256]{4,1,3,2,0:T(4,128)(2,1)S(1)}, bf16[4,4,7,2,256]{4,1,3,2,0:T(4,128)(2,1)S(1)}, u32[]{:S(2)}, u32[]{:S(2)}) collective-permute-start(bf16[4,4,7,2,256]{4,1,3,2,0:T(4,128)(2,1)S(1)} %get-tuple-element.8), channel_id=1, source_target_pairs={{1,0},{2,1},{3,2},{5,4},{6,5},{7,6},{9,8},{10,9},{11,10},{13,12},{... | collective-permute-start | bytes 344072 | tf_op jit(solution)/shard_map/ppermute | solution.py:115
  39.5 0.0 copy-done.1
  39.5 1.0 %collective-permute-done = bf16[4,4,7,2,256]{4,1,3,2,0:T(4,128)(2,1)S(1)} collective-permute-done((bf16[4,4,7,2,256]{4,1,3,2,0:T(4,128)(2,1)S(1)}, bf16[4,4,7,2,256]{4,1,3,2,0:T(4,128)(2,1)S(1)}, u32[]{:S(2)}, u32[]{:S(2)}) %collective-permute-start) | collective-permute-done | bytes 114720 | tf_op jit(solution)/shard_map/ppermute | solution.py:114
  40.5 4.3 %collective-permute-done.1 = bf16[4,4,7,2,256]{4,1,3,2,0:T(4,128)(2,1)S(1)} collective-permute-done((bf16[4,4,7,2,256]{4,1,3,2,0:T(4,128)(2,1)S(1)}, bf16[4,4,7,2,256]{4,1,3,2,0:T(4,128)(2,1)S(1)}, u32[]{:S(2)}, u32[]{:S(2)}) %collective-permute-start.1) | collective-permute-done | bytes 114720 | tf_op jit(solution)/shard_map/ppermute | solution.py:115
  44.8 0.6 %pad_maximum_fusion = bf16[4,4,7,16,256]{4,1,3,2,0:T(4,128)(2,1)S(1)} fusion(bf16[4,4,7,2,256]{4,1,3,2,0:T(4,128)(2,1)S(1)} %collective-permute-done.1, bf16[4,4,7,12,256]{4,1,3,2,0:T(4,128)(2,1)S(1)} %bitcast.24, bf16[4,4,7,2,256]{4,1,3,2,0:T(4,128)(2,1)S(1)} %collective-permute-done), kind=kLoop, calls=%fused_computation.2 | loop fusion | flops 917504 | bytes 1835008 | tf_op jit(solution)/shard_map/concatenate | solution.py:117
  45.5 0.1 copy.5
  45.6 0.1 broadcast_in_dim.4.m_ref
  45.7 3.1 %shard_map.47.x_ref = bf16[16,80,256]{2,1,0:T(8,128)(2,1)S(1)} custom-call(bf16[16,112,256]{2,1,0:T(8,128)(2,1)S(1)} %bitcast.21, bf16[3,3,256,256]{3,2,1,0:T(8,128)(2,1)S(1)} %get-tuple-element.6.w_ref, f32[16,256]{1,0:T(8,128)S(1)} %get-tuple-element.12.k_ref, bf16[256,256]{1,0:T(8,128)(2,1)S(1)} %get-tuple-element.10.p_ref, ...), custom_call_target="tpu_custom_call" | custom-call | flops 1677721600 | bytes 2883584 | tf_op jit(solution)/shard_map/pallas_call | solution.py:51
  48.8 0.1 broadcast_in_dim.5.m_ref
  48.9 1.9 %shard_map.48 = bf16[16,48,256]{2,1,0:T(8,128)(2,1)S(1)} custom-call(bf16[16,80,256]{2,1,0:T(8,128)(2,1)S(1)} %shard_map.47.x_ref, bf16[3,3,256,256]{3,2,1,0:T(8,128)(2,1)S(1)} %get-tuple-element.5.w_ref, f32[16,256]{1,0:T(8,128)S(1)} %get-tuple-element.11.k_ref, bf16[256,256]{1,0:T(8,128)(2,1)S(1)} %get-tuple-element.9.p_ref, ...), custom_call_target="tpu_custom_call" | custom-call | flops 1006632960 | bytes 2359296 | tf_op jit(solution)/shard_map/pallas_call | solution.py:51
  50.8 9.8 %all_to_all.23 = bf16[16,3,12,256]{3,2,1,0:T(8,128)(2,1)S(1)} all-to-all(bf16[16,3,12,256]{3,2,1,0:T(8,128)(2,1)S(1)} %bitcast.22), channel_id=1, replica_groups=mesh['groups'=2,'tm'=4,'width'=4] {'tm'}, dimensions={0} | all-to-all | bytes 589824 | tf_op jit(solution)/shard_map/all_to_all | solution.py:131
  60.6 0.9 %copy.6 = bf16[4,4,3,12,256]{4,1,3,2,0:T(4,128)(2,1)} copy(bf16[4,4,3,12,256]{4,3,2,1,0:T(8,128)(2,1)S(1)} %bitcast.25) | data formatting | bytes 589824 | tf_op jit(solution)/shard_map/all_to_all | solution.py:131
  (8 shorter events, 0.1 us)
Async XLA Ops:
  0.0 23.7 %copy-start = (bf16[2,256,256]{2,1,0:T(8,128)(2,1)S(1)}, bf16[2,256,256]{2,1,0:T(8,128)(2,1)}, u32[]{:S(2)}) copy-start(bf16[2,256,256]{2,1,0:T(8,128)(2,1)} %param.7) | copy-start | bytes 786436
  19.1 14.8 %all-to-all-start = ((bf16[4,7,12,4,256]{4,3,2,1,0:T(4,128)(2,1)}), bf16[4,7,12,4,256]{4,3,2,1,0:T(4,128)(2,1)S(1)}, u32[]{:S(2)}, u32[]{:S(2)}) async-start(bf16[4,7,12,4,256]{4,3,2,1,0:T(4,128)(2,1)} %shard_map.46), calls=%async_computation | async-start | bytes 1376256 | tf_op jit(solution)/shard_map/all_to_all | solution.py:109
  23.7 15.7 %copy-start.1 = (f32[2,16,256]{2,1,0:T(8,128)S(1)}, f32[2,16,256]{2,1,0:T(8,128)}, u32[]{:S(2)}) copy-start(f32[2,16,256]{2,1,0:T(8,128)} %param.6) | copy-start | bytes 98308
  34.0 6.5 %collective-permute-start = (bf16[4,4,7,2,256]{4,1,3,2,0:T(4,128)(2,1)S(1)}, bf16[4,4,7,2,256]{4,1,3,2,0:T(4,128)(2,1)S(1)}, u32[]{:S(2)}, u32[]{:S(2)}) collective-permute-start(bf16[4,4,7,2,256]{4,1,3,2,0:T(4,128)(2,1)S(1)} %get-tuple-element.7), channel_id=1, source_target_pairs={{0,1},{1,2},{2,3},{4,5},{5,6},{6,7},{8,9},{9,10},{10,11},{12,13},{... | collective-permute-start | bytes 344072 | tf_op jit(solution)/shard_map/ppermute | solution.py:114
  38.2 6.7 %collective-permute-start.1 = (bf16[4,4,7,2,256]{4,1,3,2,0:T(4,128)(2,1)S(1)}, bf16[4,4,7,2,256]{4,1,3,2,0:T(4,128)(2,1)S(1)}, u32[]{:S(2)}, u32[]{:S(2)}) collective-permute-start(bf16[4,4,7,2,256]{4,1,3,2,0:T(4,128)(2,1)S(1)} %get-tuple-element.8), channel_id=1, source_target_pairs={{1,0},{2,1},{3,2},{5,4},{6,5},{7,6},{9,8},{10,9},{11,10},{13,12},{... | collective-permute-start | bytes 344072 | tf_op jit(solution)/shard_map/ppermute | solution.py:115

commit v11 on v6

--- a/solution.py
+++ b/solution.py
@@ -18,12 +18,11 @@
     def window(dy):
         return x_ref[:, dy * pitch : dy * pitch + count, :].reshape(total, chans)
 
-    taps = [None, None, None]
-    for dy in range(3):
-        piece = window(dy)
-        for dx in range(3):
-            part = jnp.dot(piece, w_ref[dy, dx], preferred_element_type=jnp.float32)
-            taps[dx] = part if taps[dx] is None else taps[dx] + part
+    pieces = jnp.concatenate([window(dy) for dy in range(3)], axis=1)
+    taps = []
+    for dx in range(3):
+        weight = jnp.concatenate([w_ref[dy, dx] for dy in range(3)], axis=0)
+        taps.append(jnp.dot(pieces, weight, preferred_element_type=jnp.float32))
     conv = taps[0] + pltpu.roll(taps[1], total - 1, 0) + pltpu.roll(taps[2], total - 2, 0)
     hidden = (conv / (1.0 + jnp.exp(-conv))).astype(jnp.bfloat16)
 

time: 45.6 us -> 45.6 us (level)
  no operation moved by 1% of the time
where the time goes in v11:
time: 45.6 us; the launch traced here: 45.3 us
  waiting for transfers between devices  13.7 us (30%)
  blocking collectives  9.8 us (21%)
  starting transfers between devices  9.71 us (21%)
  Pallas kernels  5.06 us (11%)
  local copies, waits for them, and re-layouts  4.57 us (10%)
  other arithmetic  2.32 us (5%)
    all_to_all x1, blocking collectives, shards(): return lax.all_to_all(state, 'tm', 0, 1, tiled=True)  9.8 us
    all_to_all x1, waiting for transfers between devices, shards(): received = lax.all_to_all(pieces, 'tm', 0, 0, tiled=False)  8.35 us
    pallas_call x2, Pallas kernels, block(): pl.pallas_call(functools.partial(block_kernel, count=count, pitch=pitch),...  5.06 us
    ppermute x1, waiting for transfers between devices, shards(): after = lax.ppermute(received[:, :, :, :halo], 'width', down)  4.34 us
    all_to_all x1, starting transfers between devices, shards(): received = lax.all_to_all(pieces, 'tm', 0, 0, tiled=False)  4.24 us
    ppermute x1, starting transfers between devices, shards(): before = lax.ppermute(received[:, :, :, cols - halo:], 'width', up)  4.18 us
    squeeze x3, local copies, waits for them, and re-layouts, shards(): state = block(state, conv_w[b], depth_k[b], proj_w[b], mask, pitch)  1.81 us
    another operation x1, other arithmetic, shards(): jnp.stack([padded[:, r * rows:r * rows + rows + 2 * halo] for r in range(...  1.48 us
  transfers between devices with their start and end apart: 3, of which 3 were waited for; matrix products, arithmetic and copies ran while one was open for 5% of the time, Pallas kernels for 0%

profile of v11, /device:TPU:0, one launch (start us, length us, event | category | flops | bytes accessed | tf_op | source)
XLA Modules:
  0.0 45.3 jit_solution(2194844923865007563)
XLA Ops:
  0.0 1.4 %fusion = (bf16[1,4,7,12,256]{4,1,3,2,0:T(4,128)(2,1)S(1)}, bf16[1,4,7,12,256]{4,1,3,2,0:T(4,128)(2,1)S(1)}, bf16[1,4,7,12,256]{4,1,3,2,0:T(4,128)(2,1)S(1)}, bf16[1,4,7,12,256]{4,1,3,2,0:T(4,128)(2,1)S(1)}) fusion(bf16[4,12,12,256]{3,0,2,1:T(4,128)(2,1)} %param.4), kind=kLoop, calls=%fused_computation.6 | loop fusion | bytes 1327104 | tf_op jit(solution)/shard_map/stack | solution.py:75
  1.4 0.0 copy-start
  1.4 1.5 %pad_maximum_fusion.1 = bf16[4,4,7,12,256]{4,1,3,2,0:T(4,128)(2,1)} fusion(bf16[1,4,7,12,256]{4,1,3,2,0:T(4,128)(2,1)S(1)} %get-tuple-element.10, bf16[1,4,7,12,256]{4,1,3,2,0:T(4,128)(2,1)S(1)} %get-tuple-element.11, bf16[1,4,7,12,256]{4,1,3,2,0:T(4,128)(2,1)S(1)} %get-tuple-element.12, bf16[1,4,7,12,256]{4,1,3,2,0:T(4,128)(2,1)S(1)} %get-tuple-element.9), kind=kLoop, calls=%fused_computation.3 | loop fusion | flops 1032192 | bytes 1376256 | tf_op jit(solution)/shard_map/stack | solution.py:75
  2.9 4.2 %all-to-all-start = ((bf16[4,4,7,12,256]{4,1,3,2,0:T(4,128)(2,1)}), bf16[4,4,7,12,256]{4,1,3,2,0:T(4,128)(2,1)S(1)}, u32[]{:S(2)}, u32[]{:S(2)}) async-start(bf16[4,4,7,12,256]{4,1,3,2,0:T(4,128)(2,1)} %pad_maximum_fusion.1), calls=%async_computation | async-start | bytes 1376256 | tf_op jit(solution)/shard_map/all_to_all | solution.py:76
  7.2 0.1 and_convert_fusion
  7.2 0.1 reshape.86
  7.3 0.1 and_convert_fusion.1
  7.4 0.1 reshape.87
  7.5 0.0 copy-done
  7.5 0.0 copy-start.1
  7.5 1.8 %slice_bitcast_fusion = (bf16[3,3,256,256]{3,2,1,0:T(8,128)(2,1)S(1)}, bf16[3,3,256,256]{3,2,1,0:T(8,128)(2,1)S(1)}) fusion(bf16[2,3,3,256,256]{4,3,2,1,0:T(8,128)(2,1)} %param.5), kind=kLoop, calls=%fused_computation | loop fusion | bytes 4718592 | tf_op jit(solution)/shard_map/squeeze | solution.py:94
  9.3 8.3 %all-to-all-done = bf16[4,4,7,12,256]{4,1,3,2,0:T(4,128)(2,1)S(1)} async-done(((bf16[4,4,7,12,256]{4,1,3,2,0:T(4,128)(2,1)}), bf16[4,4,7,12,256]{4,1,3,2,0:T(4,128)(2,1)S(1)}, u32[]{:S(2)}, u32[]{:S(2)}) %all-to-all-start) | async-done | bytes 688160 | tf_op jit(solution)/shard_map/all_to_all | solution.py:76
  17.7 0.1 fusion.6
  17.8 4.2 %collective-permute-start = (bf16[4,4,7,2,256]{4,1,3,2,0:T(4,128)(2,1)S(1)}, bf16[4,4,7,2,256]{4,1,3,2,0:T(4,128)(2,1)S(1)}, u32[]{:S(2)}, u32[]{:S(2)}) collective-permute-start(bf16[4,4,7,2,256]{4,1,3,2,0:T(4,128)(2,1)S(1)} %get-tuple-element.7), channel_id=1, source_target_pairs={{0,1},{1,2},{2,3},{4,5},{5,6},{6,7},{8,9},{9,10},{10,11},{12,13},{... | collective-permute-start | bytes 344072 | tf_op jit(solution)/shard_map/ppermute | solution.py:80
  21.9 1.3 %collective-permute-start.1 = (bf16[4,4,7,2,256]{4,1,3,2,0:T(4,128)(2,1)S(1)}, bf16[4,4,7,2,256]{4,1,3,2,0:T(4,128)(2,1)S(1)}, u32[]{:S(2)}, u32[]{:S(2)}) collective-permute-start(bf16[4,4,7,2,256]{4,1,3,2,0:T(4,128)(2,1)S(1)} %get-tuple-element.8), channel_id=1, source_target_pairs={{1,0},{2,1},{3,2},{5,4},{6,5},{7,6},{9,8},{10,9},{11,10},{13,12},{... | collective-permute-start | bytes 344072 | tf_op jit(solution)/shard_map/ppermute | solution.py:81
  23.2 0.0 copy-done.1
  23.3 1.0 %collective-permute-done = bf16[4,4,7,2,256]{4,1,3,2,0:T(4,128)(2,1)S(1)} collective-permute-done((bf16[4,4,7,2,256]{4,1,3,2,0:T(4,128)(2,1)S(1)}, bf16[4,4,7,2,256]{4,1,3,2,0:T(4,128)(2,1)S(1)}, u32[]{:S(2)}, u32[]{:S(2)}) %collective-permute-start) | collective-permute-done | bytes 114720 | tf_op jit(solution)/shard_map/ppermute | solution.py:80
  24.3 4.3 %collective-permute-done.1 = bf16[4,4,7,2,256]{4,1,3,2,0:T(4,128)(2,1)S(1)} collective-permute-done((bf16[4,4,7,2,256]{4,1,3,2,0:T(4,128)(2,1)S(1)}, bf16[4,4,7,2,256]{4,1,3,2,0:T(4,128)(2,1)S(1)}, u32[]{:S(2)}, u32[]{:S(2)}) %collective-permute-start.1) | collective-permute-done | bytes 114720 | tf_op jit(solution)/shard_map/ppermute | solution.py:81
  28.6 0.6 %pad_maximum_fusion = bf16[4,4,7,16,256]{4,1,3,2,0:T(4,128)(2,1)S(1)} fusion(bf16[4,4,7,2,256]{4,1,3,2,0:T(4,128)(2,1)S(1)} %collective-permute-done.1, bf16[4,4,7,12,256]{4,1,3,2,0:T(4,128)(2,1)S(1)} %all-to-all-done, bf16[4,4,7,2,256]{4,1,3,2,0:T(4,128)(2,1)S(1)} %collective-permute-done), kind=kLoop, calls=%fused_computation.2 | loop fusion | flops 917504 | bytes 1835008 | tf_op jit(solution)/shard_map/concatenate | solution.py:83
  29.3 0.1 copy.5
  29.4 0.1 broadcast_in_dim.4.m_ref
  29.5 3.1 %shard_map.46.x_ref = bf16[16,80,256]{2,1,0:T(8,128)(2,1)S(1)} custom-call(bf16[16,112,256]{2,1,0:T(8,128)(2,1)S(1)} %bitcast.27, bf16[3,3,256,256]{3,2,1,0:T(8,128)(2,1)S(1)} %get-tuple-element.6.w_ref, f32[16,256]{1,0:T(8,128)S(1)} %get-tuple-element.16.k_ref, bf16[256,256]{1,0:T(8,128)(2,1)S(1)} %get-tuple-element.14.p_ref, ...), custom_call_target="tpu_custom_call" | custom-call | flops 1677721600 | bytes 2883584 | tf_op jit(solution)/shard_map/pallas_call | solution.py:50
  32.6 0.1 broadcast_in_dim.5.m_ref
  32.7 1.9 %shard_map.47 = bf16[16,48,256]{2,1,0:T(8,128)(2,1)S(1)} custom-call(bf16[16,80,256]{2,1,0:T(8,128)(2,1)S(1)} %shard_map.46.x_ref, bf16[3,3,256,256]{3,2,1,0:T(8,128)(2,1)S(1)} %get-tuple-element.5.w_ref, f32[16,256]{1,0:T(8,128)S(1)} %get-tuple-element.15.k_ref, bf16[256,256]{1,0:T(8,128)(2,1)S(1)} %get-tuple-element.13.p_ref, ...), custom_call_target="tpu_custom_call" | custom-call | flops 1006632960 | bytes 2359296 | tf_op jit(solution)/shard_map/pallas_call | solution.py:50
  34.6 9.8 %all_to_all.23 = bf16[16,3,12,256]{3,2,1,0:T(8,128)(2,1)S(1)} all-to-all(bf16[16,3,12,256]{3,2,1,0:T(8,128)(2,1)S(1)} %bitcast.28), channel_id=1, replica_groups=mesh['groups'=2,'tm'=4,'width'=4] {'tm'}, dimensions={0} | all-to-all | bytes 589824 | tf_op jit(solution)/shard_map/all_to_all | solution.py:97
  44.4 0.9 %copy.6 = bf16[4,4,3,12,256]{4,1,3,2,0:T(4,128)(2,1)} copy(bf16[4,4,3,12,256]{4,3,2,1,0:T(8,128)(2,1)S(1)} %bitcast.29) | data formatting | bytes 589824 | tf_op jit(solution)/shard_map/all_to_all | solution.py:97
  (8 shorter events, 0.1 us)
Async XLA Ops:
  1.4 6.1 %copy-start = (bf16[2,256,256]{2,1,0:T(8,128)(2,1)S(1)}, bf16[2,256,256]{2,1,0:T(8,128)(2,1)}, u32[]{:S(2)}) copy-start(bf16[2,256,256]{2,1,0:T(8,128)(2,1)} %param.7) | copy-start | bytes 786436
  2.9 14.8 %all-to-all-start = ((bf16[4,4,7,12,256]{4,1,3,2,0:T(4,128)(2,1)}), bf16[4,4,7,12,256]{4,1,3,2,0:T(4,128)(2,1)S(1)}, u32[]{:S(2)}, u32[]{:S(2)}) async-start(bf16[4,4,7,12,256]{4,1,3,2,0:T(4,128)(2,1)} %pad_maximum_fusion.1), calls=%async_computation | async-start | bytes 1376256 | tf_op jit(solution)/shard_map/all_to_all | solution.py:76
  7.5 15.7 %copy-start.1 = (f32[2,16,256]{2,1,0:T(8,128)S(1)}, f32[2,16,256]{2,1,0:T(8,128)}, u32[]{:S(2)}) copy-start(f32[2,16,256]{2,1,0:T(8,128)} %param.6) | copy-start | bytes 98308
  17.8 6.5 %collective-permute-start = (bf16[4,4,7,2,256]{4,1,3,2,0:T(4,128)(2,1)S(1)}, bf16[4,4,7,2,256]{4,1,3,2,0:T(4,128)(2,1)S(1)}, u32[]{:S(2)}, u32[]{:S(2)}) collective-permute-start(bf16[4,4,7,2,256]{4,1,3,2,0:T(4,128)(2,1)S(1)} %get-tuple-element.7), channel_id=1, source_target_pairs={{0,1},{1,2},{2,3},{4,5},{5,6},{6,7},{8,9},{9,10},{10,11},{12,13},{... | collective-permute-start | bytes 344072 | tf_op jit(solution)/shard_map/ppermute | solution.py:80
  21.9 6.7 %collective-permute-start.1 = (bf16[4,4,7,2,256]{4,1,3,2,0:T(4,128)(2,1)S(1)}, bf16[4,4,7,2,256]{4,1,3,2,0:T(4,128)(2,1)S(1)}, u32[]{:S(2)}, u32[]{:S(2)}) collective-permute-start(bf16[4,4,7,2,256]{4,1,3,2,0:T(4,128)(2,1)S(1)} %get-tuple-element.8), channel_id=1, source_target_pairs={{1,0},{2,1},{3,2},{5,4},{6,5},{7,6},{9,8},{10,9},{11,10},{13,12},{... | collective-permute-start | bytes 344072 | tf_op jit(solution)/shard_map/ppermute | solution.py:81

commit v12 on v6

--- a/solution.py
+++ b/solution.py
@@ -40,17 +40,25 @@
     mixed = jnp.dot(depth, p_ref[...], preferred_element_type=jnp.float32).astype(jnp.bfloat16)
     center = pltpu.roll(window(1).astype(jnp.float32), total - 1, 0)
     state = (center + mixed.astype(jnp.float32)).astype(jnp.bfloat16).reshape(frames, count, chans)
-    o_ref[...] = jnp.where(m_ref[...][None] > 0, state, jnp.zeros((), state.dtype))
+    state = jnp.where(m_ref[...][None] > 0, state, jnp.zeros((), state.dtype))
+    if o_ref.shape[0] == frames:
+        o_ref[...] = state
+    else:
+        cols = o_ref.shape[1]
+        turned = jnp.swapaxes(state.astype(jnp.float32), 0, 1).astype(state.dtype)
+        for r in range(o_ref.shape[0]):
+            o_ref[r] = turned[r * pitch : r * pitch + cols]
 
 
-def block(x, weight, kernel, proj, mask, pitch):
+def block(x, weight, kernel, proj, mask, pitch, cols=None):
     frames, length, chans = x.shape
     count = length - 2 * pitch
+    shape = (frames, count, chans) if cols is None else (count // pitch, cols, frames, chans)
     flops = 2 * frames * count * chans * chans * 10
     vmem = pltpu.VMEM
     return pl.pallas_call(
         functools.partial(block_kernel, count=count, pitch=pitch),
-        out_shape=jax.ShapeDtypeStruct((frames, count, chans), x.dtype),
+        out_shape=jax.ShapeDtypeStruct(shape, x.dtype),
         in_specs=[pl.BlockSpec(memory_space=vmem)] * 5,
         out_specs=pl.BlockSpec(memory_space=vmem),
         compiler_params=pltpu.CompilerParams(vmem_limit_bytes=48 * 1024 * 1024),
@@ -92,10 +100,13 @@
         inside = (row >= 0) & (row < height) & (col >= 0) & (col < sides * cols)
         inside = inside & (lax.broadcasted_iota(jnp.int32, (n_rows, pitch), 1) < cols + 2 * left)
         mask = jnp.broadcast_to(inside.reshape(-1, 1), (n_rows * pitch, chans)).astype(jnp.float32)
-        state = block(state, conv_w[b], depth_k[b], proj_w[b], mask, pitch)
+        last = b == BLOCKS - 1
+        state = block(state, conv_w[b], depth_k[b], proj_w[b], mask, pitch, cols if last else None)
 
-    state = state.reshape(state.shape[0], rows, pitch, chans)[:, :, :cols]
-    return lax.all_to_all(state, "tm", 0, 1, tiled=True)
+    state = state.reshape(rows, cols, bands, frames, chans)
+    state = jnp.transpose(state, (2, 0, 1, 3, 4))
+    state = lax.all_to_all(state, "tm", 0, 1, tiled=True)
+    return jnp.transpose(state[0], (2, 0, 1, 3))
 
 
 def solution(mesh):

time: 45.6 us -> 44.6 us (0.978)
  blocking collectives: 9.8 us -> 8.72 us
    all_to_all x1, blocking collectives: 9.8 us -> 8.72 us  [shards(): state = lax.all_to_all(state, 'tm', 0, 1, tiled=True)]
    all_to_all x1 -> x0, local copies, waits for them, and re-layouts: 0.87 us -> none  [shards(): return lax.all_to_all(state, 'tm', 0, 1, tiled=True)]
    unnamed x4 -> x5, local copies, waits for them, and re-layouts: 0.01 us -> 0.73 us
where the time goes in v12:
time: 44.6 us; the launch traced here: 44.3 us
  waiting for transfers between devices  13.7 us (31%)
  starting transfers between devices  9.71 us (22%)
  blocking collectives  8.72 us (20%)
  Pallas kernels  5.14 us (12%)
  local copies, waits for them, and re-layouts  4.59 us (10%)
  other arithmetic  2.32 us (5%)
    all_to_all x1, blocking collectives, shards(): state = lax.all_to_all(state, 'tm', 0, 1, tiled=True)  8.72 us
    all_to_all x1, waiting for transfers between devices, shards(): received = lax.all_to_all(pieces, 'tm', 0, 0, tiled=False)  8.35 us
    pallas_call x2, Pallas kernels, block(): pl.pallas_call(functools.partial(block_kernel, count=count, pitch=pitch),...  5.14 us
    ppermute x1, waiting for transfers between devices, shards(): after = lax.ppermute(received[:, :, :, :halo], 'width', down)  4.34 us
    all_to_all x1, starting transfers between devices, shards(): received = lax.all_to_all(pieces, 'tm', 0, 0, tiled=False)  4.24 us
    ppermute x1, starting transfers between devices, shards(): before = lax.ppermute(received[:, :, :, cols - halo:], 'width', up)  4.18 us
    squeeze x1, local copies, waits for them, and re-layouts, shards(): conv_w[b]  1.78 us
    another operation x1, other arithmetic, shards(): jnp.stack([padded[:, r * rows:r * rows + rows + 2 * halo] for r in range(...  1.48 us
  transfers between devices with their start and end apart: 3, of which 3 were waited for; matrix products, arithmetic and copies ran while one was open for 5% of the time, Pallas kernels for 0%

profile of v12, /device:TPU:0, one launch (start us, length us, event | category | flops | bytes accessed | tf_op | source)
XLA Modules:
  0.0 44.3 jit_solution(13473139986298695116)
XLA Ops:
  0.0 1.4 %fusion = (bf16[1,4,7,12,256]{4,1,3,2,0:T(4,128)(2,1)S(1)}, bf16[1,4,7,12,256]{4,1,3,2,0:T(4,128)(2,1)S(1)}, bf16[1,4,7,12,256]{4,1,3,2,0:T(4,128)(2,1)S(1)}, bf16[1,4,7,12,256]{4,1,3,2,0:T(4,128)(2,1)S(1)}) fusion(bf16[4,12,12,256]{3,0,2,1:T(4,128)(2,1)} %param.4), kind=kLoop, calls=%fused_computation.7 | loop fusion | bytes 1327104 | tf_op jit(solution)/shard_map/stack | solution.py:84
  1.4 0.0 copy-start
  1.4 1.5 %pad_maximum_fusion.1 = bf16[4,4,7,12,256]{4,1,3,2,0:T(4,128)(2,1)} fusion(bf16[1,4,7,12,256]{4,1,3,2,0:T(4,128)(2,1)S(1)} %get-tuple-element.10, bf16[1,4,7,12,256]{4,1,3,2,0:T(4,128)(2,1)S(1)} %get-tuple-element.11, bf16[1,4,7,12,256]{4,1,3,2,0:T(4,128)(2,1)S(1)} %get-tuple-element.12, bf16[1,4,7,12,256]{4,1,3,2,0:T(4,128)(2,1)S(1)} %get-tuple-element.9), kind=kLoop, calls=%fused_computation.3 | loop fusion | flops 1032192 | bytes 1376256 | tf_op jit(solution)/shard_map/stack | solution.py:84
  2.9 4.2 %all-to-all-start = ((bf16[4,4,7,12,256]{4,1,3,2,0:T(4,128)(2,1)}), bf16[4,4,7,12,256]{4,1,3,2,0:T(4,128)(2,1)S(1)}, u32[]{:S(2)}, u32[]{:S(2)}) async-start(bf16[4,4,7,12,256]{4,1,3,2,0:T(4,128)(2,1)} %pad_maximum_fusion.1), calls=%async_computation | async-start | bytes 1376256 | tf_op jit(solution)/shard_map/all_to_all | solution.py:85
  7.2 0.1 and_convert_fusion
  7.2 0.1 reshape.90
  7.3 0.1 and_convert_fusion.1
  7.4 0.1 reshape.91
  7.5 0.0 copy-done
  7.5 0.0 copy-start.1
  7.5 1.8 %slice_bitcast_fusion = (bf16[3,3,256,256]{3,2,1,0:T(8,128)(2,1)S(1)}, bf16[3,3,256,256]{3,2,1,0:T(8,128)(2,1)S(1)}) fusion(bf16[2,3,3,256,256]{4,3,2,1,0:T(8,128)(2,1)} %param.5), kind=kLoop, calls=%fused_computation | loop fusion | bytes 4718592 | tf_op jit(solution)/shard_map/squeeze | solution.py:104
  9.3 8.3 %all-to-all-done = bf16[4,4,7,12,256]{4,1,3,2,0:T(4,128)(2,1)S(1)} async-done(((bf16[4,4,7,12,256]{4,1,3,2,0:T(4,128)(2,1)}), bf16[4,4,7,12,256]{4,1,3,2,0:T(4,128)(2,1)S(1)}, u32[]{:S(2)}, u32[]{:S(2)}) %all-to-all-start) | async-done | bytes 688160 | tf_op jit(solution)/shard_map/all_to_all | solution.py:85
  17.7 0.1 fusion.6
  17.8 4.2 %collective-permute-start = (bf16[4,4,7,2,256]{4,1,3,2,0:T(4,128)(2,1)S(1)}, bf16[4,4,7,2,256]{4,1,3,2,0:T(4,128)(2,1)S(1)}, u32[]{:S(2)}, u32[]{:S(2)}) collective-permute-start(bf16[4,4,7,2,256]{4,1,3,2,0:T(4,128)(2,1)S(1)} %get-tuple-element.7), channel_id=1, source_target_pairs={{0,1},{1,2},{2,3},{4,5},{5,6},{6,7},{8,9},{9,10},{10,11},{12,13},{... | collective-permute-start | bytes 344072 | tf_op jit(solution)/shard_map/ppermute | solution.py:89
  21.9 1.3 %collective-permute-start.1 = (bf16[4,4,7,2,256]{4,1,3,2,0:T(4,128)(2,1)S(1)}, bf16[4,4,7,2,256]{4,1,3,2,0:T(4,128)(2,1)S(1)}, u32[]{:S(2)}, u32[]{:S(2)}) collective-permute-start(bf16[4,4,7,2,256]{4,1,3,2,0:T(4,128)(2,1)S(1)} %get-tuple-element.8), channel_id=1, source_target_pairs={{1,0},{2,1},{3,2},{5,4},{6,5},{7,6},{9,8},{10,9},{11,10},{13,12},{... | collective-permute-start | bytes 344072 | tf_op jit(solution)/shard_map/ppermute | solution.py:90
  23.2 0.0 copy-done.1
  23.3 1.0 %collective-permute-done = bf16[4,4,7,2,256]{4,1,3,2,0:T(4,128)(2,1)S(1)} collective-permute-done((bf16[4,4,7,2,256]{4,1,3,2,0:T(4,128)(2,1)S(1)}, bf16[4,4,7,2,256]{4,1,3,2,0:T(4,128)(2,1)S(1)}, u32[]{:S(2)}, u32[]{:S(2)}) %collective-permute-start) | collective-permute-done | bytes 114720 | tf_op jit(solution)/shard_map/ppermute | solution.py:89
  24.3 4.3 %collective-permute-done.1 = bf16[4,4,7,2,256]{4,1,3,2,0:T(4,128)(2,1)S(1)} collective-permute-done((bf16[4,4,7,2,256]{4,1,3,2,0:T(4,128)(2,1)S(1)}, bf16[4,4,7,2,256]{4,1,3,2,0:T(4,128)(2,1)S(1)}, u32[]{:S(2)}, u32[]{:S(2)}) %collective-permute-start.1) | collective-permute-done | bytes 114720 | tf_op jit(solution)/shard_map/ppermute | solution.py:90
  28.6 0.6 %pad_maximum_fusion = bf16[4,4,7,16,256]{4,1,3,2,0:T(4,128)(2,1)S(1)} fusion(bf16[4,4,7,2,256]{4,1,3,2,0:T(4,128)(2,1)S(1)} %collective-permute-done.1, bf16[4,4,7,12,256]{4,1,3,2,0:T(4,128)(2,1)S(1)} %all-to-all-done, bf16[4,4,7,2,256]{4,1,3,2,0:T(4,128)(2,1)S(1)} %collective-permute-done), kind=kLoop, calls=%fused_computation.2 | loop fusion | flops 917504 | bytes 1835008 | tf_op jit(solution)/shard_map/concatenate | solution.py:92
  29.3 0.1 copy.7
  29.4 0.1 broadcast_in_dim.4.m_ref
  29.5 3.1 %shard_map.46.x_ref = bf16[16,80,256]{2,1,0:T(8,128)(2,1)S(1)} custom-call(bf16[16,112,256]{2,1,0:T(8,128)(2,1)S(1)} %bitcast.29, bf16[3,3,256,256]{3,2,1,0:T(8,128)(2,1)S(1)} %get-tuple-element.6.w_ref, f32[16,256]{1,0:T(8,128)S(1)} %get-tuple-element.16.k_ref, bf16[256,256]{1,0:T(8,128)(2,1)S(1)} %get-tuple-element.14.p_ref, ...), custom_call_target="tpu_custom_call" | custom-call | flops 1677721600 | bytes 2883584 | tf_op jit(solution)/shard_map/pallas_call | solution.py:59
  32.6 0.1 broadcast_in_dim.5.m_ref
  32.7 2.0 %shard_map.47 = bf16[3,12,16,256]{3,2,1,0:T(8,128)(2,1)S(1)} custom-call(bf16[16,80,256]{2,1,0:T(8,128)(2,1)S(1)} %shard_map.46.x_ref, bf16[3,3,256,256]{3,2,1,0:T(8,128)(2,1)S(1)} %get-tuple-element.5.w_ref, f32[16,256]{1,0:T(8,128)S(1)} %get-tuple-element.15.k_ref, bf16[256,256]{1,0:T(8,128)(2,1)S(1)} %get-tuple-element.13.p_ref, ...), custom_call_target="tpu_custom_call" | custom-call | flops 1006632960 | bytes 2359296 | tf_op jit(solution)/shard_map/pallas_call | solution.py:59
  34.7 0.1 reshape.89
  34.8 0.1 copy.10
  34.9 8.7 %all_to_all.14 = bf16[4,3,12,4,256]{4,3,2,1,0:T(4,128)(2,1)S(1)} all-to-all(bf16[4,3,12,4,256]{4,3,2,1,0:T(4,128)(2,1)S(1)} %bitcast.30), channel_id=1, replica_groups=mesh['groups'=2,'tm'=4,'width'=4] {'tm'}, dimensions={0} | all-to-all | bytes 589824 | tf_op jit(solution)/shard_map/all_to_all | solution.py:108
  43.6 0.7 %copy.12 = bf16[4,12,12,256]{3,0,2,1:T(4,128)(2,1)} copy(bf16[4,12,12,256]{3,0,2,1:T(4,128)(2,1)S(1)} %bitcast.31) | data formatting | bytes 589824
  (8 shorter events, 0.1 us)
Async XLA Ops:
  1.4 6.1 %copy-start = (bf16[2,256,256]{2,1,0:T(8,128)(2,1)S(1)}, bf16[2,256,256]{2,1,0:T(8,128)(2,1)}, u32[]{:S(2)}) copy-start(bf16[2,256,256]{2,1,0:T(8,128)(2,1)} %param.7) | copy-start | bytes 786436
  2.9 14.8 %all-to-all-start = ((bf16[4,4,7,12,256]{4,1,3,2,0:T(4,128)(2,1)}), bf16[4,4,7,12,256]{4,1,3,2,0:T(4,128)(2,1)S(1)}, u32[]{:S(2)}, u32[]{:S(2)}) async-start(bf16[4,4,7,12,256]{4,1,3,2,0:T(4,128)(2,1)} %pad_maximum_fusion.1), calls=%async_computation | async-start | bytes 1376256 | tf_op jit(solution)/shard_map/all_to_all | solution.py:85
  7.5 15.7 %copy-start.1 = (f32[2,16,256]{2,1,0:T(8,128)S(1)}, f32[2,16,256]{2,1,0:T(8,128)}, u32[]{:S(2)}) copy-start(f32[2,16,256]{2,1,0:T(8,128)} %param.6) | copy-start | bytes 98308
  17.8 6.5 %collective-permute-start = (bf16[4,4,7,2,256]{4,1,3,2,0:T(4,128)(2,1)S(1)}, bf16[4,4,7,2,256]{4,1,3,2,0:T(4,128)(2,1)S(1)}, u32[]{:S(2)}, u32[]{:S(2)}) collective-permute-start(bf16[4,4,7,2,256]{4,1,3,2,0:T(4,128)(2,1)S(1)} %get-tuple-element.7), channel_id=1, source_target_pairs={{0,1},{1,2},{2,3},{4,5},{5,6},{6,7},{8,9},{9,10},{10,11},{12,13},{... | collective-permute-start | bytes 344072 | tf_op jit(solution)/shard_map/ppermute | solution.py:89
  21.9 6.7 %collective-permute-start.1 = (bf16[4,4,7,2,256]{4,1,3,2,0:T(4,128)(2,1)S(1)}, bf16[4,4,7,2,256]{4,1,3,2,0:T(4,128)(2,1)S(1)}, u32[]{:S(2)}, u32[]{:S(2)}) collective-permute-start(bf16[4,4,7,2,256]{4,1,3,2,0:T(4,128)(2,1)S(1)} %get-tuple-element.8), channel_id=1, source_target_pairs={{1,0},{2,1},{3,2},{5,4},{6,5},{7,6},{9,8},{10,9},{11,10},{13,12},{... | collective-permute-start | bytes 344072 | tf_op jit(solution)/shard_map/ppermute | solution.py:90

commit v13 on v12

--- a/solution.py
+++ b/solution.py
@@ -1,6 +1,7 @@
 import functools
 
 import jax
+import numpy as np
 import jax.numpy as jnp
 from jax import lax
 from jax.experimental import pallas as pl
@@ -81,7 +82,9 @@
     pitch = -(-(cols + 2 * halo) // LANES) * LANES
 
     padded = jnp.pad(video, ((0, 0), (halo, halo), (0, 0), (0, 0)))
-    pieces = jnp.stack([padded[:, r * rows : r * rows + rows + 2 * halo] for r in range(bands)])
+    picks = np.array([r * rows + i for r in range(bands) for i in range(rows + 2 * halo)], np.int32)
+    pieces = jnp.take(padded, picks, axis=1).reshape(frames, bands, rows + 2 * halo, cols, chans)
+    pieces = jnp.transpose(pieces, (1, 0, 2, 3, 4))
     received = lax.all_to_all(pieces, "tm", 0, 0, tiled=False)
 
     up = [(i, i + 1) for i in range(sides - 1)]

time: 44.6 us -> 45.6 us (1.022)
  local copies, waits for them, and re-layouts: 4.59 us -> 6.31 us
  other arithmetic: 2.32 us -> 1.5 us
    gather x0 -> x1, local copies, waits for them, and re-layouts: none -> 1.99 us  [shards(): jnp.take(padded, picks, axis=1)]
    another operation x1 -> x0, other arithmetic: 1.48 us -> none  [shards(): jnp.stack([padded[:, r * rows:r * rows + rows + 2 * halo] for r in range(...]
    another operation x1 -> x0, local copies, waits for them, and re-layouts: 1.36 us -> none  [shards(): jnp.stack([padded[:, r * rows:r * rows + rows + 2 * halo] for r in range(...]
    pad x0 -> x1, local copies, waits for them, and re-layouts: none -> 1.1 us  [shards(): padded = jnp.pad(video, ((0, 0), (halo, halo), (0, 0), (0, 0)))]
    gather x0 -> x1, other arithmetic: none -> 0.66 us  [shards(): jnp.take(padded, picks, axis=1)]
where the time goes in v13:
time: 45.6 us; the launch traced here: 45.2 us
  waiting for transfers between devices  13.7 us (30%)
  starting transfers between devices  9.71 us (21%)
  blocking collectives  8.72 us (19%)
  local copies, waits for them, and re-layouts  6.31 us (14%)
  Pallas kernels  5.14 us (11%)
  other arithmetic  1.5 us (3%)
    all_to_all x1, blocking collectives, shards(): state = lax.all_to_all(state, 'tm', 0, 1, tiled=True)  8.72 us
    all_to_all x1, waiting for transfers between devices, shards(): received = lax.all_to_all(pieces, 'tm', 0, 0, tiled=False)  8.35 us
    pallas_call x2, Pallas kernels, block(): pl.pallas_call(functools.partial(block_kernel, count=count, pitch=pitch),...  5.14 us
    ppermute x1, waiting for transfers between devices, shards(): after = lax.ppermute(received[:, :, :, :halo], 'width', down)  4.34 us
    all_to_all x1, starting transfers between devices, shards(): received = lax.all_to_all(pieces, 'tm', 0, 0, tiled=False)  4.24 us
    ppermute x1, starting transfers between devices, shards(): before = lax.ppermute(received[:, :, :, cols - halo:], 'width', up)  4.18 us
    gather x1, local copies, waits for them, and re-layouts, shards(): jnp.take(padded, picks, axis=1)  1.99 us
    squeeze x1, local copies, waits for them, and re-layouts, shards(): conv_w[b]  1.78 us
  transfers between devices with their start and end apart: 3, of which 3 were waited for; matrix products, arithmetic and copies ran while one was open for 5% of the time, Pallas kernels for 0%

profile of v13, /device:TPU:0, one launch (start us, length us, event | category | flops | bytes accessed | tf_op | source)
XLA Modules:
  0.0 45.2 jit_solution(7881079783738646886)
XLA Ops:
  0.0 0.7 %pad_clamp_fusion = s32[1024]{0:T(1024)S(1)} fusion(s32[28]{0:T(128)} %constant.58), kind=kLoop, calls=%fused_computation.9 | loop fusion | flops 1024 | bytes 4208 | tf_op jit(solution)/shard_map/jit(_take)/gather | solution.py:86
  0.7 1.1 %pad.4 = bf16[4,16,12,256]{3,0,2,1:T(4,128)(2,1)S(1)} pad(bf16[4,12,12,256]{3,0,2,1:T(4,128)(2,1)} %param.5, bf16[]{:T(256)} %constant.16.clone.1), padding=0_0x2_2x0_0x0_0 | pad | bytes 688130 | tf_op jit(solution)/shard_map/jit(_pad)/pad | solution.py:84
  1.8 0.0 copy-start
  1.8 2.0 %gather_fusion = bf16[28,4,12,256]{3,1,2,0:T(4,128)(2,1)} fusion(bf16[4,16,12,256]{3,0,2,1:T(4,128)(2,1)S(1)} %pad.4, s32[1024]{0:T(1024)S(1)} %pad_clamp_fusion), kind=kCustom, calls=%fused_computation | custom fusion | bytes 1376368 | tf_op jit(solution)/shard_map/jit(_take)/gather | solution.py:86
  3.8 4.2 %all-to-all-start = ((bf16[4,4,7,12,256]{4,1,3,2,0:T(4,128)(2,1)}), bf16[4,4,7,12,256]{4,1,3,2,0:T(4,128)(2,1)S(1)}, u32[]{:S(2)}, u32[]{:S(2)}) async-start(bf16[4,4,7,12,256]{4,1,3,2,0:T(4,128)(2,1)} %bitcast.2), calls=%async_computation | async-start | bytes 1376256 | tf_op jit(solution)/shard_map/all_to_all | solution.py:88
  8.1 0.1 and_convert_fusion
  8.1 0.1 reshape.99
  8.2 0.1 and_convert_fusion.1
  8.3 0.1 reshape.100
  8.4 0.0 copy-done
  8.4 0.0 copy-start.1
  8.4 1.8 %slice_bitcast_fusion = (bf16[3,3,256,256]{3,2,1,0:T(8,128)(2,1)S(1)}, bf16[3,3,256,256]{3,2,1,0:T(8,128)(2,1)S(1)}) fusion(bf16[2,3,3,256,256]{4,3,2,1,0:T(8,128)(2,1)} %param.6), kind=kLoop, calls=%fused_computation.1 | loop fusion | bytes 4718592 | tf_op jit(solution)/shard_map/squeeze | solution.py:107
  10.2 8.3 %all-to-all-done = bf16[4,4,7,12,256]{4,1,3,2,0:T(4,128)(2,1)S(1)} async-done(((bf16[4,4,7,12,256]{4,1,3,2,0:T(4,128)(2,1)}), bf16[4,4,7,12,256]{4,1,3,2,0:T(4,128)(2,1)S(1)}, u32[]{:S(2)}, u32[]{:S(2)}) %all-to-all-start) | async-done | bytes 688160 | tf_op jit(solution)/shard_map/all_to_all | solution.py:88
  18.6 0.1 fusion.4
  18.6 4.2 %collective-permute-start = (bf16[4,4,7,2,256]{4,1,3,2,0:T(4,128)(2,1)S(1)}, bf16[4,4,7,2,256]{4,1,3,2,0:T(4,128)(2,1)S(1)}, u32[]{:S(2)}, u32[]{:S(2)}) collective-permute-start(bf16[4,4,7,2,256]{4,1,3,2,0:T(4,128)(2,1)S(1)} %get-tuple-element.7), channel_id=1, source_target_pairs={{0,1},{1,2},{2,3},{4,5},{5,6},{6,7},{8,9},{9,10},{10,11},{12,13},{... | collective-permute-start | bytes 344072 | tf_op jit(solution)/shard_map/ppermute | solution.py:92
  22.8 1.3 %collective-permute-start.1 = (bf16[4,4,7,2,256]{4,1,3,2,0:T(4,128)(2,1)S(1)}, bf16[4,4,7,2,256]{4,1,3,2,0:T(4,128)(2,1)S(1)}, u32[]{:S(2)}, u32[]{:S(2)}) collective-permute-start(bf16[4,4,7,2,256]{4,1,3,2,0:T(4,128)(2,1)S(1)} %get-tuple-element.8), channel_id=1, source_target_pairs={{1,0},{2,1},{3,2},{5,4},{6,5},{7,6},{9,8},{10,9},{11,10},{13,12},{... | collective-permute-start | bytes 344072 | tf_op jit(solution)/shard_map/ppermute | solution.py:93
  24.1 0.0 copy-done.1
  24.2 1.0 %collective-permute-done = bf16[4,4,7,2,256]{4,1,3,2,0:T(4,128)(2,1)S(1)} collective-permute-done((bf16[4,4,7,2,256]{4,1,3,2,0:T(4,128)(2,1)S(1)}, bf16[4,4,7,2,256]{4,1,3,2,0:T(4,128)(2,1)S(1)}, u32[]{:S(2)}, u32[]{:S(2)}) %collective-permute-start) | collective-permute-done | bytes 114720 | tf_op jit(solution)/shard_map/ppermute | solution.py:92
  25.2 4.3 %collective-permute-done.1 = bf16[4,4,7,2,256]{4,1,3,2,0:T(4,128)(2,1)S(1)} collective-permute-done((bf16[4,4,7,2,256]{4,1,3,2,0:T(4,128)(2,1)S(1)}, bf16[4,4,7,2,256]{4,1,3,2,0:T(4,128)(2,1)S(1)}, u32[]{:S(2)}, u32[]{:S(2)}) %collective-permute-start.1) | collective-permute-done | bytes 114720 | tf_op jit(solution)/shard_map/ppermute | solution.py:93
  29.5 0.6 %pad_maximum_fusion = bf16[4,4,7,16,256]{4,1,3,2,0:T(4,128)(2,1)S(1)} fusion(bf16[4,4,7,2,256]{4,1,3,2,0:T(4,128)(2,1)S(1)} %collective-permute-done.1, bf16[4,4,7,12,256]{4,1,3,2,0:T(4,128)(2,1)S(1)} %all-to-all-done, bf16[4,4,7,2,256]{4,1,3,2,0:T(4,128)(2,1)S(1)} %collective-permute-done), kind=kLoop, calls=%fused_computation.3 | loop fusion | flops 917504 | bytes 1835008 | tf_op jit(solution)/shard_map/concatenate | solution.py:95
  30.2 0.1 copy.8
  30.3 0.1 broadcast_in_dim.28.m_ref
  30.4 3.1 %shard_map.55.x_ref = bf16[16,80,256]{2,1,0:T(8,128)(2,1)S(1)} custom-call(bf16[16,112,256]{2,1,0:T(8,128)(2,1)S(1)} %bitcast.26, bf16[3,3,256,256]{3,2,1,0:T(8,128)(2,1)S(1)} %get-tuple-element.6.w_ref, f32[16,256]{1,0:T(8,128)S(1)} %get-tuple-element.12.k_ref, bf16[256,256]{1,0:T(8,128)(2,1)S(1)} %get-tuple-element.10.p_ref, ...), custom_call_target="tpu_custom_call" | custom-call | flops 1677721600 | bytes 2883584 | tf_op jit(solution)/shard_map/pallas_call | solution.py:60
  33.5 0.1 broadcast_in_dim.29.m_ref
  33.6 2.0 %shard_map.56 = bf16[3,12,16,256]{3,2,1,0:T(8,128)(2,1)S(1)} custom-call(bf16[16,80,256]{2,1,0:T(8,128)(2,1)S(1)} %shard_map.55.x_ref, bf16[3,3,256,256]{3,2,1,0:T(8,128)(2,1)S(1)} %get-tuple-element.5.w_ref, f32[16,256]{1,0:T(8,128)S(1)} %get-tuple-element.11.k_ref, bf16[256,256]{1,0:T(8,128)(2,1)S(1)} %get-tuple-element.9.p_ref, ...), custom_call_target="tpu_custom_call" | custom-call | flops 1006632960 | bytes 2359296 | tf_op jit(solution)/shard_map/pallas_call | solution.py:60
  35.6 0.1 reshape.98
  35.7 0.1 copy.11
  35.8 8.7 %all_to_all.14 = bf16[4,3,12,4,256]{4,3,2,1,0:T(4,128)(2,1)S(1)} all-to-all(bf16[4,3,12,4,256]{4,3,2,1,0:T(4,128)(2,1)S(1)} %bitcast.27), channel_id=1, replica_groups=mesh['groups'=2,'tm'=4,'width'=4] {'tm'}, dimensions={0} | all-to-all | bytes 589824 | tf_op jit(solution)/shard_map/all_to_all | solution.py:111
  44.5 0.7 %copy.13 = bf16[4,12,12,256]{3,0,2,1:T(4,128)(2,1)} copy(bf16[4,12,12,256]{3,0,2,1:T(4,128)(2,1)S(1)} %bitcast.28) | data formatting | bytes 589824
  (8 shorter events, 0.1 us)
Async XLA Ops:
  1.8 6.6 %copy-start = (bf16[2,256,256]{2,1,0:T(8,128)(2,1)S(1)}, bf16[2,256,256]{2,1,0:T(8,128)(2,1)}, u32[]{:S(2)}) copy-start(bf16[2,256,256]{2,1,0:T(8,128)(2,1)} %param.8) | copy-start | bytes 786436
  3.8 14.8 %all-to-all-start = ((bf16[4,4,7,12,256]{4,1,3,2,0:T(4,128)(2,1)}), bf16[4,4,7,12,256]{4,1,3,2,0:T(4,128)(2,1)S(1)}, u32[]{:S(2)}, u32[]{:S(2)}) async-start(bf16[4,4,7,12,256]{4,1,3,2,0:T(4,128)(2,1)} %bitcast.2), calls=%async_computation | async-start | bytes 1376256 | tf_op jit(solution)/shard_map/all_to_all | solution.py:88
  8.4 15.7 %copy-start.1 = (f32[2,16,256]{2,1,0:T(8,128)S(1)}, f32[2,16,256]{2,1,0:T(8,128)}, u32[]{:S(2)}) copy-start(f32[2,16,256]{2,1,0:T(8,128)} %param.7) | copy-start | bytes 98308
  18.6 6.5 %collective-permute-start = (bf16[4,4,7,2,256]{4,1,3,2,0:T(4,128)(2,1)S(1)}, bf16[4,4,7,2,256]{4,1,3,2,0:T(4,128)(2,1)S(1)}, u32[]{:S(2)}, u32[]{:S(2)}) collective-permute-start(bf16[4,4,7,2,256]{4,1,3,2,0:T(4,128)(2,1)S(1)} %get-tuple-element.7), channel_id=1, source_target_pairs={{0,1},{1,2},{2,3},{4,5},{5,6},{6,7},{8,9},{9,10},{10,11},{12,13},{... | collective-permute-start | bytes 344072 | tf_op jit(solution)/shard_map/ppermute | solution.py:92
  22.8 6.7 %collective-permute-start.1 = (bf16[4,4,7,2,256]{4,1,3,2,0:T(4,128)(2,1)S(1)}, bf16[4,4,7,2,256]{4,1,3,2,0:T(4,128)(2,1)S(1)}, u32[]{:S(2)}, u32[]{:S(2)}) collective-permute-start(bf16[4,4,7,2,256]{4,1,3,2,0:T(4,128)(2,1)S(1)} %get-tuple-element.8), channel_id=1, source_target_pairs={{1,0},{2,1},{3,2},{5,4},{6,5},{7,6},{9,8},{10,9},{11,10},{13,12},{... | collective-permute-start | bytes 344072 | tf_op jit(solution)/shard_map/ppermute | solution.py:93

commit v14 on v12

--- a/solution.py
+++ b/solution.py
@@ -11,7 +11,7 @@
 LANES = 16
 
 
-def block_kernel(x_ref, w_ref, k_ref, p_ref, m_ref, o_ref, *, count, pitch):
+def block_kernel(x_ref, w_ref, k_ref, p_ref, m_ref, o_ref, v_ref, d_ref, *, count, pitch):
     frames, _, chans = x_ref.shape
     total = frames * count
 
@@ -25,17 +25,26 @@
             part = jnp.dot(piece, w_ref[dy, dx], preferred_element_type=jnp.float32)
             taps[dx] = part if taps[dx] is None else taps[dx] + part
     conv = taps[0] + pltpu.roll(taps[1], total - 1, 0) + pltpu.roll(taps[2], total - 2, 0)
-    hidden = (conv / (1.0 + jnp.exp(-conv))).astype(jnp.bfloat16)
+    hidden = (conv * (0.5 + 0.5 * jnp.tanh(0.5 * conv))).astype(jnp.bfloat16)
+    v_ref[...] = hidden.astype(jnp.float32).reshape(frames, count, chans)
 
-    values = hidden.astype(jnp.float32).reshape(frames, count, chans)
-    kernel = k_ref[...]
-    depth = []
-    for t in range(frames):
-        acc = values[t] * kernel[0:1]
-        for lag in range(1, t + 1):
-            acc = acc + values[t - lag] * kernel[lag : lag + 1]
-        depth.append(acc.astype(jnp.bfloat16))
-    depth = jnp.stack(depth).reshape(total, chans)
+    sub, lane = 8, 128
+    tiles = (count // sub) * (chans // lane)
+
+    def mix(i, carry):
+        rows = pl.ds(pl.multiple_of((i // (chans // lane)) * sub, sub), sub)
+        lanes = pl.ds(pl.multiple_of((i % (chans // lane)) * lane, lane), lane)
+        values = [v_ref[s, rows, lanes] for s in range(frames)]
+        taps_k = [k_ref[lag, :, lanes] for lag in range(frames)]
+        for t in range(frames):
+            acc = values[t] * taps_k[0]
+            for lag in range(1, t + 1):
+                acc = acc + values[t - lag] * taps_k[lag]
+            d_ref[t, rows, lanes] = acc
+        return carry
+
+    lax.fori_loop(0, tiles, mix, 0)
+    depth = d_ref[...].astype(jnp.bfloat16).reshape(total, chans)
 
     mixed = jnp.dot(depth, p_ref[...], preferred_element_type=jnp.float32).astype(jnp.bfloat16)
     center = pltpu.roll(window(1).astype(jnp.float32), total - 1, 0)
@@ -61,13 +70,14 @@
         out_shape=jax.ShapeDtypeStruct(shape, x.dtype),
         in_specs=[pl.BlockSpec(memory_space=vmem)] * 5,
         out_specs=pl.BlockSpec(memory_space=vmem),
+        scratch_shapes=[pltpu.VMEM((frames, count, chans), jnp.float32)] * 2,
         compiler_params=pltpu.CompilerParams(vmem_limit_bytes=48 * 1024 * 1024),
         cost_estimate=pl.CostEstimate(
             flops=flops,
             transcendentals=frames * count * chans,
             bytes_accessed=2 * frames * (length + count) * chans + 2 * 10 * chans * chans,
         ),
-    )(x, weight, kernel, proj, mask)
+    )(x, weight, jnp.broadcast_to(kernel[:, None, :], (frames, 8, chans)), proj, mask)
 
 
 def shards(video, conv_w, depth_k, proj_w):

time: 44.6 us -> 45.3 us (1.016)
  Pallas kernels: 5.14 us -> 5.81 us
    pallas_call x2, Pallas kernels: 5.14 us -> 5.81 us  [block(): pl.pallas_call(functools.partial(block_kernel, count=count, pitch=pitch),...]
where the time goes in v14:
time: 45.3 us; the launch traced here: 45 us
  waiting for transfers between devices  13.7 us (30%)
  starting transfers between devices  9.71 us (21%)
  blocking collectives  8.72 us (19%)
  Pallas kernels  5.81 us (13%)
  local copies, waits for them, and re-layouts  4.61 us (10%)
  other arithmetic  2.32 us (5%)
    all_to_all x1, blocking collectives, shards(): state = lax.all_to_all(state, 'tm', 0, 1, tiled=True)  8.72 us
    all_to_all x1, waiting for transfers between devices, shards(): received = lax.all_to_all(pieces, 'tm', 0, 0, tiled=False)  8.35 us
    pallas_call x2, Pallas kernels, block(): pl.pallas_call(functools.partial(block_kernel, count=count, pitch=pitch),...  5.81 us
    ppermute x1, waiting for transfers between devices, shards(): after = lax.ppermute(received[:, :, :, :halo], 'width', down)  4.34 us
    all_to_all x1, starting transfers between devices, shards(): received = lax.all_to_all(pieces, 'tm', 0, 0, tiled=False)  4.24 us
    ppermute x1, starting transfers between devices, shards(): before = lax.ppermute(received[:, :, :, cols - halo:], 'width', up)  4.18 us
    squeeze x1, local copies, waits for them, and re-layouts, shards(): conv_w[b]  1.78 us
    another operation x1, other arithmetic, shards(): jnp.stack([padded[:, r * rows:r * rows + rows + 2 * halo] for r in range(...  1.48 us
  transfers between devices with their start and end apart: 3, of which 3 were waited for; matrix products, arithmetic and copies ran while one was open for 5% of the time, Pallas kernels for 0%

profile of v14, /device:TPU:0, one launch (start us, length us, event | category | flops | bytes accessed | tf_op | source)
XLA Modules:
  0.0 45.0 jit_solution(12451008739038494454)
XLA Ops:
  0.0 1.4 %fusion = (bf16[1,4,7,12,256]{4,1,3,2,0:T(4,128)(2,1)S(1)}, bf16[1,4,7,12,256]{4,1,3,2,0:T(4,128)(2,1)S(1)}, bf16[1,4,7,12,256]{4,1,3,2,0:T(4,128)(2,1)S(1)}, bf16[1,4,7,12,256]{4,1,3,2,0:T(4,128)(2,1)S(1)}) fusion(bf16[4,12,12,256]{3,0,2,1:T(4,128)(2,1)} %param.4), kind=kLoop, calls=%fused_computation.7 | loop fusion | bytes 1327104 | tf_op jit(solution)/shard_map/stack | solution.py:94
  1.4 0.0 copy-start
  1.4 1.5 %pad_maximum_fusion.1 = bf16[4,4,7,12,256]{4,1,3,2,0:T(4,128)(2,1)} fusion(bf16[1,4,7,12,256]{4,1,3,2,0:T(4,128)(2,1)S(1)} %get-tuple-element.10, bf16[1,4,7,12,256]{4,1,3,2,0:T(4,128)(2,1)S(1)} %get-tuple-element.11, bf16[1,4,7,12,256]{4,1,3,2,0:T(4,128)(2,1)S(1)} %get-tuple-element.12, bf16[1,4,7,12,256]{4,1,3,2,0:T(4,128)(2,1)S(1)} %get-tuple-element.9), kind=kLoop, calls=%fused_computation.3 | loop fusion | flops 1032192 | bytes 1376256 | tf_op jit(solution)/shard_map/stack | solution.py:94
  2.9 4.2 %all-to-all-start = ((bf16[4,4,7,12,256]{4,1,3,2,0:T(4,128)(2,1)}), bf16[4,4,7,12,256]{4,1,3,2,0:T(4,128)(2,1)S(1)}, u32[]{:S(2)}, u32[]{:S(2)}) async-start(bf16[4,4,7,12,256]{4,1,3,2,0:T(4,128)(2,1)} %pad_maximum_fusion.1), calls=%async_computation | async-start | bytes 1376256 | tf_op jit(solution)/shard_map/all_to_all | solution.py:95
  7.2 0.1 and_convert_fusion
  7.2 0.1 reshape.92
  7.3 0.1 and_convert_fusion.1
  7.4 0.1 reshape.93
  7.5 0.0 copy-done
  7.5 0.0 copy-start.1
  7.5 1.8 %slice_bitcast_fusion = (bf16[3,3,256,256]{3,2,1,0:T(8,128)(2,1)S(1)}, bf16[3,3,256,256]{3,2,1,0:T(8,128)(2,1)S(1)}) fusion(bf16[2,3,3,256,256]{4,3,2,1,0:T(8,128)(2,1)} %param.5), kind=kLoop, calls=%fused_computation | loop fusion | bytes 4718592 | tf_op jit(solution)/shard_map/squeeze | solution.py:114
  9.3 8.3 %all-to-all-done = bf16[4,4,7,12,256]{4,1,3,2,0:T(4,128)(2,1)S(1)} async-done(((bf16[4,4,7,12,256]{4,1,3,2,0:T(4,128)(2,1)}), bf16[4,4,7,12,256]{4,1,3,2,0:T(4,128)(2,1)S(1)}, u32[]{:S(2)}, u32[]{:S(2)}) %all-to-all-start) | async-done | bytes 688160 | tf_op jit(solution)/shard_map/all_to_all | solution.py:95
  17.7 0.1 fusion.6
  17.8 4.2 %collective-permute-start = (bf16[4,4,7,2,256]{4,1,3,2,0:T(4,128)(2,1)S(1)}, bf16[4,4,7,2,256]{4,1,3,2,0:T(4,128)(2,1)S(1)}, u32[]{:S(2)}, u32[]{:S(2)}) collective-permute-start(bf16[4,4,7,2,256]{4,1,3,2,0:T(4,128)(2,1)S(1)} %get-tuple-element.7), channel_id=1, source_target_pairs={{0,1},{1,2},{2,3},{4,5},{5,6},{6,7},{8,9},{9,10},{10,11},{12,13},{... | collective-permute-start | bytes 344072 | tf_op jit(solution)/shard_map/ppermute | solution.py:99
  21.9 1.3 %collective-permute-start.1 = (bf16[4,4,7,2,256]{4,1,3,2,0:T(4,128)(2,1)S(1)}, bf16[4,4,7,2,256]{4,1,3,2,0:T(4,128)(2,1)S(1)}, u32[]{:S(2)}, u32[]{:S(2)}) collective-permute-start(bf16[4,4,7,2,256]{4,1,3,2,0:T(4,128)(2,1)S(1)} %get-tuple-element.8), channel_id=1, source_target_pairs={{1,0},{2,1},{3,2},{5,4},{6,5},{7,6},{9,8},{10,9},{11,10},{13,12},{... | collective-permute-start | bytes 344072 | tf_op jit(solution)/shard_map/ppermute | solution.py:100
  23.2 0.0 copy-done.1
  23.3 1.0 %collective-permute-done = bf16[4,4,7,2,256]{4,1,3,2,0:T(4,128)(2,1)S(1)} collective-permute-done((bf16[4,4,7,2,256]{4,1,3,2,0:T(4,128)(2,1)S(1)}, bf16[4,4,7,2,256]{4,1,3,2,0:T(4,128)(2,1)S(1)}, u32[]{:S(2)}, u32[]{:S(2)}) %collective-permute-start) | collective-permute-done | bytes 114720 | tf_op jit(solution)/shard_map/ppermute | solution.py:99
  24.3 4.3 %collective-permute-done.1 = bf16[4,4,7,2,256]{4,1,3,2,0:T(4,128)(2,1)S(1)} collective-permute-done((bf16[4,4,7,2,256]{4,1,3,2,0:T(4,128)(2,1)S(1)}, bf16[4,4,7,2,256]{4,1,3,2,0:T(4,128)(2,1)S(1)}, u32[]{:S(2)}, u32[]{:S(2)}) %collective-permute-start.1) | collective-permute-done | bytes 114720 | tf_op jit(solution)/shard_map/ppermute | solution.py:100
  28.6 0.6 %pad_maximum_fusion = bf16[4,4,7,16,256]{4,1,3,2,0:T(4,128)(2,1)S(1)} fusion(bf16[4,4,7,2,256]{4,1,3,2,0:T(4,128)(2,1)S(1)} %collective-permute-done.1, bf16[4,4,7,12,256]{4,1,3,2,0:T(4,128)(2,1)S(1)} %all-to-all-done, bf16[4,4,7,2,256]{4,1,3,2,0:T(4,128)(2,1)S(1)} %collective-permute-done), kind=kLoop, calls=%fused_computation.2 | loop fusion | flops 917504 | bytes 1835008 | tf_op jit(solution)/shard_map/concatenate | solution.py:102
  29.3 0.1 copy.7
  29.4 0.1 broadcast_in_dim.26.m_ref
  29.5 3.5 %shard_map.46.x_ref = bf16[16,80,256]{2,1,0:T(8,128)(2,1)S(1)} custom-call(bf16[16,112,256]{2,1,0:T(8,128)(2,1)S(1)} %bitcast.29, bf16[3,3,256,256]{3,2,1,0:T(8,128)(2,1)S(1)} %get-tuple-element.6.w_ref, f32[16,8,256]{2,1,0:T(8,128)S(1)} %broadcast_in_dim.25.k_ref, bf16[256,256]{1,0:T(8,128)(2,1)S(1)} %get-tuple-element.14.p_ref, ...), custom_call_target="tpu_custom_call" | custom-call | flops 1677721600 | bytes 2883584 | tf_op jit(solution)/shard_map/pallas_call | solution.py:68
  33.0 0.1 broadcast_in_dim.29.m_ref
  33.1 2.3 %shard_map.47 = bf16[3,12,16,256]{3,2,1,0:T(8,128)(2,1)S(1)} custom-call(bf16[16,80,256]{2,1,0:T(8,128)(2,1)S(1)} %shard_map.46.x_ref, bf16[3,3,256,256]{3,2,1,0:T(8,128)(2,1)S(1)} %get-tuple-element.5.w_ref, f32[16,8,256]{2,1,0:T(8,128)S(1)} %broadcast_in_dim.28.k_ref, bf16[256,256]{1,0:T(8,128)(2,1)S(1)} %get-tuple-element.13.p_ref, ...), custom_call_target="tpu_custom_call" | custom-call | flops 1006632960 | bytes 2359296 | tf_op jit(solution)/shard_map/pallas_call | solution.py:68
  35.4 0.1 reshape.91
  35.5 0.1 copy.10
  35.6 8.7 %all_to_all.14 = bf16[4,3,12,4,256]{4,3,2,1,0:T(4,128)(2,1)S(1)} all-to-all(bf16[4,3,12,4,256]{4,3,2,1,0:T(4,128)(2,1)S(1)} %bitcast.30), channel_id=1, replica_groups=mesh['groups'=2,'tm'=4,'width'=4] {'tm'}, dimensions={0} | all-to-all | bytes 589824 | tf_op jit(solution)/shard_map/all_to_all | solution.py:118
  44.3 0.7 %copy.12 = bf16[4,12,12,256]{3,0,2,1:T(4,128)(2,1)} copy(bf16[4,12,12,256]{3,0,2,1:T(4,128)(2,1)S(1)} %bitcast.31) | data formatting | bytes 589824
  (10 shorter events, 0.1 us)
Async XLA Ops:
  1.4 6.1 %copy-start = (bf16[2,256,256]{2,1,0:T(8,128)(2,1)S(1)}, bf16[2,256,256]{2,1,0:T(8,128)(2,1)}, u32[]{:S(2)}) copy-start(bf16[2,256,256]{2,1,0:T(8,128)(2,1)} %param.7) | copy-start | bytes 786436
  2.9 14.8 %all-to-all-start = ((bf16[4,4,7,12,256]{4,1,3,2,0:T(4,128)(2,1)}), bf16[4,4,7,12,256]{4,1,3,2,0:T(4,128)(2,1)S(1)}, u32[]{:S(2)}, u32[]{:S(2)}) async-start(bf16[4,4,7,12,256]{4,1,3,2,0:T(4,128)(2,1)} %pad_maximum_fusion.1), calls=%async_computation | async-start | bytes 1376256 | tf_op jit(solution)/shard_map/all_to_all | solution.py:95
  7.5 15.7 %copy-start.1 = (f32[2,16,256]{2,1,0:T(8,128)S(1)}, f32[2,16,256]{2,1,0:T(8,128)}, u32[]{:S(2)}) copy-start(f32[2,16,256]{2,1,0:T(8,128)} %param.6) | copy-start | bytes 98308
  17.8 6.5 %collective-permute-start = (bf16[4,4,7,2,256]{4,1,3,2,0:T(4,128)(2,1)S(1)}, bf16[4,4,7,2,256]{4,1,3,2,0:T(4,128)(2,1)S(1)}, u32[]{:S(2)}, u32[]{:S(2)}) collective-permute-start(bf16[4,4,7,2,256]{4,1,3,2,0:T(4,128)(2,1)S(1)} %get-tuple-element.7), channel_id=1, source_target_pairs={{0,1},{1,2},{2,3},{4,5},{5,6},{6,7},{8,9},{9,10},{10,11},{12,13},{... | collective-permute-start | bytes 344072 | tf_op jit(solution)/shard_map/ppermute | solution.py:99
  21.9 6.7 %collective-permute-start.1 = (bf16[4,4,7,2,256]{4,1,3,2,0:T(4,128)(2,1)S(1)}, bf16[4,4,7,2,256]{4,1,3,2,0:T(4,128)(2,1)S(1)}, u32[]{:S(2)}, u32[]{:S(2)}) collective-permute-start(bf16[4,4,7,2,256]{4,1,3,2,0:T(4,128)(2,1)S(1)} %get-tuple-element.8), channel_id=1, source_target_pairs={{1,0},{2,1},{3,2},{5,4},{6,5},{7,6},{9,8},{10,9},{11,10},{13,12},{... | collective-permute-start | bytes 344072 | tf_op jit(solution)/shard_map/ppermute | solution.py:100

commit v15 on v12

--- a/solution.py
+++ b/solution.py
@@ -88,8 +88,11 @@
     down = [(i + 1, i) for i in range(sides - 1)]
     before = lax.ppermute(received[:, :, :, cols - halo :], "width", up)
     after = lax.ppermute(received[:, :, :, :halo], "width", down)
-    spare = jnp.zeros(received.shape[:3] + (pitch - cols - 2 * halo, chans), received.dtype)
-    state = jnp.concatenate([before, received, after, spare], axis=3)
+    state = jnp.pad(received, ((0, 0), (0, 0), (0, 0), (halo, pitch - cols - halo), (0, 0)))
+    state = state.reshape(bands * frames, rows + 2 * halo, pitch, chans)
+    edge = (bands * frames, rows + 2 * halo, halo, chans)
+    state = lax.dynamic_update_slice(state, before.reshape(edge), (0, 0, 0, 0))
+    state = lax.dynamic_update_slice(state, after.reshape(edge), (0, 0, halo + cols, 0))
     state = state.reshape(bands * frames, -1, chans)
 
     for b in range(BLOCKS):

time: 44.6 us -> 44.1 us (0.989)
  local copies, waits for them, and re-layouts: 4.59 us -> 5.53 us
  waiting for transfers between devices: 13.7 us -> 12.9 us
  other arithmetic: 2.32 us -> 1.68 us
    concatenate x1 -> x0, other arithmetic: 0.65 us -> none  [shards(): state = jnp.concatenate([before, received, after, spare], axis=3)]
    ppermute x1, waiting for transfers between devices: 1.02 us -> 0.44 us  [shards(): before = lax.ppermute(received[:, :, :, cols - halo:], 'width', up)]
  transfers between devices with their start and end apart: 3 -> 3, of which waited for: 3 -> 3; matrix products, arithmetic and copies ran while one was open for 5% -> 7% of each run, Pallas kernels for 0% -> 0%
where the time goes in v15:
time: 44.1 us; the launch traced here: 43.8 us
  waiting for transfers between devices  12.9 us (29%)
  starting transfers between devices  9.71 us (22%)
  blocking collectives  8.72 us (20%)
  local copies, waits for them, and re-layouts  5.53 us (13%)
  Pallas kernels  5.14 us (12%)
  other arithmetic  1.68 us (4%)
    all_to_all x1, blocking collectives, shards(): state = lax.all_to_all(state, 'tm', 0, 1, tiled=True)  8.72 us
    all_to_all x1, waiting for transfers between devices, shards(): received = lax.all_to_all(pieces, 'tm', 0, 0, tiled=False)  8.35 us
    pallas_call x2, Pallas kernels, block(): pl.pallas_call(functools.partial(block_kernel, count=count, pitch=pitch),...  5.14 us
    all_to_all x1, starting transfers between devices, shards(): received = lax.all_to_all(pieces, 'tm', 0, 0, tiled=False)  4.24 us
    ppermute x1, starting transfers between devices, shards(): before = lax.ppermute(received[:, :, :, cols - halo:], 'width', up)  4.18 us
    ppermute x1, waiting for transfers between devices, shards(): after = lax.ppermute(received[:, :, :, :halo], 'width', down)  4.1 us
    squeeze x1, local copies, waits for them, and re-layouts, shards(): conv_w[b]  1.78 us
    another operation x1, other arithmetic, shards(): jnp.stack([padded[:, r * rows:r * rows + rows + 2 * halo] for r in range(...  1.48 us
  transfers between devices with their start and end apart: 3, of which 3 were waited for; matrix products, arithmetic and copies ran while one was open for 7% of the time, Pallas kernels for 0%

profile of v15, /device:TPU:0, one launch (start us, length us, event | category | flops | bytes accessed | tf_op | source)
XLA Modules:
  0.0 43.8 jit_solution(6609107710799804127)
XLA Ops:
  0.0 1.4 %fusion = (bf16[1,4,7,12,256]{4,1,3,2,0:T(4,128)(2,1)S(1)}, bf16[1,4,7,12,256]{4,1,3,2,0:T(4,128)(2,1)S(1)}, bf16[1,4,7,12,256]{4,1,3,2,0:T(4,128)(2,1)S(1)}, bf16[1,4,7,12,256]{4,1,3,2,0:T(4,128)(2,1)S(1)}) fusion(bf16[4,12,12,256]{3,0,2,1:T(4,128)(2,1)} %param.4), kind=kLoop, calls=%fused_computation.6 | loop fusion | bytes 1327104 | tf_op jit(solution)/shard_map/stack | solution.py:84
  1.4 0.0 copy-start
  1.4 1.5 %pad_maximum_fusion = bf16[4,4,7,12,256]{4,1,3,2,0:T(4,128)(2,1)} fusion(bf16[1,4,7,12,256]{4,1,3,2,0:T(4,128)(2,1)S(1)} %get-tuple-element.10, bf16[1,4,7,12,256]{4,1,3,2,0:T(4,128)(2,1)S(1)} %get-tuple-element.11, bf16[1,4,7,12,256]{4,1,3,2,0:T(4,128)(2,1)S(1)} %get-tuple-element.12, bf16[1,4,7,12,256]{4,1,3,2,0:T(4,128)(2,1)S(1)} %get-tuple-element.9), kind=kLoop, calls=%fused_computation.2 | loop fusion | flops 1032192 | bytes 1376256 | tf_op jit(solution)/shard_map/stack | solution.py:84
  2.9 4.2 %all-to-all-start = ((bf16[4,4,7,12,256]{4,1,3,2,0:T(4,128)(2,1)}), bf16[4,4,7,12,256]{4,1,3,2,0:T(4,128)(2,1)S(1)}, u32[]{:S(2)}, u32[]{:S(2)}) async-start(bf16[4,4,7,12,256]{4,1,3,2,0:T(4,128)(2,1)} %pad_maximum_fusion), calls=%async_computation | async-start | bytes 1376256 | tf_op jit(solution)/shard_map/all_to_all | solution.py:85
  7.2 0.1 and_convert_fusion
  7.2 0.1 reshape.102
  7.3 0.1 and_convert_fusion.1
  7.4 0.1 reshape.103
  7.5 0.0 copy-done
  7.5 0.0 copy-start.1
  7.5 1.8 %slice_bitcast_fusion = (bf16[3,3,256,256]{3,2,1,0:T(8,128)(2,1)S(1)}, bf16[3,3,256,256]{3,2,1,0:T(8,128)(2,1)S(1)}) fusion(bf16[2,3,3,256,256]{4,3,2,1,0:T(8,128)(2,1)} %param.5), kind=kLoop, calls=%fused_computation | loop fusion | bytes 4718592 | tf_op jit(solution)/shard_map/squeeze | solution.py:107
  9.3 8.3 %all-to-all-done = bf16[4,4,7,12,256]{4,1,3,2,0:T(4,128)(2,1)S(1)} async-done(((bf16[4,4,7,12,256]{4,1,3,2,0:T(4,128)(2,1)}), bf16[4,4,7,12,256]{4,1,3,2,0:T(4,128)(2,1)S(1)}, u32[]{:S(2)}, u32[]{:S(2)}) %all-to-all-start) | async-done | bytes 688160 | tf_op jit(solution)/shard_map/all_to_all | solution.py:85
  17.7 0.1 fusion.6
  17.8 4.2 %collective-permute-start = (bf16[4,4,7,2,256]{4,1,3,2,0:T(4,128)(2,1)S(1)}, bf16[4,4,7,2,256]{4,1,3,2,0:T(4,128)(2,1)S(1)}, u32[]{:S(2)}, u32[]{:S(2)}) collective-permute-start(bf16[4,4,7,2,256]{4,1,3,2,0:T(4,128)(2,1)S(1)} %get-tuple-element.8), channel_id=1, source_target_pairs={{0,1},{1,2},{2,3},{4,5},{5,6},{6,7},{8,9},{9,10},{10,11},{12,13},{... | collective-permute-start | bytes 344072 | tf_op jit(solution)/shard_map/ppermute | solution.py:89
  21.9 0.0 copy-done.1
  22.0 1.3 %collective-permute-start.1 = (bf16[4,4,7,2,256]{4,1,3,2,0:T(4,128)(2,1)S(1)}, bf16[4,4,7,2,256]{4,1,3,2,0:T(4,128)(2,1)S(1)}, u32[]{:S(2)}, u32[]{:S(2)}) collective-permute-start(bf16[4,4,7,2,256]{4,1,3,2,0:T(4,128)(2,1)S(1)} %get-tuple-element.7), channel_id=1, source_target_pairs={{1,0},{2,1},{3,2},{5,4},{6,5},{7,6},{9,8},{10,9},{11,10},{13,12},{... | collective-permute-start | bytes 344072 | tf_op jit(solution)/shard_map/ppermute | solution.py:90
  23.3 0.1 copy.10
  23.4 0.4 pad.9
  23.8 0.4 %collective-permute-done = bf16[4,4,7,2,256]{4,1,3,2,0:T(4,128)(2,1)S(1)} collective-permute-done((bf16[4,4,7,2,256]{4,1,3,2,0:T(4,128)(2,1)S(1)}, bf16[4,4,7,2,256]{4,1,3,2,0:T(4,128)(2,1)S(1)}, u32[]{:S(2)}, u32[]{:S(2)}) %collective-permute-start) | collective-permute-done | bytes 114720 | tf_op jit(solution)/shard_map/ppermute | solution.py:89
  24.3 0.1 copy.11
  24.4 0.2 constant_dynamic-update-slice_fusion.1
  24.5 4.1 %collective-permute-done.1 = bf16[4,4,7,2,256]{4,1,3,2,0:T(4,128)(2,1)S(1)} collective-permute-done((bf16[4,4,7,2,256]{4,1,3,2,0:T(4,128)(2,1)S(1)}, bf16[4,4,7,2,256]{4,1,3,2,0:T(4,128)(2,1)S(1)}, u32[]{:S(2)}, u32[]{:S(2)}) %collective-permute-start.1) | collective-permute-done | bytes 114720 | tf_op jit(solution)/shard_map/ppermute | solution.py:90
  28.7 0.1 copy.12
  28.7 0.2 constant_dynamic-update-slice_fusion
  28.9 0.1 broadcast_in_dim.4.m_ref
  29.0 3.1 %shard_map.46.x_ref = bf16[16,80,256]{2,1,0:T(8,128)(2,1)S(1)} custom-call(bf16[16,112,256]{2,1,0:T(8,128)(2,1)S(1)} %bitcast.33, bf16[3,3,256,256]{3,2,1,0:T(8,128)(2,1)S(1)} %get-tuple-element.6.w_ref, f32[16,256]{1,0:T(8,128)S(1)} %get-tuple-element.16.k_ref, bf16[256,256]{1,0:T(8,128)(2,1)S(1)} %get-tuple-element.14.p_ref, ...), custom_call_target="tpu_custom_call" | custom-call | flops 1677721600 | bytes 2883584 | tf_op jit(solution)/shard_map/pallas_call | solution.py:59
  32.1 0.1 broadcast_in_dim.5.m_ref
  32.2 2.0 %shard_map.47 = bf16[3,12,16,256]{3,2,1,0:T(8,128)(2,1)S(1)} custom-call(bf16[16,80,256]{2,1,0:T(8,128)(2,1)S(1)} %shard_map.46.x_ref, bf16[3,3,256,256]{3,2,1,0:T(8,128)(2,1)S(1)} %get-tuple-element.5.w_ref, f32[16,256]{1,0:T(8,128)S(1)} %get-tuple-element.15.k_ref, bf16[256,256]{1,0:T(8,128)(2,1)S(1)} %get-tuple-element.13.p_ref, ...), custom_call_target="tpu_custom_call" | custom-call | flops 1006632960 | bytes 2359296 | tf_op jit(solution)/shard_map/pallas_call | solution.py:59
  34.2 0.1 reshape.101
  34.3 0.1 copy.15
  34.4 8.7 %all_to_all.14 = bf16[4,3,12,4,256]{4,3,2,1,0:T(4,128)(2,1)S(1)} all-to-all(bf16[4,3,12,4,256]{4,3,2,1,0:T(4,128)(2,1)S(1)} %bitcast.34), channel_id=1, replica_groups=mesh['groups'=2,'tm'=4,'width'=4] {'tm'}, dimensions={0} | all-to-all | bytes 589824 | tf_op jit(solution)/shard_map/all_to_all | solution.py:111
  43.1 0.7 %copy.19 = bf16[4,12,12,256]{3,0,2,1:T(4,128)(2,1)} copy(bf16[4,12,12,256]{3,0,2,1:T(4,128)(2,1)S(1)} %bitcast.35) | data formatting | bytes 589824
  (8 shorter events, 0.1 us)
Async XLA Ops:
  1.4 6.1 %copy-start = (bf16[2,256,256]{2,1,0:T(8,128)(2,1)S(1)}, bf16[2,256,256]{2,1,0:T(8,128)(2,1)}, u32[]{:S(2)}) copy-start(bf16[2,256,256]{2,1,0:T(8,128)(2,1)} %param.7) | copy-start | bytes 786436
  2.9 14.8 %all-to-all-start = ((bf16[4,4,7,12,256]{4,1,3,2,0:T(4,128)(2,1)}), bf16[4,4,7,12,256]{4,1,3,2,0:T(4,128)(2,1)S(1)}, u32[]{:S(2)}, u32[]{:S(2)}) async-start(bf16[4,4,7,12,256]{4,1,3,2,0:T(4,128)(2,1)} %pad_maximum_fusion), calls=%async_computation | async-start | bytes 1376256 | tf_op jit(solution)/shard_map/all_to_all | solution.py:85
  7.5 14.4 %copy-start.1 = (f32[2,16,256]{2,1,0:T(8,128)S(1)}, f32[2,16,256]{2,1,0:T(8,128)}, u32[]{:S(2)}) copy-start(f32[2,16,256]{2,1,0:T(8,128)} %param.6) | copy-start | bytes 98308
  17.8 6.5 %collective-permute-start = (bf16[4,4,7,2,256]{4,1,3,2,0:T(4,128)(2,1)S(1)}, bf16[4,4,7,2,256]{4,1,3,2,0:T(4,128)(2,1)S(1)}, u32[]{:S(2)}, u32[]{:S(2)}) collective-permute-start(bf16[4,4,7,2,256]{4,1,3,2,0:T(4,128)(2,1)S(1)} %get-tuple-element.8), channel_id=1, source_target_pairs={{0,1},{1,2},{2,3},{4,5},{5,6},{6,7},{8,9},{9,10},{10,11},{12,13},{... | collective-permute-start | bytes 344072 | tf_op jit(solution)/shard_map/ppermute | solution.py:89
  22.0 6.7 %collective-permute-start.1 = (bf16[4,4,7,2,256]{4,1,3,2,0:T(4,128)(2,1)S(1)}, bf16[4,4,7,2,256]{4,1,3,2,0:T(4,128)(2,1)S(1)}, u32[]{:S(2)}, u32[]{:S(2)}) collective-permute-start(bf16[4,4,7,2,256]{4,1,3,2,0:T(4,128)(2,1)S(1)} %get-tuple-element.7), channel_id=1, source_target_pairs={{1,0},{2,1},{3,2},{5,4},{6,5},{7,6},{9,8},{10,9},{11,10},{13,12},{... | collective-permute-start | bytes 344072 | tf_op jit(solution)/shard_map/ppermute | solution.py:90

commit v16 on v12

--- a/solution.py
+++ b/solution.py
@@ -18,9 +18,12 @@
     def window(dy):
         return x_ref[:, dy * pitch : dy * pitch + count, :].reshape(total, chans)
 
+    def operand(dy):
+        return window(dy).astype(jnp.bfloat16)
+
     taps = [None, None, None]
     for dy in range(3):
-        piece = window(dy)
+        piece = operand(dy)
         for dx in range(3):
             part = jnp.dot(piece, w_ref[dy, dx], preferred_element_type=jnp.float32)
             taps[dx] = part if taps[dx] is None else taps[dx] + part
@@ -34,12 +37,13 @@
         acc = values[t] * kernel[0:1]
         for lag in range(1, t + 1):
             acc = acc + values[t - lag] * kernel[lag : lag + 1]
-        depth.append(acc.astype(jnp.bfloat16))
-    depth = jnp.stack(depth).reshape(total, chans)
+        depth.append(acc.astype(jnp.bfloat16) if count % 16 == 0 else acc)
+    depth = jnp.stack(depth).reshape(total, chans).astype(jnp.bfloat16)
 
     mixed = jnp.dot(depth, p_ref[...], preferred_element_type=jnp.float32).astype(jnp.bfloat16)
     center = pltpu.roll(window(1).astype(jnp.float32), total - 1, 0)
-    state = (center + mixed.astype(jnp.float32)).astype(jnp.bfloat16).reshape(frames, count, chans)
+    state = (center + mixed.astype(jnp.float32)).astype(jnp.bfloat16).astype(o_ref.dtype)
+    state = state.reshape(frames, count, chans)
     state = jnp.where(m_ref[...][None] > 0, state, jnp.zeros((), state.dtype))
     if o_ref.shape[0] == frames:
         o_ref[...] = state
@@ -54,18 +58,19 @@
     frames, length, chans = x.shape
     count = length - 2 * pitch
     shape = (frames, count, chans) if cols is None else (count // pitch, cols, frames, chans)
+    dtype = x.dtype if cols is None else jnp.bfloat16
     flops = 2 * frames * count * chans * chans * 10
     vmem = pltpu.VMEM
     return pl.pallas_call(
         functools.partial(block_kernel, count=count, pitch=pitch),
-        out_shape=jax.ShapeDtypeStruct(shape, x.dtype),
+        out_shape=jax.ShapeDtypeStruct(shape, dtype),
         in_specs=[pl.BlockSpec(memory_space=vmem)] * 5,
         out_specs=pl.BlockSpec(memory_space=vmem),
         compiler_params=pltpu.CompilerParams(vmem_limit_bytes=48 * 1024 * 1024),
         cost_estimate=pl.CostEstimate(
             flops=flops,
             transcendentals=frames * count * chans,
-            bytes_accessed=2 * frames * (length + count) * chans + 2 * 10 * chans * chans,
+            bytes_accessed=x.dtype.itemsize * frames * (length + count) * chans + 2 * 10 * chans * chans,
         ),
     )(x, weight, kernel, proj, mask)
 
@@ -88,18 +93,39 @@
     down = [(i + 1, i) for i in range(sides - 1)]
     before = lax.ppermute(received[:, :, :, cols - halo :], "width", up)
     after = lax.ppermute(received[:, :, :, :halo], "width", down)
-    spare = jnp.zeros(received.shape[:3] + (pitch - cols - 2 * halo, chans), received.dtype)
-    state = jnp.concatenate([before, received, after, spare], axis=3)
+    def image_mask(left, width, first):
+        n_rows = rows + 2 * left
+        row = band * rows - left + lax.broadcasted_iota(jnp.int32, (n_rows, width), 0)
+        col = side * cols + first + lax.broadcasted_iota(jnp.int32, (n_rows, width), 1)
+        inside = (row >= 0) & (row < height) & (col >= 0) & (col < sides * cols)
+        return jnp.broadcast_to(inside.reshape(-1, 1), (n_rows * width, chans)).astype(jnp.float32)
+
+    band_in = jnp.pad(received, ((0, 0), (0, 0), (0, 0), (halo, pitch - cols - halo), (0, 0)))
+    band_in = band_in.reshape(bands * frames, -1, chans)
+    cut = (jnp.arange(pitch) < cols + 2 * (halo - 1)).astype(jnp.float32)
+    first_mask = image_mask(halo - 1, pitch, -(halo - 1)) * jnp.tile(cut, rows + 2 * (halo - 1))[:, None]
+    state = block(band_in, conv_w[0], depth_k[0], proj_w[0], first_mask, pitch)
+
+    reach = 2 * halo
+    rim = jnp.concatenate([before, received[:, :, :, :halo], received[:, :, :, cols - halo :], after], axis=3)
+    rim = rim.astype(jnp.float32).reshape(bands * frames, -1, chans)
+    rim_left = image_mask(halo - 1, halo, -(halo - 1))
+    rim_right = image_mask(halo - 1, halo, cols - 1)
+    n_rows = rows + 2 * (halo - 1)
+    rim_mask = jnp.concatenate(
+        [rim_left.reshape(n_rows, halo, chans), jnp.zeros((n_rows, halo, chans), jnp.float32),
+         rim_right.reshape(n_rows, halo, chans), jnp.zeros((n_rows, halo, chans), jnp.float32)], axis=1
+    ).reshape(-1, chans)
+    rims = block(rim, conv_w[0], depth_k[0], proj_w[0], rim_mask, 2 * reach)
+    rims = rims.astype(state.dtype).reshape(bands * frames, n_rows, 2 * reach, chans)
+    state = state.reshape(bands * frames, n_rows, pitch, chans)
+    state = lax.dynamic_update_slice(state, rims[:, :, :halo], (0, 0, 0, 0))
+    state = lax.dynamic_update_slice(state, rims[:, :, reach : reach + halo], (0, 0, cols + halo - 2 * (halo - 1), 0))
     state = state.reshape(bands * frames, -1, chans)
 
-    for b in range(BLOCKS):
+    for b in range(1, BLOCKS):
         left = halo - 1 - b
-        n_rows = rows + 2 * left
-        row = band * rows - left + lax.broadcasted_iota(jnp.int32, (n_rows, pitch), 0)
-        col = side * cols - left + lax.broadcasted_iota(jnp.int32, (n_rows, pitch), 1)
-        inside = (row >= 0) & (row < height) & (col >= 0) & (col < sides * cols)
-        inside = inside & (lax.broadcasted_iota(jnp.int32, (n_rows, pitch), 1) < cols + 2 * left)
-        mask = jnp.broadcast_to(inside.reshape(-1, 1), (n_rows * pitch, chans)).astype(jnp.float32)
+        mask = image_mask(left, pitch, -left)
         last = b == BLOCKS - 1
         state = block(state, conv_w[b], depth_k[b], proj_w[b], mask, pitch, cols if last else None)
 

time: 44.6 us -> 43.6 us (0.978)
  waiting for transfers between devices: 13.7 us -> 9.4 us
  Pallas kernels: 5.14 us -> 6.89 us
  local copies, waits for them, and re-layouts: 4.59 us -> 5.77 us
    ppermute x1, waiting for transfers between devices: 4.34 us -> 1.52 us  [shards(): after = lax.ppermute(received[:, :, :, :halo], 'width', down)]
    pallas_call x2 -> x3, Pallas kernels: 5.14 us -> 6.89 us  [block(): pl.pallas_call(functools.partial(block_kernel, count=count, pitch=pitch),...]
    ppermute x1, waiting for transfers between devices: 1.02 us -> 0.01 us  [shards(): before = lax.ppermute(received[:, :, :, cols - halo:], 'width', up)]
    all_to_all x1, waiting for transfers between devices: 8.35 us -> 7.88 us  [shards(): received = lax.all_to_all(pieces, 'tm', 0, 0, tiled=False)]
    unnamed x5 -> x8, local copies, waits for them, and re-layouts: 0.73 us -> 1.04 us
  transfers between devices with their start and end apart: 3 -> 3, of which waited for: 3 -> 2; matrix products, arithmetic and copies ran while one was open for 5% -> 8% of each run, Pallas kernels for 0% -> 7%
where the time goes in v16:
time: 43.6 us; the launch traced here: 43.3 us
  starting transfers between devices  9.84 us (23%)
  waiting for transfers between devices  9.4 us (22%)
  blocking collectives  8.72 us (20%)
  Pallas kernels  6.89 us (16%)
  local copies, waits for them, and re-layouts  5.77 us (13%)
  other arithmetic  2.4 us (6%)
    all_to_all x1, blocking collectives, shards(): state = lax.all_to_all(state, 'tm', 0, 1, tiled=True)  8.72 us
    all_to_all x1, waiting for transfers between devices, shards(): received = lax.all_to_all(pieces, 'tm', 0, 0, tiled=False)  7.88 us
    pallas_call x3, Pallas kernels, block(): pl.pallas_call(functools.partial(block_kernel, count=count, pitch=pitch),...  6.89 us
    all_to_all x1, starting transfers between devices, shards(): received = lax.all_to_all(pieces, 'tm', 0, 0, tiled=False)  4.37 us
    ppermute x1, starting transfers between devices, shards(): before = lax.ppermute(received[:, :, :, cols - halo:], 'width', up)  4.18 us
    squeeze x1, local copies, waits for them, and re-layouts, shards(): conv_w[b]  1.78 us
    ppermute x1, waiting for transfers between devices, shards(): after = lax.ppermute(received[:, :, :, :halo], 'width', down)  1.52 us
    another operation x1, other arithmetic, shards(): jnp.stack([padded[:, r * rows:r * rows + rows + 2 * halo] for r in range(...  1.48 us
  transfers between devices with their start and end apart: 3, of which 2 were waited for; matrix products, arithmetic and copies ran while one was open for 8% of the time, Pallas kernels for 7%

profile of v16, /device:TPU:0, one launch (start us, length us, event | category | flops | bytes accessed | tf_op | source)
XLA Modules:
  0.0 43.3 jit_solution(1140191525439981476)
XLA Ops:
  0.0 1.4 %fusion = (bf16[1,4,7,12,256]{4,1,3,2,0:T(4,128)(2,1)S(1)}, bf16[1,4,7,12,256]{4,1,3,2,0:T(4,128)(2,1)S(1)}, bf16[1,4,7,12,256]{4,1,3,2,0:T(4,128)(2,1)S(1)}, bf16[1,4,7,12,256]{4,1,3,2,0:T(4,128)(2,1)S(1)}) fusion(bf16[4,12,12,256]{3,0,2,1:T(4,128)(2,1)} %param.4), kind=kLoop, calls=%fused_computation.8 | loop fusion | bytes 1327104 | tf_op jit(solution)/shard_map/stack | solution.py:89
  1.4 1.5 %pad_maximum_fusion = bf16[4,4,7,12,256]{4,1,3,2,0:T(4,128)(2,1)} fusion(bf16[1,4,7,12,256]{4,1,3,2,0:T(4,128)(2,1)S(1)} %get-tuple-element.10, bf16[1,4,7,12,256]{4,1,3,2,0:T(4,128)(2,1)S(1)} %get-tuple-element.11, bf16[1,4,7,12,256]{4,1,3,2,0:T(4,128)(2,1)S(1)} %get-tuple-element.12, bf16[1,4,7,12,256]{4,1,3,2,0:T(4,128)(2,1)S(1)} %get-tuple-element.9), kind=kLoop, calls=%fused_computation.2 | loop fusion | flops 1032192 | bytes 1376256 | tf_op jit(solution)/shard_map/stack | solution.py:89
  2.9 4.4 %all-to-all-start = ((bf16[4,4,7,12,256]{4,1,3,2,0:T(4,128)(2,1)}), bf16[4,4,7,12,256]{4,1,3,2,0:T(4,128)(2,1)S(1)}, u32[]{:S(2)}, u32[]{:S(2)}) async-start(bf16[4,4,7,12,256]{4,1,3,2,0:T(4,128)(2,1)} %pad_maximum_fusion), calls=%async_computation | async-start | bytes 1376256 | tf_op jit(solution)/shard_map/all_to_all | solution.py:90
  7.3 0.1 and_convert_fusion.2
  7.4 0.1 copy.20
  7.5 0.1 copy.21
  7.6 0.1 and_select_fusion
  7.7 0.1 mul.25
  7.8 0.1 and_convert_fusion
  7.8 0.1 reshape.168
  8.1 1.8 %slice_bitcast_fusion = (bf16[3,3,256,256]{3,2,1,0:T(8,128)(2,1)S(1)}, bf16[3,3,256,256]{3,2,1,0:T(8,128)(2,1)S(1)}) fusion(bf16[2,3,3,256,256]{4,3,2,1,0:T(8,128)(2,1)} %param.5), kind=kLoop, calls=%fused_computation | loop fusion | bytes 4718592 | tf_op jit(solution)/shard_map/squeeze | solution.py:130
  9.9 7.9 %all-to-all-done = bf16[4,4,7,12,256]{4,1,3,2,0:T(4,128)(2,1)S(1)} async-done(((bf16[4,4,7,12,256]{4,1,3,2,0:T(4,128)(2,1)}), bf16[4,4,7,12,256]{4,1,3,2,0:T(4,128)(2,1)S(1)}, u32[]{:S(2)}, u32[]{:S(2)}) %all-to-all-start) | async-done | bytes 688160 | tf_op jit(solution)/shard_map/all_to_all | solution.py:90
  17.8 0.1 fusion.10
  17.9 0.1 copy.23
  18.0 4.2 %collective-permute-start = (bf16[4,4,7,2,256]{4,3,2,1,0:T(2,128)(2,1)S(1)}, bf16[4,4,7,2,256]{4,3,2,1,0:T(2,128)(2,1)S(1)}, u32[]{:S(2)}, u32[]{:S(2)}) collective-permute-start(bf16[4,4,7,2,256]{4,3,2,1,0:T(2,128)(2,1)S(1)} %copy.23), channel_id=1, source_target_pairs={{0,1},{1,2},{2,3},{4,5},{5,6},{6,7},{8,9},{9,10},{10,11},{12,13},{... | collective-permute-start | bytes 344072 | tf_op jit(solution)/shard_map/ppermute | solution.py:94
  22.2 0.1 copy.24
  22.3 1.3 %collective-permute-start.1 = (bf16[4,4,7,2,256]{4,3,2,1,0:T(2,128)(2,1)S(1)}, bf16[4,4,7,2,256]{4,3,2,1,0:T(2,128)(2,1)S(1)}, u32[]{:S(2)}, u32[]{:S(2)}) collective-permute-start(bf16[4,4,7,2,256]{4,3,2,1,0:T(2,128)(2,1)S(1)} %copy.24), channel_id=1, source_target_pairs={{1,0},{2,1},{3,2},{5,4},{6,5},{7,6},{9,8},{10,9},{11,10},{13,12},{... | collective-permute-start | bytes 344072 | tf_op jit(solution)/shard_map/ppermute | solution.py:95
  23.6 0.1 copy.25
  23.7 0.4 pad.9.clone
  24.1 0.1 mul.26.m_ref
  24.2 3.2 %shard_map.46 = bf16[16,80,256]{2,1,0:T(8,128)(2,1)S(1)} custom-call(bf16[16,112,256]{2,1,0:T(8,128)(2,1)S(1)} %bitcast.37, bf16[3,3,256,256]{3,2,1,0:T(8,128)(2,1)S(1)} %get-tuple-element.6.w_ref, f32[16,256]{1,0:T(8,128)S(1)} %get-tuple-element.16.k_ref, bf16[256,256]{1,0:T(8,128)(2,1)S(1)} %get-tuple-element.14.p_ref, f32[80,256]{1,0:T(8,128)S(1)} %mul.26.m_ref), custom_call_target="tpu_custom_call" | custom-call | flops 1677721600 | bytes 2883584 | tf_op jit(solution)/shard_map/pallas_call | solution.py:64
  27.4 1.5 %collective-permute-done.1 = bf16[4,4,7,2,256]{4,3,2,1,0:T(2,128)(2,1)S(1)} collective-permute-done((bf16[4,4,7,2,256]{4,3,2,1,0:T(2,128)(2,1)S(1)}, bf16[4,4,7,2,256]{4,3,2,1,0:T(2,128)(2,1)S(1)}, u32[]{:S(2)}, u32[]{:S(2)}) %collective-permute-start.1) | collective-permute-done | bytes 114720 | tf_op jit(solution)/shard_map/ppermute | solution.py:95
  29.0 0.5 %pad_maximum_fusion.1 = bf16[4,4,7,8,256]{4,3,2,1,0:T(8,128)(2,1)S(1)} fusion(bf16[4,4,7,2,256]{4,3,2,1,0:T(2,128)(2,1)S(1)} %collective-permute-done.1, bf16[4,4,7,2,256]{4,3,2,1,0:T(2,128)(2,1)S(1)} %copy.23, bf16[4,4,7,2,256]{4,3,2,1,0:T(2,128)(2,1)S(1)} %copy.24, bf16[4,4,7,2,256]{4,3,2,1,0:T(2,128)(2,1)S(1)} %collective-permute-done), kind=kLoop, calls=%fused_computation.3 | loop fusion | flops 1835008 | bytes 917504 | tf_op jit(solution)/shard_map/concatenate | solution.py:110
  29.6 1.7 %shard_map.47 = f32[16,40,256]{2,1,0:T(8,128)S(1)} custom-call(f32[16,56,256]{2,1,0:T(8,128)S(1)} %convert.2.x_ref, bf16[3,3,256,256]{3,2,1,0:T(8,128)(2,1)S(1)} %get-tuple-element.6.w_ref, f32[16,256]{1,0:T(8,128)S(1)} %get-tuple-element.16.k_ref, bf16[256,256]{1,0:T(8,128)(2,1)S(1)} %get-tuple-element.14.p_ref, f32[40,256]{1,0:T(8,128)S(1)} %maximum_bitcast_fusion.m_ref), custom_call_target="tpu_custom_call" | custom-call | flops 838860800 | bytes 2883584 | tf_op jit(solution)/shard_map/pallas_call | solution.py:64
  31.3 0.1 slice_dynamic-update-slice_fusion.1
  31.4 0.1 slice_dynamic-update-slice_fusion
  31.5 0.1 broadcast_in_dim.8.m_ref
  31.6 2.0 %shard_map.48 = bf16[3,12,16,256]{3,2,1,0:T(8,128)(2,1)S(1)} custom-call(bf16[16,80,256]{2,1,0:T(8,128)(2,1)S(1)} %bitcast.39, bf16[3,3,256,256]{3,2,1,0:T(8,128)(2,1)S(1)} %get-tuple-element.5.w_ref, f32[16,256]{1,0:T(8,128)S(1)} %get-tuple-element.15.k_ref, bf16[256,256]{1,0:T(8,128)(2,1)S(1)} %get-tuple-element.13.p_ref, f32[48,256]{1,0:T(8,128)S(1)} %broadcast_in_dim.8.m_ref), custom_call_target="tpu_custom_call" | custom-call | flops 1006632960 | bytes 2359296 | tf_op jit(solution)/shard_map/pallas_call | solution.py:64
  33.6 0.1 reshape.166
  33.7 0.1 copy.27
  33.8 8.7 %all_to_all.14 = bf16[4,3,12,4,256]{4,3,2,1,0:T(4,128)(2,1)S(1)} all-to-all(bf16[4,3,12,4,256]{4,3,2,1,0:T(4,128)(2,1)S(1)} %bitcast.41), channel_id=1, replica_groups=mesh['groups'=2,'tm'=4,'width'=4] {'tm'}, dimensions={0} | all-to-all | bytes 589824 | tf_op jit(solution)/shard_map/all_to_all | solution.py:134
  42.5 0.7 %copy.31 = bf16[4,12,12,256]{3,0,2,1:T(4,128)(2,1)} copy(bf16[4,12,12,256]{3,0,2,1:T(4,128)(2,1)S(1)} %bitcast.42) | data formatting | bytes 589824
  (20 shorter events, 0.4 us)
Async XLA Ops:
  1.4 6.2 %copy-start = (bf16[2,256,256]{2,1,0:T(8,128)(2,1)S(1)}, bf16[2,256,256]{2,1,0:T(8,128)(2,1)}, u32[]{:S(2)}) copy-start(bf16[2,256,256]{2,1,0:T(8,128)(2,1)} %param.7) | copy-start | bytes 786436
  2.9 5.3 %copy-start.1 = (f32[2,16,256]{2,1,0:T(8,128)S(1)}, f32[2,16,256]{2,1,0:T(8,128)}, u32[]{:S(2)}) copy-start(f32[2,16,256]{2,1,0:T(8,128)} %param.6) | copy-start | bytes 98308
  2.9 14.9 %all-to-all-start = ((bf16[4,4,7,12,256]{4,1,3,2,0:T(4,128)(2,1)}), bf16[4,4,7,12,256]{4,1,3,2,0:T(4,128)(2,1)S(1)}, u32[]{:S(2)}, u32[]{:S(2)}) async-start(bf16[4,4,7,12,256]{4,1,3,2,0:T(4,128)(2,1)} %pad_maximum_fusion), calls=%async_computation | async-start | bytes 1376256 | tf_op jit(solution)/shard_map/all_to_all | solution.py:90
  18.0 9.4 %collective-permute-start = (bf16[4,4,7,2,256]{4,3,2,1,0:T(2,128)(2,1)S(1)}, bf16[4,4,7,2,256]{4,3,2,1,0:T(2,128)(2,1)S(1)}, u32[]{:S(2)}, u32[]{:S(2)}) collective-permute-start(bf16[4,4,7,2,256]{4,3,2,1,0:T(2,128)(2,1)S(1)} %copy.23), channel_id=1, source_target_pairs={{0,1},{1,2},{2,3},{4,5},{5,6},{6,7},{8,9},{9,10},{10,11},{12,13},{... | collective-permute-start | bytes 344072 | tf_op jit(solution)/shard_map/ppermute | solution.py:94
  22.3 6.7 %collective-permute-start.1 = (bf16[4,4,7,2,256]{4,3,2,1,0:T(2,128)(2,1)S(1)}, bf16[4,4,7,2,256]{4,3,2,1,0:T(2,128)(2,1)S(1)}, u32[]{:S(2)}, u32[]{:S(2)}) collective-permute-start(bf16[4,4,7,2,256]{4,3,2,1,0:T(2,128)(2,1)S(1)} %copy.24), channel_id=1, source_target_pairs={{1,0},{2,1},{3,2},{5,4},{6,5},{7,6},{9,8},{10,9},{11,10},{13,12},{... | collective-permute-start | bytes 344072 | tf_op jit(solution)/shard_map/ppermute | solution.py:95

commit v17 on v16

--- a/solution.py
+++ b/solution.py
@@ -28,7 +28,7 @@
             part = jnp.dot(piece, w_ref[dy, dx], preferred_element_type=jnp.float32)
             taps[dx] = part if taps[dx] is None else taps[dx] + part
     conv = taps[0] + pltpu.roll(taps[1], total - 1, 0) + pltpu.roll(taps[2], total - 2, 0)
-    hidden = (conv / (1.0 + jnp.exp(-conv))).astype(jnp.bfloat16)
+    hidden = (conv * (0.5 + 0.5 * jnp.tanh(0.5 * conv))).astype(jnp.bfloat16)
 
     values = hidden.astype(jnp.float32).reshape(frames, count, chans)
     kernel = k_ref[...]
@@ -107,8 +107,13 @@
     state = block(band_in, conv_w[0], depth_k[0], proj_w[0], first_mask, pitch)
 
     reach = 2 * halo
-    rim = jnp.concatenate([before, received[:, :, :, :halo], received[:, :, :, cols - halo :], after], axis=3)
-    rim = rim.astype(jnp.float32).reshape(bands * frames, -1, chans)
+    rim = jnp.concatenate([received[:, :, :, :halo], received[:, :, :, cols - halo :]], axis=3).astype(jnp.float32)
+    rim = jnp.pad(rim, ((0, 0), (0, 0), (0, 0), (halo, halo), (0, 0)))
+    rim = rim.reshape((bands * frames,) + rim.shape[2:])
+    edge = (bands * frames, rows + 2 * halo, halo, chans)
+    rim = lax.dynamic_update_slice(rim, before.astype(jnp.float32).reshape(edge), (0, 0, 0, 0))
+    rim = lax.dynamic_update_slice(rim, after.astype(jnp.float32).reshape(edge), (0, 0, 3 * halo, 0))
+    rim = rim.reshape(bands * frames, -1, chans)
     rim_left = image_mask(halo - 1, halo, -(halo - 1))
     rim_right = image_mask(halo - 1, halo, cols - 1)
     n_rows = rows + 2 * (halo - 1)

time: 43.6 us -> 43.5 us (level)
  transfers between devices with their start and end apart: 3 -> 3, of which waited for: 2 -> 2; matrix products, arithmetic and copies ran while one was open for 8% -> 9% of each run, Pallas kernels for 7% -> 7%
where the time goes in v17:
time: 43.5 us; the launch traced here: 43.1 us
  starting transfers between devices  9.84 us (23%)
  waiting for transfers between devices  9.18 us (21%)
  blocking collectives  8.72 us (20%)
  Pallas kernels  6.8 us (16%)
  local copies, waits for them, and re-layouts  5.77 us (13%)
  other arithmetic  2.57 us (6%)
    all_to_all x1, blocking collectives, shards(): state = lax.all_to_all(state, 'tm', 0, 1, tiled=True)  8.72 us
    all_to_all x1, waiting for transfers between devices, shards(): received = lax.all_to_all(pieces, 'tm', 0, 0, tiled=False)  7.88 us
    pallas_call x3, Pallas kernels, block(): pl.pallas_call(functools.partial(block_kernel, count=count, pitch=pitch),...  6.8 us
    all_to_all x1, starting transfers between devices, shards(): received = lax.all_to_all(pieces, 'tm', 0, 0, tiled=False)  4.37 us
    ppermute x1, starting transfers between devices, shards(): before = lax.ppermute(received[:, :, :, cols - halo:], 'width', up)  4.18 us
    squeeze x1, local copies, waits for them, and re-layouts, shards(): conv_w[b]  1.78 us
    another operation x1, other arithmetic, shards(): jnp.stack([padded[:, r * rows:r * rows + rows + 2 * halo] for r in range(...  1.48 us
    another operation x1, local copies, waits for them, and re-layouts, shards(): jnp.stack([padded[:, r * rows:r * rows + rows + 2 * halo] for r in range(...  1.36 us
  transfers between devices with their start and end apart: 3, of which 2 were waited for; matrix products, arithmetic and copies ran while one was open for 9% of the time, Pallas kernels for 7%

profile of v17, /device:TPU:0, one launch (start us, length us, event | category | flops | bytes accessed | tf_op | source)
XLA Modules:
  0.0 43.1 jit_solution(4543533287196520963)
XLA Ops:
  0.0 1.4 %fusion.4 = (bf16[1,4,7,12,256]{4,1,3,2,0:T(4,128)(2,1)S(1)}, bf16[1,4,7,12,256]{4,1,3,2,0:T(4,128)(2,1)S(1)}, bf16[1,4,7,12,256]{4,1,3,2,0:T(4,128)(2,1)S(1)}, bf16[1,4,7,12,256]{4,1,3,2,0:T(4,128)(2,1)S(1)}) fusion(bf16[4,12,12,256]{3,0,2,1:T(4,128)(2,1)} %param.4), kind=kLoop, calls=%fused_computation.16 | loop fusion | bytes 1327104 | tf_op jit(solution)/shard_map/stack | solution.py:89
  1.4 1.5 %pad_maximum_fusion = bf16[4,4,7,12,256]{4,1,3,2,0:T(4,128)(2,1)} fusion(bf16[1,4,7,12,256]{4,1,3,2,0:T(4,128)(2,1)S(1)} %get-tuple-element.10, bf16[1,4,7,12,256]{4,1,3,2,0:T(4,128)(2,1)S(1)} %get-tuple-element.11, bf16[1,4,7,12,256]{4,1,3,2,0:T(4,128)(2,1)S(1)} %get-tuple-element.12, bf16[1,4,7,12,256]{4,1,3,2,0:T(4,128)(2,1)S(1)} %get-tuple-element.9), kind=kLoop, calls=%fused_computation.7 | loop fusion | flops 1032192 | bytes 1376256 | tf_op jit(solution)/shard_map/stack | solution.py:89
  2.9 4.4 %all-to-all-start = ((bf16[4,4,7,12,256]{4,1,3,2,0:T(4,128)(2,1)}), bf16[4,4,7,12,256]{4,1,3,2,0:T(4,128)(2,1)S(1)}, u32[]{:S(2)}, u32[]{:S(2)}) async-start(bf16[4,4,7,12,256]{4,1,3,2,0:T(4,128)(2,1)} %pad_maximum_fusion), calls=%async_computation | async-start | bytes 1376256 | tf_op jit(solution)/shard_map/all_to_all | solution.py:90
  7.3 0.1 and_convert_fusion.2
  7.4 0.1 copy.18
  7.5 0.1 copy.19
  7.6 0.1 and_select_fusion
  7.7 0.1 mul.25
  7.8 0.1 reshape.197
  8.1 1.8 %slice_bitcast_fusion = (bf16[3,3,256,256]{3,2,1,0:T(8,128)(2,1)S(1)}, bf16[3,3,256,256]{3,2,1,0:T(8,128)(2,1)S(1)}) fusion(bf16[2,3,3,256,256]{4,3,2,1,0:T(8,128)(2,1)} %param.5), kind=kLoop, calls=%fused_computation.2 | loop fusion | bytes 4718592 | tf_op jit(solution)/shard_map/squeeze | solution.py:135
  9.9 7.9 %all-to-all-done = bf16[4,4,7,12,256]{4,1,3,2,0:T(4,128)(2,1)S(1)} async-done(((bf16[4,4,7,12,256]{4,1,3,2,0:T(4,128)(2,1)}), bf16[4,4,7,12,256]{4,1,3,2,0:T(4,128)(2,1)S(1)}, u32[]{:S(2)}, u32[]{:S(2)}) %all-to-all-start) | async-done | bytes 688160 | tf_op jit(solution)/shard_map/all_to_all | solution.py:90
  17.8 0.1 fusion.14
  17.9 0.1 copy.21
  18.0 0.1 copy.22
  18.1 4.2 %collective-permute-start = (bf16[4,4,7,2,256]{4,3,2,1,0:T(2,128)(2,1)S(1)}, bf16[4,4,7,2,256]{4,3,2,1,0:T(2,128)(2,1)S(1)}, u32[]{:S(2)}, u32[]{:S(2)}) collective-permute-start(bf16[4,4,7,2,256]{4,3,2,1,0:T(2,128)(2,1)S(1)} %copy.22), channel_id=1, source_target_pairs={{0,1},{1,2},{2,3},{4,5},{5,6},{6,7},{8,9},{9,10},{10,11},{12,13},{... | collective-permute-start | bytes 344072 | tf_op jit(solution)/shard_map/ppermute | solution.py:94
  22.3 0.3 fusion.3
  22.6 1.3 %collective-permute-start.1 = (bf16[4,4,7,2,256]{4,3,2,1,0:T(2,128)(2,1)S(1)}, bf16[4,4,7,2,256]{4,3,2,1,0:T(2,128)(2,1)S(1)}, u32[]{:S(2)}, u32[]{:S(2)}) collective-permute-start(bf16[4,4,7,2,256]{4,3,2,1,0:T(2,128)(2,1)S(1)} %copy.21), channel_id=1, source_target_pairs={{1,0},{2,1},{3,2},{5,4},{6,5},{7,6},{9,8},{10,9},{11,10},{13,12},{... | collective-permute-start | bytes 344072 | tf_op jit(solution)/shard_map/ppermute | solution.py:95
  23.9 0.1 bitcast_convert_fusion
  24.0 0.1 copy.23
  24.2 0.4 pad.14.clone
  24.7 3.1 %shard_map.46 = bf16[16,80,256]{2,1,0:T(8,128)(2,1)S(1)} custom-call(bf16[16,112,256]{2,1,0:T(8,128)(2,1)S(1)} %bitcast.44, bf16[3,3,256,256]{3,2,1,0:T(8,128)(2,1)S(1)} %get-tuple-element.6.w_ref, f32[16,256]{1,0:T(8,128)S(1)} %get-tuple-element.16.k_ref, bf16[256,256]{1,0:T(8,128)(2,1)S(1)} %get-tuple-element.14.p_ref, f32[80,256]{1,0:T(8,128)S(1)} %mul.26.m_ref), custom_call_target="tpu_custom_call" | custom-call | flops 1677721600 | bytes 2883584 | tf_op jit(solution)/shard_map/pallas_call | solution.py:64
  27.8 0.2 convert_dynamic-update-slice_fusion.1
  28.0 1.3 %collective-permute-done.1 = bf16[4,4,7,2,256]{4,3,2,1,0:T(2,128)(2,1)S(1)} collective-permute-done((bf16[4,4,7,2,256]{4,3,2,1,0:T(2,128)(2,1)S(1)}, bf16[4,4,7,2,256]{4,3,2,1,0:T(2,128)(2,1)S(1)}, u32[]{:S(2)}, u32[]{:S(2)}) %collective-permute-start.1) | collective-permute-done | bytes 114720 | tf_op jit(solution)/shard_map/ppermute | solution.py:95
  29.3 0.2 convert_dynamic-update-slice_fusion
  29.5 1.7 %shard_map.47 = f32[16,40,256]{2,1,0:T(8,128)S(1)} custom-call(f32[16,56,256]{2,1,0:T(8,128)S(1)} %bitcast.43, bf16[3,3,256,256]{3,2,1,0:T(8,128)(2,1)S(1)} %get-tuple-element.6.w_ref, f32[16,256]{1,0:T(8,128)S(1)} %get-tuple-element.16.k_ref, bf16[256,256]{1,0:T(8,128)(2,1)S(1)} %get-tuple-element.14.p_ref, f32[40,256]{1,0:T(8,128)S(1)} %maximum_bitcast_fusion.m_ref), custom_call_target="tpu_custom_call" | custom-call | flops 838860800 | bytes 2883584 | tf_op jit(solution)/shard_map/pallas_call | solution.py:64
  31.2 0.1 slice_dynamic-update-slice_fusion.1
  31.3 0.1 slice_dynamic-update-slice_fusion
  31.5 2.0 %shard_map.48 = bf16[3,12,16,256]{3,2,1,0:T(8,128)(2,1)S(1)} custom-call(bf16[16,80,256]{2,1,0:T(8,128)(2,1)S(1)} %bitcast.46, bf16[3,3,256,256]{3,2,1,0:T(8,128)(2,1)S(1)} %get-tuple-element.5.w_ref, f32[16,256]{1,0:T(8,128)S(1)} %get-tuple-element.15.k_ref, bf16[256,256]{1,0:T(8,128)(2,1)S(1)} %get-tuple-element.13.p_ref, f32[48,256]{1,0:T(8,128)S(1)} %broadcast_in_dim.8.m_ref), custom_call_target="tpu_custom_call" | custom-call | flops 1006632960 | bytes 2359296 | tf_op jit(solution)/shard_map/pallas_call | solution.py:64
  33.5 0.1 reshape.190
  33.6 0.1 copy.25
  33.7 8.7 %all_to_all.14 = bf16[4,3,12,4,256]{4,3,2,1,0:T(4,128)(2,1)S(1)} all-to-all(bf16[4,3,12,4,256]{4,3,2,1,0:T(4,128)(2,1)S(1)} %bitcast.47), channel_id=1, replica_groups=mesh['groups'=2,'tm'=4,'width'=4] {'tm'}, dimensions={0} | all-to-all | bytes 589824 | tf_op jit(solution)/shard_map/all_to_all | solution.py:139
  42.4 0.7 %copy.31 = bf16[4,12,12,256]{3,0,2,1:T(4,128)(2,1)} copy(bf16[4,12,12,256]{3,0,2,1:T(4,128)(2,1)S(1)} %bitcast.48) | data formatting | bytes 589824
  (22 shorter events, 0.5 us)
Async XLA Ops:
  1.4 6.2 %copy-start = (bf16[2,256,256]{2,1,0:T(8,128)(2,1)S(1)}, bf16[2,256,256]{2,1,0:T(8,128)(2,1)}, u32[]{:S(2)}) copy-start(bf16[2,256,256]{2,1,0:T(8,128)(2,1)} %param.7) | copy-start | bytes 786436
  2.9 5.3 %copy-start.1 = (f32[2,16,256]{2,1,0:T(8,128)S(1)}, f32[2,16,256]{2,1,0:T(8,128)}, u32[]{:S(2)}) copy-start(f32[2,16,256]{2,1,0:T(8,128)} %param.6) | copy-start | bytes 98308
  2.9 14.9 %all-to-all-start = ((bf16[4,4,7,12,256]{4,1,3,2,0:T(4,128)(2,1)}), bf16[4,4,7,12,256]{4,1,3,2,0:T(4,128)(2,1)S(1)}, u32[]{:S(2)}, u32[]{:S(2)}) async-start(bf16[4,4,7,12,256]{4,1,3,2,0:T(4,128)(2,1)} %pad_maximum_fusion), calls=%async_computation | async-start | bytes 1376256 | tf_op jit(solution)/shard_map/all_to_all | solution.py:90
  18.1 9.8 %collective-permute-start = (bf16[4,4,7,2,256]{4,3,2,1,0:T(2,128)(2,1)S(1)}, bf16[4,4,7,2,256]{4,3,2,1,0:T(2,128)(2,1)S(1)}, u32[]{:S(2)}, u32[]{:S(2)}) collective-permute-start(bf16[4,4,7,2,256]{4,3,2,1,0:T(2,128)(2,1)S(1)} %copy.22), channel_id=1, source_target_pairs={{0,1},{1,2},{2,3},{4,5},{5,6},{6,7},{8,9},{9,10},{10,11},{12,13},{... | collective-permute-start | bytes 344072 | tf_op jit(solution)/shard_map/ppermute | solution.py:94
  22.6 6.7 %collective-permute-start.1 = (bf16[4,4,7,2,256]{4,3,2,1,0:T(2,128)(2,1)S(1)}, bf16[4,4,7,2,256]{4,3,2,1,0:T(2,128)(2,1)S(1)}, u32[]{:S(2)}, u32[]{:S(2)}) collective-permute-start(bf16[4,4,7,2,256]{4,3,2,1,0:T(2,128)(2,1)S(1)} %copy.21), channel_id=1, source_target_pairs={{1,0},{2,1},{3,2},{5,4},{6,5},{7,6},{9,8},{10,9},{11,10},{13,12},{... | collective-permute-start | bytes 344072 | tf_op jit(solution)/shard_map/ppermute | solution.py:95

commit v18 on v17

--- a/solution.py
+++ b/solution.py
@@ -107,7 +107,8 @@
     state = block(band_in, conv_w[0], depth_k[0], proj_w[0], first_mask, pitch)
 
     reach = 2 * halo
-    rim = jnp.concatenate([received[:, :, :, :halo], received[:, :, :, cols - halo :]], axis=3).astype(jnp.float32)
+    late, before = lax.optimization_barrier((received, before))
+    rim = jnp.concatenate([late[:, :, :, :halo], late[:, :, :, cols - halo :]], axis=3).astype(jnp.float32)
     rim = jnp.pad(rim, ((0, 0), (0, 0), (0, 0), (halo, halo), (0, 0)))
     rim = rim.reshape((bands * frames,) + rim.shape[2:])
     edge = (bands * frames, rows + 2 * halo, halo, chans)

time: 43.5 us -> 43 us (0.989)
  waiting for transfers between devices: 9.18 us -> 8.46 us
  local copies, waits for them, and re-layouts: 5.77 us -> 6.29 us
    ppermute x1, waiting for transfers between devices: 1.3 us -> 0.57 us  [shards(): after = lax.ppermute(received[:, :, :, :halo], 'width', down)]
    unnamed x8 -> x6, local copies, waits for them, and re-layouts: 1.04 us -> 0.86 us
  transfers between devices with their start and end apart: 3 -> 3, of which waited for: 2 -> 2; matrix products, arithmetic and copies ran while one was open for 9% -> 10% of each run, Pallas kernels for 7% -> 7%
where the time goes in v18:
time: 43 us; the launch traced here: 42.6 us
  starting transfers between devices  9.84 us (23%)
  blocking collectives  8.72 us (20%)
  waiting for transfers between devices  8.46 us (20%)
  Pallas kernels  6.8 us (16%)
  local copies, waits for them, and re-layouts  6.29 us (15%)
  other arithmetic  2.25 us (5%)
    all_to_all x1, blocking collectives, shards(): state = lax.all_to_all(state, 'tm', 0, 1, tiled=True)  8.72 us
    all_to_all x1, waiting for transfers between devices, shards(): received = lax.all_to_all(pieces, 'tm', 0, 0, tiled=False)  7.88 us
    pallas_call x3, Pallas kernels, block(): pl.pallas_call(functools.partial(block_kernel, count=count, pitch=pitch),...  6.8 us
    all_to_all x1, starting transfers between devices, shards(): received = lax.all_to_all(pieces, 'tm', 0, 0, tiled=False)  4.37 us
    ppermute x1, starting transfers between devices, shards(): before = lax.ppermute(received[:, :, :, cols - halo:], 'width', up)  4.18 us
    squeeze x1, local copies, waits for them, and re-layouts, shards(): conv_w[b]  1.78 us
    another operation x1, other arithmetic, shards(): jnp.stack([padded[:, r * rows:r * rows + rows + 2 * halo] for r in range(...  1.47 us
    another operation x1, local copies, waits for them, and re-layouts, shards(): jnp.stack([padded[:, r * rows:r * rows + rows + 2 * halo] for r in range(...  1.36 us
  transfers between devices with their start and end apart: 3, of which 2 were waited for; matrix products, arithmetic and copies ran while one was open for 10% of the time, Pallas kernels for 7%

profile of v18, /device:TPU:0, one launch (start us, length us, event | category | flops | bytes accessed | tf_op | source)
XLA Modules:
  0.0 42.6 jit_solution(1718263790347492074)
XLA Ops:
  0.0 1.4 %fusion.4 = (bf16[1,4,7,12,256]{4,1,3,2,0:T(4,128)(2,1)S(1)}, bf16[1,4,7,12,256]{4,1,3,2,0:T(4,128)(2,1)S(1)}, bf16[1,4,7,12,256]{4,1,3,2,0:T(4,128)(2,1)S(1)}, bf16[1,4,7,12,256]{4,1,3,2,0:T(4,128)(2,1)S(1)}) fusion(bf16[4,12,12,256]{3,0,2,1:T(4,128)(2,1)} %param.4), kind=kLoop, calls=%fused_computation.14 | loop fusion | bytes 1327104 | tf_op jit(solution)/shard_map/stack | solution.py:89
  1.4 1.5 %pad_maximum_fusion = bf16[4,4,7,12,256]{4,1,3,2,0:T(4,128)(2,1)} fusion(bf16[1,4,7,12,256]{4,1,3,2,0:T(4,128)(2,1)S(1)} %get-tuple-element.16, bf16[1,4,7,12,256]{4,1,3,2,0:T(4,128)(2,1)S(1)} %get-tuple-element.17, bf16[1,4,7,12,256]{4,1,3,2,0:T(4,128)(2,1)S(1)} %get-tuple-element.18, bf16[1,4,7,12,256]{4,1,3,2,0:T(4,128)(2,1)S(1)} %get-tuple-element.15), kind=kLoop, calls=%fused_computation.7 | loop fusion | flops 1032192 | bytes 1376256 | tf_op jit(solution)/shard_map/stack | solution.py:89
  2.9 4.4 %all-to-all-start = ((bf16[4,4,7,12,256]{4,1,3,2,0:T(4,128)(2,1)}), bf16[4,4,7,12,256]{4,1,3,2,0:T(4,128)(2,1)S(1)}, u32[]{:S(2)}, u32[]{:S(2)}) async-start(bf16[4,4,7,12,256]{4,1,3,2,0:T(4,128)(2,1)} %pad_maximum_fusion), calls=%async_computation | async-start | bytes 1376256 | tf_op jit(solution)/shard_map/all_to_all | solution.py:90
  7.3 0.1 and_convert_fusion.2
  7.4 0.1 copy.22
  7.5 0.1 copy.23
  7.7 0.1 mul.25
  7.8 0.1 reshape.197
  8.1 1.8 %slice_bitcast_fusion = (bf16[3,3,256,256]{3,2,1,0:T(8,128)(2,1)S(1)}, bf16[3,3,256,256]{3,2,1,0:T(8,128)(2,1)S(1)}) fusion(bf16[2,3,3,256,256]{4,3,2,1,0:T(8,128)(2,1)} %param.5), kind=kLoop, calls=%fused_computation.2 | loop fusion | bytes 4718592 | tf_op jit(solution)/shard_map/squeeze | solution.py:136
  9.9 7.9 %all-to-all-done = bf16[4,4,7,12,256]{4,1,3,2,0:T(4,128)(2,1)S(1)} async-done(((bf16[4,4,7,12,256]{4,1,3,2,0:T(4,128)(2,1)}), bf16[4,4,7,12,256]{4,1,3,2,0:T(4,128)(2,1)S(1)}, u32[]{:S(2)}, u32[]{:S(2)}) %all-to-all-start) | async-done | bytes 688160 | tf_op jit(solution)/shard_map/all_to_all | solution.py:90
  17.8 0.1 fusion.15
  17.9 4.2 %collective-permute-start = (bf16[4,4,7,2,256]{4,1,3,2,0:T(4,128)(2,1)S(1)}, bf16[4,4,7,2,256]{4,1,3,2,0:T(4,128)(2,1)S(1)}, u32[]{:S(2)}, u32[]{:S(2)}) collective-permute-start(bf16[4,4,7,2,256]{4,1,3,2,0:T(4,128)(2,1)S(1)} %get-tuple-element.14), channel_id=1, source_target_pairs={{0,1},{1,2},{2,3},{4,5},{5,6},{6,7},{8,9},{9,10},{10,11},{12,13},{... | collective-permute-start | bytes 344072 | tf_op jit(solution)/shard_map/ppermute | solution.py:94
  22.1 1.3 %collective-permute-start.1 = (bf16[4,4,7,2,256]{4,1,3,2,0:T(4,128)(2,1)S(1)}, bf16[4,4,7,2,256]{4,1,3,2,0:T(4,128)(2,1)S(1)}, u32[]{:S(2)}, u32[]{:S(2)}) collective-permute-start(bf16[4,4,7,2,256]{4,1,3,2,0:T(4,128)(2,1)S(1)} %get-tuple-element.13), channel_id=1, source_target_pairs={{1,0},{2,1},{3,2},{5,4},{6,5},{7,6},{9,8},{10,9},{11,10},{13,12},{... | collective-permute-start | bytes 344072 | tf_op jit(solution)/shard_map/ppermute | solution.py:95
  23.4 0.1 copy.25
  23.5 0.4 %pad.14.clone = bf16[4,4,7,16,256]{4,3,2,1,0:T(8,128)(2,1)S(1)} pad(bf16[4,4,7,12,256]{4,3,2,1,0:T(8,128)(2,1)S(1)} %copy.25, bf16[]{:T(256)} %constant.12.clone.1), padding=0_0x0_0x0_0x2_2x0_0 | pad | bytes 1605634 | tf_op jit(solution)/shard_map/jit(_pad)/pad | solution.py:103
  24.0 3.1 %shard_map.46 = bf16[16,80,256]{2,1,0:T(8,128)(2,1)S(1)} custom-call(bf16[16,112,256]{2,1,0:T(8,128)(2,1)S(1)} %bitcast.41, bf16[3,3,256,256]{3,2,1,0:T(8,128)(2,1)S(1)} %get-tuple-element.10.w_ref, f32[16,256]{1,0:T(8,128)S(1)} %get-tuple-element.22.k_ref, bf16[256,256]{1,0:T(8,128)(2,1)S(1)} %get-tuple-element.20.p_ref, f32[80,256]{1,0:T(8,128)S(1)} %mul.26.m_ref), custom_call_target="tpu_custom_call" | custom-call | flops 1677721600 | bytes 2883584 | tf_op jit(solution)/shard_map/pallas_call | solution.py:64
  27.2 0.1 copy.18
  27.3 0.2 fusion.14
  27.5 0.3 fusion.3
  27.9 0.1 bitcast_convert_fusion
  28.0 0.1 copy.20
  28.1 0.1 constant_dynamic-update-slice_fusion.1
  28.2 0.6 %collective-permute-done.1 = bf16[4,4,7,2,256]{4,1,3,2,0:T(4,128)(2,1)S(1)} collective-permute-done((bf16[4,4,7,2,256]{4,1,3,2,0:T(4,128)(2,1)S(1)}, bf16[4,4,7,2,256]{4,1,3,2,0:T(4,128)(2,1)S(1)}, u32[]{:S(2)}, u32[]{:S(2)}) %collective-permute-start.1) | collective-permute-done | bytes 114720 | tf_op jit(solution)/shard_map/ppermute | solution.py:95
  28.8 0.1 copy.21
  28.8 0.1 constant_dynamic-update-slice_fusion
  29.0 1.7 %shard_map.47 = f32[16,40,256]{2,1,0:T(8,128)S(1)} custom-call(f32[16,56,256]{2,1,0:T(8,128)S(1)} %bitcast.42, bf16[3,3,256,256]{3,2,1,0:T(8,128)(2,1)S(1)} %get-tuple-element.10.w_ref, f32[16,256]{1,0:T(8,128)S(1)} %get-tuple-element.22.k_ref, bf16[256,256]{1,0:T(8,128)(2,1)S(1)} %get-tuple-element.20.p_ref, f32[40,256]{1,0:T(8,128)S(1)} %maximum_bitcast_fusion.m_ref), custom_call_target="tpu_custom_call" | custom-call | flops 838860800 | bytes 2883584 | tf_op jit(solution)/shard_map/pallas_call | solution.py:64
  30.7 0.1 slice_dynamic-update-slice_fusion.1
  30.8 0.1 slice_dynamic-update-slice_fusion
  31.0 2.0 %shard_map.48 = bf16[3,12,16,256]{3,2,1,0:T(8,128)(2,1)S(1)} custom-call(bf16[16,80,256]{2,1,0:T(8,128)(2,1)S(1)} %bitcast.44, bf16[3,3,256,256]{3,2,1,0:T(8,128)(2,1)S(1)} %get-tuple-element.9.w_ref, f32[16,256]{1,0:T(8,128)S(1)} %get-tuple-element.21.k_ref, bf16[256,256]{1,0:T(8,128)(2,1)S(1)} %get-tuple-element.19.p_ref, f32[48,256]{1,0:T(8,128)S(1)} %broadcast_in_dim.8.m_ref), custom_call_target="tpu_custom_call" | custom-call | flops 1006632960 | bytes 2359296 | tf_op jit(solution)/shard_map/pallas_call | solution.py:64
  33.1 0.1 copy.27
  33.2 8.7 %all_to_all.14 = bf16[4,3,12,4,256]{4,3,2,1,0:T(4,128)(2,1)S(1)} all-to-all(bf16[4,3,12,4,256]{4,3,2,1,0:T(4,128)(2,1)S(1)} %bitcast.45), channel_id=1, replica_groups=mesh['groups'=2,'tm'=4,'width'=4] {'tm'}, dimensions={0} | all-to-all | bytes 589824 | tf_op jit(solution)/shard_map/all_to_all | solution.py:140
  41.9 0.7 %copy.33 = bf16[4,12,12,256]{3,0,2,1:T(4,128)(2,1)} copy(bf16[4,12,12,256]{3,0,2,1:T(4,128)(2,1)S(1)} %bitcast.46) | data formatting | bytes 589824
  (24 shorter events, 0.7 us)
Async XLA Ops:
  1.4 6.2 %copy-start = (bf16[2,256,256]{2,1,0:T(8,128)(2,1)S(1)}, bf16[2,256,256]{2,1,0:T(8,128)(2,1)}, u32[]{:S(2)}) copy-start(bf16[2,256,256]{2,1,0:T(8,128)(2,1)} %param.7) | copy-start | bytes 786436
  2.8 5.3 %copy-start.1 = (f32[2,16,256]{2,1,0:T(8,128)S(1)}, f32[2,16,256]{2,1,0:T(8,128)}, u32[]{:S(2)}) copy-start(f32[2,16,256]{2,1,0:T(8,128)} %param.6) | copy-start | bytes 98308
  2.9 14.9 %all-to-all-start = ((bf16[4,4,7,12,256]{4,1,3,2,0:T(4,128)(2,1)}), bf16[4,4,7,12,256]{4,1,3,2,0:T(4,128)(2,1)S(1)}, u32[]{:S(2)}, u32[]{:S(2)}) async-start(bf16[4,4,7,12,256]{4,1,3,2,0:T(4,128)(2,1)} %pad_maximum_fusion), calls=%async_computation | async-start | bytes 1376256 | tf_op jit(solution)/shard_map/all_to_all | solution.py:90
  17.9 9.3 %collective-permute-start = (bf16[4,4,7,2,256]{4,1,3,2,0:T(4,128)(2,1)S(1)}, bf16[4,4,7,2,256]{4,1,3,2,0:T(4,128)(2,1)S(1)}, u32[]{:S(2)}, u32[]{:S(2)}) collective-permute-start(bf16[4,4,7,2,256]{4,1,3,2,0:T(4,128)(2,1)S(1)} %get-tuple-element.14), channel_id=1, source_target_pairs={{0,1},{1,2},{2,3},{4,5},{5,6},{6,7},{8,9},{9,10},{10,11},{12,13},{... | collective-permute-start | bytes 344072 | tf_op jit(solution)/shard_map/ppermute | solution.py:94
  22.1 6.7 %collective-permute-start.1 = (bf16[4,4,7,2,256]{4,1,3,2,0:T(4,128)(2,1)S(1)}, bf16[4,4,7,2,256]{4,1,3,2,0:T(4,128)(2,1)S(1)}, u32[]{:S(2)}, u32[]{:S(2)}) collective-permute-start(bf16[4,4,7,2,256]{4,1,3,2,0:T(4,128)(2,1)S(1)} %get-tuple-element.13), channel_id=1, source_target_pairs={{1,0},{2,1},{3,2},{5,4},{6,5},{7,6},{9,8},{10,9},{11,10},{13,12},{... | collective-permute-start | bytes 344072 | tf_op jit(solution)/shard_map/ppermute | solution.py:95

commit v19 on v18

--- a/solution.py
+++ b/solution.py
@@ -91,8 +91,8 @@
 
     up = [(i, i + 1) for i in range(sides - 1)]
     down = [(i + 1, i) for i in range(sides - 1)]
+    after = lax.ppermute(received[:, :, :, :halo], "width", down)
     before = lax.ppermute(received[:, :, :, cols - halo :], "width", up)
-    after = lax.ppermute(received[:, :, :, :halo], "width", down)
     def image_mask(left, width, first):
         n_rows = rows + 2 * left
         row = band * rows - left + lax.broadcasted_iota(jnp.int32, (n_rows, width), 0)
@@ -107,7 +107,7 @@
     state = block(band_in, conv_w[0], depth_k[0], proj_w[0], first_mask, pitch)
 
     reach = 2 * halo
-    late, before = lax.optimization_barrier((received, before))
+    late, after = lax.optimization_barrier((received, after))
     rim = jnp.concatenate([late[:, :, :, :halo], late[:, :, :, cols - halo :]], axis=3).astype(jnp.float32)
     rim = jnp.pad(rim, ((0, 0), (0, 0), (0, 0), (halo, halo), (0, 0)))
     rim = rim.reshape((bands * frames,) + rim.shape[2:])

time: 43 us -> 43 us (level)
  starting transfers between devices: 9.84 us -> 10.5 us
  waiting for transfers between devices: 8.46 us -> 7.89 us
    ppermute x1, starting transfers between devices: 4.18 us -> 4.81 us  [shards(): before = lax.ppermute(received[:, :, :, cols - halo:], 'width', up)]
    ppermute x1, waiting for transfers between devices: 0.57 us -> 0.01 us  [shards(): after = lax.ppermute(received[:, :, :, :halo], 'width', down)]
  transfers between devices with their start and end apart: 3 -> 3, of which waited for: 2 -> 1; matrix products, arithmetic and copies ran while one was open for 10% -> 10% of each run, Pallas kernels for 7% -> 7%
where the time goes in v19:
time: 43 us; the launch traced here: 42.7 us
  starting transfers between devices  10.5 us (24%)
  blocking collectives  8.72 us (20%)
  waiting for transfers between devices  7.89 us (18%)
  Pallas kernels  6.8 us (16%)
  local copies, waits for them, and re-layouts  6.29 us (15%)
  other arithmetic  2.25 us (5%)
    all_to_all x1, blocking collectives, shards(): state = lax.all_to_all(state, 'tm', 0, 1, tiled=True)  8.72 us
    all_to_all x1, waiting for transfers between devices, shards(): received = lax.all_to_all(pieces, 'tm', 0, 0, tiled=False)  7.88 us
    pallas_call x3, Pallas kernels, block(): pl.pallas_call(functools.partial(block_kernel, count=count, pitch=pitch),...  6.8 us
    ppermute x1, starting transfers between devices, shards(): before = lax.ppermute(received[:, :, :, cols - halo:], 'width', up)  4.81 us
    all_to_all x1, starting transfers between devices, shards(): received = lax.all_to_all(pieces, 'tm', 0, 0, tiled=False)  4.37 us
    squeeze x1, local copies, waits for them, and re-layouts, shards(): conv_w[b]  1.78 us
    another operation x1, other arithmetic, shards(): jnp.stack([padded[:, r * rows:r * rows + rows + 2 * halo] for r in range(...  1.47 us
    another operation x1, local copies, waits for them, and re-layouts, shards(): jnp.stack([padded[:, r * rows:r * rows + rows + 2 * halo] for r in range(...  1.36 us
  transfers between devices with their start and end apart: 3, of which 1 were waited for; matrix products, arithmetic and copies ran while one was open for 10% of the time, Pallas kernels for 7%

profile of v19, /device:TPU:0, one launch (start us, length us, event | category | flops | bytes accessed | tf_op | source)
XLA Modules:
  0.0 42.7 jit_solution(7655577411933136326)
XLA Ops:
  0.0 1.4 %fusion.4 = (bf16[1,4,7,12,256]{4,1,3,2,0:T(4,128)(2,1)S(1)}, bf16[1,4,7,12,256]{4,1,3,2,0:T(4,128)(2,1)S(1)}, bf16[1,4,7,12,256]{4,1,3,2,0:T(4,128)(2,1)S(1)}, bf16[1,4,7,12,256]{4,1,3,2,0:T(4,128)(2,1)S(1)}) fusion(bf16[4,12,12,256]{3,0,2,1:T(4,128)(2,1)} %param.4), kind=kLoop, calls=%fused_computation.14 | loop fusion | bytes 1327104 | tf_op jit(solution)/shard_map/stack | solution.py:89
  1.4 1.5 %pad_maximum_fusion = bf16[4,4,7,12,256]{4,1,3,2,0:T(4,128)(2,1)} fusion(bf16[1,4,7,12,256]{4,1,3,2,0:T(4,128)(2,1)S(1)} %get-tuple-element.16, bf16[1,4,7,12,256]{4,1,3,2,0:T(4,128)(2,1)S(1)} %get-tuple-element.17, bf16[1,4,7,12,256]{4,1,3,2,0:T(4,128)(2,1)S(1)} %get-tuple-element.18, bf16[1,4,7,12,256]{4,1,3,2,0:T(4,128)(2,1)S(1)} %get-tuple-element.15), kind=kLoop, calls=%fused_computation.7 | loop fusion | flops 1032192 | bytes 1376256 | tf_op jit(solution)/shard_map/stack | solution.py:89
  2.9 4.4 %all-to-all-start = ((bf16[4,4,7,12,256]{4,1,3,2,0:T(4,128)(2,1)}), bf16[4,4,7,12,256]{4,1,3,2,0:T(4,128)(2,1)S(1)}, u32[]{:S(2)}, u32[]{:S(2)}) async-start(bf16[4,4,7,12,256]{4,1,3,2,0:T(4,128)(2,1)} %pad_maximum_fusion), calls=%async_computation | async-start | bytes 1376256 | tf_op jit(solution)/shard_map/all_to_all | solution.py:90
  7.3 0.1 and_convert_fusion.2
  7.4 0.1 copy.22
  7.5 0.1 copy.23
  7.6 0.1 and_select_fusion
  7.7 0.1 mul.25
  7.8 0.1 reshape.197
  8.1 1.8 %slice_bitcast_fusion = (bf16[3,3,256,256]{3,2,1,0:T(8,128)(2,1)S(1)}, bf16[3,3,256,256]{3,2,1,0:T(8,128)(2,1)S(1)}) fusion(bf16[2,3,3,256,256]{4,3,2,1,0:T(8,128)(2,1)} %param.5), kind=kLoop, calls=%fused_computation.2 | loop fusion | bytes 4718592 | tf_op jit(solution)/shard_map/squeeze | solution.py:136
  9.9 7.9 %all-to-all-done = bf16[4,4,7,12,256]{4,1,3,2,0:T(4,128)(2,1)S(1)} async-done(((bf16[4,4,7,12,256]{4,1,3,2,0:T(4,128)(2,1)}), bf16[4,4,7,12,256]{4,1,3,2,0:T(4,128)(2,1)S(1)}, u32[]{:S(2)}, u32[]{:S(2)}) %all-to-all-start) | async-done | bytes 688160 | tf_op jit(solution)/shard_map/all_to_all | solution.py:90
  17.8 0.1 fusion.15
  17.9 1.3 %collective-permute-start = (bf16[4,4,7,2,256]{4,1,3,2,0:T(4,128)(2,1)S(1)}, bf16[4,4,7,2,256]{4,1,3,2,0:T(4,128)(2,1)S(1)}, u32[]{:S(2)}, u32[]{:S(2)}) collective-permute-start(bf16[4,4,7,2,256]{4,1,3,2,0:T(4,128)(2,1)S(1)} %get-tuple-element.14), channel_id=1, source_target_pairs={{1,0},{2,1},{3,2},{5,4},{6,5},{7,6},{9,8},{10,9},{11,10},{13,12},{... | collective-permute-start | bytes 344072 | tf_op jit(solution)/shard_map/ppermute | solution.py:94
  19.2 4.8 %collective-permute-start.1 = (bf16[4,4,7,2,256]{4,1,3,2,0:T(4,128)(2,1)S(1)}, bf16[4,4,7,2,256]{4,1,3,2,0:T(4,128)(2,1)S(1)}, u32[]{:S(2)}, u32[]{:S(2)}) collective-permute-start(bf16[4,4,7,2,256]{4,1,3,2,0:T(4,128)(2,1)S(1)} %get-tuple-element.13), channel_id=1, source_target_pairs={{0,1},{1,2},{2,3},{4,5},{5,6},{6,7},{8,9},{9,10},{10,11},{12,13},{... | collective-permute-start | bytes 344072 | tf_op jit(solution)/shard_map/ppermute | solution.py:95
  24.0 0.1 copy.25
  24.1 0.4 %pad.14.clone = bf16[4,4,7,16,256]{4,3,2,1,0:T(8,128)(2,1)S(1)} pad(bf16[4,4,7,12,256]{4,3,2,1,0:T(8,128)(2,1)S(1)} %copy.25, bf16[]{:T(256)} %constant.12.clone.1), padding=0_0x0_0x0_0x2_2x0_0 | pad | bytes 1605634 | tf_op jit(solution)/shard_map/jit(_pad)/pad | solution.py:103
  24.6 3.1 %shard_map.46 = bf16[16,80,256]{2,1,0:T(8,128)(2,1)S(1)} custom-call(bf16[16,112,256]{2,1,0:T(8,128)(2,1)S(1)} %bitcast.42, bf16[3,3,256,256]{3,2,1,0:T(8,128)(2,1)S(1)} %get-tuple-element.10.w_ref, f32[16,256]{1,0:T(8,128)S(1)} %get-tuple-element.22.k_ref, bf16[256,256]{1,0:T(8,128)(2,1)S(1)} %get-tuple-element.20.p_ref, f32[80,256]{1,0:T(8,128)S(1)} %mul.26.m_ref), custom_call_target="tpu_custom_call" | custom-call | flops 1677721600 | bytes 2883584 | tf_op jit(solution)/shard_map/pallas_call | solution.py:64
  27.8 0.1 copy.18
  28.0 0.2 fusion.14
  28.1 0.3 fusion.3
  28.5 0.1 bitcast_convert_fusion
  28.6 0.1 copy.21
  28.7 0.1 copy.20
  28.8 0.1 constant_dynamic-update-slice_fusion.1
  28.9 0.1 constant_dynamic-update-slice_fusion
  29.0 1.7 %shard_map.47 = f32[16,40,256]{2,1,0:T(8,128)S(1)} custom-call(f32[16,56,256]{2,1,0:T(8,128)S(1)} %bitcast.41, bf16[3,3,256,256]{3,2,1,0:T(8,128)(2,1)S(1)} %get-tuple-element.10.w_ref, f32[16,256]{1,0:T(8,128)S(1)} %get-tuple-element.22.k_ref, bf16[256,256]{1,0:T(8,128)(2,1)S(1)} %get-tuple-element.20.p_ref, f32[40,256]{1,0:T(8,128)S(1)} %maximum_bitcast_fusion.m_ref), custom_call_target="tpu_custom_call" | custom-call | flops 838860800 | bytes 2883584 | tf_op jit(solution)/shard_map/pallas_call | solution.py:64
  30.7 0.1 slice_dynamic-update-slice_fusion.1
  30.8 0.1 slice_dynamic-update-slice_fusion
  31.0 2.0 %shard_map.48 = bf16[3,12,16,256]{3,2,1,0:T(8,128)(2,1)S(1)} custom-call(bf16[16,80,256]{2,1,0:T(8,128)(2,1)S(1)} %bitcast.44, bf16[3,3,256,256]{3,2,1,0:T(8,128)(2,1)S(1)} %get-tuple-element.9.w_ref, f32[16,256]{1,0:T(8,128)S(1)} %get-tuple-element.21.k_ref, bf16[256,256]{1,0:T(8,128)(2,1)S(1)} %get-tuple-element.19.p_ref, f32[48,256]{1,0:T(8,128)S(1)} %broadcast_in_dim.8.m_ref), custom_call_target="tpu_custom_call" | custom-call | flops 1006632960 | bytes 2359296 | tf_op jit(solution)/shard_map/pallas_call | solution.py:64
  33.1 0.1 copy.27
  33.2 8.7 %all_to_all.14 = bf16[4,3,12,4,256]{4,3,2,1,0:T(4,128)(2,1)S(1)} all-to-all(bf16[4,3,12,4,256]{4,3,2,1,0:T(4,128)(2,1)S(1)} %bitcast.45), channel_id=1, replica_groups=mesh['groups'=2,'tm'=4,'width'=4] {'tm'}, dimensions={0} | all-to-all | bytes 589824 | tf_op jit(solution)/shard_map/all_to_all | solution.py:140
  42.0 0.7 %copy.33 = bf16[4,12,12,256]{3,0,2,1:T(4,128)(2,1)} copy(bf16[4,12,12,256]{3,0,2,1:T(4,128)(2,1)S(1)} %bitcast.46) | data formatting | bytes 589824
  (24 shorter events, 0.6 us)
Async XLA Ops:
  1.4 6.2 %copy-start = (bf16[2,256,256]{2,1,0:T(8,128)(2,1)S(1)}, bf16[2,256,256]{2,1,0:T(8,128)(2,1)}, u32[]{:S(2)}) copy-start(bf16[2,256,256]{2,1,0:T(8,128)(2,1)} %param.7) | copy-start | bytes 786436
  2.8 5.3 %copy-start.1 = (f32[2,16,256]{2,1,0:T(8,128)S(1)}, f32[2,16,256]{2,1,0:T(8,128)}, u32[]{:S(2)}) copy-start(f32[2,16,256]{2,1,0:T(8,128)} %param.6) | copy-start | bytes 98308
  2.9 14.9 %all-to-all-start = ((bf16[4,4,7,12,256]{4,1,3,2,0:T(4,128)(2,1)}), bf16[4,4,7,12,256]{4,1,3,2,0:T(4,128)(2,1)S(1)}, u32[]{:S(2)}, u32[]{:S(2)}) async-start(bf16[4,4,7,12,256]{4,1,3,2,0:T(4,128)(2,1)} %pad_maximum_fusion), calls=%async_computation | async-start | bytes 1376256 | tf_op jit(solution)/shard_map/all_to_all | solution.py:90
  17.9 9.9 %collective-permute-start = (bf16[4,4,7,2,256]{4,1,3,2,0:T(4,128)(2,1)S(1)}, bf16[4,4,7,2,256]{4,1,3,2,0:T(4,128)(2,1)S(1)}, u32[]{:S(2)}, u32[]{:S(2)}) collective-permute-start(bf16[4,4,7,2,256]{4,1,3,2,0:T(4,128)(2,1)S(1)} %get-tuple-element.14), channel_id=1, source_target_pairs={{1,0},{2,1},{3,2},{5,4},{6,5},{7,6},{9,8},{10,9},{11,10},{13,12},{... | collective-permute-start | bytes 344072 | tf_op jit(solution)/shard_map/ppermute | solution.py:94
  19.2 9.5 %collective-permute-start.1 = (bf16[4,4,7,2,256]{4,1,3,2,0:T(4,128)(2,1)S(1)}, bf16[4,4,7,2,256]{4,1,3,2,0:T(4,128)(2,1)S(1)}, u32[]{:S(2)}, u32[]{:S(2)}) collective-permute-start(bf16[4,4,7,2,256]{4,1,3,2,0:T(4,128)(2,1)S(1)} %get-tuple-element.13), channel_id=1, source_target_pairs={{0,1},{1,2},{2,3},{4,5},{5,6},{6,7},{8,9},{9,10},{10,11},{12,13},{... | collective-permute-start | bytes 344072 | tf_op jit(solution)/shard_map/ppermute | solution.py:95

commit v20 on v18

--- a/solution.py
+++ b/solution.py
@@ -85,8 +85,11 @@
     halo = BLOCKS
     pitch = -(-(cols + 2 * halo) // LANES) * LANES
 
-    padded = jnp.pad(video, ((0, 0), (halo, halo), (0, 0), (0, 0)))
-    pieces = jnp.stack([padded[:, r * rows : r * rows + rows + 2 * halo] for r in range(bands)])
+    pieces = jnp.zeros((bands, frames, rows + 2 * halo, cols, chans), video.dtype)
+    for r in range(bands):
+        first, last = max(r * rows - halo, 0), min(r * rows + rows + halo, height)
+        start = first - (r * rows - halo)
+        pieces = lax.dynamic_update_slice(pieces, video[None, :, first:last], (r, 0, start, 0, 0))
     received = lax.all_to_all(pieces, "tm", 0, 0, tiled=False)
 
     up = [(i, i + 1) for i in range(sides - 1)]

time: 43 us -> 45.1 us (1.049)
  local copies, waits for them, and re-layouts: 6.29 us -> 10.1 us
  other arithmetic: 2.25 us -> 0.77 us
    dynamic_update_slice x0 -> x4, local copies, waits for them, and re-layouts: none -> 4.15 us  [shards(): lax.dynamic_update_slice(pieces, video[None, :, first:last], (r, 0, start...]
    another operation x1 -> x0, other arithmetic: 1.47 us -> none  [shards(): jnp.stack([padded[:, r * rows:r * rows + rows + 2 * halo] for r in range(...]
    another operation x2 -> x1, local copies, waits for them, and re-layouts: 1.36 us -> 0.01 us  [the longest x1 1.36 us: shards(): jnp.stack([padded[:, r * rows:r * rows + rows + 2 * halo] for r in range(...]
    broadcast_in_dim x0 -> x1, local copies, waits for them, and re-layouts: none -> 1.02 us  [shards(): video[None, :, first:last]]
  transfers between devices with their start and end apart: 3 -> 3, of which waited for: 2 -> 2; matrix products, arithmetic and copies ran while one was open for 10% -> 9% of each run, Pallas kernels for 7% -> 7%
where the time goes in v20:
time: 45.1 us; the launch traced here: 44.8 us
  local copies, waits for them, and re-layouts  10.1 us (22%)
  starting transfers between devices  9.71 us (22%)
  blocking collectives  8.72 us (19%)
  waiting for transfers between devices  8.46 us (19%)
  Pallas kernels  6.8 us (15%)
  other arithmetic  0.77 us (2%)
    all_to_all x1, blocking collectives, shards(): state = lax.all_to_all(state, 'tm', 0, 1, tiled=True)  8.72 us
    all_to_all x1, waiting for transfers between devices, shards(): received = lax.all_to_all(pieces, 'tm', 0, 0, tiled=False)  7.88 us
    pallas_call x3, Pallas kernels, block(): pl.pallas_call(functools.partial(block_kernel, count=count, pitch=pitch),...  6.8 us
    all_to_all x1, starting transfers between devices, shards(): received = lax.all_to_all(pieces, 'tm', 0, 0, tiled=False)  4.24 us
    ppermute x1, starting transfers between devices, shards(): before = lax.ppermute(received[:, :, :, cols - halo:], 'width', up)  4.18 us
    dynamic_update_slice x4, local copies, waits for them, and re-layouts, shards(): lax.dynamic_update_slice(pieces, video[None, :, first:last], (r, 0, start...  4.15 us
    squeeze x1, local copies, waits for them, and re-layouts, shards(): conv_w[b]  1.78 us
    ppermute x1, starting transfers between devices, shards(): after = lax.ppermute(received[:, :, :, :halo], 'width', down)  1.29 us
  transfers between devices with their start and end apart: 3, of which 2 were waited for; matrix products, arithmetic and copies ran while one was open for 9% of the time, Pallas kernels for 7%

profile of v20, /device:TPU:0, one launch (start us, length us, event | category | flops | bytes accessed | tf_op | source)
XLA Modules:
  0.0 44.8 jit_solution(3272926014691948038)
XLA Ops:
  0.0 1.0 %slice_bitcast_fusion.4 = bf16[1,4,5,12,256]{4,1,3,2,0:T(4,128)(2,1)S(1)} fusion(bf16[4,12,12,256]{3,0,2,1:T(4,128)(2,1)} %param.4), kind=kLoop, calls=%fused_computation.16 | loop fusion | bytes 245760 | tf_op jit(solution)/shard_map/broadcast_in_dim | solution.py:92
  1.0 1.0 %dynamic_update_slice.24 = bf16[4,4,7,12,256]{4,1,3,2,0:T(4,128)(2,1)} pad(bf16[1,4,5,12,256]{4,1,3,2,0:T(4,128)(2,1)S(1)} %slice_bitcast_fusion.4, bf16[]{:T(256)} %constant.14.clone.1), padding=0_3x0_0x2_0x0_0x0_0 | pad | bytes 811010 | tf_op jit(solution)/shard_map/dynamic_update_slice | solution.py:92
  2.1 1.7 %bitcast_dynamic-update-slice_fusion.1 = bf16[4,4,7,12,256]{4,1,3,2,0:T(4,128)(2,1)} fusion(bf16[4,4,7,12,256]{4,1,3,2,0:T(4,128)(2,1)} %dynamic_update_slice.24, bf16[4,12,12,256]{3,0,2,1:T(4,128)(2,1)} %param.4), kind=kLoop, calls=%fused_computation.12 | loop fusion | bytes 344064 | tf_op jit(solution)/shard_map/dynamic_update_slice | solution.py:92
  3.8 0.7 %bitcast_dynamic-update-slice_fusion = bf16[4,4,7,12,256]{4,1,3,2,0:T(4,128)(2,1)} fusion(bf16[4,4,7,12,256]{4,1,3,2,0:T(4,128)(2,1)} %bitcast_dynamic-update-slice_fusion.1, bf16[4,12,12,256]{3,0,2,1:T(4,128)(2,1)S(1)} %copy-done), kind=kLoop, calls=%fused_computation.11 | loop fusion | bytes 344064 | tf_op jit(solution)/shard_map/dynamic_update_slice | solution.py:92
  4.5 0.7 %bitcast_dynamic-update-slice_fusion.2 = bf16[4,4,7,12,256]{4,1,3,2,0:T(4,128)(2,1)} fusion(bf16[4,4,7,12,256]{4,1,3,2,0:T(4,128)(2,1)} %bitcast_dynamic-update-slice_fusion, bf16[4,12,12,256]{3,0,2,1:T(4,128)(2,1)S(1)} %copy-done), kind=kLoop, calls=%fused_computation.15 | loop fusion | bytes 245760 | tf_op jit(solution)/shard_map/dynamic_update_slice | solution.py:92
  5.2 4.2 %all-to-all-start = ((bf16[4,4,7,12,256]{4,1,3,2,0:T(4,128)(2,1)}), bf16[4,4,7,12,256]{4,1,3,2,0:T(4,128)(2,1)S(1)}, u32[]{:S(2)}, u32[]{:S(2)}) async-start(bf16[4,4,7,12,256]{4,1,3,2,0:T(4,128)(2,1)} %bitcast_dynamic-update-slice_fusion.2), calls=%async_computation | async-start | bytes 1376256 | tf_op jit(solution)/shard_map/all_to_all | solution.py:93
  9.6 0.1 copy.23
  9.7 0.1 copy.24
  10.0 0.1 reshape.197
  10.3 1.8 %slice_bitcast_fusion = (bf16[3,3,256,256]{3,2,1,0:T(8,128)(2,1)S(1)}, bf16[3,3,256,256]{3,2,1,0:T(8,128)(2,1)S(1)}) fusion(bf16[2,3,3,256,256]{4,3,2,1,0:T(8,128)(2,1)} %param.5), kind=kLoop, calls=%fused_computation.2 | loop fusion | bytes 4718592 | tf_op jit(solution)/shard_map/squeeze | solution.py:139
  12.1 7.9 %all-to-all-done = bf16[4,4,7,12,256]{4,1,3,2,0:T(4,128)(2,1)S(1)} async-done(((bf16[4,4,7,12,256]{4,1,3,2,0:T(4,128)(2,1)}), bf16[4,4,7,12,256]{4,1,3,2,0:T(4,128)(2,1)S(1)}, u32[]{:S(2)}, u32[]{:S(2)}) %all-to-all-start) | async-done | bytes 688160 | tf_op jit(solution)/shard_map/all_to_all | solution.py:93
  20.1 4.2 %collective-permute-start = (bf16[4,4,7,2,256]{4,1,3,2,0:T(4,128)(2,1)S(1)}, bf16[4,4,7,2,256]{4,1,3,2,0:T(4,128)(2,1)S(1)}, u32[]{:S(2)}, u32[]{:S(2)}) collective-permute-start(bf16[4,4,7,2,256]{4,1,3,2,0:T(4,128)(2,1)S(1)} %get-tuple-element.14), channel_id=1, source_target_pairs={{0,1},{1,2},{2,3},{4,5},{5,6},{6,7},{8,9},{9,10},{10,11},{12,13},{... | collective-permute-start | bytes 344072 | tf_op jit(solution)/shard_map/ppermute | solution.py:97
  24.3 1.3 %collective-permute-start.1 = (bf16[4,4,7,2,256]{4,1,3,2,0:T(4,128)(2,1)S(1)}, bf16[4,4,7,2,256]{4,1,3,2,0:T(4,128)(2,1)S(1)}, u32[]{:S(2)}, u32[]{:S(2)}) collective-permute-start(bf16[4,4,7,2,256]{4,1,3,2,0:T(4,128)(2,1)S(1)} %get-tuple-element.13), channel_id=1, source_target_pairs={{1,0},{2,1},{3,2},{5,4},{6,5},{7,6},{9,8},{10,9},{11,10},{13,12},{... | collective-permute-start | bytes 344072 | tf_op jit(solution)/shard_map/ppermute | solution.py:98
  25.6 0.1 copy.26
  25.7 0.4 pad.10.clone
  26.2 3.1 %shard_map.46 = bf16[16,80,256]{2,1,0:T(8,128)(2,1)S(1)} custom-call(bf16[16,112,256]{2,1,0:T(8,128)(2,1)S(1)} %bitcast.41, bf16[3,3,256,256]{3,2,1,0:T(8,128)(2,1)S(1)} %get-tuple-element.10.w_ref, f32[16,256]{1,0:T(8,128)S(1)} %get-tuple-element.18.k_ref, bf16[256,256]{1,0:T(8,128)(2,1)S(1)} %get-tuple-element.16.p_ref, f32[80,256]{1,0:T(8,128)S(1)} %mul.26.m_ref), custom_call_target="tpu_custom_call" | custom-call | flops 1677721600 | bytes 2883584 | tf_op jit(solution)/shard_map/pallas_call | solution.py:64
  29.4 0.1 copy.19
  29.5 0.2 fusion.12
  29.7 0.3 fusion.3
  30.1 0.1 bitcast_convert_fusion
  30.2 0.1 copy.21
  30.3 0.1 constant_dynamic-update-slice_fusion.1
  30.4 0.6 %collective-permute-done.1 = bf16[4,4,7,2,256]{4,1,3,2,0:T(4,128)(2,1)S(1)} collective-permute-done((bf16[4,4,7,2,256]{4,1,3,2,0:T(4,128)(2,1)S(1)}, bf16[4,4,7,2,256]{4,1,3,2,0:T(4,128)(2,1)S(1)}, u32[]{:S(2)}, u32[]{:S(2)}) %collective-permute-start.1) | collective-permute-done | bytes 114720 | tf_op jit(solution)/shard_map/ppermute | solution.py:98
  30.9 0.1 copy.22
  31.0 0.1 constant_dynamic-update-slice_fusion
  31.1 1.7 %shard_map.47 = f32[16,40,256]{2,1,0:T(8,128)S(1)} custom-call(f32[16,56,256]{2,1,0:T(8,128)S(1)} %bitcast.42, bf16[3,3,256,256]{3,2,1,0:T(8,128)(2,1)S(1)} %get-tuple-element.10.w_ref, f32[16,256]{1,0:T(8,128)S(1)} %get-tuple-element.18.k_ref, bf16[256,256]{1,0:T(8,128)(2,1)S(1)} %get-tuple-element.16.p_ref, f32[40,256]{1,0:T(8,128)S(1)} %maximum_bitcast_fusion.m_ref), custom_call_target="tpu_custom_call" | custom-call | flops 838860800 | bytes 2883584 | tf_op jit(solution)/shard_map/pallas_call | solution.py:64
  32.9 0.1 slice_dynamic-update-slice_fusion.1
  33.0 0.1 slice_dynamic-update-slice_fusion
  33.2 2.0 %shard_map.48 = bf16[3,12,16,256]{3,2,1,0:T(8,128)(2,1)S(1)} custom-call(bf16[16,80,256]{2,1,0:T(8,128)(2,1)S(1)} %bitcast.44, bf16[3,3,256,256]{3,2,1,0:T(8,128)(2,1)S(1)} %get-tuple-element.9.w_ref, f32[16,256]{1,0:T(8,128)S(1)} %get-tuple-element.17.k_ref, bf16[256,256]{1,0:T(8,128)(2,1)S(1)} %get-tuple-element.15.p_ref, f32[48,256]{1,0:T(8,128)S(1)} %broadcast_in_dim.37.m_ref), custom_call_target="tpu_custom_call" | custom-call | flops 1006632960 | bytes 2359296 | tf_op jit(solution)/shard_map/pallas_call | solution.py:64
  35.3 0.1 copy.28
  35.4 8.7 %all_to_all.14 = bf16[4,3,12,4,256]{4,3,2,1,0:T(4,128)(2,1)S(1)} all-to-all(bf16[4,3,12,4,256]{4,3,2,1,0:T(4,128)(2,1)S(1)} %bitcast.45), channel_id=1, replica_groups=mesh['groups'=2,'tm'=4,'width'=4] {'tm'}, dimensions={0} | all-to-all | bytes 589824 | tf_op jit(solution)/shard_map/all_to_all | solution.py:143
  44.1 0.7 %copy.37 = bf16[4,12,12,256]{3,0,2,1:T(4,128)(2,1)} copy(bf16[4,12,12,256]{3,0,2,1:T(4,128)(2,1)S(1)} %bitcast.46) | data formatting | bytes 589824
  (29 shorter events, 0.9 us)
Async XLA Ops:
  0.0 3.8 %copy-start = (bf16[4,12,12,256]{3,0,2,1:T(4,128)(2,1)S(1)}, bf16[4,12,12,256]{3,0,2,1:T(4,128)(2,1)}, u32[]{:S(2)}) copy-start(bf16[4,12,12,256]{3,0,2,1:T(4,128)(2,1)} %param.4) | copy-start | bytes 884740
  2.1 7.7 %copy-start.1 = (bf16[2,256,256]{2,1,0:T(8,128)(2,1)S(1)}, bf16[2,256,256]{2,1,0:T(8,128)(2,1)}, u32[]{:S(2)}) copy-start(bf16[2,256,256]{2,1,0:T(8,128)(2,1)} %param.7) | copy-start | bytes 786436
  4.5 5.8 %copy-start.2 = (f32[2,16,256]{2,1,0:T(8,128)S(1)}, f32[2,16,256]{2,1,0:T(8,128)}, u32[]{:S(2)}) copy-start(f32[2,16,256]{2,1,0:T(8,128)} %param.6) | copy-start | bytes 98308
  5.2 14.8 %all-to-all-start = ((bf16[4,4,7,12,256]{4,1,3,2,0:T(4,128)(2,1)}), bf16[4,4,7,12,256]{4,1,3,2,0:T(4,128)(2,1)S(1)}, u32[]{:S(2)}, u32[]{:S(2)}) async-start(bf16[4,4,7,12,256]{4,1,3,2,0:T(4,128)(2,1)} %bitcast_dynamic-update-slice_fusion.2), calls=%async_computation | async-start | bytes 1376256 | tf_op jit(solution)/shard_map/all_to_all | solution.py:93
  20.1 9.3 %collective-permute-start = (bf16[4,4,7,2,256]{4,1,3,2,0:T(4,128)(2,1)S(1)}, bf16[4,4,7,2,256]{4,1,3,2,0:T(4,128)(2,1)S(1)}, u32[]{:S(2)}, u32[]{:S(2)}) collective-permute-start(bf16[4,4,7,2,256]{4,1,3,2,0:T(4,128)(2,1)S(1)} %get-tuple-element.14), channel_id=1, source_target_pairs={{0,1},{1,2},{2,3},{4,5},{5,6},{6,7},{8,9},{9,10},{10,11},{12,13},{... | collective-permute-start | bytes 344072 | tf_op jit(solution)/shard_map/ppermute | solution.py:97
  24.3 6.7 %collective-permute-start.1 = (bf16[4,4,7,2,256]{4,1,3,2,0:T(4,128)(2,1)S(1)}, bf16[4,4,7,2,256]{4,1,3,2,0:T(4,128)(2,1)S(1)}, u32[]{:S(2)}, u32[]{:S(2)}) collective-permute-start(bf16[4,4,7,2,256]{4,1,3,2,0:T(4,128)(2,1)S(1)} %get-tuple-element.13), channel_id=1, source_target_pairs={{1,0},{2,1},{3,2},{5,4},{6,5},{7,6},{9,8},{10,9},{11,10},{13,12},{... | collective-permute-start | bytes 344072 | tf_op jit(solution)/shard_map/ppermute | solution.py:98

commit v21 on v18

--- a/solution.py
+++ b/solution.py
@@ -11,7 +11,7 @@
 LANES = 16
 
 
-def block_kernel(x_ref, w_ref, k_ref, p_ref, m_ref, o_ref, *, count, pitch):
+def block_kernel(x_ref, w_ref, k_ref, p_ref, m_ref, o_ref, *, count, pitch, index):
     frames, _, chans = x_ref.shape
     total = frames * count
 
@@ -25,7 +25,7 @@
     for dy in range(3):
         piece = operand(dy)
         for dx in range(3):
-            part = jnp.dot(piece, w_ref[dy, dx], preferred_element_type=jnp.float32)
+            part = jnp.dot(piece, w_ref[index, dy, dx], preferred_element_type=jnp.float32)
             taps[dx] = part if taps[dx] is None else taps[dx] + part
     conv = taps[0] + pltpu.roll(taps[1], total - 1, 0) + pltpu.roll(taps[2], total - 2, 0)
     hidden = (conv * (0.5 + 0.5 * jnp.tanh(0.5 * conv))).astype(jnp.bfloat16)
@@ -54,7 +54,7 @@
             o_ref[r] = turned[r * pitch : r * pitch + cols]
 
 
-def block(x, weight, kernel, proj, mask, pitch, cols=None):
+def block(x, weights, index, kernel, proj, mask, pitch, cols=None):
     frames, length, chans = x.shape
     count = length - 2 * pitch
     shape = (frames, count, chans) if cols is None else (count // pitch, cols, frames, chans)
@@ -62,7 +62,7 @@
     flops = 2 * frames * count * chans * chans * 10
     vmem = pltpu.VMEM
     return pl.pallas_call(
-        functools.partial(block_kernel, count=count, pitch=pitch),
+        functools.partial(block_kernel, count=count, pitch=pitch, index=index),
         out_shape=jax.ShapeDtypeStruct(shape, dtype),
         in_specs=[pl.BlockSpec(memory_space=vmem)] * 5,
         out_specs=pl.BlockSpec(memory_space=vmem),
@@ -72,7 +72,7 @@
             transcendentals=frames * count * chans,
             bytes_accessed=x.dtype.itemsize * frames * (length + count) * chans + 2 * 10 * chans * chans,
         ),
-    )(x, weight, kernel, proj, mask)
+    )(x, weights, kernel, proj, mask)
 
 
 def shards(video, conv_w, depth_k, proj_w):
@@ -104,7 +104,7 @@
     band_in = band_in.reshape(bands * frames, -1, chans)
     cut = (jnp.arange(pitch) < cols + 2 * (halo - 1)).astype(jnp.float32)
     first_mask = image_mask(halo - 1, pitch, -(halo - 1)) * jnp.tile(cut, rows + 2 * (halo - 1))[:, None]
-    state = block(band_in, conv_w[0], depth_k[0], proj_w[0], first_mask, pitch)
+    state = block(band_in, conv_w, 0, depth_k[0], proj_w[0], first_mask, pitch)
 
     reach = 2 * halo
     late, before = lax.optimization_barrier((received, before))
@@ -122,7 +122,7 @@
         [rim_left.reshape(n_rows, halo, chans), jnp.zeros((n_rows, halo, chans), jnp.float32),
          rim_right.reshape(n_rows, halo, chans), jnp.zeros((n_rows, halo, chans), jnp.float32)], axis=1
     ).reshape(-1, chans)
-    rims = block(rim, conv_w[0], depth_k[0], proj_w[0], rim_mask, 2 * reach)
+    rims = block(rim, conv_w, 0, depth_k[0], proj_w[0], rim_mask, 2 * reach)
     rims = rims.astype(state.dtype).reshape(bands * frames, n_rows, 2 * reach, chans)
     state = state.reshape(bands * frames, n_rows, pitch, chans)
     state = lax.dynamic_update_slice(state, rims[:, :, :halo], (0, 0, 0, 0))
@@ -133,7 +133,7 @@
         left = halo - 1 - b
         mask = image_mask(left, pitch, -left)
         last = b == BLOCKS - 1
-        state = block(state, conv_w[b], depth_k[b], proj_w[b], mask, pitch, cols if last else None)
+        state = block(state, conv_w, b, depth_k[b], proj_w[b], mask, pitch, cols if last else None)
 
     state = state.reshape(rows, cols, bands, frames, chans)
     state = jnp.transpose(state, (2, 0, 1, 3, 4))

time: 43 us -> 42.8 us (level)
  waiting for transfers between devices: 8.46 us -> 9.09 us
  local copies, waits for them, and re-layouts: 6.29 us -> 5.67 us
    squeeze x1 -> x0, local copies, waits for them, and re-layouts: 1.78 us -> none  [shards(): conv_w[b]]
    squeeze x1, local copies, waits for them, and re-layouts: 0.02 us -> 1.17 us  [shards(): proj_w[b]]
    all_to_all x1, waiting for transfers between devices: 7.88 us -> 8.51 us  [shards(): received = lax.all_to_all(pieces, 'tm', 0, 0, tiled=False)]
  transfers between devices with their start and end apart: 3 -> 3, of which waited for: 2 -> 2; matrix products, arithmetic and copies ran while one was open for 10% -> 8% of each run, Pallas kernels for 7% -> 7%
where the time goes in v21:
time: 42.8 us; the launch traced here: 42.5 us
  starting transfers between devices  9.71 us (23%)
  waiting for transfers between devices  9.09 us (21%)
  blocking collectives  8.72 us (20%)
  Pallas kernels  6.78 us (16%)
  local copies, waits for them, and re-layouts  5.67 us (13%)
  other arithmetic  2.25 us (5%)
    all_to_all x1, blocking collectives, shards(): state = lax.all_to_all(state, 'tm', 0, 1, tiled=True)  8.72 us
    all_to_all x1, waiting for transfers between devices, shards(): received = lax.all_to_all(pieces, 'tm', 0, 0, tiled=False)  8.51 us
    pallas_call x3, Pallas kernels, block(): pl.pallas_call(functools.partial(block_kernel, count=count, pitch=pitch,...  6.78 us
    all_to_all x1, starting transfers between devices, shards(): received = lax.all_to_all(pieces, 'tm', 0, 0, tiled=False)  4.24 us
    ppermute x1, starting transfers between devices, shards(): before = lax.ppermute(received[:, :, :, cols - halo:], 'width', up)  4.18 us
    another operation x1, other arithmetic, shards(): jnp.stack([padded[:, r * rows:r * rows + rows + 2 * halo] for r in range(...  1.48 us
    another operation x1, local copies, waits for them, and re-layouts, shards(): jnp.stack([padded[:, r * rows:r * rows + rows + 2 * halo] for r in range(...  1.37 us
    ppermute x1, starting transfers between devices, shards(): after = lax.ppermute(received[:, :, :, :halo], 'width', down)  1.29 us
  transfers between devices with their start and end apart: 3, of which 2 were waited for; matrix products, arithmetic and copies ran while one was open for 8% of the time, Pallas kernels for 7%

profile of v21, /device:TPU:0, one launch (start us, length us, event | category | flops | bytes accessed | tf_op | source)
XLA Modules:
  0.0 42.5 jit_solution(12999768360895063945)
XLA Ops:
  0.0 1.4 %fusion.4 = (bf16[1,4,7,12,256]{4,1,3,2,0:T(4,128)(2,1)S(1)}, bf16[1,4,7,12,256]{4,1,3,2,0:T(4,128)(2,1)S(1)}, bf16[1,4,7,12,256]{4,1,3,2,0:T(4,128)(2,1)S(1)}, bf16[1,4,7,12,256]{4,1,3,2,0:T(4,128)(2,1)S(1)}) fusion(bf16[4,12,12,256]{3,0,2,1:T(4,128)(2,1)} %param.4), kind=kLoop, calls=%fused_computation.12 | loop fusion | bytes 1327104 | tf_op jit(solution)/shard_map/stack | solution.py:89
  1.4 1.5 %pad_maximum_fusion = bf16[4,4,7,12,256]{4,1,3,2,0:T(4,128)(2,1)} fusion(bf16[1,4,7,12,256]{4,1,3,2,0:T(4,128)(2,1)S(1)} %get-tuple-element.14, bf16[1,4,7,12,256]{4,1,3,2,0:T(4,128)(2,1)S(1)} %get-tuple-element.15, bf16[1,4,7,12,256]{4,1,3,2,0:T(4,128)(2,1)S(1)} %get-tuple-element.16, bf16[1,4,7,12,256]{4,1,3,2,0:T(4,128)(2,1)S(1)} %get-tuple-element.13), kind=kLoop, calls=%fused_computation.5 | loop fusion | flops 1032192 | bytes 1376256 | tf_op jit(solution)/shard_map/stack | solution.py:89
  2.9 4.2 %all-to-all-start = ((bf16[4,4,7,12,256]{4,1,3,2,0:T(4,128)(2,1)}), bf16[4,4,7,12,256]{4,1,3,2,0:T(4,128)(2,1)S(1)}, u32[]{:S(2)}, u32[]{:S(2)}) async-start(bf16[4,4,7,12,256]{4,1,3,2,0:T(4,128)(2,1)} %pad_maximum_fusion), calls=%async_computation | async-start | bytes 1376256 | tf_op jit(solution)/shard_map/all_to_all | solution.py:90
  7.2 0.1 and_convert_fusion.2
  7.3 0.1 copy.22
  7.4 0.1 copy.23
  7.5 0.1 mul.25
  7.7 0.1 reshape.197
  8.0 1.2 %slice_bitcast_fusion.2 = (bf16[256,256]{1,0:T(8,128)(2,1)S(1)}, bf16[256,256]{1,0:T(8,128)(2,1)S(1)}) fusion(bf16[2,256,256]{2,1,0:T(8,128)(2,1)} %param.7), kind=kLoop, calls=%fused_computation.16 | loop fusion | bytes 524288 | tf_op jit(solution)/shard_map/squeeze | solution.py:136
  9.1 8.5 %all-to-all-done = bf16[4,4,7,12,256]{4,1,3,2,0:T(4,128)(2,1)S(1)} async-done(((bf16[4,4,7,12,256]{4,1,3,2,0:T(4,128)(2,1)}), bf16[4,4,7,12,256]{4,1,3,2,0:T(4,128)(2,1)S(1)}, u32[]{:S(2)}, u32[]{:S(2)}) %all-to-all-start) | async-done | bytes 688160 | tf_op jit(solution)/shard_map/all_to_all | solution.py:90
  17.7 0.1 fusion.15
  17.7 4.2 %collective-permute-start = (bf16[4,4,7,2,256]{4,1,3,2,0:T(4,128)(2,1)S(1)}, bf16[4,4,7,2,256]{4,1,3,2,0:T(4,128)(2,1)S(1)}, u32[]{:S(2)}, u32[]{:S(2)}) collective-permute-start(bf16[4,4,7,2,256]{4,1,3,2,0:T(4,128)(2,1)S(1)} %get-tuple-element.12), channel_id=1, source_target_pairs={{0,1},{1,2},{2,3},{4,5},{5,6},{6,7},{8,9},{9,10},{10,11},{12,13},{... | collective-permute-start | bytes 344072 | tf_op jit(solution)/shard_map/ppermute | solution.py:94
  21.9 1.3 %collective-permute-start.1 = (bf16[4,4,7,2,256]{4,1,3,2,0:T(4,128)(2,1)S(1)}, bf16[4,4,7,2,256]{4,1,3,2,0:T(4,128)(2,1)S(1)}, u32[]{:S(2)}, u32[]{:S(2)}) collective-permute-start(bf16[4,4,7,2,256]{4,1,3,2,0:T(4,128)(2,1)S(1)} %get-tuple-element.11), channel_id=1, source_target_pairs={{1,0},{2,1},{3,2},{5,4},{6,5},{7,6},{9,8},{10,9},{11,10},{13,12},{... | collective-permute-start | bytes 344072 | tf_op jit(solution)/shard_map/ppermute | solution.py:95
  23.2 0.1 copy.25
  23.4 0.4 %pad.14.clone = bf16[4,4,7,16,256]{4,3,2,1,0:T(8,128)(2,1)S(1)} pad(bf16[4,4,7,12,256]{4,3,2,1,0:T(8,128)(2,1)S(1)} %copy.25, bf16[]{:T(256)} %constant.12.clone.1), padding=0_0x0_0x0_0x2_2x0_0 | pad | bytes 1605634 | tf_op jit(solution)/shard_map/jit(_pad)/pad | solution.py:103
  23.9 3.1 %shard_map.46 = bf16[16,80,256]{2,1,0:T(8,128)(2,1)S(1)} custom-call(bf16[16,112,256]{2,1,0:T(8,128)(2,1)S(1)} %bitcast.38, bf16[2,3,3,256,256]{4,3,2,1,0:T(8,128)(2,1)S(1)} %copy-done, f32[16,256]{1,0:T(8,128)S(1)} %get-tuple-element.20.k_ref, bf16[256,256]{1,0:T(8,128)(2,1)S(1)} %get-tuple-element.18.p_ref, f32[80,256]{1,0:T(8,128)S(1)} %mul.26.m_ref), custom_call_target="tpu_custom_call" | custom-call | flops 1677721600 | bytes 2883584 | tf_op jit(solution)/shard_map/pallas_call | solution.py:64
  27.0 0.1 copy.18
  27.2 0.2 fusion.14
  27.4 0.3 fusion.3
  27.7 0.1 bitcast_convert_fusion
  27.8 0.1 copy.20
  27.9 0.1 constant_dynamic-update-slice_fusion.1
  28.0 0.6 %collective-permute-done.1 = bf16[4,4,7,2,256]{4,1,3,2,0:T(4,128)(2,1)S(1)} collective-permute-done((bf16[4,4,7,2,256]{4,1,3,2,0:T(4,128)(2,1)S(1)}, bf16[4,4,7,2,256]{4,1,3,2,0:T(4,128)(2,1)S(1)}, u32[]{:S(2)}, u32[]{:S(2)}) %collective-permute-start.1) | collective-permute-done | bytes 114720 | tf_op jit(solution)/shard_map/ppermute | solution.py:95
  28.6 0.1 copy.21
  28.7 0.1 constant_dynamic-update-slice_fusion
  28.8 1.7 %shard_map.47 = f32[16,40,256]{2,1,0:T(8,128)S(1)} custom-call(f32[16,56,256]{2,1,0:T(8,128)S(1)} %bitcast.37, bf16[2,3,3,256,256]{4,3,2,1,0:T(8,128)(2,1)S(1)} %copy-done, f32[16,256]{1,0:T(8,128)S(1)} %get-tuple-element.20.k_ref, bf16[256,256]{1,0:T(8,128)(2,1)S(1)} %get-tuple-element.18.p_ref, f32[40,256]{1,0:T(8,128)S(1)} %maximum_bitcast_fusion.m_ref), custom_call_target="tpu_custom_call" | custom-call | flops 838860800 | bytes 2883584 | tf_op jit(solution)/shard_map/pallas_call | solution.py:64
  30.5 0.1 slice_dynamic-update-slice_fusion.1
  30.6 0.1 slice_dynamic-update-slice_fusion
  30.8 2.0 %shard_map.48 = bf16[3,12,16,256]{3,2,1,0:T(8,128)(2,1)S(1)} custom-call(bf16[16,80,256]{2,1,0:T(8,128)(2,1)S(1)} %bitcast.40, bf16[2,3,3,256,256]{4,3,2,1,0:T(8,128)(2,1)S(1)} %copy-done, f32[16,256]{1,0:T(8,128)S(1)} %get-tuple-element.19.k_ref, bf16[256,256]{1,0:T(8,128)(2,1)S(1)} %get-tuple-element.17.p_ref, f32[48,256]{1,0:T(8,128)S(1)} %broadcast_in_dim.8.m_ref), custom_call_target="tpu_custom_call" | custom-call | flops 1006632960 | bytes 2359296 | tf_op jit(solution)/shard_map/pallas_call | solution.py:64
  32.9 0.1 copy.27
  33.0 8.7 %all_to_all.14 = bf16[4,3,12,4,256]{4,3,2,1,0:T(4,128)(2,1)S(1)} all-to-all(bf16[4,3,12,4,256]{4,3,2,1,0:T(4,128)(2,1)S(1)} %bitcast.41), channel_id=1, replica_groups=mesh['groups'=2,'tm'=4,'width'=4] {'tm'}, dimensions={0} | all-to-all | bytes 589824 | tf_op jit(solution)/shard_map/all_to_all | solution.py:140
  41.8 0.7 %copy.33 = bf16[4,12,12,256]{3,0,2,1:T(4,128)(2,1)} copy(bf16[4,12,12,256]{3,0,2,1:T(4,128)(2,1)S(1)} %bitcast.42) | data formatting | bytes 589824
  (23 shorter events, 0.6 us)
Async XLA Ops:
  0.0 7.9 %copy-start.1 = (f32[2,16,256]{2,1,0:T(8,128)S(1)}, f32[2,16,256]{2,1,0:T(8,128)}, u32[]{:S(2)}) copy-start(f32[2,16,256]{2,1,0:T(8,128)} %param.6) | copy-start | bytes 98308
  2.9 14.8 %all-to-all-start = ((bf16[4,4,7,12,256]{4,1,3,2,0:T(4,128)(2,1)}), bf16[4,4,7,12,256]{4,1,3,2,0:T(4,128)(2,1)S(1)}, u32[]{:S(2)}, u32[]{:S(2)}) async-start(bf16[4,4,7,12,256]{4,1,3,2,0:T(4,128)(2,1)} %pad_maximum_fusion), calls=%async_computation | async-start | bytes 1376256 | tf_op jit(solution)/shard_map/all_to_all | solution.py:90
  7.4 16.4 %copy-start = (bf16[2,3,3,256,256]{4,3,2,1,0:T(8,128)(2,1)S(1)}, bf16[2,3,3,256,256]{4,3,2,1,0:T(8,128)(2,1)}, u32[]{:S(2)}) copy-start(bf16[2,3,3,256,256]{4,3,2,1,0:T(8,128)(2,1)} %w_ref.5) | copy-start | bytes 7077892
  17.7 9.3 %collective-permute-start = (bf16[4,4,7,2,256]{4,1,3,2,0:T(4,128)(2,1)S(1)}, bf16[4,4,7,2,256]{4,1,3,2,0:T(4,128)(2,1)S(1)}, u32[]{:S(2)}, u32[]{:S(2)}) collective-permute-start(bf16[4,4,7,2,256]{4,1,3,2,0:T(4,128)(2,1)S(1)} %get-tuple-element.12), channel_id=1, source_target_pairs={{0,1},{1,2},{2,3},{4,5},{5,6},{6,7},{8,9},{9,10},{10,11},{12,13},{... | collective-permute-start | bytes 344072 | tf_op jit(solution)/shard_map/ppermute | solution.py:94
  21.9 6.7 %collective-permute-start.1 = (bf16[4,4,7,2,256]{4,1,3,2,0:T(4,128)(2,1)S(1)}, bf16[4,4,7,2,256]{4,1,3,2,0:T(4,128)(2,1)S(1)}, u32[]{:S(2)}, u32[]{:S(2)}) collective-permute-start(bf16[4,4,7,2,256]{4,1,3,2,0:T(4,128)(2,1)S(1)} %get-tuple-element.11), channel_id=1, source_target_pairs={{1,0},{2,1},{3,2},{5,4},{6,5},{7,6},{9,8},{10,9},{11,10},{13,12},{... | collective-permute-start | bytes 344072 | tf_op jit(solution)/shard_map/ppermute | solution.py:95

commit v22 on v21

--- a/solution.py
+++ b/solution.py
@@ -11,7 +11,8 @@
 LANES = 16
 
 
-def block_kernel(x_ref, w_ref, k_ref, p_ref, m_ref, o_ref, *, count, pitch, index):
+def block_kernel(x_ref, w_ref, k_ref, p_ref, *refs, count, pitch, index):
+    m_ref, o_ref = refs if len(refs) == 2 else (None,) + refs
     frames, _, chans = x_ref.shape
     total = frames * count
 
@@ -44,7 +45,8 @@
     center = pltpu.roll(window(1).astype(jnp.float32), total - 1, 0)
     state = (center + mixed.astype(jnp.float32)).astype(jnp.bfloat16).astype(o_ref.dtype)
     state = state.reshape(frames, count, chans)
-    state = jnp.where(m_ref[...][None] > 0, state, jnp.zeros((), state.dtype))
+    if m_ref is not None:
+        state = jnp.where(m_ref[...][None] > 0, state, jnp.zeros((), state.dtype))
     if o_ref.shape[0] == frames:
         o_ref[...] = state
     else:
@@ -64,7 +66,7 @@
     return pl.pallas_call(
         functools.partial(block_kernel, count=count, pitch=pitch, index=index),
         out_shape=jax.ShapeDtypeStruct(shape, dtype),
-        in_specs=[pl.BlockSpec(memory_space=vmem)] * 5,
+        in_specs=[pl.BlockSpec(memory_space=vmem)] * (4 + (mask is not None)),
         out_specs=pl.BlockSpec(memory_space=vmem),
         compiler_params=pltpu.CompilerParams(vmem_limit_bytes=48 * 1024 * 1024),
         cost_estimate=pl.CostEstimate(
@@ -72,7 +74,7 @@
             transcendentals=frames * count * chans,
             bytes_accessed=x.dtype.itemsize * frames * (length + count) * chans + 2 * 10 * chans * chans,
         ),
-    )(x, weights, kernel, proj, mask)
+    )(x, weights, kernel, proj, *([] if mask is None else [mask]))
 
 
 def shards(video, conv_w, depth_k, proj_w):
@@ -131,8 +133,8 @@
 
     for b in range(1, BLOCKS):
         left = halo - 1 - b
-        mask = image_mask(left, pitch, -left)
         last = b == BLOCKS - 1
+        mask = None if last else image_mask(left, pitch, -left)
         state = block(state, conv_w, b, depth_k[b], proj_w[b], mask, pitch, cols if last else None)
 
     state = state.reshape(rows, cols, bands, frames, chans)

time: 42.8 us -> 42.7 us (level)
  no operation moved by 1% of the time
where the time goes in v22:
time: 42.7 us; the launch traced here: 42.4 us
  starting transfers between devices  9.71 us (23%)
  waiting for transfers between devices  9.3 us (22%)
  blocking collectives  8.72 us (20%)
  Pallas kernels  6.77 us (16%)
  local copies, waits for them, and re-layouts  5.49 us (13%)
  other arithmetic  2.16 us (5%)
    all_to_all x1, waiting for transfers between devices, shards(): received = lax.all_to_all(pieces, 'tm', 0, 0, tiled=False)  8.73 us
    all_to_all x1, blocking collectives, shards(): state = lax.all_to_all(state, 'tm', 0, 1, tiled=True)  8.72 us
    pallas_call x3, Pallas kernels, block(): pl.pallas_call(functools.partial(block_kernel, count=count, pitch=pitch,...  6.77 us
    all_to_all x1, starting transfers between devices, shards(): received = lax.all_to_all(pieces, 'tm', 0, 0, tiled=False)  4.24 us
    ppermute x1, starting transfers between devices, shards(): before = lax.ppermute(received[:, :, :, cols - halo:], 'width', up)  4.18 us
    another operation x1, other arithmetic, shards(): jnp.stack([padded[:, r * rows:r * rows + rows + 2 * halo] for r in range(...  1.48 us
    another operation x1, local copies, waits for them, and re-layouts, shards(): jnp.stack([padded[:, r * rows:r * rows + rows + 2 * halo] for r in range(...  1.37 us
    ppermute x1, starting transfers between devices, shards(): after = lax.ppermute(received[:, :, :, :halo], 'width', down)  1.29 us
  transfers between devices with their start and end apart: 3, of which 2 were waited for; matrix products, arithmetic and copies ran while one was open for 8% of the time, Pallas kernels for 7%

profile of v22, /device:TPU:0, one launch (start us, length us, event | category | flops | bytes accessed | tf_op | source)
XLA Modules:
  0.0 42.4 jit_solution(12621409495085738331)
XLA Ops:
  0.0 1.4 %fusion.4 = (bf16[1,4,7,12,256]{4,1,3,2,0:T(4,128)(2,1)S(1)}, bf16[1,4,7,12,256]{4,1,3,2,0:T(4,128)(2,1)S(1)}, bf16[1,4,7,12,256]{4,1,3,2,0:T(4,128)(2,1)S(1)}, bf16[1,4,7,12,256]{4,1,3,2,0:T(4,128)(2,1)S(1)}) fusion(bf16[4,12,12,256]{3,0,2,1:T(4,128)(2,1)} %param.4), kind=kLoop, calls=%fused_computation.12 | loop fusion | bytes 1327104 | tf_op jit(solution)/shard_map/stack | solution.py:91
  1.4 1.5 %pad_maximum_fusion = bf16[4,4,7,12,256]{4,1,3,2,0:T(4,128)(2,1)} fusion(bf16[1,4,7,12,256]{4,1,3,2,0:T(4,128)(2,1)S(1)} %get-tuple-element.14, bf16[1,4,7,12,256]{4,1,3,2,0:T(4,128)(2,1)S(1)} %get-tuple-element.15, bf16[1,4,7,12,256]{4,1,3,2,0:T(4,128)(2,1)S(1)} %get-tuple-element.16, bf16[1,4,7,12,256]{4,1,3,2,0:T(4,128)(2,1)S(1)} %get-tuple-element.13), kind=kLoop, calls=%fused_computation.5 | loop fusion | flops 1032192 | bytes 1376256 | tf_op jit(solution)/shard_map/stack | solution.py:91
  2.9 4.2 %all-to-all-start = ((bf16[4,4,7,12,256]{4,1,3,2,0:T(4,128)(2,1)}), bf16[4,4,7,12,256]{4,1,3,2,0:T(4,128)(2,1)S(1)}, u32[]{:S(2)}, u32[]{:S(2)}) async-start(bf16[4,4,7,12,256]{4,1,3,2,0:T(4,128)(2,1)} %pad_maximum_fusion), calls=%async_computation | async-start | bytes 1376256 | tf_op jit(solution)/shard_map/all_to_all | solution.py:92
  7.2 0.1 and_convert_fusion.1
  7.2 0.1 copy.22
  7.3 0.1 copy.23
  7.5 0.1 mul.23
  7.8 1.1 %slice_bitcast_fusion.2 = (bf16[256,256]{1,0:T(8,128)(2,1)S(1)}, bf16[256,256]{1,0:T(8,128)(2,1)S(1)}) fusion(bf16[2,256,256]{2,1,0:T(8,128)(2,1)} %param.7), kind=kLoop, calls=%fused_computation.16 | loop fusion | bytes 524288 | tf_op jit(solution)/shard_map/squeeze | solution.py:138
  8.9 8.7 %all-to-all-done = bf16[4,4,7,12,256]{4,1,3,2,0:T(4,128)(2,1)S(1)} async-done(((bf16[4,4,7,12,256]{4,1,3,2,0:T(4,128)(2,1)}), bf16[4,4,7,12,256]{4,1,3,2,0:T(4,128)(2,1)S(1)}, u32[]{:S(2)}, u32[]{:S(2)}) %all-to-all-start) | async-done | bytes 688160 | tf_op jit(solution)/shard_map/all_to_all | solution.py:92
  17.7 0.1 fusion.13
  17.7 4.2 %collective-permute-start = (bf16[4,4,7,2,256]{4,1,3,2,0:T(4,128)(2,1)S(1)}, bf16[4,4,7,2,256]{4,1,3,2,0:T(4,128)(2,1)S(1)}, u32[]{:S(2)}, u32[]{:S(2)}) collective-permute-start(bf16[4,4,7,2,256]{4,1,3,2,0:T(4,128)(2,1)S(1)} %get-tuple-element.12), channel_id=1, source_target_pairs={{0,1},{1,2},{2,3},{4,5},{5,6},{6,7},{8,9},{9,10},{10,11},{12,13},{... | collective-permute-start | bytes 344072 | tf_op jit(solution)/shard_map/ppermute | solution.py:96
  21.9 1.3 %collective-permute-start.1 = (bf16[4,4,7,2,256]{4,1,3,2,0:T(4,128)(2,1)S(1)}, bf16[4,4,7,2,256]{4,1,3,2,0:T(4,128)(2,1)S(1)}, u32[]{:S(2)}, u32[]{:S(2)}) collective-permute-start(bf16[4,4,7,2,256]{4,1,3,2,0:T(4,128)(2,1)S(1)} %get-tuple-element.11), channel_id=1, source_target_pairs={{1,0},{2,1},{3,2},{5,4},{6,5},{7,6},{9,8},{10,9},{11,10},{13,12},{... | collective-permute-start | bytes 344072 | tf_op jit(solution)/shard_map/ppermute | solution.py:97
  23.2 0.1 copy.25
  23.4 0.4 %pad.14.clone = bf16[4,4,7,16,256]{4,3,2,1,0:T(8,128)(2,1)S(1)} pad(bf16[4,4,7,12,256]{4,3,2,1,0:T(8,128)(2,1)S(1)} %copy.25, bf16[]{:T(256)} %constant.12.clone.1), padding=0_0x0_0x0_0x2_2x0_0 | pad | bytes 1605634 | tf_op jit(solution)/shard_map/jit(_pad)/pad | solution.py:105
  23.9 3.1 %shard_map.46 = bf16[16,80,256]{2,1,0:T(8,128)(2,1)S(1)} custom-call(bf16[16,112,256]{2,1,0:T(8,128)(2,1)S(1)} %bitcast.38, bf16[2,3,3,256,256]{4,3,2,1,0:T(8,128)(2,1)S(1)} %copy-done, f32[16,256]{1,0:T(8,128)S(1)} %get-tuple-element.20.k_ref, bf16[256,256]{1,0:T(8,128)(2,1)S(1)} %get-tuple-element.18.p_ref, f32[80,256]{1,0:T(8,128)S(1)} %mul.24.refs_0_), custom_call_target="tpu_custom_call" | custom-call | flops 1677721600 | bytes 2883584 | tf_op jit(solution)/shard_map/pallas_call | solution.py:66
  27.1 0.1 copy.18
  27.2 0.2 fusion.12
  27.4 0.3 fusion.3
  27.7 0.1 bitcast_convert_fusion
  27.8 0.1 copy.20
  27.9 0.1 constant_dynamic-update-slice_fusion.1
  28.1 0.6 %collective-permute-done.1 = bf16[4,4,7,2,256]{4,1,3,2,0:T(4,128)(2,1)S(1)} collective-permute-done((bf16[4,4,7,2,256]{4,1,3,2,0:T(4,128)(2,1)S(1)}, bf16[4,4,7,2,256]{4,1,3,2,0:T(4,128)(2,1)S(1)}, u32[]{:S(2)}, u32[]{:S(2)}) %collective-permute-start.1) | collective-permute-done | bytes 114720 | tf_op jit(solution)/shard_map/ppermute | solution.py:97
  28.6 0.1 copy.21
  28.7 0.1 constant_dynamic-update-slice_fusion
  28.8 1.7 %shard_map.47 = f32[16,40,256]{2,1,0:T(8,128)S(1)} custom-call(f32[16,56,256]{2,1,0:T(8,128)S(1)} %bitcast.37, bf16[2,3,3,256,256]{4,3,2,1,0:T(8,128)(2,1)S(1)} %copy-done, f32[16,256]{1,0:T(8,128)S(1)} %get-tuple-element.20.k_ref, bf16[256,256]{1,0:T(8,128)(2,1)S(1)} %get-tuple-element.18.p_ref, f32[40,256]{1,0:T(8,128)S(1)} %maximum_bitcast_fusion.refs_0_), custom_call_target="tpu_custom_call" | custom-call | flops 838860800 | bytes 2883584 | tf_op jit(solution)/shard_map/pallas_call | solution.py:66
  30.5 0.1 slice_dynamic-update-slice_fusion.1
  30.6 0.1 slice_dynamic-update-slice_fusion
  30.8 2.0 %shard_map.48 = bf16[3,12,16,256]{3,2,1,0:T(8,128)(2,1)S(1)} custom-call(bf16[16,80,256]{2,1,0:T(8,128)(2,1)S(1)} %bitcast.40, bf16[2,3,3,256,256]{4,3,2,1,0:T(8,128)(2,1)S(1)} %copy-done, f32[16,256]{1,0:T(8,128)S(1)} %get-tuple-element.19.k_ref, bf16[256,256]{1,0:T(8,128)(2,1)S(1)} %get-tuple-element.17.p_ref), custom_call_target="tpu_custom_call" | custom-call | flops 1006632960 | bytes 2359296 | tf_op jit(solution)/shard_map/pallas_call | solution.py:66
  32.8 0.1 reshape.157
  32.8 0.1 copy.27
  33.0 8.7 %all_to_all.14 = bf16[4,3,12,4,256]{4,3,2,1,0:T(4,128)(2,1)S(1)} all-to-all(bf16[4,3,12,4,256]{4,3,2,1,0:T(4,128)(2,1)S(1)} %bitcast.41), channel_id=1, replica_groups=mesh['groups'=2,'tm'=4,'width'=4] {'tm'}, dimensions={0} | all-to-all | bytes 589824 | tf_op jit(solution)/shard_map/all_to_all | solution.py:142
  41.7 0.7 %copy.33 = bf16[4,12,12,256]{3,0,2,1:T(4,128)(2,1)} copy(bf16[4,12,12,256]{3,0,2,1:T(4,128)(2,1)S(1)} %bitcast.42) | data formatting | bytes 589824
  (18 shorter events, 0.4 us)
Async XLA Ops:
  0.0 7.8 %copy-start.1 = (f32[2,16,256]{2,1,0:T(8,128)S(1)}, f32[2,16,256]{2,1,0:T(8,128)}, u32[]{:S(2)}) copy-start(f32[2,16,256]{2,1,0:T(8,128)} %param.6) | copy-start | bytes 98308
  2.9 14.8 %all-to-all-start = ((bf16[4,4,7,12,256]{4,1,3,2,0:T(4,128)(2,1)}), bf16[4,4,7,12,256]{4,1,3,2,0:T(4,128)(2,1)S(1)}, u32[]{:S(2)}, u32[]{:S(2)}) async-start(bf16[4,4,7,12,256]{4,1,3,2,0:T(4,128)(2,1)} %pad_maximum_fusion), calls=%async_computation | async-start | bytes 1376256 | tf_op jit(solution)/shard_map/all_to_all | solution.py:92
  7.2 16.7 %copy-start = (bf16[2,3,3,256,256]{4,3,2,1,0:T(8,128)(2,1)S(1)}, bf16[2,3,3,256,256]{4,3,2,1,0:T(8,128)(2,1)}, u32[]{:S(2)}) copy-start(bf16[2,3,3,256,256]{4,3,2,1,0:T(8,128)(2,1)} %w_ref.5) | copy-start | bytes 7077892
  17.7 9.3 %collective-permute-start = (bf16[4,4,7,2,256]{4,1,3,2,0:T(4,128)(2,1)S(1)}, bf16[4,4,7,2,256]{4,1,3,2,0:T(4,128)(2,1)S(1)}, u32[]{:S(2)}, u32[]{:S(2)}) collective-permute-start(bf16[4,4,7,2,256]{4,1,3,2,0:T(4,128)(2,1)S(1)} %get-tuple-element.12), channel_id=1, source_target_pairs={{0,1},{1,2},{2,3},{4,5},{5,6},{6,7},{8,9},{9,10},{10,11},{12,13},{... | collective-permute-start | bytes 344072 | tf_op jit(solution)/shard_map/ppermute | solution.py:96
  21.9 6.7 %collective-permute-start.1 = (bf16[4,4,7,2,256]{4,1,3,2,0:T(4,128)(2,1)S(1)}, bf16[4,4,7,2,256]{4,1,3,2,0:T(4,128)(2,1)S(1)}, u32[]{:S(2)}, u32[]{:S(2)}) collective-permute-start(bf16[4,4,7,2,256]{4,1,3,2,0:T(4,128)(2,1)S(1)} %get-tuple-element.11), channel_id=1, source_target_pairs={{1,0},{2,1},{3,2},{5,4},{6,5},{7,6},{9,8},{10,9},{11,10},{13,12},{... | collective-permute-start | bytes 344072 | tf_op jit(solution)/shard_map/ppermute | solution.py:97

commit v23 on v22

--- a/solution.py
+++ b/solution.py
@@ -32,7 +32,7 @@
     hidden = (conv * (0.5 + 0.5 * jnp.tanh(0.5 * conv))).astype(jnp.bfloat16)
 
     values = hidden.astype(jnp.float32).reshape(frames, count, chans)
-    kernel = k_ref[...]
+    kernel = k_ref[index]
     depth = []
     for t in range(frames):
         acc = values[t] * kernel[0:1]
@@ -41,7 +41,7 @@
         depth.append(acc.astype(jnp.bfloat16) if count % 16 == 0 else acc)
     depth = jnp.stack(depth).reshape(total, chans).astype(jnp.bfloat16)
 
-    mixed = jnp.dot(depth, p_ref[...], preferred_element_type=jnp.float32).astype(jnp.bfloat16)
+    mixed = jnp.dot(depth, p_ref[index], preferred_element_type=jnp.float32).astype(jnp.bfloat16)
     center = pltpu.roll(window(1).astype(jnp.float32), total - 1, 0)
     state = (center + mixed.astype(jnp.float32)).astype(jnp.bfloat16).astype(o_ref.dtype)
     state = state.reshape(frames, count, chans)
@@ -106,7 +106,7 @@
     band_in = band_in.reshape(bands * frames, -1, chans)
     cut = (jnp.arange(pitch) < cols + 2 * (halo - 1)).astype(jnp.float32)
     first_mask = image_mask(halo - 1, pitch, -(halo - 1)) * jnp.tile(cut, rows + 2 * (halo - 1))[:, None]
-    state = block(band_in, conv_w, 0, depth_k[0], proj_w[0], first_mask, pitch)
+    state = block(band_in, conv_w, 0, depth_k, proj_w, first_mask, pitch)
 
     reach = 2 * halo
     late, before = lax.optimization_barrier((received, before))
@@ -124,7 +124,7 @@
         [rim_left.reshape(n_rows, halo, chans), jnp.zeros((n_rows, halo, chans), jnp.float32),
          rim_right.reshape(n_rows, halo, chans), jnp.zeros((n_rows, halo, chans), jnp.float32)], axis=1
     ).reshape(-1, chans)
-    rims = block(rim, conv_w, 0, depth_k[0], proj_w[0], rim_mask, 2 * reach)
+    rims = block(rim, conv_w, 0, depth_k, proj_w, rim_mask, 2 * reach)
     rims = rims.astype(state.dtype).reshape(bands * frames, n_rows, 2 * reach, chans)
     state = state.reshape(bands * frames, n_rows, pitch, chans)
     state = lax.dynamic_update_slice(state, rims[:, :, :halo], (0, 0, 0, 0))
@@ -135,7 +135,7 @@
         left = halo - 1 - b
         last = b == BLOCKS - 1
         mask = None if last else image_mask(left, pitch, -left)
-        state = block(state, conv_w, b, depth_k[b], proj_w[b], mask, pitch, cols if last else None)
+        state = block(state, conv_w, b, depth_k, proj_w, mask, pitch, cols if last else None)
 
     state = state.reshape(rows, cols, bands, frames, chans)
     state = jnp.transpose(state, (2, 0, 1, 3, 4))

time: 42.7 us -> 46.1 us (1.080)
  local copies, waits for them, and re-layouts: 5.49 us -> 7.5 us
  waiting for transfers between devices: 9.3 us -> 10.6 us
    all_to_all x1, waiting for transfers between devices: 8.73 us -> 10.6 us  [shards(): received = lax.all_to_all(pieces, 'tm', 0, 0, tiled=False)]
    squeeze x2 -> x0, local copies, waits for them, and re-layouts: 1.15 us -> none  [the longest x1 1.15 us: shards(): proj_w[b]]
    unnamed x6 -> x8, local copies, waits for them, and re-layouts: 0.86 us -> 1.97 us
    optimization_barrier x1, local copies, waits for them, and re-layouts: 0.14 us -> 1.24 us  [shards(): late, before = lax.optimization_barrier((received, before))]
    slice x1, local copies, waits for them, and re-layouts: 0.08 us -> 1.04 us  [shards(): after = lax.ppermute(received[:, :, :, :halo], 'width', down)]
    ppermute x1, waiting for transfers between devices: 0.57 us -> 0.01 us  [shards(): after = lax.ppermute(received[:, :, :, :halo], 'width', down)]
  transfers between devices with their start and end apart: 3 -> 3, of which waited for: 2 -> 1; matrix products, arithmetic and copies ran while one was open for 8% -> 10% of each run, Pallas kernels for 7% -> 7%
where the time goes in v23:
time: 46.1 us; the launch traced here: 45.7 us
  waiting for transfers between devices  10.6 us (23%)
  starting transfers between devices  9.83 us (21%)
  blocking collectives  8.72 us (19%)
  local copies, waits for them, and re-layouts  7.5 us (16%)
  Pallas kernels  6.69 us (15%)
  other arithmetic  2.18 us (5%)
    all_to_all x1, waiting for transfers between devices, shards(): received = lax.all_to_all(pieces, 'tm', 0, 0, tiled=False)  10.6 us
    all_to_all x1, blocking collectives, shards(): state = lax.all_to_all(state, 'tm', 0, 1, tiled=True)  8.72 us
    pallas_call x3, Pallas kernels, block(): pl.pallas_call(functools.partial(block_kernel, count=count, pitch=pitch,...  6.69 us
    ppermute x1, starting transfers between devices, shards(): before = lax.ppermute(received[:, :, :, cols - halo:], 'width', up)  4.3 us
    all_to_all x1, starting transfers between devices, shards(): received = lax.all_to_all(pieces, 'tm', 0, 0, tiled=False)  4.24 us
    unnamed x8, local copies, waits for them, and re-layouts  1.97 us
    another operation x1, other arithmetic, shards(): jnp.stack([padded[:, r * rows:r * rows + rows + 2 * halo] for r in range(...  1.49 us
    another operation x1, local copies, waits for them, and re-layouts, shards(): jnp.stack([padded[:, r * rows:r * rows + rows + 2 * halo] for r in range(...  1.36 us
  transfers between devices with their start and end apart: 3, of which 1 were waited for; matrix products, arithmetic and copies ran while one was open for 10% of the time, Pallas kernels for 7%

profile of v23, /device:TPU:0, one launch (start us, length us, event | category | flops | bytes accessed | tf_op | source)
XLA Modules:
  0.0 45.7 jit_solution(9866293937347667550)
XLA Ops:
  0.0 1.4 %fusion.4 = (bf16[1,4,7,12,256]{4,1,3,2,0:T(4,128)(2,1)S(1)}, bf16[1,4,7,12,256]{4,1,3,2,0:T(4,128)(2,1)S(1)}, bf16[1,4,7,12,256]{4,1,3,2,0:T(4,128)(2,1)S(1)}, bf16[1,4,7,12,256]{4,1,3,2,0:T(4,128)(2,1)S(1)}) fusion(bf16[4,12,12,256]{3,0,2,1:T(4,128)(2,1)} %param.4), kind=kLoop, calls=%fused_computation.12 | loop fusion | bytes 1327104 | tf_op jit(solution)/shard_map/stack | solution.py:91
  1.4 1.5 %pad_maximum_fusion = bf16[4,4,7,12,256]{4,1,3,2,0:T(4,128)(2,1)} fusion(bf16[1,4,7,12,256]{4,1,3,2,0:T(4,128)(2,1)S(1)} %get-tuple-element.14, bf16[1,4,7,12,256]{4,1,3,2,0:T(4,128)(2,1)S(1)} %get-tuple-element.15, bf16[1,4,7,12,256]{4,1,3,2,0:T(4,128)(2,1)S(1)} %get-tuple-element.16, bf16[1,4,7,12,256]{4,1,3,2,0:T(4,128)(2,1)S(1)} %get-tuple-element.13), kind=kLoop, calls=%fused_computation.5 | loop fusion | flops 1032192 | bytes 1376256 | tf_op jit(solution)/shard_map/stack | solution.py:91
  2.9 4.2 %all-to-all-start = ((bf16[4,4,7,12,256]{4,1,3,2,0:T(4,128)(2,1)}), bf16[4,4,7,12,256]{4,1,3,2,0:T(4,128)(2,1)}, u32[]{:S(2)}, u32[]{:S(2)}) async-start(bf16[4,4,7,12,256]{4,1,3,2,0:T(4,128)(2,1)} %pad_maximum_fusion), calls=%async_computation | async-start | bytes 1376256 | tf_op jit(solution)/shard_map/all_to_all | solution.py:92
  7.2 0.1 and_select_fusion
  7.2 0.1 mul.23
  7.3 0.1 and_convert_fusion.1
  7.4 0.1 copy.23
  7.5 0.1 copy.22
  7.8 10.6 %all-to-all-done = bf16[4,4,7,12,256]{4,1,3,2,0:T(4,128)(2,1)} async-done(((bf16[4,4,7,12,256]{4,1,3,2,0:T(4,128)(2,1)}), bf16[4,4,7,12,256]{4,1,3,2,0:T(4,128)(2,1)}, u32[]{:S(2)}, u32[]{:S(2)}) %all-to-all-start) | async-done | bytes 688160 | tf_op jit(solution)/shard_map/all_to_all | solution.py:92
  18.3 1.0 %fusion.13 = (bf16[4,4,7,2,256]{4,1,3,2,0:T(4,128)(2,1)S(1)}, bf16[4,4,7,2,256]{4,1,3,2,0:T(4,128)(2,1)S(1)}) fusion(bf16[4,4,7,12,256]{4,1,3,2,0:T(4,128)(2,1)} %all-to-all-done), kind=kLoop, calls=%fused_computation.36 | loop fusion | bytes 458752 | tf_op jit(solution)/shard_map/slice | solution.py:97
  19.4 4.3 %collective-permute-start = (bf16[4,4,7,2,256]{4,1,3,2,0:T(4,128)(2,1)S(1)}, bf16[4,4,7,2,256]{4,1,3,2,0:T(4,128)(2,1)S(1)}, u32[]{:S(2)}, u32[]{:S(2)}) collective-permute-start(bf16[4,4,7,2,256]{4,1,3,2,0:T(4,128)(2,1)S(1)} %get-tuple-element.12), channel_id=1, source_target_pairs={{0,1},{1,2},{2,3},{4,5},{5,6},{6,7},{8,9},{9,10},{10,11},{12,13},{... | collective-permute-start | bytes 344072 | tf_op jit(solution)/shard_map/ppermute | solution.py:96
  23.7 1.3 %collective-permute-start.1 = (bf16[4,4,7,2,256]{4,1,3,2,0:T(4,128)(2,1)S(1)}, bf16[4,4,7,2,256]{4,1,3,2,0:T(4,128)(2,1)S(1)}, u32[]{:S(2)}, u32[]{:S(2)}) collective-permute-start(bf16[4,4,7,2,256]{4,1,3,2,0:T(4,128)(2,1)S(1)} %get-tuple-element.11), channel_id=1, source_target_pairs={{1,0},{2,1},{3,2},{5,4},{6,5},{7,6},{9,8},{10,9},{11,10},{13,12},{... | collective-permute-start | bytes 344072 | tf_op jit(solution)/shard_map/ppermute | solution.py:97
  25.0 1.2 %copy.25 = bf16[4,4,7,12,256]{4,3,2,1,0:T(8,128)(2,1)S(1)} copy(bf16[4,4,7,12,256]{4,1,3,2,0:T(4,128)(2,1)} %all-to-all-done) | data formatting | bytes 1376256
  26.2 0.4 pad.14.clone
  26.7 0.1 mul.24.refs_0_
  26.8 3.1 %shard_map.46 = bf16[16,80,256]{2,1,0:T(8,128)(2,1)S(1)} custom-call(bf16[16,112,256]{2,1,0:T(8,128)(2,1)S(1)} %bitcast.30, bf16[2,3,3,256,256]{4,3,2,1,0:T(8,128)(2,1)S(1)} %copy-done, f32[2,16,256]{2,1,0:T(8,128)S(1)} %copy-done.2, bf16[2,256,256]{2,1,0:T(8,128)(2,1)S(1)} %copy-done.1, f32[80,256]{1,0:T(8,128)S(1)} %mul.24.refs_0_), custom_call_target="tpu_custom_call" | custom-call | flops 1677721600 | bytes 2883584 | tf_op jit(solution)/shard_map/pallas_call | solution.py:66
  29.8 1.2 %copy.18 = bf16[4,4,7,12,256]{4,3,2,1,0:T(8,128)(2,1)S(1)} copy(bf16[4,4,7,12,256]{4,1,3,2,0:T(4,128)(2,1)} %all-to-all-done) | data formatting | bytes 1376256 | tf_op jit(solution)/shard_map/optimization_barrier | solution.py:112
  31.1 0.2 fusion.12
  31.3 0.4 fusion.3
  31.6 0.1 bitcast_convert_fusion
  31.7 0.1 copy.20
  31.8 0.1 constant_dynamic-update-slice_fusion.1
  32.0 0.1 copy.21
  32.1 0.1 constant_dynamic-update-slice_fusion
  32.2 1.6 %shard_map.47 = f32[16,40,256]{2,1,0:T(8,128)S(1)} custom-call(f32[16,56,256]{2,1,0:T(8,128)S(1)} %bitcast.29, bf16[2,3,3,256,256]{4,3,2,1,0:T(8,128)(2,1)S(1)} %copy-done, f32[2,16,256]{2,1,0:T(8,128)S(1)} %copy-done.2, bf16[2,256,256]{2,1,0:T(8,128)(2,1)S(1)} %copy-done.1, f32[40,256]{1,0:T(8,128)S(1)} %maximum_bitcast_fusion.refs_0_), custom_call_target="tpu_custom_call" | custom-call | flops 838860800 | bytes 2883584 | tf_op jit(solution)/shard_map/pallas_call | solution.py:66
  33.9 0.1 slice_dynamic-update-slice_fusion.1
  34.0 0.1 slice_dynamic-update-slice_fusion
  34.1 2.0 %shard_map.48 = bf16[3,12,16,256]{3,2,1,0:T(8,128)(2,1)S(1)} custom-call(bf16[16,80,256]{2,1,0:T(8,128)(2,1)S(1)} %bitcast.32, bf16[2,3,3,256,256]{4,3,2,1,0:T(8,128)(2,1)S(1)} %copy-done, f32[2,16,256]{2,1,0:T(8,128)S(1)} %copy-done.2, bf16[2,256,256]{2,1,0:T(8,128)(2,1)S(1)} %copy-done.1), custom_call_target="tpu_custom_call" | custom-call | flops 1006632960 | bytes 2359296 | tf_op jit(solution)/shard_map/pallas_call | solution.py:66
  36.1 0.1 reshape.157
  36.2 0.1 copy.27
  36.3 8.7 %all_to_all.14 = bf16[4,3,12,4,256]{4,3,2,1,0:T(4,128)(2,1)S(1)} all-to-all(bf16[4,3,12,4,256]{4,3,2,1,0:T(4,128)(2,1)S(1)} %bitcast.33), channel_id=1, replica_groups=mesh['groups'=2,'tm'=4,'width'=4] {'tm'}, dimensions={0} | all-to-all | bytes 589824 | tf_op jit(solution)/shard_map/all_to_all | solution.py:142
  45.0 0.7 %copy.33 = bf16[4,12,12,256]{3,0,2,1:T(4,128)(2,1)} copy(bf16[4,12,12,256]{3,0,2,1:T(4,128)(2,1)S(1)} %bitcast.34) | data formatting | bytes 589824
  (18 shorter events, 0.3 us)
Async XLA Ops:
  2.9 15.5 %all-to-all-start = ((bf16[4,4,7,12,256]{4,1,3,2,0:T(4,128)(2,1)}), bf16[4,4,7,12,256]{4,1,3,2,0:T(4,128)(2,1)}, u32[]{:S(2)}, u32[]{:S(2)}) async-start(bf16[4,4,7,12,256]{4,1,3,2,0:T(4,128)(2,1)} %pad_maximum_fusion), calls=%async_computation | async-start | bytes 1376256 | tf_op jit(solution)/shard_map/all_to_all | solution.py:92
  7.1 19.6 %copy-start = (bf16[2,3,3,256,256]{4,3,2,1,0:T(8,128)(2,1)S(1)}, bf16[2,3,3,256,256]{4,3,2,1,0:T(8,128)(2,1)}, u32[]{:S(2)}) copy-start(bf16[2,3,3,256,256]{4,3,2,1,0:T(8,128)(2,1)} %w_ref.5) | copy-start | bytes 7077892
  7.1 19.7 %copy-start.1 = (bf16[2,256,256]{2,1,0:T(8,128)(2,1)S(1)}, bf16[2,256,256]{2,1,0:T(8,128)(2,1)}, u32[]{:S(2)}) copy-start(bf16[2,256,256]{2,1,0:T(8,128)(2,1)} %p_ref.5) | copy-start | bytes 786436
  7.1 19.7 %copy-start.2 = (f32[2,16,256]{2,1,0:T(8,128)S(1)}, f32[2,16,256]{2,1,0:T(8,128)}, u32[]{:S(2)}) copy-start(f32[2,16,256]{2,1,0:T(8,128)} %k_ref.5) | copy-start | bytes 98308
  19.4 10.5 %collective-permute-start = (bf16[4,4,7,2,256]{4,1,3,2,0:T(4,128)(2,1)S(1)}, bf16[4,4,7,2,256]{4,1,3,2,0:T(4,128)(2,1)S(1)}, u32[]{:S(2)}, u32[]{:S(2)}) collective-permute-start(bf16[4,4,7,2,256]{4,1,3,2,0:T(4,128)(2,1)S(1)} %get-tuple-element.12), channel_id=1, source_target_pairs={{0,1},{1,2},{2,3},{4,5},{5,6},{6,7},{8,9},{9,10},{10,11},{12,13},{... | collective-permute-start | bytes 344072 | tf_op jit(solution)/shard_map/ppermute | solution.py:96
  23.7 8.3 %collective-permute-start.1 = (bf16[4,4,7,2,256]{4,1,3,2,0:T(4,128)(2,1)S(1)}, bf16[4,4,7,2,256]{4,1,3,2,0:T(4,128)(2,1)S(1)}, u32[]{:S(2)}, u32[]{:S(2)}) collective-permute-start(bf16[4,4,7,2,256]{4,1,3,2,0:T(4,128)(2,1)S(1)} %get-tuple-element.11), channel_id=1, source_target_pairs={{1,0},{2,1},{3,2},{5,4},{6,5},{7,6},{9,8},{10,9},{11,10},{13,12},{... | collective-permute-start | bytes 344072 | tf_op jit(solution)/shard_map/ppermute | solution.py:97

commit v24 on v22

--- a/solution.py
+++ b/solution.py
@@ -87,8 +87,12 @@
     halo = BLOCKS
     pitch = -(-(cols + 2 * halo) // LANES) * LANES
 
-    padded = jnp.pad(video, ((0, 0), (halo, halo), (0, 0), (0, 0)))
-    pieces = jnp.stack([padded[:, r * rows : r * rows + rows + 2 * halo] for r in range(bands)])
+    def band_rows(r):
+        first, last = max(r * rows - halo, 0), min(r * rows + rows + halo, height)
+        pad = ((0, 0), (first - (r * rows - halo), r * rows + rows + halo - last), (0, 0), (0, 0))
+        return jnp.pad(video[:, first:last], pad)
+
+    pieces = jnp.stack([band_rows(r) for r in range(bands)])
     received = lax.all_to_all(pieces, "tm", 0, 0, tiled=False)
 
     up = [(i, i + 1) for i in range(sides - 1)]

time: 42.7 us -> 43.6 us (1.021)
  local copies, waits for them, and re-layouts: 5.49 us -> 6.43 us
    slice x0 -> x1, local copies, waits for them, and re-layouts: none -> 1.05 us  [band_rows(): return jnp.pad(video[:, first:last], pad)]
    another operation x2 -> x3, local copies, waits for them, and re-layouts: 1.37 us -> 1.26 us  [the longest x2 1.26 us: shards(): pieces = jnp.stack([band_rows(r) for r in range(bands)])]
where the time goes in v24:
time: 43.6 us; the launch traced here: 43.3 us
  starting transfers between devices  9.71 us (22%)
  waiting for transfers between devices  9.31 us (21%)
  blocking collectives  8.72 us (20%)
  Pallas kernels  6.77 us (16%)
  local copies, waits for them, and re-layouts  6.43 us (15%)
  other arithmetic  2.15 us (5%)
    all_to_all x1, waiting for transfers between devices, shards(): received = lax.all_to_all(pieces, 'tm', 0, 0, tiled=False)  8.73 us
    all_to_all x1, blocking collectives, shards(): state = lax.all_to_all(state, 'tm', 0, 1, tiled=True)  8.72 us
    pallas_call x3, Pallas kernels, block(): pl.pallas_call(functools.partial(block_kernel, count=count, pitch=pitch,...  6.77 us
    all_to_all x1, starting transfers between devices, shards(): received = lax.all_to_all(pieces, 'tm', 0, 0, tiled=False)  4.24 us
    ppermute x1, starting transfers between devices, shards(): before = lax.ppermute(received[:, :, :, cols - halo:], 'width', up)  4.18 us
    another operation x1, other arithmetic, shards(): pieces = jnp.stack([band_rows(r) for r in range(bands)])  1.47 us
    ppermute x1, starting transfers between devices, shards(): after = lax.ppermute(received[:, :, :, :halo], 'width', down)  1.29 us
    another operation x2, local copies, waits for them, and re-layouts, shards(): pieces = jnp.stack([band_rows(r) for r in range(bands)])  1.26 us
  transfers between devices with their start and end apart: 3, of which 2 were waited for; matrix products, arithmetic and copies ran while one was open for 8% of the time, Pallas kernels for 7%

profile of v24, /device:TPU:0, one launch (start us, length us, event | category | flops | bytes accessed | tf_op | source)
XLA Modules:
  0.0 43.3 jit_solution(15580621176157769032)
XLA Ops:
  0.0 1.1 %fusion.12 = (bf16[4,5,12,256]{3,0,2,1:T(4,128)(2,1)S(1)}, bf16[4,5,12,256]{3,0,2,1:T(4,128)(2,1)S(1)}) fusion(bf16[4,12,12,256]{3,0,2,1:T(4,128)(2,1)} %param.4), kind=kLoop, calls=%fused_computation.39 | loop fusion | bytes 491520 | tf_op jit(solution)/shard_map/slice | solution.py:93
  1.1 1.1 %slice_bitcast_fusion.1 = (bf16[1,4,7,12,256]{4,1,3,2,0:T(4,128)(2,1)S(1)}, bf16[1,4,7,12,256]{4,1,3,2,0:T(4,128)(2,1)S(1)}) fusion(bf16[4,12,12,256]{3,0,2,1:T(4,128)(2,1)} %param.4), kind=kLoop, calls=%fused_computation.12 | loop fusion | bytes 688128 | tf_op jit(solution)/shard_map/stack | solution.py:95
  2.2 0.1 pad_bitcast_fusion
  2.3 1.5 %pad_maximum_fusion = bf16[4,4,7,12,256]{4,1,3,2,0:T(4,128)(2,1)} fusion(bf16[1,4,7,12,256]{4,1,3,2,0:T(4,128)(2,1)S(1)} %get-tuple-element.23, bf16[1,4,7,12,256]{4,1,3,2,0:T(4,128)(2,1)S(1)} %get-tuple-element.16, bf16[1,4,7,12,256]{4,1,3,2,0:T(4,128)(2,1)S(1)} %get-tuple-element.15, bf16[1,4,7,12,256]{4,1,3,2,0:T(4,128)(2,1)S(1)} %get-tuple-element.24), kind=kLoop, calls=%fused_computation.5 | loop fusion | flops 1032192 | bytes 1376256 | tf_op jit(solution)/shard_map/stack | solution.py:95
  3.8 4.2 %all-to-all-start = ((bf16[4,4,7,12,256]{4,1,3,2,0:T(4,128)(2,1)}), bf16[4,4,7,12,256]{4,1,3,2,0:T(4,128)(2,1)S(1)}, u32[]{:S(2)}, u32[]{:S(2)}) async-start(bf16[4,4,7,12,256]{4,1,3,2,0:T(4,128)(2,1)} %pad_maximum_fusion), calls=%async_computation | async-start | bytes 1376256 | tf_op jit(solution)/shard_map/all_to_all | solution.py:96
  8.2 0.1 copy.23
  8.3 0.1 copy.24
  8.4 0.1 mul.23
  8.7 1.1 %slice_bitcast_fusion.2 = (bf16[256,256]{1,0:T(8,128)(2,1)S(1)}, bf16[256,256]{1,0:T(8,128)(2,1)S(1)}) fusion(bf16[2,256,256]{2,1,0:T(8,128)(2,1)} %param.7), kind=kLoop, calls=%fused_computation.14 | loop fusion | bytes 524288 | tf_op jit(solution)/shard_map/squeeze | solution.py:142
  9.9 8.7 %all-to-all-done = bf16[4,4,7,12,256]{4,1,3,2,0:T(4,128)(2,1)S(1)} async-done(((bf16[4,4,7,12,256]{4,1,3,2,0:T(4,128)(2,1)}), bf16[4,4,7,12,256]{4,1,3,2,0:T(4,128)(2,1)S(1)}, u32[]{:S(2)}, u32[]{:S(2)}) %all-to-all-start) | async-done | bytes 688160 | tf_op jit(solution)/shard_map/all_to_all | solution.py:96
  18.6 0.1 fusion.11
  18.7 4.2 %collective-permute-start = (bf16[4,4,7,2,256]{4,1,3,2,0:T(4,128)(2,1)S(1)}, bf16[4,4,7,2,256]{4,1,3,2,0:T(4,128)(2,1)S(1)}, u32[]{:S(2)}, u32[]{:S(2)}) collective-permute-start(bf16[4,4,7,2,256]{4,1,3,2,0:T(4,128)(2,1)S(1)} %get-tuple-element.12), channel_id=1, source_target_pairs={{0,1},{1,2},{2,3},{4,5},{5,6},{6,7},{8,9},{9,10},{10,11},{12,13},{... | collective-permute-start | bytes 344072 | tf_op jit(solution)/shard_map/ppermute | solution.py:100
  22.9 1.3 %collective-permute-start.1 = (bf16[4,4,7,2,256]{4,1,3,2,0:T(4,128)(2,1)S(1)}, bf16[4,4,7,2,256]{4,1,3,2,0:T(4,128)(2,1)S(1)}, u32[]{:S(2)}, u32[]{:S(2)}) collective-permute-start(bf16[4,4,7,2,256]{4,1,3,2,0:T(4,128)(2,1)S(1)} %get-tuple-element.11), channel_id=1, source_target_pairs={{1,0},{2,1},{3,2},{5,4},{6,5},{7,6},{9,8},{10,9},{11,10},{13,12},{... | collective-permute-start | bytes 344072 | tf_op jit(solution)/shard_map/ppermute | solution.py:101
  24.2 0.1 copy.26
  24.3 0.4 pad.19.clone
  24.8 3.1 %shard_map.46 = bf16[16,80,256]{2,1,0:T(8,128)(2,1)S(1)} custom-call(bf16[16,112,256]{2,1,0:T(8,128)(2,1)S(1)} %bitcast.38, bf16[2,3,3,256,256]{4,3,2,1,0:T(8,128)(2,1)S(1)} %copy-done, f32[16,256]{1,0:T(8,128)S(1)} %get-tuple-element.20.k_ref, bf16[256,256]{1,0:T(8,128)(2,1)S(1)} %get-tuple-element.18.p_ref, f32[80,256]{1,0:T(8,128)S(1)} %mul.24.refs_0_), custom_call_target="tpu_custom_call" | custom-call | flops 1677721600 | bytes 2883584 | tf_op jit(solution)/shard_map/pallas_call | solution.py:66
  28.0 0.1 copy.19
  28.1 0.2 fusion.10
  28.3 0.3 fusion.3
  28.7 0.1 bitcast_convert_fusion
  28.8 0.1 copy.21
  28.9 0.1 constant_dynamic-update-slice_fusion.1
  29.0 0.6 %collective-permute-done.1 = bf16[4,4,7,2,256]{4,1,3,2,0:T(4,128)(2,1)S(1)} collective-permute-done((bf16[4,4,7,2,256]{4,1,3,2,0:T(4,128)(2,1)S(1)}, bf16[4,4,7,2,256]{4,1,3,2,0:T(4,128)(2,1)S(1)}, u32[]{:S(2)}, u32[]{:S(2)}) %collective-permute-start.1) | collective-permute-done | bytes 114720 | tf_op jit(solution)/shard_map/ppermute | solution.py:101
  29.6 0.1 copy.22
  29.7 0.1 constant_dynamic-update-slice_fusion
  29.8 1.7 %shard_map.47 = f32[16,40,256]{2,1,0:T(8,128)S(1)} custom-call(f32[16,56,256]{2,1,0:T(8,128)S(1)} %bitcast.37, bf16[2,3,3,256,256]{4,3,2,1,0:T(8,128)(2,1)S(1)} %copy-done, f32[16,256]{1,0:T(8,128)S(1)} %get-tuple-element.20.k_ref, bf16[256,256]{1,0:T(8,128)(2,1)S(1)} %get-tuple-element.18.p_ref, f32[40,256]{1,0:T(8,128)S(1)} %maximum_bitcast_fusion.refs_0_), custom_call_target="tpu_custom_call" | custom-call | flops 838860800 | bytes 2883584 | tf_op jit(solution)/shard_map/pallas_call | solution.py:66
  31.5 0.1 slice_dynamic-update-slice_fusion.1
  31.6 0.1 slice_dynamic-update-slice_fusion
  31.7 2.0 %shard_map.48 = bf16[3,12,16,256]{3,2,1,0:T(8,128)(2,1)S(1)} custom-call(bf16[16,80,256]{2,1,0:T(8,128)(2,1)S(1)} %bitcast.40, bf16[2,3,3,256,256]{4,3,2,1,0:T(8,128)(2,1)S(1)} %copy-done, f32[16,256]{1,0:T(8,128)S(1)} %get-tuple-element.19.k_ref, bf16[256,256]{1,0:T(8,128)(2,1)S(1)} %get-tuple-element.17.p_ref), custom_call_target="tpu_custom_call" | custom-call | flops 1006632960 | bytes 2359296 | tf_op jit(solution)/shard_map/pallas_call | solution.py:66
  33.8 0.1 copy.28
  33.9 8.7 %all_to_all.14 = bf16[4,3,12,4,256]{4,3,2,1,0:T(4,128)(2,1)S(1)} all-to-all(bf16[4,3,12,4,256]{4,3,2,1,0:T(4,128)(2,1)S(1)} %bitcast.41), channel_id=1, replica_groups=mesh['groups'=2,'tm'=4,'width'=4] {'tm'}, dimensions={0} | all-to-all | bytes 589824 | tf_op jit(solution)/shard_map/all_to_all | solution.py:146
  42.6 0.7 %copy.34 = bf16[4,12,12,256]{3,0,2,1:T(4,128)(2,1)} copy(bf16[4,12,12,256]{3,0,2,1:T(4,128)(2,1)S(1)} %bitcast.42) | data formatting | bytes 589824
  (20 shorter events, 0.5 us)
Async XLA Ops:
  0.0 8.7 %copy-start.1 = (f32[2,16,256]{2,1,0:T(8,128)S(1)}, f32[2,16,256]{2,1,0:T(8,128)}, u32[]{:S(2)}) copy-start(f32[2,16,256]{2,1,0:T(8,128)} %param.6) | copy-start | bytes 98308
  3.8 14.8 %all-to-all-start = ((bf16[4,4,7,12,256]{4,1,3,2,0:T(4,128)(2,1)}), bf16[4,4,7,12,256]{4,1,3,2,0:T(4,128)(2,1)S(1)}, u32[]{:S(2)}, u32[]{:S(2)}) async-start(bf16[4,4,7,12,256]{4,1,3,2,0:T(4,128)(2,1)} %pad_maximum_fusion), calls=%async_computation | async-start | bytes 1376256 | tf_op jit(solution)/shard_map/all_to_all | solution.py:96
  8.2 16.7 %copy-start = (bf16[2,3,3,256,256]{4,3,2,1,0:T(8,128)(2,1)S(1)}, bf16[2,3,3,256,256]{4,3,2,1,0:T(8,128)(2,1)}, u32[]{:S(2)}) copy-start(bf16[2,3,3,256,256]{4,3,2,1,0:T(8,128)(2,1)} %w_ref.5) | copy-start | bytes 7077892
  18.7 9.3 %collective-permute-start = (bf16[4,4,7,2,256]{4,1,3,2,0:T(4,128)(2,1)S(1)}, bf16[4,4,7,2,256]{4,1,3,2,0:T(4,128)(2,1)S(1)}, u32[]{:S(2)}, u32[]{:S(2)}) collective-permute-start(bf16[4,4,7,2,256]{4,1,3,2,0:T(4,128)(2,1)S(1)} %get-tuple-element.12), channel_id=1, source_target_pairs={{0,1},{1,2},{2,3},{4,5},{5,6},{6,7},{8,9},{9,10},{10,11},{12,13},{... | collective-permute-start | bytes 344072 | tf_op jit(solution)/shard_map/ppermute | solution.py:100
  22.9 6.7 %collective-permute-start.1 = (bf16[4,4,7,2,256]{4,1,3,2,0:T(4,128)(2,1)S(1)}, bf16[4,4,7,2,256]{4,1,3,2,0:T(4,128)(2,1)S(1)}, u32[]{:S(2)}, u32[]{:S(2)}) collective-permute-start(bf16[4,4,7,2,256]{4,1,3,2,0:T(4,128)(2,1)S(1)} %get-tuple-element.11), channel_id=1, source_target_pairs={{1,0},{2,1},{3,2},{5,4},{6,5},{7,6},{9,8},{10,9},{11,10},{13,12},{... | collective-permute-start | bytes 344072 | tf_op jit(solution)/shard_map/ppermute | solution.py:101
